TPU v7x, 32 devices: a whole 2x2x4 slice. The times are simulated.
32 devices in a mesh: grp: 2 (over x), smp: 16 (over z, y, core).
Axes of the slice: x: 2, y: 2, z: 4, core: 2. Of those that a mesh axis runs over, the one named last changes fastest.
Arguments:
- state: bfloat16 [512, 16, 1024], P(('grp', 'smp')), parts along dimension 0, may hold values from -40 to 40
- unit_slot: int32 [512, 64], P(('grp', 'smp')), parts along dimension 0, may hold values from 0 to 511
- token_count: int32 [512], P(('grp', 'smp')), parts along dimension 0, may hold values from 48 to 64, as said below
- session: int32 [512], P(('grp', 'smp')), parts along dimension 0, may hold values from 0 to 15, as said below
- session_row: int32 [32], P('grp'), parts along dimension 0, may hold values from 0 to 15, as said below
- unit_count: int32 [16], replicated, may hold values from 128 to 512, as said below
- panels: bfloat16 [16, 512, 1024], P('smp'), may hold values from -40 to 40
- memory_key: bfloat16 [512, 1024], P(('grp', 'smp')), parts along dimension 0, may hold values from -240 to 240
- memory_value: bfloat16 [512, 1024], P(('grp', 'smp')), parts along dimension 0, may hold values from -24 to 24
- q1_weight: bfloat16 [1024, 1024], replicated, may hold values from -0.1875 to 0.1875
- o1_weight: bfloat16 [1024, 1024], replicated, may hold values from -0.1875 to 0.1875
- kv_weight: bfloat16 [1024, 2048], replicated, may hold values from -6 to 6
- q2_weight: bfloat16 [1024, 1024], replicated, may hold values from -0.1875 to 0.1875
- o2_weight: bfloat16 [1024, 1024], replicated, may hold values from -0.1875 to 0.1875
Outputs:
- latent_out: bfloat16 [512, 16, 1024], P(('grp', 'smp')), parts along dimension 0
There are 2 independent parts, one for each index of `grp`. A program takes and returns all parts, laid end to end along the dimension named above; an argument that names none is the same for every part. Nothing has to cross between parts.
Inputs may be any that keep to these rules, and one draw needn't show every extreme that they name: The panel row of session s is session_row[s]; it lies on the device of index session_row[s]. session_row is a permutation. The 16 samples of one device have sessions on 16 different devices; one device holds the session of one sample on every device. `token_count`: some sample on every device has 64 tokens. `unit_count`: some panel row has 512 units.
All inputs are finite; a program needn't handle non-finite values.
Results may differ from a plain program's by a relative error of at most 0.007.
The roundings to bfloat16 on the way count: a program that leaves them out, or rounds other values in their place, can miss the bound.
Values may be sent and summed in bfloat16 or wider, within the bound.
No kernel may reach another device: no remote copies, remote signals or barrier semaphores. Data moves between devices by JAX's collectives and lax.ppermute only.
A program may use at most 128 MiB of HBM per device.

v0:
```python
import jax
import jax.numpy as jnp
from jax import lax
from jax.sharding import PartitionSpec as P

HEAD_DIM = 64


masked_score = -1e30


def normed(values):
    wide = values.astype(jnp.float32)
    return (wide * lax.rsqrt(jnp.mean(wide * wide, axis=-1, keepdims=True) + 1e-05)).astype(
        jnp.bfloat16
    )


def attend(queries, key_rows, value_rows, live_tokens):
    samples, latents, head_count, head_size = queries.shape
    spike_scores = jnp.einsum(
        "blhd,bkhd->bhlk", queries, key_rows, preferred_element_type=jnp.float32
    ) * HEAD_DIM ** (-0.5)
    spike_scores = jnp.where(live_tokens[:, None, None, :], spike_scores, masked_score)
    spike_max = jnp.max(spike_scores, axis=-1, keepdims=True)
    spike_exp = jnp.exp(spike_scores - spike_max)
    denominator = jnp.transpose(jnp.sum(spike_exp, axis=-1, keepdims=True), (0, 2, 1, 3))
    spike_mix = (
        jnp.einsum(
            "bhlk,bkhd->blhd",
            spike_exp.astype(jnp.bfloat16),
            value_rows,
            preferred_element_type=jnp.float32,
        )
        / denominator
    )
    return spike_mix.reshape(samples, latents, head_count * head_size).astype(jnp.bfloat16)


def per_device(
    state,
    unit_slot,
    token_count,
    session,
    session_row,
    unit_count,
    panels,
    memory_key,
    memory_value,
    q1_weight,
    o1_weight,
    kv_weight,
    q2_weight,
    o2_weight,
):
    local_samples, latents, model_width = state.shape
    token_total = unit_slot.shape[1]
    owners = lax.axis_size("smp")
    sess_dev, unit_total = (panels.shape[0], panels.shape[1])
    head_count = model_width // HEAD_DIM
    session_ids = jnp.arange(session_row.shape[0], dtype=jnp.int32)
    panel_row = jnp.sum(
        jnp.where(session[:, None] == session_ids[None, :], session_row[None, :], 0), axis=1
    )
    unit_limit = jnp.sum(
        jnp.where(panel_row[:, None] == session_ids[None, :], unit_count[None, :], 0), axis=1
    )
    owner_rank = panel_row // sess_dev
    token_index = (panel_row % sess_dev * unit_total)[:, None] + unit_slot % unit_limit[:, None]
    slot_pick = owner_rank[None, :] == jnp.arange(owners, dtype=jnp.int32)[:, None]
    request = jnp.sum(jnp.where(slot_pick[:, :, None], token_index[None, :, :], 0), axis=1)
    live_tokens = jnp.arange(token_total, dtype=jnp.int32)[None, :] < token_count[:, None]
    panel_table = panels.reshape(sess_dev * unit_total, model_width)
    arrived = lax.all_to_all(
        panel_table[lax.all_to_all(request, "smp", split_axis=0, concat_axis=0, tiled=True)],
        "smp",
        split_axis=0,
        concat_axis=0,
        tiled=True,
    )
    row_total = local_samples * latents
    flat_state = state.reshape(row_total, model_width)
    queries = jnp.dot(normed(flat_state), q1_weight, preferred_element_type=jnp.float32).astype(
        jnp.bfloat16
    )
    queries = queries.reshape(row_total, head_count, HEAD_DIM)
    running_max = jnp.full((head_count, row_total), masked_score, jnp.float32)
    key_rows = lax.all_gather(memory_key, "smp", axis=0, tiled=True).reshape(
        -1, head_count, HEAD_DIM
    )
    value_rows = lax.all_gather(memory_value, "smp", axis=0, tiled=True).reshape(
        -1, head_count, HEAD_DIM
    )
    scores = jnp.einsum(
        "rhd,khd->hrk", queries, key_rows, preferred_element_type=jnp.float32
    ) * HEAD_DIM ** (-0.5)
    new_max = jnp.maximum(running_max, jnp.max(scores, axis=-1))
    exponent = jnp.exp(scores - new_max[:, :, None])
    denominator = jnp.sum(exponent, axis=-1)
    weighted = jnp.einsum(
        "hrk,khd->hrd",
        exponent.astype(jnp.bfloat16),
        value_rows,
        preferred_element_type=jnp.float32,
    )
    running_max, denominator, weighted = (new_max, denominator, weighted)
    read_mem = (
        jnp.transpose(weighted / denominator[:, :, None], (1, 0, 2))
        .reshape(row_total, model_width)
        .astype(jnp.bfloat16)
    )
    hidden = (
        flat_state.astype(jnp.float32)
        + jnp.dot(read_mem, o1_weight, preferred_element_type=jnp.float32)
    ).astype(jnp.bfloat16)
    queries2 = jnp.dot(normed(hidden), q2_weight, preferred_element_type=jnp.float32).astype(
        jnp.bfloat16
    )
    queries2 = queries2.reshape(local_samples, latents, model_width)
    embed = arrived[owner_rank]
    key_value = jnp.dot(
        normed(embed.reshape(local_samples * token_total, model_width)),
        kv_weight,
        preferred_element_type=jnp.float32,
    ).astype(jnp.bfloat16)
    key_value = key_value.reshape(local_samples, token_total, 2 * model_width)
    key_rows = key_value[:, :, :model_width].reshape(
        local_samples, token_total, head_count, HEAD_DIM
    )
    value_rows = key_value[:, :, model_width:].reshape(
        local_samples, token_total, head_count, HEAD_DIM
    )
    read_spike = attend(
        queries2.reshape(local_samples, latents, head_count, HEAD_DIM),
        key_rows,
        value_rows,
        live_tokens,
    )
    result = hidden.astype(jnp.float32) + jnp.dot(
        read_spike.reshape(row_total, model_width), o2_weight, preferred_element_type=jnp.float32
    )
    return result.astype(jnp.bfloat16).reshape(local_samples, latents, model_width)


def solution(mesh):
    in_specs = (
        P(("grp", "smp"), None, None),
        P(("grp", "smp"), None),
        P(("grp", "smp")),
        P(("grp", "smp")),
        P("grp"),
        P(),
        P("smp", None, None),
        P(("grp", "smp"), None),
        P(("grp", "smp"), None),
        P(),
        P(),
        P(),
        P(),
        P(),
    )
    out_specs = P(("grp", "smp"), None, None)
    return jax.shard_map(
        per_device, mesh=mesh, in_specs=in_specs, out_specs=out_specs, check_vma=False
    )
```

profile of v0, /device:TPU:0, one launch (start us, length us, event | category | flops | bytes accessed | tf_op | source)
XLA Modules:
  0.0 167.4 jit_solution(13503824719128611106)
XLA Ops:
  0.0 0.0 copy-start
  0.0 1.0 select_reduce_fusion.2
  1.0 0.8 select_reduce_fusion.1
  1.9 0.9 add_select_fusion
  2.8 0.7 select_reduce_fusion
  3.5 7.4 %all-to-all-start = ((s32[16,1,64]{2,1,0:T(1,128)}), s32[16,1,64]{2,1,0:T(1,128)S(1)}, u32[]{:S(2)}, u32[]{:S(2)}) async-start(s32[16,1,64]{2,1,0:T(1,128)} %bitcast.9), calls=%async_computation | async-start | bytes 16384 | tf_op jit(solution)/shard_map/all_to_all | solution.py:75
  10.9 1.2 multiply_reduce_fusion.2
  12.1 5.1 %all-to-all-done = s32[16,1,64]{2,1,0:T(1,128)S(1)} async-done(((s32[16,1,64]{2,1,0:T(1,128)}), s32[16,1,64]{2,1,0:T(1,128)S(1)}, u32[]{:S(2)}, u32[]{:S(2)}) %all-to-all-start) | async-done | bytes 4128 | tf_op jit(solution)/shard_map/all_to_all | solution.py:75
  17.2 0.1 reshape.192
  17.3 7.4 %gather_fusion = bf16[1024,1024]{1,0:T(8,128)(2,1)} fusion(bf16[512,1024]{1,0:T(8,128)(2,1)} %bitcast.57, s32[1024]{0:T(1024)S(1)} %broadcast_clamp_fusion), kind=kCustom, calls=%fused_computation | custom fusion | bytes 4198400 | tf_op jit(solution)/shard_map/gather | solution.py:75
  24.7 0.0 copy-start.1
  24.7 4.6 %all-to-all-start.1 = ((bf16[16,64,1024]{2,1,0:T(8,128)(2,1)}), bf16[16,64,1024]{2,1,0:T(8,128)(2,1)}, u32[]{:S(2)}, u32[]{:S(2)}) async-start(bf16[16,64,1024]{2,1,0:T(8,128)(2,1)} %bitcast.58), calls=%async_computation.1 | async-start | bytes 4194304 | tf_op jit(solution)/shard_map/all_to_all | solution.py:74
  29.3 0.1 rsqrt.31
  29.4 0.0 copy-done.1
  29.4 0.2 fusion.31
  29.5 0.0 copy-start.5
  29.6 3.1 %convolution_convert_fusion.2 = bf16[256,1024]{1,0:T(8,128)(2,1)} fusion(bf16[256,1024]{1,0:T(8,128)(2,1)S(1)} %fusion.31, bf16[1024,1024]{1,0:T(8,128)(2,1)} %param.23), kind=kOutput, calls=%fused_computation.31 | convolution fusion | flops 537133056 | bytes 3145728 | tf_op jit(solution)/shard_map/dot_general | solution.py:83
  32.7 0.0 copy-start.6
  32.7 1.2 copy.36
  33.9 0.0 copy-done.5
  33.9 52.9 %all_gather.6 = bf16[256,1024]{1,0:T(8,128)(2,1)} all-gather(bf16[16,1024]{1,0:T(8,128)(2,1)S(1)} %copy-done.5), channel_id=1, replica_groups=mesh['grp'=2,'smp'=16] {'smp'}, dimensions={0}, use_global_device_ids=true | all-gather | bytes 557056 | tf_op jit(solution)/shard_map/all_gather | solution.py:88
  86.8 2.0 %copy.37 = bf16[256,1024]{0,1:T(8,128)(2,1)} copy(bf16[256,1024]{1,0:T(8,128)(2,1)} %all_gather.6) | data formatting | bytes 1048576 | tf_op jit(solution)/shard_map/all_gather | solution.py:88
  88.9 0.0 copy-done.6
  88.9 25.8 %all_gather.7 = bf16[256,1024]{1,0:T(8,128)(2,1)} all-gather(bf16[16,1024]{1,0:T(8,128)(2,1)S(1)} %copy-done.6), channel_id=1, replica_groups=mesh['grp'=2,'smp'=16] {'smp'}, dimensions={0}, use_global_device_ids=true | all-gather | bytes 557056 | tf_op jit(solution)/shard_map/all_gather | solution.py:91
  114.7 2.0 %copy.38 = bf16[256,1024]{0,1:T(8,128)(2,1)} copy(bf16[256,1024]{1,0:T(8,128)(2,1)} %all_gather.7) | data formatting | bytes 1048576 | tf_op jit(solution)/shard_map/all_gather | solution.py:91
  116.8 1.8 %multiply_reduce_fusion.1 = (f32[16,256]{1,0:T(8,128)S(1)}, f32[16,256,256]{1,2,0:T(8,128)S(1)}) fusion(bf16[256,16,64]{0,2,1:T(8,128)(2,1)S(1)} %bitcast.61, bf16[256,16,64]{0,2,1:T(8,128)(2,1)} %bitcast.62), kind=kOutput, calls=%fused_computation.10 | convolution fusion | flops 136310784 | bytes 5259264 | tf_op jit(solution)/shard_map/rhd,khd->hrk/dot_general | solution.py:94
  118.6 0.0 copy-start.3
  118.6 0.7 fusion.5
  119.3 0.3 copy-done.3
  119.6 0.9 fusion.25
  120.5 0.0 copy-start.9
  120.5 0.0 copy-done
  120.5 0.8 fusion.28
  121.4 0.0 copy-start.4
  121.4 0.8 copy-done.4
  122.2 0.0 copy-done.9
  122.2 0.0 copy-start.7
  122.2 1.6 convolution_convert_fusion.1
  123.8 1.8 %reshape_reshape.3 = bf16[16,16,16,64]{3,2,1,0:T(8,128)(2,1)S(1)} reshape(bf16[256,1024]{1,0:T(8,128)(2,1)} %convolution_convert_fusion.1) | data formatting | bytes 1048576 | tf_op jit(solution)/shard_map/reshape;reshape | solution.py:134
  125.5 0.0 copy-done.7
  125.6 0.1 iota_compare_fusion
  125.6 0.0 all-to-all-done.1
  125.6 3.6 %gather_fusion.1 = bf16[16,64,1024]{2,1,0:T(8,128)(2,1)} fusion(bf16[16,64,1024]{2,1,0:T(8,128)(2,1)} %all-to-all-done.1, s32[1024]{0:T(1024)S(1)} %pad_clamp_fusion), kind=kCustom, calls=%fused_computation.1 | custom fusion | bytes 4194368 | tf_op jit(solution)/shard_map/gather | solution.py:120
  129.2 2.1 %multiply_reduce_fusion = f32[16,64]{1,0:T(8,128)S(1)} fusion(bf16[16,64,1024]{2,1,0:T(8,128)(2,1)} %gather_fusion.1), kind=kLoop, calls=%fused_computation.8 | loop fusion | flops 3144704 | bytes 2101248 | tf_op jit(solution)/shard_map/reduce_sum | solution.py:14
  131.3 0.1 rsqrt.33
  131.4 0.0 copy-start.8
  131.4 2.1 %fusion = bf16[1024,1024]{1,0:T(8,128)(2,1)S(1)} fusion(f32[1024]{0:T(1024)S(1)} %rsqrt.33, bf16[16,64,1024]{2,1,0:T(8,128)(2,1)} %gather_fusion.1), kind=kLoop, calls=%fused_computation.3 | loop fusion | flops 3145728 | bytes 4198400 | tf_op jit(solution)/shard_map/convert_element_type | solution.py:14
  133.5 0.7 copy-done.8
  134.2 4.7 %convolution_convert_fusion = bf16[1024,2048]{1,0:T(8,128)(2,1)S(1)} fusion(bf16[1024,1024]{1,0:T(8,128)(2,1)S(1)} %fusion, bf16[1024,2048]{1,0:T(8,128)(2,1)S(1)} %copy-done.8), kind=kOutput, calls=%fused_computation.11 | convolution fusion | flops 4297064448 | bytes 10485760 | tf_op jit(solution)/shard_map/dot_general | solution.py:121
  138.9 2.6 %fusion.43 = (bf16[16,64,1024]{2,1,0:T(8,128)(2,1)}, bf16[16,64,1024]{2,1,0:T(8,128)(2,1)}) fusion(bf16[16,64,2048]{2,1,0:T(8,128)(2,1)S(1)} %bitcast.60), kind=kLoop, calls=%fused_computation.68 | loop fusion | bytes 8388608 | tf_op jit(solution)/shard_map/slice | solution.py:127
  141.5 6.4 %reshape.186 = bf16[16,64,16,64]{3,2,1,0:T(8,128)(2,1)} reshape(bf16[16,64,1024]{2,1,0:T(8,128)(2,1)} %get-tuple-element.5) | data formatting | bytes 4194304 | tf_op jit(solution)/shard_map/reshape | solution.py:127
  147.9 6.4 %reshape.185 = bf16[16,64,16,64]{3,2,1,0:T(8,128)(2,1)} reshape(bf16[16,64,1024]{2,1,0:T(8,128)(2,1)} %get-tuple-element.6) | data formatting | bytes 4194304 | tf_op jit(solution)/shard_map/reshape | solution.py:130
  154.3 0.0 copy-start.2
  154.3 4.7 %fusion.12 = (f32[16,16,16]{2,1,0:T(8,128)S(1)}, f32[16,16,16,64]{3,2,1,0:T(8,128)S(1)}) fusion(pred[16,64]{1,0:T(8,128)(4,1)S(1)} %iota_compare_fusion, bf16[16,64,16,64]{3,2,1,0:T(8,128)(2,1)} %reshape.186, bf16[16,16,16,64]{3,2,1,0:T(8,128)(2,1)S(1)} %reshape_reshape.3), kind=kOutput, calls=%fused_computation.21 | convolution fusion | flops 34336768 | bytes 3687424 | tf_op jit(solution)/shard_map/blhd,bkhd->bhlk/dot_general | solution.py:21
  159.0 1.3 fusion.15
  160.3 0.0 copy-done.2
  160.3 2.0 %fusion.9 = bf16[16,16,16,64]{3,1,2,0:T(8,128)(2,1)S(1)} fusion(bf16[16,64,16,64]{3,2,1,0:T(8,128)(2,1)S(1)} %copy-done.2, f32[16,16,16,64]{3,2,1,0:T(8,128)S(1)} %get-tuple-element.12, f32[16,16,16]{1,2,0:T(8,128)S(1)} %bitcast.65, f32[16,16,16]{2,1,0:T(8,128)S(1)} %get-tuple-element.11, pred[16,64]{1,0:T(8,128)(4,1)S(1)} %iota_compare_fusion), kind=kOutput, calls=%fused_computation.16 | convolution fusion | flops 35127296 | bytes 3703808 | tf_op jit(solution)/shard_map/bhlk,bkhd->blhd/dot_general | solution.py:29
  162.3 0.3 copy.44
  162.6 1.5 convert_element_type.85
  164.1 3.3 %fusion.20 = bf16[256,1024]{1,0:T(8,128)(2,1)} fusion(bf16[256,1024]{1,0:T(8,128)(2,1)} %convert_element_type.85, bf16[1024,1024]{1,0:T(8,128)(2,1)} %param.27, bf16[256,1024]{1,0:T(8,128)(2,1)} %copy-done.4), kind=kOutput, calls=%fused_computation.29 | convolution fusion | flops 537657344 | bytes 3670016 | tf_op jit(solution)/shard_map/dot_general | solution.py:139
  (11 shorter events, 0.1 us)
Async XLA Ops:
  0.0 120.5 %copy-start = (bf16[1024,1024]{1,0:T(8,128)(2,1)S(1)}, bf16[1024,1024]{1,0:T(8,128)(2,1)}, u32[]{:S(2)}) copy-start(bf16[1024,1024]{1,0:T(8,128)(2,1)} %param.24) | copy-start | bytes 6291460
  3.5 13.7 %all-to-all-start = ((s32[16,1,64]{2,1,0:T(1,128)}), s32[16,1,64]{2,1,0:T(1,128)S(1)}, u32[]{:S(2)}, u32[]{:S(2)}) async-start(s32[16,1,64]{2,1,0:T(1,128)} %bitcast.9), calls=%async_computation | async-start | bytes 16384 | tf_op jit(solution)/shard_map/all_to_all | solution.py:75
  24.7 4.7 %copy-start.1 = (bf16[16,16,1024]{2,1,0:T(8,128)(2,1)S(1)}, bf16[16,16,1024]{2,1,0:T(8,128)(2,1)}, u32[]{:S(2)}) copy-start(bf16[16,16,1024]{2,1,0:T(8,128)(2,1)} %param.14) | copy-start | bytes 1572868
  24.7 100.9 %all-to-all-start.1 = ((bf16[16,64,1024]{2,1,0:T(8,128)(2,1)}), bf16[16,64,1024]{2,1,0:T(8,128)(2,1)}, u32[]{:S(2)}, u32[]{:S(2)}) async-start(bf16[16,64,1024]{2,1,0:T(8,128)(2,1)} %bitcast.58), calls=%async_computation.1 | async-start | bytes 4194304 | tf_op jit(solution)/shard_map/all_to_all | solution.py:74
  29.5 4.4 %copy-start.5 = (bf16[16,1024]{1,0:T(8,128)(2,1)S(1)}, bf16[16,1024]{1,0:T(8,128)(2,1)}, u32[]{:S(2)}) copy-start(bf16[16,1024]{1,0:T(8,128)(2,1)} %param.21) | copy-start | bytes 98308
  32.7 56.2 %copy-start.6 = (bf16[16,1024]{1,0:T(8,128)(2,1)S(1)}, bf16[16,1024]{1,0:T(8,128)(2,1)}, u32[]{:S(2)}) copy-start(bf16[16,1024]{1,0:T(8,128)(2,1)} %param.22) | copy-start | bytes 98308
  118.6 1.0 copy-start.3
  120.5 1.7 %copy-start.9 = (bf16[1024,1024]{1,0:T(8,128)(2,1)S(1)}, bf16[1024,1024]{1,0:T(8,128)(2,1)}, u32[]{:S(2)}) copy-start(bf16[1024,1024]{1,0:T(8,128)(2,1)} %param.26) | copy-start | bytes 6291460
  121.4 0.8 copy-start.4
  122.2 3.4 %copy-start.7 = (s32[16]{0:T(128)S(1)}, s32[16]{0:T(128)}, u32[]{:S(2)}) copy-start(s32[16]{0:T(128)} %param.16) | copy-start | bytes 196
  131.4 2.8 %copy-start.8 = (bf16[1024,2048]{1,0:T(8,128)(2,1)S(1)}, bf16[1024,2048]{1,0:T(8,128)(2,1)}, u32[]{:S(2)}) copy-start(bf16[1024,2048]{1,0:T(8,128)(2,1)} %param.25) | copy-start | bytes 12582916
  154.3 6.1 %copy-start.2 = (bf16[16,64,16,64]{3,2,1,0:T(8,128)(2,1)S(1)}, bf16[16,64,16,64]{3,2,1,0:T(8,128)(2,1)}, u32[]{:S(2)}) copy-start(bf16[16,64,16,64]{3,2,1,0:T(8,128)(2,1)} %reshape.185) | copy-start | bytes 6291460
where the time goes:
time: 168 us; the launch traced here: 167 us
  blocking collectives  78.8 us (47%)
  local copies, waits for them, and re-layouts  37.3 us (22%)
  matrix products  22.9 us (14%)
  starting transfers between devices  11.9 us (7%)
  other arithmetic  11.2 us (7%)
  waiting for transfers between devices  5.11 us (3%)
    all_gather x1, blocking collectives, per_device(): lax.all_gather(memory_key, 'smp', axis=0, tiled=True)  52.9 us
    all_gather x1, blocking collectives, per_device(): lax.all_gather(memory_value, 'smp', axis=0, tiled=True)  25.8 us
    gather x1, local copies, waits for them, and re-layouts, per_device(): panel_table[lax.all_to_all(request, 'smp', split_axis=0, concat_axis=0, t...  7.42 us
    all_to_all x1, starting transfers between devices, per_device(): lax.all_to_all(request, 'smp', split_axis=0, concat_axis=0, tiled=True)  7.39 us
    reshape x1, local copies, waits for them, and re-layouts, per_device(): key_value[:, :, :model_width]  6.37 us
    reshape x1, local copies, waits for them, and re-layouts, per_device(): key_value[:, :, model_width:]  6.37 us
    all_to_all x1, waiting for transfers between devices, per_device(): lax.all_to_all(request, 'smp', split_axis=0, concat_axis=0, tiled=True)  5.11 us
    dot_general x1, matrix products, per_device(): jnp.dot(normed(embed.reshape(local_samples * token_total, model_width)),...  4.71 us
  transfers between devices with their start and end apart: 2, of which 1 were waited for; matrix products, arithmetic and copies ran while one was open for 10% of the time, Pallas kernels for 0%

commit v1 on v0

--- a/solution.py
+++ b/solution.py
@@ -85,12 +85,11 @@
     )
     queries = queries.reshape(row_total, head_count, HEAD_DIM)
     running_max = jnp.full((head_count, row_total), masked_score, jnp.float32)
-    key_rows = lax.all_gather(memory_key, "smp", axis=0, tiled=True).reshape(
-        -1, head_count, HEAD_DIM
+    memory_rows = lax.all_gather(
+        jnp.concatenate([memory_key, memory_value], axis=1), "smp", axis=0, tiled=True
     )
-    value_rows = lax.all_gather(memory_value, "smp", axis=0, tiled=True).reshape(
-        -1, head_count, HEAD_DIM
-    )
+    key_rows = memory_rows[:, :model_width].reshape(-1, head_count, HEAD_DIM)
+    value_rows = memory_rows[:, model_width:].reshape(-1, head_count, HEAD_DIM)
     scores = jnp.einsum(
         "rhd,khd->hrk", queries, key_rows, preferred_element_type=jnp.float32
     ) * HEAD_DIM ** (-0.5)

time: 168 us -> 136 us (0.81)
  the two profiles are of different devices: /device:TPU:0 before, /device:TPU:15 now
where the time goes in v1:
time: 136 us; the launch traced here: 135 us
  local copies, waits for them, and re-layouts  39.5 us (29%)
  waiting for transfers between devices  30.8 us (23%)
  matrix products  22.9 us (17%)
  between operations  13.6 us (10%)
  other arithmetic  11 us (8%)
  blocking collectives  10.2 us (7%)
  starting transfers between devices  7.03 us (5%)
    all_to_all x1, waiting for transfers between devices, per_device(): lax.all_to_all(panel_table[lax.all_to_all(request, 'smp', split_axis=0, c...  15.6 us
    all_gather x1, waiting for transfers between devices, per_device(): lax.all_gather(jnp.concatenate([memory_key, memory_value], axis=1), 'smp'...  15.2 us
    all_to_all x1, blocking collectives, per_device(): lax.all_to_all(request, 'smp', split_axis=0, concat_axis=0, tiled=True)  10.2 us
    gather x1, local copies, waits for them, and re-layouts, per_device(): panel_table[lax.all_to_all(request, 'smp', split_axis=0, concat_axis=0, t...  7.42 us
    all_to_all x1, starting transfers between devices, per_device(): lax.all_to_all(panel_table[lax.all_to_all(request, 'smp', split_axis=0, c...  7.03 us
    reshape x1, local copies, waits for them, and re-layouts, per_device(): key_value[:, :, :model_width]  6.37 us
    reshape x1, local copies, waits for them, and re-layouts, per_device(): key_value[:, :, model_width:]  6.37 us
    dot_general x1, matrix products, per_device(): jnp.dot(normed(embed.reshape(local_samples * token_total, model_width)),...  4.71 us
  transfers between devices with their start and end apart: 2, of which 2 were waited for; matrix products, arithmetic and copies ran while one was open for 21% of the time, Pallas kernels for 0%

profile of v1, /device:TPU:15, one launch (start us, length us, event | category | flops | bytes accessed | tf_op | source)
XLA Modules:
  0.0 135.0 jit_solution(4492190522715917087)
XLA Ops:
  6.5 0.0 copy-start
  6.5 0.0 all-gather.2.cloned.1.call-start
  6.5 1.5 %pad_maximum_fusion = bf16[16,2048]{1,0:T(8,128)(2,1)} fusion(bf16[16,1024]{1,0:T(8,128)(2,1)} %param.22, bf16[16,1024]{1,0:T(8,128)(2,1)} %param.21), kind=kLoop, calls=%fused_computation.47 | loop fusion | flops 131072 | bytes 131072 | tf_op jit(solution)/shard_map/concatenate | solution.py:89
  8.1 0.0 all-gather.2.cloned.1.call-update
  8.1 0.9 select_reduce_fusion.2
  9.0 0.8 select_reduce_fusion.1
  9.8 0.9 add_select_fusion
  10.7 0.1 select_reduce_fusion
  10.9 10.2 %all_to_all.17 = s32[16,1,64]{2,1,0:T(1,128)S(1)} all-to-all(s32[16,1,64]{2,1,0:T(1,128)S(1)} %bitcast.66), channel_id=1, replica_groups=mesh['grp'=2,'smp'=16] {'smp'}, dimensions={0} | all-to-all | bytes 8192 | tf_op jit(solution)/shard_map/all_to_all | solution.py:75
  21.0 0.1 reshape.192
  21.1 7.4 %gather_fusion = bf16[1024,1024]{1,0:T(8,128)(2,1)} fusion(bf16[512,1024]{1,0:T(8,128)(2,1)} %bitcast.57, s32[1024]{0:T(1024)S(1)} %broadcast_clamp_fusion), kind=kCustom, calls=%fused_computation | custom fusion | bytes 4198400 | tf_op jit(solution)/shard_map/gather | solution.py:75
  28.5 0.0 copy-start.1
  28.5 7.0 %all-to-all-start.1 = ((bf16[16,64,1024]{2,1,0:T(8,128)(2,1)}), bf16[16,64,1024]{2,1,0:T(8,128)(2,1)}, u32[]{:S(2)}, u32[]{:S(2)}) async-start(bf16[16,64,1024]{2,1,0:T(8,128)(2,1)} %bitcast.58), calls=%async_computation.1 | async-start | bytes 4194304 | tf_op jit(solution)/shard_map/all_to_all | solution.py:74
  35.5 0.0 copy-done.1
  35.6 0.2 multiply_reduce_fusion.2
  35.7 0.1 rsqrt.31
  35.8 0.2 fusion.31
  36.0 0.0 copy-start.5
  36.0 3.1 %convolution_convert_fusion.2 = bf16[256,1024]{1,0:T(8,128)(2,1)} fusion(bf16[256,1024]{1,0:T(8,128)(2,1)S(1)} %fusion.31, bf16[1024,1024]{1,0:T(8,128)(2,1)} %param.23), kind=kOutput, calls=%fused_computation.31 | convolution fusion | flops 537133056 | bytes 3145728 | tf_op jit(solution)/shard_map/dot_general | solution.py:83
  39.1 1.2 copy.36
  40.4 0.0 copy-done.5
  40.4 0.1 iota_compare_fusion
  40.5 15.2 %all-gather.2.cloned.1.call-done = bf16[256,2048]{1,0:T(8,128)(2,1)} async-done(((bf16[16,2048]{1,0:T(8,128)(2,1)}), bf16[256,2048]{1,0:T(8,128)(2,1)}) %all-gather.2.cloned.1.call-update) | async-done | bytes 1048592 | tf_op jit(solution)/shard_map/all_gather | solution.py:88
  55.7 2.2 %fusion.44 = (bf16[256,1024]{1,0:T(8,128)(2,1)}, bf16[256,1024]{1,0:T(8,128)(2,1)}) fusion(bf16[256,2048]{1,0:T(8,128)(2,1)} %all-gather.2.cloned.1.call-done), kind=kLoop, calls=%fused_computation.70 | loop fusion | bytes 2097152 | tf_op jit(solution)/shard_map/slice | solution.py:91
  57.9 2.0 %copy.37 = bf16[256,1024]{0,1:T(8,128)(2,1)} copy(bf16[256,1024]{1,0:T(8,128)(2,1)} %get-tuple-element.7) | data formatting | bytes 1048576 | tf_op jit(solution)/shard_map/slice | solution.py:91
  60.0 2.0 %copy.38 = bf16[256,1024]{0,1:T(8,128)(2,1)} copy(bf16[256,1024]{1,0:T(8,128)(2,1)} %get-tuple-element.8) | data formatting | bytes 1048576 | tf_op jit(solution)/shard_map/slice | solution.py:92
  62.0 1.8 %multiply_reduce_fusion.1 = (f32[16,256]{1,0:T(8,128)S(1)}, f32[16,256,256]{1,2,0:T(8,128)S(1)}) fusion(bf16[256,16,64]{0,2,1:T(8,128)(2,1)S(1)} %bitcast.61, bf16[256,16,64]{0,2,1:T(8,128)(2,1)} %bitcast.62), kind=kOutput, calls=%fused_computation.10 | convolution fusion | flops 136310784 | bytes 5259264 | tf_op jit(solution)/shard_map/rhd,khd->hrk/dot_general | solution.py:93
  63.8 0.0 copy-start.3
  63.8 0.7 fusion.5
  64.5 0.3 copy-done.3
  64.9 0.9 fusion.25
  65.7 0.0 copy-start.7
  65.7 0.0 copy-done
  65.8 0.8 fusion.28
  66.6 0.0 copy-start.4
  66.6 0.8 copy-done.4
  67.4 0.0 copy-done.7
  67.4 1.6 %convolution_convert_fusion.1 = bf16[256,1024]{1,0:T(8,128)(2,1)} fusion(bf16[1024,1024]{1,0:T(8,128)(2,1)S(1)} %copy-done.7, bf16[256,1024]{1,0:T(8,128)(2,1)S(1)} %get-tuple-element.12, f32[256]{0:T(256)S(1)} %add_rsqrt_fusion.2), kind=kOutput, calls=%fused_computation.30 | convolution fusion | flops 537919488 | bytes 3146752 | tf_op jit(solution)/shard_map/dot_general | solution.py:115
  69.0 1.8 %reshape_reshape.3 = bf16[16,16,16,64]{3,2,1,0:T(8,128)(2,1)S(1)} reshape(bf16[256,1024]{1,0:T(8,128)(2,1)} %convolution_convert_fusion.1) | data formatting | bytes 1048576 | tf_op jit(solution)/shard_map/reshape;reshape | solution.py:133
  70.8 15.6 %all-to-all-done.1 = bf16[16,64,1024]{2,1,0:T(8,128)(2,1)} async-done(((bf16[16,64,1024]{2,1,0:T(8,128)(2,1)}), bf16[16,64,1024]{2,1,0:T(8,128)(2,1)}, u32[]{:S(2)}, u32[]{:S(2)}) %all-to-all-start.1) | async-done | bytes 2097184 | tf_op jit(solution)/shard_map/all_to_all | solution.py:74
  86.4 3.6 %gather_fusion.1 = bf16[16,64,1024]{2,1,0:T(8,128)(2,1)} fusion(bf16[16,64,1024]{2,1,0:T(8,128)(2,1)} %all-to-all-done.1, s32[1024]{0:T(1024)S(1)} %pad_clamp_fusion), kind=kCustom, calls=%fused_computation.1 | custom fusion | bytes 4194368 | tf_op jit(solution)/shard_map/gather | solution.py:119
  89.9 2.1 %multiply_reduce_fusion = f32[16,64]{1,0:T(8,128)S(1)} fusion(bf16[16,64,1024]{2,1,0:T(8,128)(2,1)} %gather_fusion.1), kind=kLoop, calls=%fused_computation.8 | loop fusion | flops 3144704 | bytes 2101248 | tf_op jit(solution)/shard_map/reduce_sum | solution.py:14
  92.0 0.1 rsqrt.33
  92.1 0.0 copy-start.6
  92.1 2.1 %fusion = bf16[1024,1024]{1,0:T(8,128)(2,1)S(1)} fusion(f32[1024]{0:T(1024)S(1)} %rsqrt.33, bf16[16,64,1024]{2,1,0:T(8,128)(2,1)} %gather_fusion.1), kind=kLoop, calls=%fused_computation.3 | loop fusion | flops 3145728 | bytes 4198400 | tf_op jit(solution)/shard_map/convert_element_type | solution.py:14
  94.2 0.7 copy-done.6
  94.9 4.7 %convolution_convert_fusion = bf16[1024,2048]{1,0:T(8,128)(2,1)S(1)} fusion(bf16[1024,1024]{1,0:T(8,128)(2,1)S(1)} %fusion, bf16[1024,2048]{1,0:T(8,128)(2,1)S(1)} %copy-done.6), kind=kOutput, calls=%fused_computation.11 | convolution fusion | flops 4297064448 | bytes 10485760 | tf_op jit(solution)/shard_map/dot_general | solution.py:120
  99.6 2.6 %fusion.43 = (bf16[16,64,1024]{2,1,0:T(8,128)(2,1)}, bf16[16,64,1024]{2,1,0:T(8,128)(2,1)}) fusion(bf16[16,64,2048]{2,1,0:T(8,128)(2,1)S(1)} %bitcast.60), kind=kLoop, calls=%fused_computation.69 | loop fusion | bytes 8388608 | tf_op jit(solution)/shard_map/slice | solution.py:126
  102.2 6.4 %reshape.186 = bf16[16,64,16,64]{3,2,1,0:T(8,128)(2,1)} reshape(bf16[16,64,1024]{2,1,0:T(8,128)(2,1)} %get-tuple-element.5) | data formatting | bytes 4194304 | tf_op jit(solution)/shard_map/reshape | solution.py:126
  108.6 6.4 %reshape.185 = bf16[16,64,16,64]{3,2,1,0:T(8,128)(2,1)} reshape(bf16[16,64,1024]{2,1,0:T(8,128)(2,1)} %get-tuple-element.6) | data formatting | bytes 4194304 | tf_op jit(solution)/shard_map/reshape | solution.py:129
  115.0 0.0 copy-start.2
  115.0 4.7 %fusion.12 = (f32[16,16,16]{2,1,0:T(8,128)S(1)}, f32[16,16,16,64]{3,2,1,0:T(8,128)S(1)}) fusion(pred[16,64]{1,0:T(8,128)(4,1)S(1)} %iota_compare_fusion, bf16[16,64,16,64]{3,2,1,0:T(8,128)(2,1)} %reshape.186, bf16[16,16,16,64]{3,2,1,0:T(8,128)(2,1)S(1)} %reshape_reshape.3), kind=kOutput, calls=%fused_computation.21 | convolution fusion | flops 34336768 | bytes 3687424 | tf_op jit(solution)/shard_map/blhd,bkhd->bhlk/dot_general | solution.py:21
  119.7 1.3 fusion.15
  121.0 0.0 copy-done.2
  121.0 2.0 %fusion.9 = bf16[16,16,16,64]{3,1,2,0:T(8,128)(2,1)S(1)} fusion(bf16[16,64,16,64]{3,2,1,0:T(8,128)(2,1)S(1)} %copy-done.2, f32[16,16,16,64]{3,2,1,0:T(8,128)S(1)} %get-tuple-element.14, f32[16,16,16]{1,2,0:T(8,128)S(1)} %bitcast.65, f32[16,16,16]{2,1,0:T(8,128)S(1)} %get-tuple-element.13, pred[16,64]{1,0:T(8,128)(4,1)S(1)} %iota_compare_fusion), kind=kOutput, calls=%fused_computation.16 | convolution fusion | flops 35127296 | bytes 3703808 | tf_op jit(solution)/shard_map/bhlk,bkhd->blhd/dot_general | solution.py:29
  123.0 0.3 copy.44
  123.3 1.5 %convert_element_type.85 = bf16[256,1024]{1,0:T(8,128)(2,1)} reshape(bf16[16,16,16,64]{3,2,1,0:T(8,128)(2,1)S(1)} %copy.44) | data formatting | bytes 1048576 | tf_op jit(solution)/shard_map/convert_element_type | solution.py:37
  124.8 3.3 %fusion.20 = bf16[256,1024]{1,0:T(8,128)(2,1)} fusion(bf16[256,1024]{1,0:T(8,128)(2,1)} %convert_element_type.85, bf16[1024,1024]{1,0:T(8,128)(2,1)} %param.27, bf16[256,1024]{1,0:T(8,128)(2,1)} %copy-done.4), kind=kOutput, calls=%fused_computation.29 | convolution fusion | flops 537657344 | bytes 3670016 | tf_op jit(solution)/shard_map/dot_general | solution.py:138
  (11 shorter events, 0.1 us)
Async XLA Ops:
  6.5 59.2 %copy-start = (bf16[1024,1024]{1,0:T(8,128)(2,1)S(1)}, bf16[1024,1024]{1,0:T(8,128)(2,1)}, u32[]{:S(2)}) copy-start(bf16[1024,1024]{1,0:T(8,128)(2,1)} %param.24) | copy-start | bytes 6291460
  6.5 49.1 %all-gather.2.cloned.1.call-start = ((), (), s32[]{:S(2)}) async-start(), calls=%async_computation.2 | async-start | bytes 1114112 | tf_op jit(solution)/shard_map/all_gather | solution.py:88
  28.5 7.0 %copy-start.1 = (bf16[16,16,1024]{2,1,0:T(8,128)(2,1)S(1)}, bf16[16,16,1024]{2,1,0:T(8,128)(2,1)}, u32[]{:S(2)}) copy-start(bf16[16,16,1024]{2,1,0:T(8,128)(2,1)} %param.14) | copy-start | bytes 1572868
  28.5 57.8 %all-to-all-start.1 = ((bf16[16,64,1024]{2,1,0:T(8,128)(2,1)}), bf16[16,64,1024]{2,1,0:T(8,128)(2,1)}, u32[]{:S(2)}, u32[]{:S(2)}) async-start(bf16[16,64,1024]{2,1,0:T(8,128)(2,1)} %bitcast.58), calls=%async_computation.1 | async-start | bytes 4194304 | tf_op jit(solution)/shard_map/all_to_all | solution.py:74
  36.0 4.4 %copy-start.5 = (s32[16]{0:T(128)S(1)}, s32[16]{0:T(128)}, u32[]{:S(2)}) copy-start(s32[16]{0:T(128)} %param.16) | copy-start | bytes 196
  63.8 1.0 copy-start.3
  65.7 1.7 %copy-start.7 = (bf16[1024,1024]{1,0:T(8,128)(2,1)S(1)}, bf16[1024,1024]{1,0:T(8,128)(2,1)}, u32[]{:S(2)}) copy-start(bf16[1024,1024]{1,0:T(8,128)(2,1)} %param.26) | copy-start | bytes 6291460
  66.6 0.8 copy-start.4
  92.1 2.8 %copy-start.6 = (bf16[1024,2048]{1,0:T(8,128)(2,1)S(1)}, bf16[1024,2048]{1,0:T(8,128)(2,1)}, u32[]{:S(2)}) copy-start(bf16[1024,2048]{1,0:T(8,128)(2,1)} %param.25) | copy-start | bytes 12582916
  115.0 6.1 %copy-start.2 = (bf16[16,64,16,64]{3,2,1,0:T(8,128)(2,1)S(1)}, bf16[16,64,16,64]{3,2,1,0:T(8,128)(2,1)}, u32[]{:S(2)}) copy-start(bf16[16,64,16,64]{3,2,1,0:T(8,128)(2,1)} %reshape.185) | copy-start | bytes 6291460
Sparse Core Ops, SparseCore 0:
  9.5 46.1 all-gather.1

commit v2 on v1

--- a/solution.py
+++ b/solution.py
@@ -85,9 +85,14 @@
     )
     queries = queries.reshape(row_total, head_count, HEAD_DIM)
     running_max = jnp.full((head_count, row_total), masked_score, jnp.float32)
-    memory_rows = lax.all_gather(
-        jnp.concatenate([memory_key, memory_value], axis=1), "smp", axis=0, tiled=True
-    )
+    memory_pair = jnp.concatenate([memory_key, memory_value], axis=1)
+    memory_rows = lax.all_to_all(
+        jnp.broadcast_to(memory_pair[None], (owners,) + memory_pair.shape),
+        "smp",
+        split_axis=0,
+        concat_axis=0,
+        tiled=True,
+    ).reshape(-1, 2 * model_width)
     key_rows = memory_rows[:, :model_width].reshape(-1, head_count, HEAD_DIM)
     value_rows = memory_rows[:, model_width:].reshape(-1, head_count, HEAD_DIM)
     scores = jnp.einsum(

time: 136 us -> 142 us (1.044)
  the two profiles are of different devices: /device:TPU:15 before, /device:TPU:13 now
where the time goes in v2:
time: 142 us; the launch traced here: 141 us
  waiting for transfers between devices  50 us (35%)
  local copies, waits for them, and re-layouts  38.6 us (27%)
  matrix products  22.9 us (16%)
  starting transfers between devices  18.4 us (13%)
  other arithmetic  11 us (8%)
    all_to_all x1, waiting for transfers between devices, per_device(): lax.all_to_all(panel_table[lax.all_to_all(request, 'smp', split_axis=0, c...  27.5 us
    all_to_all x1, waiting for transfers between devices, per_device(): lax.all_to_all(jnp.broadcast_to(memory_pair[None], (owners,) + memory_pai...  19.5 us
    all_to_all x1, starting transfers between devices, per_device(): lax.all_to_all(jnp.broadcast_to(memory_pair[None], (owners,) + memory_pai...  6.81 us
    all_to_all x1, starting transfers between devices, per_device(): lax.all_to_all(request, 'smp', split_axis=0, concat_axis=0, tiled=True)  6.55 us
    reshape x1, local copies, waits for them, and re-layouts, per_device(): key_value[:, :, :model_width]  6.37 us
    reshape x1, local copies, waits for them, and re-layouts, per_device(): key_value[:, :, model_width:]  6.37 us
    gather x1, local copies, waits for them, and re-layouts, per_device(): panel_table[lax.all_to_all(request, 'smp', split_axis=0, concat_axis=0, t...  5.39 us
    all_to_all x1, starting transfers between devices, per_device(): lax.all_to_all(panel_table[lax.all_to_all(request, 'smp', split_axis=0, c...  5.04 us
  transfers between devices with their start and end apart: 3, of which 3 were waited for; matrix products, arithmetic and copies ran while one was open for 18% of the time, Pallas kernels for 0%

profile of v2, /device:TPU:13, one launch (start us, length us, event | category | flops | bytes accessed | tf_op | source)
XLA Modules:
  0.0 141.1 jit_solution(10532160137987151399)
XLA Ops:
  0.0 0.0 copy-start
  0.0 0.0 copy-start.1
  0.0 1.0 select_reduce_fusion.2
  1.0 0.8 select_reduce_fusion.1
  1.9 0.9 add_select_fusion
  2.8 0.7 select_reduce_fusion
  3.5 6.6 %all-to-all-start.1 = ((s32[16,1,64]{2,1,0:T(1,128)}), s32[16,1,64]{2,1,0:T(1,128)S(1)}, u32[]{:S(2)}, u32[]{:S(2)}) async-start(s32[16,1,64]{2,1,0:T(1,128)} %bitcast.10), calls=%async_computation.1 | async-start | bytes 16384 | tf_op jit(solution)/shard_map/all_to_all | solution.py:75
  10.1 0.8 pad_maximum_fusion
  10.8 2.9 %all-to-all-done.1 = s32[16,1,64]{2,1,0:T(1,128)S(1)} async-done(((s32[16,1,64]{2,1,0:T(1,128)}), s32[16,1,64]{2,1,0:T(1,128)S(1)}, u32[]{:S(2)}, u32[]{:S(2)}) %all-to-all-start.1) | async-done | bytes 4128 | tf_op jit(solution)/shard_map/all_to_all | solution.py:75
  13.8 1.1 broadcast_in_dim.52
  14.9 6.8 %all-to-all-start = ((bf16[16,16,2048]{2,1,0:T(8,128)(2,1)}), bf16[16,16,2048]{2,1,0:T(8,128)(2,1)}, u32[]{:S(2)}, u32[]{:S(2)}) async-start(bf16[16,16,2048]{2,1,0:T(8,128)(2,1)} %broadcast_in_dim.52), calls=%async_computation | async-start | bytes 2097152 | tf_op jit(solution)/shard_map/all_to_all | solution.py:89
  21.7 0.1 reshape.197
  21.8 0.0 copy-done.1
  21.8 5.4 %gather_fusion = bf16[1024,1024]{1,0:T(8,128)(2,1)} fusion(bf16[512,1024]{1,0:T(8,128)(2,1)S(1)} %bitcast.58, s32[1024]{0:T(1024)S(1)} %broadcast_clamp_fusion), kind=kCustom, calls=%fused_computation | custom fusion | bytes 4198400 | tf_op jit(solution)/shard_map/gather | solution.py:75
  27.2 19.5 %all-to-all-done = bf16[16,16,2048]{2,1,0:T(8,128)(2,1)} async-done(((bf16[16,16,2048]{2,1,0:T(8,128)(2,1)}), bf16[16,16,2048]{2,1,0:T(8,128)(2,1)}, u32[]{:S(2)}, u32[]{:S(2)}) %all-to-all-start) | async-done | bytes 1048608 | tf_op jit(solution)/shard_map/all_to_all | solution.py:89
  46.7 0.0 copy-start.2
  46.7 5.0 %all-to-all-start.2 = ((bf16[16,64,1024]{2,1,0:T(8,128)(2,1)}), bf16[16,64,1024]{2,1,0:T(8,128)(2,1)}, u32[]{:S(2)}, u32[]{:S(2)}) async-start(bf16[16,64,1024]{2,1,0:T(8,128)(2,1)} %bitcast.59), calls=%async_computation.2 | async-start | bytes 4194304 | tf_op jit(solution)/shard_map/all_to_all | solution.py:74
  51.7 0.0 copy-done.2
  51.8 0.2 multiply_reduce_fusion.2
  51.9 0.1 rsqrt.31
  52.0 0.2 fusion.31
  52.2 0.0 copy-start.6
  52.2 3.1 %convolution_convert_fusion.2 = bf16[256,1024]{1,0:T(8,128)(2,1)} fusion(bf16[256,1024]{1,0:T(8,128)(2,1)S(1)} %fusion.31, bf16[1024,1024]{1,0:T(8,128)(2,1)} %param.23), kind=kOutput, calls=%fused_computation.31 | convolution fusion | flops 537133056 | bytes 3145728 | tf_op jit(solution)/shard_map/dot_general | solution.py:83
  55.3 1.2 copy.35
  56.6 0.0 copy-done.6
  56.6 0.1 iota_compare_fusion
  56.7 2.2 %fusion.44 = (bf16[256,1024]{1,0:T(8,128)(2,1)}, bf16[256,1024]{1,0:T(8,128)(2,1)}) fusion(bf16[256,2048]{1,0:T(8,128)(2,1)} %bitcast.2), kind=kLoop, calls=%fused_computation.70 | loop fusion | bytes 2097152 | tf_op jit(solution)/shard_map/slice | solution.py:96
  58.9 2.0 %copy.36 = bf16[256,1024]{0,1:T(8,128)(2,1)} copy(bf16[256,1024]{1,0:T(8,128)(2,1)} %get-tuple-element.7) | data formatting | bytes 1048576 | tf_op jit(solution)/shard_map/slice | solution.py:96
  61.0 2.0 %copy.37 = bf16[256,1024]{0,1:T(8,128)(2,1)} copy(bf16[256,1024]{1,0:T(8,128)(2,1)} %get-tuple-element.8) | data formatting | bytes 1048576 | tf_op jit(solution)/shard_map/slice | solution.py:97
  63.0 1.8 %multiply_reduce_fusion.1 = (f32[16,256]{1,0:T(8,128)S(1)}, f32[16,256,256]{1,2,0:T(8,128)S(1)}) fusion(bf16[256,16,64]{0,2,1:T(8,128)(2,1)S(1)} %bitcast.62, bf16[256,16,64]{0,2,1:T(8,128)(2,1)} %bitcast.63), kind=kOutput, calls=%fused_computation.10 | convolution fusion | flops 136310784 | bytes 5259264 | tf_op jit(solution)/shard_map/rhd,khd->hrk/dot_general | solution.py:98
  64.8 0.0 copy-start.4
  64.8 0.7 fusion.5
  65.6 0.3 copy-done.4
  65.9 0.9 fusion.25
  66.7 0.0 copy-start.8
  66.7 0.0 copy-done
  66.8 0.8 fusion.28
  67.6 0.0 copy-start.5
  67.6 0.8 copy-done.5
  68.4 0.0 copy-done.8
  68.4 1.6 %convolution_convert_fusion.1 = bf16[256,1024]{1,0:T(8,128)(2,1)} fusion(bf16[1024,1024]{1,0:T(8,128)(2,1)S(1)} %copy-done.8, bf16[256,1024]{1,0:T(8,128)(2,1)S(1)} %get-tuple-element.12, f32[256]{0:T(256)S(1)} %add_rsqrt_fusion.2), kind=kOutput, calls=%fused_computation.30 | convolution fusion | flops 537919488 | bytes 3146752 | tf_op jit(solution)/shard_map/dot_general | solution.py:120
  70.0 1.8 %reshape_reshape.3 = bf16[16,16,16,64]{3,2,1,0:T(8,128)(2,1)S(1)} reshape(bf16[256,1024]{1,0:T(8,128)(2,1)} %convolution_convert_fusion.1) | data formatting | bytes 1048576 | tf_op jit(solution)/shard_map/reshape;reshape | solution.py:138
  71.8 27.5 %all-to-all-done.2 = bf16[16,64,1024]{2,1,0:T(8,128)(2,1)} async-done(((bf16[16,64,1024]{2,1,0:T(8,128)(2,1)}), bf16[16,64,1024]{2,1,0:T(8,128)(2,1)}, u32[]{:S(2)}, u32[]{:S(2)}) %all-to-all-start.2) | async-done | bytes 2097184 | tf_op jit(solution)/shard_map/all_to_all | solution.py:74
  99.3 3.6 %gather_fusion.1 = bf16[16,64,1024]{2,1,0:T(8,128)(2,1)} fusion(bf16[16,64,1024]{2,1,0:T(8,128)(2,1)} %all-to-all-done.2, s32[1024]{0:T(1024)S(1)} %pad_clamp_fusion), kind=kCustom, calls=%fused_computation.1 | custom fusion | bytes 4194368 | tf_op jit(solution)/shard_map/gather | solution.py:124
  102.8 2.1 %multiply_reduce_fusion = f32[16,64]{1,0:T(8,128)S(1)} fusion(bf16[16,64,1024]{2,1,0:T(8,128)(2,1)} %gather_fusion.1), kind=kLoop, calls=%fused_computation.8 | loop fusion | flops 3144704 | bytes 2101248 | tf_op jit(solution)/shard_map/reduce_sum | solution.py:14
  104.9 0.1 rsqrt.33
  105.0 0.0 copy-start.7
  105.0 2.1 %fusion = bf16[1024,1024]{1,0:T(8,128)(2,1)S(1)} fusion(f32[1024]{0:T(1024)S(1)} %rsqrt.33, bf16[16,64,1024]{2,1,0:T(8,128)(2,1)} %gather_fusion.1), kind=kLoop, calls=%fused_computation.3 | loop fusion | flops 3145728 | bytes 4198400 | tf_op jit(solution)/shard_map/convert_element_type | solution.py:14
  107.1 0.7 copy-done.7
  107.8 4.7 %convolution_convert_fusion = bf16[1024,2048]{1,0:T(8,128)(2,1)S(1)} fusion(bf16[1024,1024]{1,0:T(8,128)(2,1)S(1)} %fusion, bf16[1024,2048]{1,0:T(8,128)(2,1)S(1)} %copy-done.7), kind=kOutput, calls=%fused_computation.11 | convolution fusion | flops 4297064448 | bytes 10485760 | tf_op jit(solution)/shard_map/dot_general | solution.py:125
  112.5 2.6 %fusion.43 = (bf16[16,64,1024]{2,1,0:T(8,128)(2,1)}, bf16[16,64,1024]{2,1,0:T(8,128)(2,1)}) fusion(bf16[16,64,2048]{2,1,0:T(8,128)(2,1)S(1)} %bitcast.61), kind=kLoop, calls=%fused_computation.69 | loop fusion | bytes 8388608 | tf_op jit(solution)/shard_map/slice | solution.py:131
  115.2 6.4 %reshape.191 = bf16[16,64,16,64]{3,2,1,0:T(8,128)(2,1)} reshape(bf16[16,64,1024]{2,1,0:T(8,128)(2,1)} %get-tuple-element.5) | data formatting | bytes 4194304 | tf_op jit(solution)/shard_map/reshape | solution.py:131
  121.5 6.4 %reshape.190 = bf16[16,64,16,64]{3,2,1,0:T(8,128)(2,1)} reshape(bf16[16,64,1024]{2,1,0:T(8,128)(2,1)} %get-tuple-element.6) | data formatting | bytes 4194304 | tf_op jit(solution)/shard_map/reshape | solution.py:134
  127.9 0.0 copy-start.3
  127.9 4.7 %fusion.12 = (f32[16,16,16]{2,1,0:T(8,128)S(1)}, f32[16,16,16,64]{3,2,1,0:T(8,128)S(1)}) fusion(pred[16,64]{1,0:T(8,128)(4,1)S(1)} %iota_compare_fusion, bf16[16,64,16,64]{3,2,1,0:T(8,128)(2,1)} %reshape.191, bf16[16,16,16,64]{3,2,1,0:T(8,128)(2,1)S(1)} %reshape_reshape.3), kind=kOutput, calls=%fused_computation.21 | convolution fusion | flops 34336768 | bytes 3687424 | tf_op jit(solution)/shard_map/blhd,bkhd->bhlk/dot_general | solution.py:21
  132.6 1.3 fusion.15
  133.9 0.0 copy-done.3
  134.0 2.0 %fusion.9 = bf16[16,16,16,64]{3,1,2,0:T(8,128)(2,1)S(1)} fusion(bf16[16,64,16,64]{3,2,1,0:T(8,128)(2,1)S(1)} %copy-done.3, f32[16,16,16,64]{3,2,1,0:T(8,128)S(1)} %get-tuple-element.14, f32[16,16,16]{1,2,0:T(8,128)S(1)} %bitcast.66, f32[16,16,16]{2,1,0:T(8,128)S(1)} %get-tuple-element.13, pred[16,64]{1,0:T(8,128)(4,1)S(1)} %iota_compare_fusion), kind=kOutput, calls=%fused_computation.16 | convolution fusion | flops 35127296 | bytes 3703808 | tf_op jit(solution)/shard_map/bhlk,bkhd->blhd/dot_general | solution.py:29
  135.9 0.3 copy.43
  136.2 1.5 %convert_element_type.85 = bf16[256,1024]{1,0:T(8,128)(2,1)} reshape(bf16[16,16,16,64]{3,2,1,0:T(8,128)(2,1)S(1)} %copy.43) | data formatting | bytes 1048576 | tf_op jit(solution)/shard_map/convert_element_type | solution.py:37
  137.7 3.3 %fusion.20 = bf16[256,1024]{1,0:T(8,128)(2,1)} fusion(bf16[256,1024]{1,0:T(8,128)(2,1)} %convert_element_type.85, bf16[1024,1024]{1,0:T(8,128)(2,1)} %param.27, bf16[256,1024]{1,0:T(8,128)(2,1)} %copy-done.5), kind=kOutput, calls=%fused_computation.29 | convolution fusion | flops 537657344 | bytes 3670016 | tf_op jit(solution)/shard_map/dot_general | solution.py:143
  (11 shorter events, 0.1 us)
Async XLA Ops:
  0.0 66.7 %copy-start = (bf16[1024,1024]{1,0:T(8,128)(2,1)S(1)}, bf16[1024,1024]{1,0:T(8,128)(2,1)}, u32[]{:S(2)}) copy-start(bf16[1024,1024]{1,0:T(8,128)(2,1)} %param.24) | copy-start | bytes 6291460
  0.0 21.8 %copy-start.1 = (bf16[1,512,1024]{2,1,0:T(8,128)(2,1)S(1)}, bf16[1,512,1024]{2,1,0:T(8,128)(2,1)}, u32[]{:S(2)}) copy-start(bf16[1,512,1024]{2,1,0:T(8,128)(2,1)} %param.20) | copy-start | bytes 3145732
  3.5 10.3 %all-to-all-start.1 = ((s32[16,1,64]{2,1,0:T(1,128)}), s32[16,1,64]{2,1,0:T(1,128)S(1)}, u32[]{:S(2)}, u32[]{:S(2)}) async-start(s32[16,1,64]{2,1,0:T(1,128)} %bitcast.10), calls=%async_computation.1 | async-start | bytes 16384 | tf_op jit(solution)/shard_map/all_to_all | solution.py:75
  14.9 31.8 %all-to-all-start = ((bf16[16,16,2048]{2,1,0:T(8,128)(2,1)}), bf16[16,16,2048]{2,1,0:T(8,128)(2,1)}, u32[]{:S(2)}, u32[]{:S(2)}) async-start(bf16[16,16,2048]{2,1,0:T(8,128)(2,1)} %broadcast_in_dim.52), calls=%async_computation | async-start | bytes 2097152 | tf_op jit(solution)/shard_map/all_to_all | solution.py:89
  46.7 5.0 %copy-start.2 = (bf16[16,16,1024]{2,1,0:T(8,128)(2,1)S(1)}, bf16[16,16,1024]{2,1,0:T(8,128)(2,1)}, u32[]{:S(2)}) copy-start(bf16[16,16,1024]{2,1,0:T(8,128)(2,1)} %param.14) | copy-start | bytes 1572868
  46.7 52.6 %all-to-all-start.2 = ((bf16[16,64,1024]{2,1,0:T(8,128)(2,1)}), bf16[16,64,1024]{2,1,0:T(8,128)(2,1)}, u32[]{:S(2)}, u32[]{:S(2)}) async-start(bf16[16,64,1024]{2,1,0:T(8,128)(2,1)} %bitcast.59), calls=%async_computation.2 | async-start | bytes 4194304 | tf_op jit(solution)/shard_map/all_to_all | solution.py:74
  52.2 4.4 %copy-start.6 = (s32[16]{0:T(128)S(1)}, s32[16]{0:T(128)}, u32[]{:S(2)}) copy-start(s32[16]{0:T(128)} %param.16) | copy-start | bytes 196
  64.8 1.0 copy-start.4
  66.7 1.7 %copy-start.8 = (bf16[1024,1024]{1,0:T(8,128)(2,1)S(1)}, bf16[1024,1024]{1,0:T(8,128)(2,1)}, u32[]{:S(2)}) copy-start(bf16[1024,1024]{1,0:T(8,128)(2,1)} %param.26) | copy-start | bytes 6291460
  67.6 0.8 copy-start.5
  105.0 2.8 %copy-start.7 = (bf16[1024,2048]{1,0:T(8,128)(2,1)S(1)}, bf16[1024,2048]{1,0:T(8,128)(2,1)}, u32[]{:S(2)}) copy-start(bf16[1024,2048]{1,0:T(8,128)(2,1)} %param.25) | copy-start | bytes 12582916
  127.9 6.1 %copy-start.3 = (bf16[16,64,16,64]{3,2,1,0:T(8,128)(2,1)S(1)}, bf16[16,64,16,64]{3,2,1,0:T(8,128)(2,1)}, u32[]{:S(2)}) copy-start(bf16[16,64,16,64]{3,2,1,0:T(8,128)(2,1)} %reshape.190) | copy-start | bytes 6291460

commit v3 on v2

--- a/solution.py
+++ b/solution.py
@@ -69,15 +69,21 @@
     token_index = (panel_row % sess_dev * unit_total)[:, None] + unit_slot % unit_limit[:, None]
     slot_pick = owner_rank[None, :] == jnp.arange(owners, dtype=jnp.int32)[:, None]
     request = jnp.sum(jnp.where(slot_pick[:, :, None], token_index[None, :, :], 0), axis=1)
-    live_tokens = jnp.arange(token_total, dtype=jnp.int32)[None, :] < token_count[:, None]
-    panel_table = panels.reshape(sess_dev * unit_total, model_width)
-    arrived = lax.all_to_all(
-        panel_table[lax.all_to_all(request, "smp", split_axis=0, concat_axis=0, tiled=True)],
+    count_pick = jnp.sum(jnp.where(slot_pick, token_count[None, :], 0), axis=1)
+    sample_pick = jnp.sum(
+        jnp.where(slot_pick, jnp.arange(local_samples, dtype=jnp.int32)[None, :], 0), axis=1
+    )
+    served = lax.all_to_all(
+        jnp.concatenate([request, count_pick[:, None]], axis=1),
         "smp",
         split_axis=0,
         concat_axis=0,
         tiled=True,
     )
+    served_index = served[:, :token_total]
+    live_tokens = jnp.arange(token_total, dtype=jnp.int32)[None, :] < served[:, token_total:]
+    panel_table = panels.reshape(sess_dev * unit_total, model_width)
+    served_embed = panel_table[served_index.reshape(-1)]
     row_total = local_samples * latents
     flat_state = state.reshape(row_total, model_width)
     queries = jnp.dot(normed(flat_state), q1_weight, preferred_element_type=jnp.float32).astype(
@@ -121,25 +127,30 @@
         jnp.bfloat16
     )
     queries2 = queries2.reshape(local_samples, latents, model_width)
-    embed = arrived[owner_rank]
+    served_queries = lax.all_to_all(
+        queries2[sample_pick], "smp", split_axis=0, concat_axis=0, tiled=True
+    )
     key_value = jnp.dot(
-        normed(embed.reshape(local_samples * token_total, model_width)),
+        normed(served_embed),
         kv_weight,
         preferred_element_type=jnp.float32,
     ).astype(jnp.bfloat16)
-    key_value = key_value.reshape(local_samples, token_total, 2 * model_width)
-    key_rows = key_value[:, :, :model_width].reshape(
-        local_samples, token_total, head_count, HEAD_DIM
-    )
-    value_rows = key_value[:, :, model_width:].reshape(
-        local_samples, token_total, head_count, HEAD_DIM
-    )
-    read_spike = attend(
-        queries2.reshape(local_samples, latents, head_count, HEAD_DIM),
+    key_value = key_value.reshape(owners, token_total, 2 * model_width)
+    key_rows = key_value[:, :, :model_width].reshape(owners, token_total, head_count, HEAD_DIM)
+    value_rows = key_value[:, :, model_width:].reshape(owners, token_total, head_count, HEAD_DIM)
+    served_read = attend(
+        served_queries.reshape(owners, latents, head_count, HEAD_DIM),
         key_rows,
         value_rows,
         live_tokens,
     )
+    read_spike = lax.all_to_all(
+        served_read.reshape(owners, latents, model_width),
+        "smp",
+        split_axis=0,
+        concat_axis=0,
+        tiled=True,
+    )[owner_rank]
     result = hidden.astype(jnp.float32) + jnp.dot(
         read_spike.reshape(row_total, model_width), o2_weight, preferred_element_type=jnp.float32
     )

time: 142 us -> 128 us (0.901)
  the two profiles are of different devices: /device:TPU:13 before, /device:TPU:0 now
where the time goes in v3:
time: 128 us; the launch traced here: 127 us
  local copies, waits for them, and re-layouts  35.9 us (28%)
  waiting for transfers between devices  28.6 us (22%)
  matrix products  25.6 us (20%)
  starting transfers between devices  24.5 us (19%)
  other arithmetic  12.3 us (10%)
    all_to_all x1, waiting for transfers between devices, per_device(): lax.all_to_all(served_read.reshape(owners, latents, model_width), 'smp',...  14.4 us
    all_to_all x1, waiting for transfers between devices, per_device(): lax.all_to_all(jnp.broadcast_to(memory_pair[None], (owners,) + memory_pai...  9.85 us
    all_to_all x1, starting transfers between devices, per_device(): lax.all_to_all(jnp.concatenate([request, count_pick[:, None]], axis=1), '...  7.39 us
    dot_general x1, matrix products, per_device(): jnp.dot(normed(served_embed), kv_weight, preferred_element_type=jnp.float32)  7.36 us
    all_to_all x1, starting transfers between devices, per_device(): lax.all_to_all(queries2[sample_pick], 'smp', split_axis=0, concat_axis=0,...  6.88 us
    reshape x1, local copies, waits for them, and re-layouts, per_device(): key_value[:, :, :model_width]  6.37 us
    reshape x1, local copies, waits for them, and re-layouts, per_device(): key_value[:, :, model_width:]  6.37 us
    all_to_all x1, starting transfers between devices, per_device(): lax.all_to_all(served_read.reshape(owners, latents, model_width), 'smp',...  5.94 us
  transfers between devices with their start and end apart: 4, of which 3 were waited for; matrix products, arithmetic and copies ran while one was open for 30% of the time, Pallas kernels for 0%

profile of v3, /device:TPU:0, one launch (start us, length us, event | category | flops | bytes accessed | tf_op | source)
XLA Modules:
  0.0 127.3 jit_solution(2849705791000934286)
XLA Ops:
  0.0 0.0 copy-start
  0.0 0.0 copy-start.3
  0.0 1.0 select_reduce_fusion.4
  1.0 0.9 select_reduce_fusion.1
  1.9 0.1 copy.49
  2.0 0.9 add_select_fusion
  2.9 0.1 select_reduce_fusion
  3.0 0.7 pad_add_fusion
  3.7 7.4 %all-to-all-start.1 = ((s32[16,1,65]{2,1,0:T(1,128)}), s32[16,1,65]{2,1,0:T(1,128)S(1)}, u32[]{:S(2)}, u32[]{:S(2)}) async-start(s32[16,1,65]{2,1,0:T(1,128)} %bitcast.10), calls=%async_computation.1 | async-start | bytes 16384 | tf_op jit(solution)/shard_map/all_to_all | solution.py:76
  11.1 0.8 pad_maximum_fusion
  11.9 1.2 multiply_reduce_fusion.1
  13.1 4.3 %all-to-all-done.1 = s32[16,1,65]{2,1,0:T(1,128)S(1)} async-done(((s32[16,1,65]{2,1,0:T(1,128)}), s32[16,1,65]{2,1,0:T(1,128)S(1)}, u32[]{:S(2)}, u32[]{:S(2)}) %all-to-all-start.1) | async-done | bytes 4192 | tf_op jit(solution)/shard_map/all_to_all | solution.py:76
  17.4 1.2 broadcast_in_dim.100
  18.6 4.3 %all-to-all-start = ((bf16[16,16,2048]{2,1,0:T(8,128)(2,1)}), bf16[16,16,2048]{2,1,0:T(8,128)(2,1)}, u32[]{:S(2)}, u32[]{:S(2)}) async-start(bf16[16,16,2048]{2,1,0:T(8,128)(2,1)} %broadcast_in_dim.100), calls=%async_computation | async-start | bytes 2097152 | tf_op jit(solution)/shard_map/all_to_all | solution.py:95
  22.9 0.1 rsqrt.28
  23.0 0.0 copy-done.3
  23.0 0.2 fusion.34
  23.2 0.0 copy-start.1
  23.2 3.2 %convolution_convert_fusion.2 = bf16[256,1024]{1,0:T(8,128)(2,1)} fusion(bf16[256,1024]{1,0:T(8,128)(2,1)S(1)} %fusion.34, bf16[1024,1024]{1,0:T(8,128)(2,1)} %param.23), kind=kOutput, calls=%fused_computation.34 | convolution fusion | flops 537133056 | bytes 3145728 | tf_op jit(solution)/shard_map/dot_general | solution.py:89
  26.4 2.0 %copy.45 = bf16[256,1024]{0,1:T(8,128)(2,1)} copy(bf16[256,1024]{1,0:T(8,128)(2,1)} %convolution_convert_fusion.2) | data formatting | bytes 1048576 | tf_op jit(solution)/shard_map/convert_element_type | solution.py:89
  28.4 0.1 reshape.202
  28.5 0.0 copy-done.1
  28.6 5.4 %gather_fusion = bf16[1024,1024]{1,0:T(8,128)(2,1)} fusion(bf16[512,1024]{1,0:T(8,128)(2,1)S(1)} %bitcast.57, s32[1024]{0:T(1024)S(1)} %broadcast_clamp_fusion), kind=kCustom, calls=%fused_computation | custom fusion | bytes 4198400 | tf_op jit(solution)/shard_map/gather | solution.py:86
  33.9 2.1 %fusion = f32[1024]{0:T(1024)S(1)} fusion(bf16[1024,1024]{1,0:T(8,128)(2,1)} %gather_fusion), kind=kLoop, calls=%fused_computation.5 | loop fusion | flops 3144704 | bytes 2101248 | tf_op jit(solution)/shard_map/reduce_sum | solution.py:14
  36.0 0.0 copy-start.6
  36.0 9.9 %all-to-all-done = bf16[16,16,2048]{2,1,0:T(8,128)(2,1)} async-done(((bf16[16,16,2048]{2,1,0:T(8,128)(2,1)}), bf16[16,16,2048]{2,1,0:T(8,128)(2,1)}, u32[]{:S(2)}, u32[]{:S(2)}) %all-to-all-start) | async-done | bytes 1048608 | tf_op jit(solution)/shard_map/all_to_all | solution.py:95
  45.9 2.2 %fusion.48 = (bf16[256,1024]{1,0:T(8,128)(2,1)}, bf16[256,1024]{1,0:T(8,128)(2,1)}) fusion(bf16[256,2048]{1,0:T(8,128)(2,1)} %bitcast.2), kind=kLoop, calls=%fused_computation.80 | loop fusion | bytes 2097152 | tf_op jit(solution)/shard_map/slice | solution.py:102
  48.1 1.2 copy.46
  49.4 0.0 copy-done.6
  49.4 2.7 %multiply_reduce_fusion = (f32[16,256]{1,0:T(8,128)S(1)}, f32[16,256,256]{1,2,0:T(8,128)}) fusion(bf16[256,16,64]{0,2,1:T(8,128)(2,1)S(1)} %bitcast.60, bf16[256,16,64]{0,2,1:T(8,128)(2,1)S(1)} %bitcast.61), kind=kOutput, calls=%fused_computation.12 | convolution fusion | flops 136310784 | bytes 5259264 | tf_op jit(solution)/shard_map/rhd,khd->hrk/dot_general | solution.py:104
  52.1 1.2 copy.47
  53.3 0.0 copy-start.2
  53.3 3.0 %fusion.6 = f32[16,256]{1,0:T(8,128)S(1)} fusion(f32[16,256,256]{1,2,0:T(8,128)} %get-tuple-element.13, f32[16,256]{1,0:T(8,128)S(1)} %broadcast_maximum_fusion), kind=kLoop, calls=%fused_computation.14 | loop fusion | flops 3141632 | bytes 4227072 | tf_op jit(solution)/shard_map/reduce_sum | solution.py:109
  56.4 0.4 copy-done.2
  56.8 0.0 copy-start.4
  56.8 0.9 fusion.28
  57.6 0.0 copy-start.8
  57.7 0.0 copy-done
  57.7 0.1 copy-done.4
  57.8 0.8 fusion.31
  58.7 0.8 copy-done.7
  59.5 0.0 copy-done.8
  59.5 0.8 convolution_convert_fusion.1
  60.3 1.4 %gather_fusion.1 = bf16[16,16,1024]{2,1,0:T(8,128)(2,1)} fusion(bf16[16,16,1024]{2,1,0:T(8,128)(2,1)S(1)} %bitcast.64, s32[1024]{0:T(1024)S(1)} %pad_clamp_fusion.1), kind=kCustom, calls=%fused_computation.1 | custom fusion | bytes 1048640 | tf_op jit(solution)/shard_map/gather | solution.py:131
  61.6 6.9 %all-to-all-start.2 = ((bf16[16,16,1024]{2,1,0:T(8,128)(2,1)}), bf16[16,16,1024]{2,1,0:T(8,128)(2,1)}, u32[]{:S(2)}, u32[]{:S(2)}) async-start(bf16[16,16,1024]{2,1,0:T(8,128)(2,1)} %gather_fusion.1), calls=%async_computation.2 | async-start | bytes 1048576 | tf_op jit(solution)/shard_map/all_to_all | solution.py:130
  68.5 7.4 %convolution_convert_fusion = bf16[1024,2048]{1,0:T(8,128)(2,1)S(1)} fusion(bf16[1024,2048]{1,0:T(8,128)(2,1)} %param.25, bf16[1024,1024]{1,0:T(8,128)(2,1)} %gather_fusion, f32[1024]{0:T(1024)S(1)} %add_rsqrt_fusion.1), kind=kOutput, calls=%fused_computation.13 | convolution fusion | flops 4300210176 | bytes 10489856 | tf_op jit(solution)/shard_map/dot_general | solution.py:133
  75.9 2.6 %fusion.47 = (bf16[16,64,1024]{2,1,0:T(8,128)(2,1)}, bf16[16,64,1024]{2,1,0:T(8,128)(2,1)}) fusion(bf16[16,64,2048]{2,1,0:T(8,128)(2,1)S(1)} %bitcast.59), kind=kLoop, calls=%fused_computation.79 | loop fusion | bytes 8388608 | tf_op jit(solution)/shard_map/slice | solution.py:139
  78.5 6.4 %reshape.207 = bf16[16,64,16,64]{3,2,1,0:T(8,128)(2,1)} reshape(bf16[16,64,1024]{2,1,0:T(8,128)(2,1)} %get-tuple-element.8) | data formatting | bytes 4194304 | tf_op jit(solution)/shard_map/reshape | solution.py:139
  84.8 6.4 %reshape.204 = bf16[16,64,16,64]{3,2,1,0:T(8,128)(2,1)} reshape(bf16[16,64,1024]{2,1,0:T(8,128)(2,1)} %get-tuple-element.9) | data formatting | bytes 4194304 | tf_op jit(solution)/shard_map/reshape | solution.py:140
  91.2 0.2 slice_reduce_fusion
  91.4 0.1 iota_compare_fusion
  91.5 0.0 all-to-all-done.2
  91.5 1.8 %reshape.206 = bf16[16,16,16,64]{3,2,1,0:T(8,128)(2,1)S(1)} reshape(bf16[16,16,1024]{2,1,0:T(8,128)(2,1)} %all-to-all-done.2) | data formatting | bytes 1048576 | tf_op jit(solution)/shard_map/reshape | solution.py:142
  93.2 0.0 copy-start.5
  93.2 4.7 %fusion.15 = (f32[16,16,16]{2,1,0:T(8,128)S(1)}, f32[16,16,16,64]{3,2,1,0:T(8,128)S(1)}) fusion(pred[16,64]{1,0:T(8,128)(4,1)S(1)} %iota_compare_fusion, bf16[16,64,16,64]{3,2,1,0:T(8,128)(2,1)} %reshape.207, bf16[16,16,16,64]{3,2,1,0:T(8,128)(2,1)S(1)} %reshape.206), kind=kOutput, calls=%fused_computation.24 | convolution fusion | flops 34336768 | bytes 3687424 | tf_op jit(solution)/shard_map/blhd,bkhd->bhlk/dot_general | solution.py:21
  97.9 1.3 %fusion.18 = f32[16,16,16]{2,1,0:T(8,128)S(1)} fusion(f32[16,16,16,64]{3,2,1,0:T(8,128)S(1)} %get-tuple-element.17, f32[16,16,16]{2,1,0:T(8,128)S(1)} %get-tuple-element.16, pred[16,64]{1,0:T(8,128)(4,1)S(1)} %iota_compare_fusion), kind=kLoop, calls=%fused_computation.25 | loop fusion | flops 1044480 | bytes 1082368 | tf_op jit(solution)/shard_map/reduce_sum | solution.py:27
  99.3 0.0 copy-done.5
  99.3 2.0 %fusion.11 = bf16[16,16,16,64]{3,1,2,0:T(8,128)(2,1)S(1)} fusion(bf16[16,64,16,64]{3,2,1,0:T(8,128)(2,1)S(1)} %copy-done.5, f32[16,16,16,64]{3,2,1,0:T(8,128)S(1)} %get-tuple-element.17, f32[16,16,16]{1,2,0:T(8,128)S(1)} %bitcast.66, f32[16,16,16]{2,1,0:T(8,128)S(1)} %get-tuple-element.16, pred[16,64]{1,0:T(8,128)(4,1)S(1)} %iota_compare_fusion), kind=kOutput, calls=%fused_computation.18 | convolution fusion | flops 35127296 | bytes 3703808 | tf_op jit(solution)/shard_map/bhlk,bkhd->blhd/dot_general | solution.py:29
  101.3 0.3 copy.53
  101.6 1.5 %convert_element_type.76 = bf16[16,16,1024]{2,1,0:T(8,128)(2,1)} reshape(bf16[16,16,16,64]{3,2,1,0:T(8,128)(2,1)S(1)} %copy.53) | data formatting | bytes 1048576 | tf_op jit(solution)/shard_map/convert_element_type | solution.py:37
  103.1 5.9 %all-to-all-start.3 = ((bf16[16,16,1024]{2,1,0:T(8,128)(2,1)}), bf16[16,16,1024]{2,1,0:T(8,128)(2,1)S(1)}, u32[]{:S(2)}, u32[]{:S(2)}) async-start(bf16[16,16,1024]{2,1,0:T(8,128)(2,1)} %convert_element_type.76), calls=%async_computation.3 | async-start | bytes 1048576 | tf_op jit(solution)/shard_map/all_to_all | solution.py:147
  109.1 14.4 %all-to-all-done.3 = bf16[16,16,1024]{2,1,0:T(8,128)(2,1)S(1)} async-done(((bf16[16,16,1024]{2,1,0:T(8,128)(2,1)}), bf16[16,16,1024]{2,1,0:T(8,128)(2,1)S(1)}, u32[]{:S(2)}, u32[]{:S(2)}) %all-to-all-start.3) | async-done | bytes 524320 | tf_op jit(solution)/shard_map/all_to_all | solution.py:147
  123.5 0.6 gather_fusion.2
  124.1 3.2 %fusion.23 = bf16[256,1024]{1,0:T(8,128)(2,1)} fusion(bf16[256,1024]{1,0:T(8,128)(2,1)S(1)} %bitcast.63, bf16[1024,1024]{1,0:T(8,128)(2,1)} %param.27, bf16[256,1024]{1,0:T(8,128)(2,1)} %copy-done.7), kind=kOutput, calls=%fused_computation.32 | convolution fusion | flops 537657344 | bytes 3670016 | tf_op jit(solution)/shard_map/dot_general | solution.py:154
  (14 shorter events, 0.1 us)
Async XLA Ops:
  0.0 57.7 %copy-start = (bf16[1024,1024]{1,0:T(8,128)(2,1)S(1)}, bf16[1024,1024]{1,0:T(8,128)(2,1)}, u32[]{:S(2)}) copy-start(bf16[1024,1024]{1,0:T(8,128)(2,1)} %param.24) | copy-start | bytes 6291460
  0.0 23.0 %copy-start.3 = (bf16[16,16,1024]{2,1,0:T(8,128)(2,1)S(1)}, bf16[16,16,1024]{2,1,0:T(8,128)(2,1)}, u32[]{:S(2)}) copy-start(bf16[16,16,1024]{2,1,0:T(8,128)(2,1)} %param.14) | copy-start | bytes 1572868
  3.7 13.7 %all-to-all-start.1 = ((s32[16,1,65]{2,1,0:T(1,128)}), s32[16,1,65]{2,1,0:T(1,128)S(1)}, u32[]{:S(2)}, u32[]{:S(2)}) async-start(s32[16,1,65]{2,1,0:T(1,128)} %bitcast.10), calls=%async_computation.1 | async-start | bytes 16384 | tf_op jit(solution)/shard_map/all_to_all | solution.py:76
  18.6 27.3 %all-to-all-start = ((bf16[16,16,2048]{2,1,0:T(8,128)(2,1)}), bf16[16,16,2048]{2,1,0:T(8,128)(2,1)}, u32[]{:S(2)}, u32[]{:S(2)}) async-start(bf16[16,16,2048]{2,1,0:T(8,128)(2,1)} %broadcast_in_dim.100), calls=%async_computation | async-start | bytes 2097152 | tf_op jit(solution)/shard_map/all_to_all | solution.py:95
  23.2 5.4 %copy-start.1 = (bf16[1,512,1024]{2,1,0:T(8,128)(2,1)S(1)}, bf16[1,512,1024]{2,1,0:T(8,128)(2,1)}, u32[]{:S(2)}) copy-start(bf16[1,512,1024]{2,1,0:T(8,128)(2,1)} %param.20) | copy-start | bytes 3145732
  36.0 13.4 %copy-start.6 = (bf16[256,1024]{0,1:T(8,128)(2,1)S(1)}, bf16[256,1024]{0,1:T(8,128)(2,1)}, u32[]{:S(2)}) copy-start(bf16[256,1024]{0,1:T(8,128)(2,1)} %copy.45) | copy-start | bytes 1572868
  53.3 3.5 %copy-start.2 = (f32[16,256,256]{1,2,0:T(8,128)S(1)}, f32[16,256,256]{1,2,0:T(8,128)}, u32[]{:S(2)}) copy-start(f32[16,256,256]{1,2,0:T(8,128)} %get-tuple-element.13) | copy-start | bytes 12582916
  56.8 1.0 copy-start.4
  57.6 1.8 %copy-start.8 = (bf16[1024,1024]{1,0:T(8,128)(2,1)S(1)}, bf16[1024,1024]{1,0:T(8,128)(2,1)}, u32[]{:S(2)}) copy-start(bf16[1024,1024]{1,0:T(8,128)(2,1)} %param.26) | copy-start | bytes 6291460
  58.6 0.8 copy-start.7
  61.6 29.8 %all-to-all-start.2 = ((bf16[16,16,1024]{2,1,0:T(8,128)(2,1)}), bf16[16,16,1024]{2,1,0:T(8,128)(2,1)}, u32[]{:S(2)}, u32[]{:S(2)}) async-start(bf16[16,16,1024]{2,1,0:T(8,128)(2,1)} %gather_fusion.1), calls=%async_computation.2 | async-start | bytes 1048576 | tf_op jit(solution)/shard_map/all_to_all | solution.py:130
  93.2 6.1 %copy-start.5 = (bf16[16,64,16,64]{3,2,1,0:T(8,128)(2,1)S(1)}, bf16[16,64,16,64]{3,2,1,0:T(8,128)(2,1)}, u32[]{:S(2)}) copy-start(bf16[16,64,16,64]{3,2,1,0:T(8,128)(2,1)} %reshape.204) | copy-start | bytes 6291460
  103.1 20.4 %all-to-all-start.3 = ((bf16[16,16,1024]{2,1,0:T(8,128)(2,1)}), bf16[16,16,1024]{2,1,0:T(8,128)(2,1)S(1)}, u32[]{:S(2)}, u32[]{:S(2)}) async-start(bf16[16,16,1024]{2,1,0:T(8,128)(2,1)} %convert_element_type.76), calls=%async_computation.3 | async-start | bytes 1048576 | tf_op jit(solution)/shard_map/all_to_all | solution.py:147

commit v4 on v3

--- a/solution.py
+++ b/solution.py
@@ -1,6 +1,8 @@
 import jax
 import jax.numpy as jnp
 from jax import lax
+from jax.experimental import pallas as pl
+from jax.experimental.pallas import tpu as pltpu
 from jax.sharding import PartitionSpec as P
 
 HEAD_DIM = 64
@@ -35,6 +37,55 @@
         / denominator
     )
     return spike_mix.reshape(samples, latents, head_count * head_size).astype(jnp.bfloat16)
+
+
+def attend_block(counts_ref, query_ref, key_ref, value_ref, out_ref):
+    group = pl.program_id(0)
+    latents = query_ref.shape[1]
+    tokens = key_ref.shape[1]
+    live = lax.broadcasted_iota(jnp.int32, (latents, tokens), 1) < counts_ref[group]
+    first_head = lax.broadcasted_iota(jnp.int32, (1, 2 * HEAD_DIM), 1) < HEAD_DIM
+    for pair in range(query_ref.shape[2] // (2 * HEAD_DIM)):
+        cols = pl.ds(pair * 2 * HEAD_DIM, 2 * HEAD_DIM)
+        query = query_ref[0, :, cols]
+        key = key_ref[0, :, cols]
+        value = value_ref[0, :, cols]
+        mixes = []
+        for half in (first_head, jnp.logical_not(first_head)):
+            scores = lax.dot_general(
+                jnp.where(half, query, jnp.zeros_like(query)),
+                key,
+                (((1,), (1,)), ((), ())),
+                preferred_element_type=jnp.float32,
+            ) * HEAD_DIM ** (-0.5)
+            scores = jnp.where(live, scores, masked_score)
+            row_max = jnp.max(scores, axis=1, keepdims=True)
+            exponent = jnp.exp(scores - row_max)
+            denominator = jnp.sum(exponent, axis=1, keepdims=True)
+            mix = jnp.dot(
+                exponent.astype(jnp.bfloat16), value, preferred_element_type=jnp.float32
+            )
+            mixes.append(mix / denominator)
+        out_ref[0, :, cols] = jnp.where(first_head, mixes[0], mixes[1]).astype(jnp.bfloat16)
+
+
+def attend_kernel(queries, key_value, counts):
+    groups, latents, width = queries.shape
+    tokens = key_value.shape[1]
+    return pl.pallas_call(
+        attend_block,
+        grid_spec=pltpu.PrefetchScalarGridSpec(
+            num_scalar_prefetch=1,
+            grid=(groups,),
+            in_specs=[
+                pl.BlockSpec((1, latents, width), lambda g, c: (g, 0, 0)),
+                pl.BlockSpec((1, tokens, width), lambda g, c: (g, 0, 0)),
+                pl.BlockSpec((1, tokens, width), lambda g, c: (g, 0, 1)),
+            ],
+            out_specs=pl.BlockSpec((1, latents, width), lambda g, c: (g, 0, 0)),
+        ),
+        out_shape=jax.ShapeDtypeStruct((groups, latents, width), jnp.bfloat16),
+    )(counts, queries, key_value, key_value)
 
 
 def per_device(
@@ -81,7 +132,6 @@
         tiled=True,
     )
     served_index = served[:, :token_total]
-    live_tokens = jnp.arange(token_total, dtype=jnp.int32)[None, :] < served[:, token_total:]
     panel_table = panels.reshape(sess_dev * unit_total, model_width)
     served_embed = panel_table[served_index.reshape(-1)]
     row_total = local_samples * latents
@@ -89,8 +139,6 @@
     queries = jnp.dot(normed(flat_state), q1_weight, preferred_element_type=jnp.float32).astype(
         jnp.bfloat16
     )
-    queries = queries.reshape(row_total, head_count, HEAD_DIM)
-    running_max = jnp.full((head_count, row_total), masked_score, jnp.float32)
     memory_pair = jnp.concatenate([memory_key, memory_value], axis=1)
     memory_rows = lax.all_to_all(
         jnp.broadcast_to(memory_pair[None], (owners,) + memory_pair.shape),
@@ -98,27 +146,13 @@
         split_axis=0,
         concat_axis=0,
         tiled=True,
-    ).reshape(-1, 2 * model_width)
-    key_rows = memory_rows[:, :model_width].reshape(-1, head_count, HEAD_DIM)
-    value_rows = memory_rows[:, model_width:].reshape(-1, head_count, HEAD_DIM)
-    scores = jnp.einsum(
-        "rhd,khd->hrk", queries, key_rows, preferred_element_type=jnp.float32
-    ) * HEAD_DIM ** (-0.5)
-    new_max = jnp.maximum(running_max, jnp.max(scores, axis=-1))
-    exponent = jnp.exp(scores - new_max[:, :, None])
-    denominator = jnp.sum(exponent, axis=-1)
-    weighted = jnp.einsum(
-        "hrk,khd->hrd",
-        exponent.astype(jnp.bfloat16),
-        value_rows,
-        preferred_element_type=jnp.float32,
-    )
-    running_max, denominator, weighted = (new_max, denominator, weighted)
-    read_mem = (
-        jnp.transpose(weighted / denominator[:, :, None], (1, 0, 2))
-        .reshape(row_total, model_width)
-        .astype(jnp.bfloat16)
-    )
+    ).reshape(1, -1, 2 * model_width)
+    memory_total = memory_rows.shape[1]
+    read_mem = attend_kernel(
+        queries.reshape(1, row_total, model_width),
+        memory_rows,
+        jnp.full((1,), memory_total, jnp.int32),
+    ).reshape(row_total, model_width)
     hidden = (
         flat_state.astype(jnp.float32)
         + jnp.dot(read_mem, o1_weight, preferred_element_type=jnp.float32)
@@ -136,14 +170,7 @@
         preferred_element_type=jnp.float32,
     ).astype(jnp.bfloat16)
     key_value = key_value.reshape(owners, token_total, 2 * model_width)
-    key_rows = key_value[:, :, :model_width].reshape(owners, token_total, head_count, HEAD_DIM)
-    value_rows = key_value[:, :, model_width:].reshape(owners, token_total, head_count, HEAD_DIM)
-    served_read = attend(
-        served_queries.reshape(owners, latents, head_count, HEAD_DIM),
-        key_rows,
-        value_rows,
-        live_tokens,
-    )
+    served_read = attend_kernel(served_queries, key_value, served[:, token_total])
     read_spike = lax.all_to_all(
         served_read.reshape(owners, latents, model_width),
         "smp",

time: 128 us -> 159 us (1.24)
  Pallas kernels: 0 us -> 63.9 us
  local copies, waits for them, and re-layouts: 35.9 us -> 10.3 us
  matrix products: 25.6 us -> 18.4 us
  waiting for transfers between devices: 28.6 us -> 34 us
  other arithmetic: 12.3 us -> 8.99 us
  starting transfers between devices: 24.5 us -> 22.6 us
    pallas_call x0 -> x2, Pallas kernels: none -> 63.9 us  [attend_kernel(): pl.pallas_call(attend_block, grid_spec=pltpu.PrefetchScalarGridSpec(num_s...]
    reshape x3 -> x0, local copies, waits for them, and re-layouts: 14.5 us -> none  [the longest x1 6.37 us: per_device(): key_value[:, :, :model_width]]
    dot_general x4 -> x0, matrix products: 10.2 us -> none  [the longest x1 4.7 us: attend(): jnp.einsum('blhd,bkhd->bhlk', queries, key_rows, preferred_element_type=j...]
    slice x5 -> x1, local copies, waits for them, and re-layouts: 7.49 us -> 0.78 us  [per_device(): served[:, token_total]]
    all_to_all x1, waiting for transfers between devices: 0.01 us -> 4.4 us  [per_device(): lax.all_to_all(queries2[sample_pick], 'smp', split_axis=0, concat_axis=0,...]
    reduce_sum x2 -> x0, other arithmetic: 4.39 us -> none  [the longest x1 3.05 us: per_device(): denominator = jnp.sum(exponent, axis=-1)]
    convert_element_type x3 -> x0, local copies, waits for them, and re-layouts: 3.83 us -> none  [the longest x1 2.04 us: per_device(): jnp.dot(normed(flat_state), q1_weight, preferred_element_type=jnp.float32)]
    dot_general x1, matrix products: 7.36 us -> 9.29 us  [per_device(): jnp.dot(normed(served_embed), kv_weight, preferred_element_type=jnp.float32)]
  transfers between devices with their start and end apart: 4 -> 4, of which waited for: 3 -> 4; matrix products, arithmetic and copies ran while one was open for 30% -> 15% of each run, Pallas kernels for 0% -> 0%
where the time goes in v4:
time: 159 us; the launch traced here: 158 us
  Pallas kernels  63.9 us (40%)
  waiting for transfers between devices  34 us (21%)
  starting transfers between devices  22.6 us (14%)
  matrix products  18.4 us (12%)
  local copies, waits for them, and re-layouts  10.3 us (6%)
  other arithmetic  8.99 us (6%)
    pallas_call x2, Pallas kernels, attend_kernel(): pl.pallas_call(attend_block, grid_spec=pltpu.PrefetchScalarGridSpec(num_s...  63.9 us
    all_to_all x1, waiting for transfers between devices, per_device(): lax.all_to_all(served_read.reshape(owners, latents, model_width), 'smp',...  14.4 us
    all_to_all x1, waiting for transfers between devices, per_device(): lax.all_to_all(jnp.broadcast_to(memory_pair[None], (owners,) + memory_pai...  10.8 us
    dot_general x1, matrix products, per_device(): jnp.dot(normed(served_embed), kv_weight, preferred_element_type=jnp.float32)  9.29 us
    all_to_all x1, starting transfers between devices, per_device(): lax.all_to_all(jnp.concatenate([request, count_pick[:, None]], axis=1), '...  7.39 us
    all_to_all x1, starting transfers between devices, per_device(): lax.all_to_all(queries2[sample_pick], 'smp', split_axis=0, concat_axis=0,...  6.81 us
    gather x1, local copies, waits for them, and re-layouts, per_device(): served_embed = panel_table[served_index.reshape(-1)]  5.37 us
    all_to_all x1, waiting for transfers between devices, per_device(): lax.all_to_all(queries2[sample_pick], 'smp', split_axis=0, concat_axis=0,...  4.4 us
  transfers between devices with their start and end apart: 4, of which 4 were waited for; matrix products, arithmetic and copies ran while one was open for 15% of the time, Pallas kernels for 0%

profile of v4, /device:TPU:0, one launch (start us, length us, event | category | flops | bytes accessed | tf_op | source)
XLA Modules:
  0.0 158.5 jit_solution(5801784580853881685)
XLA Ops:
  0.0 0.0 copy-start
  0.0 1.0 select_reduce_fusion.4
  1.0 0.9 select_reduce_fusion.1
  1.9 0.1 copy.18
  2.0 0.9 add_select_fusion
  2.9 0.1 select_reduce_fusion
  3.0 0.7 pad_add_fusion
  3.7 7.4 %all-to-all-start.1 = ((s32[16,1,65]{2,1,0:T(1,128)}), s32[16,1,65]{2,1,0:T(1,128)S(1)}, u32[]{:S(2)}, u32[]{:S(2)}) async-start(s32[16,1,65]{2,1,0:T(1,128)} %bitcast.6), calls=%async_computation.1 | async-start | bytes 16384 | tf_op jit(solution)/shard_map/all_to_all | solution.py:127
  11.1 0.8 pad_maximum_fusion
  11.9 1.2 multiply_reduce_fusion
  13.1 4.3 %all-to-all-done.1 = s32[16,1,65]{2,1,0:T(1,128)S(1)} async-done(((s32[16,1,65]{2,1,0:T(1,128)}), s32[16,1,65]{2,1,0:T(1,128)S(1)}, u32[]{:S(2)}, u32[]{:S(2)}) %all-to-all-start.1) | async-done | bytes 4192 | tf_op jit(solution)/shard_map/all_to_all | solution.py:127
  17.4 1.2 broadcast_in_dim.77
  18.6 4.3 %all-to-all-start = ((bf16[16,16,2048]{2,1,0:T(8,128)(2,1)}), bf16[16,16,2048]{2,1,0:T(8,128)(2,1)}, u32[]{:S(2)}, u32[]{:S(2)}) async-start(bf16[16,16,2048]{2,1,0:T(8,128)(2,1)} %broadcast_in_dim.77), calls=%async_computation | async-start | bytes 2097152 | tf_op jit(solution)/shard_map/all_to_all | solution.py:143
  22.9 0.1 rsqrt.28
  23.0 0.0 copy-start.1
  23.1 1.3 fusion.9
  24.3 3.1 %fusion.6.query_ref = bf16[1,256,1024]{2,1,0:T(8,128)(2,1)} fusion(bf16[256,1024]{1,0:T(8,128)(2,1)S(1)} %fusion.9, bf16[1024,1024]{1,0:T(8,128)(2,1)} %param.23), kind=kOutput, calls=%fused_computation.17 | convolution fusion | flops 537133056 | bytes 3145728 | tf_op jit(solution)/shard_map/dot_general | solution.py:139
  27.5 0.1 reshape.163
  27.6 0.0 copy-done.1
  27.6 5.4 %gather_fusion.1 = bf16[1024,1024]{1,0:T(8,128)(2,1)} fusion(bf16[512,1024]{1,0:T(8,128)(2,1)S(1)} %bitcast.40, s32[1024]{0:T(1024)S(1)} %broadcast_clamp_fusion), kind=kCustom, calls=%fused_computation.1 | custom fusion | bytes 4198400 | tf_op jit(solution)/shard_map/gather | solution.py:136
  33.0 2.1 %fusion = f32[1024]{0:T(1024)S(1)} fusion(bf16[1024,1024]{1,0:T(8,128)(2,1)} %gather_fusion.1), kind=kLoop, calls=%fused_computation.5 | loop fusion | flops 3144704 | bytes 2101248 | tf_op jit(solution)/shard_map/reduce_sum | solution.py:16
  35.0 0.0 copy-start.3
  35.0 10.8 %all-to-all-done = bf16[16,16,2048]{2,1,0:T(8,128)(2,1)} async-done(((bf16[16,16,2048]{2,1,0:T(8,128)(2,1)}), bf16[16,16,2048]{2,1,0:T(8,128)(2,1)}, u32[]{:S(2)}, u32[]{:S(2)}) %all-to-all-start) | async-done | bytes 1048608 | tf_op jit(solution)/shard_map/all_to_all | solution.py:143
  45.9 4.1 %shard_map.136 = bf16[1,256,1024]{2,1,0:T(8,128)(2,1)} custom-call(s32[1]{0:T(128)} %constant.45.clone.1.counts_ref, bf16[1,256,1024]{2,1,0:T(8,128)(2,1)} %fusion.6.query_ref, bf16[1,256,2048]{2,1,0:T(8,128)(2,1)} %bitcast.2.key_ref.value_ref, bf16[1,256,2048]{2,1,0:T(8,128)(2,1)} %bitcast.2.key_ref.value_ref), custom_call_target="tpu_custom_call" | custom-call | tf_op jit(solution)/shard_map/pallas_call | solution.py:75
  50.0 0.0 copy-done
  50.0 0.0 copy-done.3
  50.0 0.0 copy-start.4
  50.0 2.0 %fusion.7 = (f32[256]{0:T(256)S(1)}, bf16[256,1024]{1,0:T(8,128)(2,1)S(1)}) fusion(bf16[1024,1024]{1,0:T(8,128)(2,1)S(1)} %copy-done, bf16[1,256,1024]{2,1,0:T(8,128)(2,1)} %shard_map.136, bf16[256,1024]{1,0:T(8,128)(2,1)S(1)} %bitcast.43), kind=kOutput, calls=%fused_computation.18 | convolution fusion | flops 538443520 | bytes 3671040 | tf_op jit(solution)/shard_map/dot_general | solution.py:158
  52.0 0.0 copy-start.5
  52.1 0.0 copy-done.4
  52.1 0.8 convolution_convert_fusion.1
  52.8 0.0 copy-done.5
  52.8 1.4 gather_fusion
  54.2 6.8 %all-to-all-start.2 = ((bf16[16,16,1024]{2,1,0:T(8,128)(2,1)}), bf16[16,16,1024]{2,1,0:T(8,128)(2,1)S(1)}, u32[]{:S(2)}, u32[]{:S(2)}) async-start(bf16[16,16,1024]{2,1,0:T(8,128)(2,1)} %gather_fusion), calls=%async_computation.2 | async-start | bytes 1048576 | tf_op jit(solution)/shard_map/all_to_all | solution.py:164
  61.0 0.8 slice_reduce_fusion.counts_ref
  61.8 9.3 %convolution_convert_fusion = bf16[1024,2048]{1,0:T(8,128)(2,1)} fusion(bf16[1024,2048]{1,0:T(8,128)(2,1)} %param.25, bf16[1024,1024]{1,0:T(8,128)(2,1)} %gather_fusion.1, f32[1024]{0:T(1024)S(1)} %add_rsqrt_fusion.1), kind=kOutput, calls=%fused_computation.7 | convolution fusion | flops 4300210176 | bytes 10489856 | tf_op jit(solution)/shard_map/dot_general | solution.py:167
  71.1 4.4 %all-to-all-done.2.query_ref = bf16[16,16,1024]{2,1,0:T(8,128)(2,1)S(1)} async-done(((bf16[16,16,1024]{2,1,0:T(8,128)(2,1)}), bf16[16,16,1024]{2,1,0:T(8,128)(2,1)S(1)}, u32[]{:S(2)}, u32[]{:S(2)}) %all-to-all-start.2) | async-done | bytes 524320 | tf_op jit(solution)/shard_map/all_to_all | solution.py:164
  75.5 0.0 copy-start.2
  75.5 0.8 copy-done.2
  76.3 59.8 %shard_map.137 = bf16[16,16,1024]{2,1,0:T(8,128)(2,1)} custom-call(s32[16]{0:T(128)} %slice_reduce_fusion.counts_ref, bf16[16,16,1024]{2,1,0:T(8,128)(2,1)} %copy-done.2, bf16[16,64,2048]{2,1,0:T(8,128)(2,1)} %bitcast.41, bf16[16,64,2048]{2,1,0:T(8,128)(2,1)} %bitcast.42), custom_call_target="tpu_custom_call" | custom-call | tf_op jit(solution)/shard_map/pallas_call | solution.py:75
  136.1 4.1 %all-to-all-start.3 = ((bf16[16,16,1024]{2,1,0:T(8,128)(2,1)}), bf16[16,16,1024]{2,1,0:T(8,128)(2,1)S(1)}, u32[]{:S(2)}, u32[]{:S(2)}) async-start(bf16[16,16,1024]{2,1,0:T(8,128)(2,1)} %shard_map.137), calls=%async_computation.3 | async-start | bytes 1048576 | tf_op jit(solution)/shard_map/all_to_all | solution.py:174
  140.2 14.4 %all-to-all-done.3 = bf16[16,16,1024]{2,1,0:T(8,128)(2,1)S(1)} async-done(((bf16[16,16,1024]{2,1,0:T(8,128)(2,1)}), bf16[16,16,1024]{2,1,0:T(8,128)(2,1)S(1)}, u32[]{:S(2)}, u32[]{:S(2)}) %all-to-all-start.3) | async-done | bytes 524320 | tf_op jit(solution)/shard_map/all_to_all | solution.py:174
  154.7 0.6 gather_fusion.2
  155.3 3.2 %fusion.4 = bf16[256,1024]{1,0:T(8,128)(2,1)} fusion(bf16[256,1024]{1,0:T(8,128)(2,1)S(1)} %bitcast.44, bf16[1024,1024]{1,0:T(8,128)(2,1)} %param.27, bf16[256,1024]{1,0:T(8,128)(2,1)} %copy-done.5), kind=kOutput, calls=%fused_computation.13 | convolution fusion | flops 537657344 | bytes 3670016 | tf_op jit(solution)/shard_map/dot_general | solution.py:181
  (12 shorter events, 0.1 us)
Async XLA Ops:
  0.0 50.0 %copy-start = (bf16[1024,1024]{1,0:T(8,128)(2,1)S(1)}, bf16[1024,1024]{1,0:T(8,128)(2,1)}, u32[]{:S(2)}) copy-start(bf16[1024,1024]{1,0:T(8,128)(2,1)} %param.24) | copy-start | bytes 6291460
  3.7 13.7 %all-to-all-start.1 = ((s32[16,1,65]{2,1,0:T(1,128)}), s32[16,1,65]{2,1,0:T(1,128)S(1)}, u32[]{:S(2)}, u32[]{:S(2)}) async-start(s32[16,1,65]{2,1,0:T(1,128)} %bitcast.6), calls=%async_computation.1 | async-start | bytes 16384 | tf_op jit(solution)/shard_map/all_to_all | solution.py:127
  18.6 27.3 %all-to-all-start = ((bf16[16,16,2048]{2,1,0:T(8,128)(2,1)}), bf16[16,16,2048]{2,1,0:T(8,128)(2,1)}, u32[]{:S(2)}, u32[]{:S(2)}) async-start(bf16[16,16,2048]{2,1,0:T(8,128)(2,1)} %broadcast_in_dim.77), calls=%async_computation | async-start | bytes 2097152 | tf_op jit(solution)/shard_map/all_to_all | solution.py:143
  23.0 4.5 %copy-start.1 = (bf16[1,512,1024]{2,1,0:T(8,128)(2,1)S(1)}, bf16[1,512,1024]{2,1,0:T(8,128)(2,1)}, u32[]{:S(2)}) copy-start(bf16[1,512,1024]{2,1,0:T(8,128)(2,1)} %param.20) | copy-start | bytes 3145732
  35.0 15.0 %copy-start.3 = (bf16[16,16,1024]{2,1,0:T(8,128)(2,1)S(1)}, bf16[16,16,1024]{2,1,0:T(8,128)(2,1)}, u32[]{:S(2)}) copy-start(bf16[16,16,1024]{2,1,0:T(8,128)(2,1)} %param.14) | copy-start | bytes 1572868
  50.0 2.0 %copy-start.4 = (bf16[1024,1024]{1,0:T(8,128)(2,1)S(1)}, bf16[1024,1024]{1,0:T(8,128)(2,1)}, u32[]{:S(2)}) copy-start(bf16[1024,1024]{1,0:T(8,128)(2,1)} %param.26) | copy-start | bytes 6291460
  52.0 0.8 copy-start.5
  54.2 21.3 %all-to-all-start.2 = ((bf16[16,16,1024]{2,1,0:T(8,128)(2,1)}), bf16[16,16,1024]{2,1,0:T(8,128)(2,1)S(1)}, u32[]{:S(2)}, u32[]{:S(2)}) async-start(bf16[16,16,1024]{2,1,0:T(8,128)(2,1)} %gather_fusion), calls=%async_computation.2 | async-start | bytes 1048576 | tf_op jit(solution)/shard_map/all_to_all | solution.py:164
  75.5 0.8 copy-start.2
  136.1 18.6 %all-to-all-start.3 = ((bf16[16,16,1024]{2,1,0:T(8,128)(2,1)}), bf16[16,16,1024]{2,1,0:T(8,128)(2,1)S(1)}, u32[]{:S(2)}, u32[]{:S(2)}) async-start(bf16[16,16,1024]{2,1,0:T(8,128)(2,1)} %shard_map.137), calls=%async_computation.3 | async-start | bytes 1048576 | tf_op jit(solution)/shard_map/all_to_all | solution.py:174

commit v5 on v4

--- a/solution.py
+++ b/solution.py
@@ -170,7 +170,15 @@
         preferred_element_type=jnp.float32,
     ).astype(jnp.bfloat16)
     key_value = key_value.reshape(owners, token_total, 2 * model_width)
-    served_read = attend_kernel(served_queries, key_value, served[:, token_total])
+    key_rows = key_value[:, :, :model_width].reshape(owners, token_total, head_count, HEAD_DIM)
+    value_rows = key_value[:, :, model_width:].reshape(owners, token_total, head_count, HEAD_DIM)
+    live_tokens = jnp.arange(token_total, dtype=jnp.int32)[None, :] < served[:, token_total:]
+    served_read = attend(
+        served_queries.reshape(owners, latents, head_count, HEAD_DIM),
+        key_rows,
+        value_rows,
+        live_tokens,
+    )
     read_spike = lax.all_to_all(
         served_read.reshape(owners, latents, model_width),
         "smp",

time: 159 us -> 121 us (0.76)
  Pallas kernels: 63.9 us -> 4.11 us
  local copies, waits for them, and re-layouts: 10.3 us -> 27.7 us
  matrix products: 18.4 us -> 23.1 us
  waiting for transfers between devices: 34 us -> 29.6 us
  starting transfers between devices: 22.6 us -> 24.5 us
    pallas_call x2 -> x1, Pallas kernels: 63.9 us -> 4.11 us  [attend_kernel(): pl.pallas_call(attend_block, grid_spec=pltpu.PrefetchScalarGridSpec(num_s...]
    reshape x0 -> x3, local copies, waits for them, and re-layouts: none -> 14.5 us  [the longest x1 6.37 us: per_device(): key_value[:, :, :model_width]]
    dot_general x0 -> x2, matrix products: none -> 6.67 us  [the longest x1 4.7 us: attend(): jnp.einsum('blhd,bkhd->bhlk', queries, key_rows, preferred_element_type=j...]
    all_to_all x1, waiting for transfers between devices: 4.4 us -> 0.01 us  [per_device(): lax.all_to_all(queries2[sample_pick], 'smp', split_axis=0, concat_axis=0,...]
    slice x1 -> x2, local copies, waits for them, and re-layouts: 0.78 us -> 2.76 us  [the longest x1 2.58 us: per_device(): key_value[:, :, :model_width]]
    dot_general x1, matrix products: 9.29 us -> 7.36 us  [per_device(): jnp.dot(normed(served_embed), kv_weight, preferred_element_type=jnp.float32)]
    all_to_all x1, starting transfers between devices: 4.1 us -> 5.94 us  [per_device(): lax.all_to_all(served_read.reshape(owners, latents, model_width), 'smp',...]
    convert_element_type x0 -> x2, local copies, waits for them, and re-layouts: none -> 1.79 us  [attend(): spike_mix.reshape(samples, latents, head_count * head_size)]
  transfers between devices with their start and end apart: 4 -> 4, of which waited for: 4 -> 3; matrix products, arithmetic and copies ran while one was open for 15% -> 31% of each run, Pallas kernels for 0% -> 0%
where the time goes in v5:
time: 121 us; the launch traced here: 120 us
  waiting for transfers between devices  29.6 us (24%)
  local copies, waits for them, and re-layouts  27.7 us (23%)
  starting transfers between devices  24.5 us (20%)
  matrix products  23.1 us (19%)
  other arithmetic  10.4 us (9%)
  Pallas kernels  4.11 us (3%)
    all_to_all x1, waiting for transfers between devices, per_device(): lax.all_to_all(served_read.reshape(owners, latents, model_width), 'smp',...  14.4 us
    all_to_all x1, waiting for transfers between devices, per_device(): lax.all_to_all(jnp.broadcast_to(memory_pair[None], (owners,) + memory_pai...  10.9 us
    all_to_all x1, starting transfers between devices, per_device(): lax.all_to_all(jnp.concatenate([request, count_pick[:, None]], axis=1), '...  7.39 us
    dot_general x1, matrix products, per_device(): jnp.dot(normed(served_embed), kv_weight, preferred_element_type=jnp.float32)  7.36 us
    all_to_all x1, starting transfers between devices, per_device(): lax.all_to_all(queries2[sample_pick], 'smp', split_axis=0, concat_axis=0,...  6.88 us
    reshape x1, local copies, waits for them, and re-layouts, per_device(): key_value[:, :, :model_width]  6.37 us
    reshape x1, local copies, waits for them, and re-layouts, per_device(): key_value[:, :, model_width:]  6.37 us
    all_to_all x1, starting transfers between devices, per_device(): lax.all_to_all(served_read.reshape(owners, latents, model_width), 'smp',...  5.94 us
  transfers between devices with their start and end apart: 4, of which 3 were waited for; matrix products, arithmetic and copies ran while one was open for 31% of the time, Pallas kernels for 0%

profile of v5, /device:TPU:0, one launch (start us, length us, event | category | flops | bytes accessed | tf_op | source)
XLA Modules:
  0.0 119.8 jit_solution(9543490535156801801)
XLA Ops:
  0.0 0.0 copy-start
  0.0 1.0 select_reduce_fusion.4
  1.0 0.9 select_reduce_fusion.1
  1.9 0.1 copy.30
  2.0 0.9 add_select_fusion
  2.9 0.1 select_reduce_fusion
  3.0 0.7 pad_add_fusion
  3.7 7.4 %all-to-all-start.1 = ((s32[16,1,65]{2,1,0:T(1,128)}), s32[16,1,65]{2,1,0:T(1,128)S(1)}, u32[]{:S(2)}, u32[]{:S(2)}) async-start(s32[16,1,65]{2,1,0:T(1,128)} %bitcast.6), calls=%async_computation.1 | async-start | bytes 16384 | tf_op jit(solution)/shard_map/all_to_all | solution.py:127
  11.1 0.8 pad_maximum_fusion
  11.9 1.2 %multiply_reduce_fusion = f32[16,16]{1,0:T(8,128)S(1)} fusion(bf16[16,16,1024]{2,1,0:T(8,128)(2,1)} %param.14), kind=kLoop, calls=%fused_computation.37 | loop fusion | flops 786176 | bytes 525312 | tf_op jit(solution)/shard_map/reduce_sum | solution.py:16
  13.1 4.3 %all-to-all-done.1 = s32[16,1,65]{2,1,0:T(1,128)S(1)} async-done(((s32[16,1,65]{2,1,0:T(1,128)}), s32[16,1,65]{2,1,0:T(1,128)S(1)}, u32[]{:S(2)}, u32[]{:S(2)}) %all-to-all-start.1) | async-done | bytes 4192 | tf_op jit(solution)/shard_map/all_to_all | solution.py:127
  17.4 1.1 broadcast_in_dim.95
  18.5 4.3 %all-to-all-start = ((bf16[16,16,2048]{2,1,0:T(8,128)(2,1)}), bf16[16,16,2048]{2,1,0:T(8,128)(2,1)}, u32[]{:S(2)}, u32[]{:S(2)}) async-start(bf16[16,16,2048]{2,1,0:T(8,128)(2,1)} %broadcast_in_dim.95), calls=%async_computation | async-start | bytes 2097152 | tf_op jit(solution)/shard_map/all_to_all | solution.py:143
  22.9 0.1 rsqrt.28
  23.0 0.0 copy-start.1
  23.0 1.3 %fusion.20 = bf16[256,1024]{1,0:T(8,128)(2,1)S(1)} fusion(bf16[16,16,1024]{2,1,0:T(8,128)(2,1)} %param.14, f32[256]{0:T(256)S(1)} %rsqrt.28), kind=kLoop, calls=%fused_computation.32 | loop fusion | flops 786432 | bytes 1049600 | tf_op jit(solution)/shard_map/convert_element_type | solution.py:16
  24.3 3.1 %fusion.16.query_ref = bf16[1,256,1024]{2,1,0:T(8,128)(2,1)} fusion(bf16[256,1024]{1,0:T(8,128)(2,1)S(1)} %fusion.20, bf16[1024,1024]{1,0:T(8,128)(2,1)} %param.23), kind=kOutput, calls=%fused_computation.28 | convolution fusion | flops 537133056 | bytes 3145728 | tf_op jit(solution)/shard_map/dot_general | solution.py:139
  27.4 0.1 reshape.192
  27.5 0.0 copy-done.1
  27.5 5.4 %gather_fusion = bf16[1024,1024]{1,0:T(8,128)(2,1)} fusion(bf16[512,1024]{1,0:T(8,128)(2,1)S(1)} %bitcast.49, s32[1024]{0:T(1024)S(1)} %broadcast_clamp_fusion), kind=kCustom, calls=%fused_computation | custom fusion | bytes 4198400 | tf_op jit(solution)/shard_map/gather | solution.py:136
  32.9 2.1 %fusion = f32[1024]{0:T(1024)S(1)} fusion(bf16[1024,1024]{1,0:T(8,128)(2,1)} %gather_fusion), kind=kLoop, calls=%fused_computation.5 | loop fusion | flops 3144704 | bytes 2101248 | tf_op jit(solution)/shard_map/reduce_sum | solution.py:16
  34.9 0.0 copy-start.3
  34.9 10.9 %all-to-all-done = bf16[16,16,2048]{2,1,0:T(8,128)(2,1)} async-done(((bf16[16,16,2048]{2,1,0:T(8,128)(2,1)}), bf16[16,16,2048]{2,1,0:T(8,128)(2,1)}, u32[]{:S(2)}, u32[]{:S(2)}) %all-to-all-start) | async-done | bytes 1048608 | tf_op jit(solution)/shard_map/all_to_all | solution.py:143
  45.8 4.1 %shard_map.136 = bf16[1,256,1024]{2,1,0:T(8,128)(2,1)} custom-call(s32[1]{0:T(128)} %constant.48.clone.1.counts_ref, bf16[1,256,1024]{2,1,0:T(8,128)(2,1)} %fusion.16.query_ref, bf16[1,256,2048]{2,1,0:T(8,128)(2,1)} %bitcast.2.key_ref.value_ref, bf16[1,256,2048]{2,1,0:T(8,128)(2,1)} %bitcast.2.key_ref.value_ref), custom_call_target="tpu_custom_call" | custom-call | tf_op jit(solution)/shard_map/pallas_call | solution.py:75
  49.9 0.0 copy-done
  49.9 0.0 copy-done.3
  49.9 0.0 copy-start.4
  49.9 2.0 %fusion.17 = (f32[256]{0:T(256)S(1)}, bf16[256,1024]{1,0:T(8,128)(2,1)S(1)}) fusion(bf16[1024,1024]{1,0:T(8,128)(2,1)S(1)} %copy-done, bf16[1,256,1024]{2,1,0:T(8,128)(2,1)} %shard_map.136, bf16[256,1024]{1,0:T(8,128)(2,1)S(1)} %bitcast.51), kind=kOutput, calls=%fused_computation.29 | convolution fusion | flops 538443520 | bytes 3671040 | tf_op jit(solution)/shard_map/dot_general | solution.py:158
  51.9 0.0 copy-start.5
  52.0 0.0 copy-done.4
  52.0 0.8 convolution_convert_fusion.1
  52.7 0.0 copy-done.5
  52.8 1.4 %gather_fusion.1 = bf16[16,16,1024]{2,1,0:T(8,128)(2,1)} fusion(bf16[16,16,1024]{2,1,0:T(8,128)(2,1)S(1)} %bitcast.53, s32[1024]{0:T(1024)S(1)} %pad_clamp_fusion.1), kind=kCustom, calls=%fused_computation.1 | custom fusion | bytes 1048640 | tf_op jit(solution)/shard_map/gather | solution.py:165
  54.1 6.9 %all-to-all-start.2 = ((bf16[16,16,1024]{2,1,0:T(8,128)(2,1)}), bf16[16,16,1024]{2,1,0:T(8,128)(2,1)}, u32[]{:S(2)}, u32[]{:S(2)}) async-start(bf16[16,16,1024]{2,1,0:T(8,128)(2,1)} %gather_fusion.1), calls=%async_computation.2 | async-start | bytes 1048576 | tf_op jit(solution)/shard_map/all_to_all | solution.py:164
  61.0 7.4 %convolution_convert_fusion = bf16[1024,2048]{1,0:T(8,128)(2,1)S(1)} fusion(bf16[1024,2048]{1,0:T(8,128)(2,1)} %param.25, bf16[1024,1024]{1,0:T(8,128)(2,1)} %gather_fusion, f32[1024]{0:T(1024)S(1)} %add_rsqrt_fusion.1), kind=kOutput, calls=%fused_computation.11 | convolution fusion | flops 4300210176 | bytes 10489856 | tf_op jit(solution)/shard_map/dot_general | solution.py:167
  68.4 2.6 %fusion.33 = (bf16[16,64,1024]{2,1,0:T(8,128)(2,1)}, bf16[16,64,1024]{2,1,0:T(8,128)(2,1)}) fusion(bf16[16,64,2048]{2,1,0:T(8,128)(2,1)S(1)} %bitcast.50), kind=kLoop, calls=%fused_computation.69 | loop fusion | bytes 8388608 | tf_op jit(solution)/shard_map/slice | solution.py:173
  71.0 6.4 %reshape.197 = bf16[16,64,16,64]{3,2,1,0:T(8,128)(2,1)} reshape(bf16[16,64,1024]{2,1,0:T(8,128)(2,1)} %get-tuple-element.8) | data formatting | bytes 4194304 | tf_op jit(solution)/shard_map/reshape | solution.py:173
  77.4 6.4 %reshape.194 = bf16[16,64,16,64]{3,2,1,0:T(8,128)(2,1)} reshape(bf16[16,64,1024]{2,1,0:T(8,128)(2,1)} %get-tuple-element.9) | data formatting | bytes 4194304 | tf_op jit(solution)/shard_map/reshape | solution.py:174
  83.7 0.2 slice_reduce_fusion
  83.9 0.1 iota_compare_fusion
  84.0 0.0 all-to-all-done.2
  84.0 1.8 %reshape.196 = bf16[16,16,16,64]{3,2,1,0:T(8,128)(2,1)S(1)} reshape(bf16[16,16,1024]{2,1,0:T(8,128)(2,1)} %all-to-all-done.2) | data formatting | bytes 1048576 | tf_op jit(solution)/shard_map/reshape | solution.py:177
  85.7 0.0 copy-start.2
  85.8 4.7 %fusion.9 = (f32[16,16,16]{2,1,0:T(8,128)S(1)}, f32[16,16,16,64]{3,2,1,0:T(8,128)S(1)}) fusion(pred[16,64]{1,0:T(8,128)(4,1)S(1)} %iota_compare_fusion, bf16[16,64,16,64]{3,2,1,0:T(8,128)(2,1)} %reshape.197, bf16[16,16,16,64]{3,2,1,0:T(8,128)(2,1)S(1)} %reshape.196), kind=kOutput, calls=%fused_computation.17 | convolution fusion | flops 34336768 | bytes 3687424 | tf_op jit(solution)/shard_map/blhd,bkhd->bhlk/dot_general | solution.py:23
  90.5 1.3 %fusion.12 = f32[16,16,16]{2,1,0:T(8,128)S(1)} fusion(f32[16,16,16,64]{3,2,1,0:T(8,128)S(1)} %get-tuple-element.13, f32[16,16,16]{2,1,0:T(8,128)S(1)} %get-tuple-element.12, pred[16,64]{1,0:T(8,128)(4,1)S(1)} %iota_compare_fusion), kind=kLoop, calls=%fused_computation.18 | loop fusion | flops 1044480 | bytes 1082368 | tf_op jit(solution)/shard_map/reduce_sum | solution.py:29
  91.8 0.0 copy-done.2
  91.8 2.0 %fusion.7 = bf16[16,16,16,64]{3,1,2,0:T(8,128)(2,1)S(1)} fusion(bf16[16,64,16,64]{3,2,1,0:T(8,128)(2,1)S(1)} %copy-done.2, f32[16,16,16,64]{3,2,1,0:T(8,128)S(1)} %get-tuple-element.13, f32[16,16,16]{1,2,0:T(8,128)S(1)} %bitcast.54, f32[16,16,16]{2,1,0:T(8,128)S(1)} %get-tuple-element.12, pred[16,64]{1,0:T(8,128)(4,1)S(1)} %iota_compare_fusion), kind=kOutput, calls=%fused_computation.13 | convolution fusion | flops 35127296 | bytes 3703808 | tf_op jit(solution)/shard_map/bhlk,bkhd->blhd/dot_general | solution.py:31
  93.8 0.3 copy.34
  94.1 1.5 %convert_element_type.64 = bf16[16,16,1024]{2,1,0:T(8,128)(2,1)} reshape(bf16[16,16,16,64]{3,2,1,0:T(8,128)(2,1)S(1)} %copy.34) | data formatting | bytes 1048576 | tf_op jit(solution)/shard_map/convert_element_type | solution.py:39
  95.6 5.9 %all-to-all-start.3 = ((bf16[16,16,1024]{2,1,0:T(8,128)(2,1)}), bf16[16,16,1024]{2,1,0:T(8,128)(2,1)S(1)}, u32[]{:S(2)}, u32[]{:S(2)}) async-start(bf16[16,16,1024]{2,1,0:T(8,128)(2,1)} %convert_element_type.64), calls=%async_computation.3 | async-start | bytes 1048576 | tf_op jit(solution)/shard_map/all_to_all | solution.py:182
  101.6 14.4 %all-to-all-done.3 = bf16[16,16,1024]{2,1,0:T(8,128)(2,1)S(1)} async-done(((bf16[16,16,1024]{2,1,0:T(8,128)(2,1)}), bf16[16,16,1024]{2,1,0:T(8,128)(2,1)S(1)}, u32[]{:S(2)}, u32[]{:S(2)}) %all-to-all-start.3) | async-done | bytes 524320 | tf_op jit(solution)/shard_map/all_to_all | solution.py:182
  116.0 0.6 gather_fusion.2
  116.6 3.2 %fusion.14 = bf16[256,1024]{1,0:T(8,128)(2,1)} fusion(bf16[256,1024]{1,0:T(8,128)(2,1)S(1)} %bitcast.52, bf16[1024,1024]{1,0:T(8,128)(2,1)} %param.27, bf16[256,1024]{1,0:T(8,128)(2,1)} %copy-done.5), kind=kOutput, calls=%fused_computation.24 | convolution fusion | flops 537657344 | bytes 3670016 | tf_op jit(solution)/shard_map/dot_general | solution.py:189
  (12 shorter events, 0.1 us)
Async XLA Ops:
  0.0 49.9 %copy-start = (bf16[1024,1024]{1,0:T(8,128)(2,1)S(1)}, bf16[1024,1024]{1,0:T(8,128)(2,1)}, u32[]{:S(2)}) copy-start(bf16[1024,1024]{1,0:T(8,128)(2,1)} %param.24) | copy-start | bytes 6291460
  3.7 13.7 %all-to-all-start.1 = ((s32[16,1,65]{2,1,0:T(1,128)}), s32[16,1,65]{2,1,0:T(1,128)S(1)}, u32[]{:S(2)}, u32[]{:S(2)}) async-start(s32[16,1,65]{2,1,0:T(1,128)} %bitcast.6), calls=%async_computation.1 | async-start | bytes 16384 | tf_op jit(solution)/shard_map/all_to_all | solution.py:127
  18.5 27.3 %all-to-all-start = ((bf16[16,16,2048]{2,1,0:T(8,128)(2,1)}), bf16[16,16,2048]{2,1,0:T(8,128)(2,1)}, u32[]{:S(2)}, u32[]{:S(2)}) async-start(bf16[16,16,2048]{2,1,0:T(8,128)(2,1)} %broadcast_in_dim.95), calls=%async_computation | async-start | bytes 2097152 | tf_op jit(solution)/shard_map/all_to_all | solution.py:143
  23.0 4.5 %copy-start.1 = (bf16[1,512,1024]{2,1,0:T(8,128)(2,1)S(1)}, bf16[1,512,1024]{2,1,0:T(8,128)(2,1)}, u32[]{:S(2)}) copy-start(bf16[1,512,1024]{2,1,0:T(8,128)(2,1)} %param.20) | copy-start | bytes 3145732
  34.9 15.0 %copy-start.3 = (bf16[16,16,1024]{2,1,0:T(8,128)(2,1)S(1)}, bf16[16,16,1024]{2,1,0:T(8,128)(2,1)}, u32[]{:S(2)}) copy-start(bf16[16,16,1024]{2,1,0:T(8,128)(2,1)} %param.14) | copy-start | bytes 1572868
  49.9 2.0 %copy-start.4 = (bf16[1024,1024]{1,0:T(8,128)(2,1)S(1)}, bf16[1024,1024]{1,0:T(8,128)(2,1)}, u32[]{:S(2)}) copy-start(bf16[1024,1024]{1,0:T(8,128)(2,1)} %param.26) | copy-start | bytes 6291460
  51.9 0.8 copy-start.5
  54.1 29.8 %all-to-all-start.2 = ((bf16[16,16,1024]{2,1,0:T(8,128)(2,1)}), bf16[16,16,1024]{2,1,0:T(8,128)(2,1)}, u32[]{:S(2)}, u32[]{:S(2)}) async-start(bf16[16,16,1024]{2,1,0:T(8,128)(2,1)} %gather_fusion.1), calls=%async_computation.2 | async-start | bytes 1048576 | tf_op jit(solution)/shard_map/all_to_all | solution.py:164
  85.7 6.1 %copy-start.2 = (bf16[16,64,16,64]{3,2,1,0:T(8,128)(2,1)S(1)}, bf16[16,64,16,64]{3,2,1,0:T(8,128)(2,1)}, u32[]{:S(2)}) copy-start(bf16[16,64,16,64]{3,2,1,0:T(8,128)(2,1)} %reshape.194) | copy-start | bytes 6291460
  95.6 20.4 %all-to-all-start.3 = ((bf16[16,16,1024]{2,1,0:T(8,128)(2,1)}), bf16[16,16,1024]{2,1,0:T(8,128)(2,1)S(1)}, u32[]{:S(2)}, u32[]{:S(2)}) async-start(bf16[16,16,1024]{2,1,0:T(8,128)(2,1)} %convert_element_type.64), calls=%async_computation.3 | async-start | bytes 1048576 | tf_op jit(solution)/shard_map/all_to_all | solution.py:182

commit v6 on v5

--- a/solution.py
+++ b/solution.py
@@ -147,6 +147,18 @@
         concat_axis=0,
         tiled=True,
     ).reshape(1, -1, 2 * model_width)
+    key_value = jnp.dot(
+        normed(served_embed),
+        kv_weight,
+        preferred_element_type=jnp.float32,
+    ).astype(jnp.bfloat16)
+    key_value = key_value.reshape(owners, token_total, 2 * model_width)
+    key_rows = key_value[:, :, :model_width].reshape(owners, token_total, head_count, HEAD_DIM)
+    value_rows = key_value[:, :, model_width:].reshape(owners, token_total, head_count, HEAD_DIM)
+    live_tokens = jnp.arange(token_total, dtype=jnp.int32)[None, :] < served[:, token_total:]
+    key_rows, value_rows, live_tokens, memory_rows = lax.optimization_barrier(
+        (key_rows, value_rows, live_tokens, memory_rows)
+    )
     memory_total = memory_rows.shape[1]
     read_mem = attend_kernel(
         queries.reshape(1, row_total, model_width),
@@ -164,15 +176,6 @@
     served_queries = lax.all_to_all(
         queries2[sample_pick], "smp", split_axis=0, concat_axis=0, tiled=True
     )
-    key_value = jnp.dot(
-        normed(served_embed),
-        kv_weight,
-        preferred_element_type=jnp.float32,
-    ).astype(jnp.bfloat16)
-    key_value = key_value.reshape(owners, token_total, 2 * model_width)
-    key_rows = key_value[:, :, :model_width].reshape(owners, token_total, head_count, HEAD_DIM)
-    value_rows = key_value[:, :, model_width:].reshape(owners, token_total, head_count, HEAD_DIM)
-    live_tokens = jnp.arange(token_total, dtype=jnp.int32)[None, :] < served[:, token_total:]
     served_read = attend(
         served_queries.reshape(owners, latents, head_count, HEAD_DIM),
         key_rows,

time: 121 us -> 118 us (0.975)
  blocking collectives: 0 us -> 20.3 us
  waiting for transfers between devices: 29.6 us -> 14.4 us
  starting transfers between devices: 24.5 us -> 17.5 us
    all_to_all x0 -> x1, blocking collectives: none -> 20.3 us  [per_device(): lax.all_to_all(queries2[sample_pick], 'smp', split_axis=0, concat_axis=0,...]
    all_to_all x1, waiting for transfers between devices: 10.9 us -> 0.01 us  [per_device(): lax.all_to_all(jnp.broadcast_to(memory_pair[None], (owners,) + memory_pai...]
    all_to_all x1 -> x0, starting transfers between devices: 6.88 us -> none  [per_device(): lax.all_to_all(queries2[sample_pick], 'smp', split_axis=0, concat_axis=0,...]
    all_to_all x1, waiting for transfers between devices: 4.33 us -> 0.01 us  [per_device(): lax.all_to_all(jnp.concatenate([request, count_pick[:, None]], axis=1), '...]
    all_to_all x1, starting transfers between devices: 5.94 us -> 4.1 us  [per_device(): lax.all_to_all(served_read.reshape(owners, latents, model_width), 'smp',...]
    all_to_all x1, starting transfers between devices: 4.34 us -> 6.06 us  [per_device(): lax.all_to_all(jnp.broadcast_to(memory_pair[None], (owners,) + memory_pai...]
  transfers between devices with their start and end apart: 4 -> 3, of which waited for: 3 -> 1; matrix products, arithmetic and copies ran while one was open for 31% -> 31% of each run, Pallas kernels for 0% -> 0%
where the time goes in v6:
time: 118 us; the launch traced here: 117 us
  local copies, waits for them, and re-layouts  27 us (23%)
  matrix products  22.9 us (19%)
  blocking collectives  20.3 us (17%)
  starting transfers between devices  17.5 us (15%)
  waiting for transfers between devices  14.4 us (12%)
  other arithmetic  10.5 us (9%)
  Pallas kernels  4.17 us (4%)
    all_to_all x1, blocking collectives, per_device(): lax.all_to_all(queries2[sample_pick], 'smp', split_axis=0, concat_axis=0,...  20.3 us
    all_to_all x1, waiting for transfers between devices, per_device(): lax.all_to_all(served_read.reshape(owners, latents, model_width), 'smp',...  14.4 us
    all_to_all x1, starting transfers between devices, per_device(): lax.all_to_all(jnp.concatenate([request, count_pick[:, None]], axis=1), '...  7.39 us
    dot_general x1, matrix products, per_device(): jnp.dot(normed(served_embed), kv_weight, preferred_element_type=jnp.float32)  7.15 us
    reshape x1, local copies, waits for them, and re-layouts, per_device(): key_value[:, :, :model_width]  6.37 us
    reshape x1, local copies, waits for them, and re-layouts, per_device(): key_value[:, :, model_width:]  6.37 us
    all_to_all x1, starting transfers between devices, per_device(): lax.all_to_all(jnp.broadcast_to(memory_pair[None], (owners,) + memory_pai...  6.06 us
    gather x1, local copies, waits for them, and re-layouts, per_device(): served_embed = panel_table[served_index.reshape(-1)]  5.36 us
  transfers between devices with their start and end apart: 3, of which 1 were waited for; matrix products, arithmetic and copies ran while one was open for 31% of the time, Pallas kernels for 0%

profile of v6, /device:TPU:0, one launch (start us, length us, event | category | flops | bytes accessed | tf_op | source)
XLA Modules:
  0.0 117.0 jit_solution(17515703133196470488)
XLA Ops:
  0.0 0.0 copy-start
  0.0 1.0 select_reduce_fusion.4
  1.0 0.9 select_reduce_fusion.1
  1.9 0.1 copy.30
  2.0 0.9 add_select_fusion
  2.9 0.1 select_reduce_fusion
  3.0 0.7 pad_add_fusion
  3.7 7.4 %all-to-all-start = ((s32[16,1,65]{2,1,0:T(1,128)}), s32[16,1,65]{2,1,0:T(1,128)S(1)}, u32[]{:S(2)}, u32[]{:S(2)}) async-start(s32[16,1,65]{2,1,0:T(1,128)} %bitcast.4), calls=%async_computation | async-start | bytes 16384 | tf_op jit(solution)/shard_map/all_to_all | solution.py:127
  11.1 1.2 %multiply_reduce_fusion = f32[16,16]{1,0:T(8,128)S(1)} fusion(bf16[16,16,1024]{2,1,0:T(8,128)(2,1)} %param.14), kind=kLoop, calls=%fused_computation.37 | loop fusion | flops 786176 | bytes 525312 | tf_op jit(solution)/shard_map/reduce_sum | solution.py:16
  12.3 0.1 rsqrt.28
  12.4 1.2 %fusion.20 = bf16[256,1024]{1,0:T(8,128)(2,1)S(1)} fusion(bf16[16,16,1024]{2,1,0:T(8,128)(2,1)} %param.14, f32[256]{0:T(256)S(1)} %rsqrt.28), kind=kLoop, calls=%fused_computation.32 | loop fusion | flops 786432 | bytes 1049600 | tf_op jit(solution)/shard_map/convert_element_type | solution.py:16
  13.6 0.8 pad_maximum_fusion
  14.4 3.1 %fusion.16.query_ref = bf16[1,256,1024]{2,1,0:T(8,128)(2,1)} fusion(bf16[256,1024]{1,0:T(8,128)(2,1)S(1)} %fusion.20, bf16[1024,1024]{1,0:T(8,128)(2,1)} %param.23), kind=kOutput, calls=%fused_computation.28 | convolution fusion | flops 537133056 | bytes 3145728 | tf_op jit(solution)/shard_map/dot_general | solution.py:139
  17.5 0.0 copy-start.1
  17.5 0.0 all-to-all-done
  17.5 1.1 broadcast_in_dim.103
  18.6 6.1 %all-to-all-start.1 = ((bf16[16,16,2048]{2,1,0:T(8,128)(2,1)}), bf16[16,16,2048]{2,1,0:T(8,128)(2,1)}, u32[]{:S(2)}, u32[]{:S(2)}) async-start(bf16[16,16,2048]{2,1,0:T(8,128)(2,1)} %broadcast_in_dim.103), calls=%async_computation.1 | async-start | bytes 2097152 | tf_op jit(solution)/shard_map/all_to_all | solution.py:143
  24.7 0.1 reshape.173
  24.8 0.0 copy-done.1
  24.8 5.4 %gather_fusion = bf16[1024,1024]{1,0:T(8,128)(2,1)} fusion(bf16[512,1024]{1,0:T(8,128)(2,1)S(1)} %bitcast.49, s32[1024]{0:T(1024)S(1)} %broadcast_clamp_fusion), kind=kCustom, calls=%fused_computation | custom fusion | bytes 4198400 | tf_op jit(solution)/shard_map/gather | solution.py:136
  30.2 0.0 copy-start.2
  30.2 2.2 %fusion = f32[1024]{0:T(1024)S(1)} fusion(bf16[1024,1024]{1,0:T(8,128)(2,1)} %gather_fusion), kind=kLoop, calls=%fused_computation.5 | loop fusion | flops 3144704 | bytes 2101248 | tf_op jit(solution)/shard_map/reduce_sum | solution.py:16
  32.4 0.0 copy-done.2
  32.4 7.1 %convolution_convert_fusion = bf16[1024,2048]{1,0:T(8,128)(2,1)S(1)} fusion(bf16[1024,2048]{1,0:T(8,128)(2,1)} %param.25, bf16[1024,1024]{1,0:T(8,128)(2,1)S(1)} %copy-done.2, f32[1024]{0:T(1024)S(1)} %add_rsqrt_fusion.1), kind=kOutput, calls=%fused_computation.11 | convolution fusion | flops 4300210176 | bytes 10489856 | tf_op jit(solution)/shard_map/dot_general | solution.py:150
  39.6 2.6 %fusion.33 = (bf16[16,64,1024]{2,1,0:T(8,128)(2,1)}, bf16[16,64,1024]{2,1,0:T(8,128)(2,1)}) fusion(bf16[16,64,2048]{2,1,0:T(8,128)(2,1)S(1)} %bitcast.50), kind=kLoop, calls=%fused_computation.69 | loop fusion | bytes 8388608 | tf_op jit(solution)/shard_map/slice | solution.py:157
  42.1 6.4 %reshape.175 = bf16[16,64,16,64]{3,2,1,0:T(8,128)(2,1)} reshape(bf16[16,64,1024]{2,1,0:T(8,128)(2,1)} %get-tuple-element.17) | data formatting | bytes 4194304 | tf_op jit(solution)/shard_map/reshape | solution.py:156
  48.5 6.4 %reshape.176 = bf16[16,64,16,64]{3,2,1,0:T(8,128)(2,1)} reshape(bf16[16,64,1024]{2,1,0:T(8,128)(2,1)} %get-tuple-element.16) | data formatting | bytes 4194304 | tf_op jit(solution)/shard_map/reshape | solution.py:157
  54.9 0.0 copy-start.4
  54.9 0.2 slice_reduce_fusion
  55.1 0.1 iota_compare_fusion
  55.1 0.0 all-to-all-done.1
  55.1 4.2 %shard_map.136 = bf16[1,256,1024]{2,1,0:T(8,128)(2,1)} custom-call(s32[1]{0:T(128)} %constant.48.clone.1.counts_ref, bf16[1,256,1024]{2,1,0:T(8,128)(2,1)} %fusion.16.query_ref, bf16[1,256,2048]{2,1,0:T(8,128)(2,1)} %bitcast.8.key_ref.value_ref, bf16[1,256,2048]{2,1,0:T(8,128)(2,1)} %bitcast.8.key_ref.value_ref), custom_call_target="tpu_custom_call" | custom-call | tf_op jit(solution)/shard_map/pallas_call | solution.py:75
  59.3 0.0 copy-done
  59.3 0.0 copy-done.4
  59.3 0.0 copy-start.5
  59.3 2.0 %fusion.17 = (f32[256]{0:T(256)S(1)}, bf16[256,1024]{1,0:T(8,128)(2,1)S(1)}) fusion(bf16[1024,1024]{1,0:T(8,128)(2,1)S(1)} %copy-done, bf16[1,256,1024]{2,1,0:T(8,128)(2,1)} %shard_map.136, bf16[256,1024]{1,0:T(8,128)(2,1)S(1)} %bitcast.51), kind=kOutput, calls=%fused_computation.29 | convolution fusion | flops 538443520 | bytes 3671040 | tf_op jit(solution)/shard_map/dot_general | solution.py:170
  61.3 0.0 copy-start.6
  61.3 0.0 copy-done.5
  61.4 0.8 convolution_convert_fusion.1
  62.1 0.1 copy-done.6
  62.2 0.6 gather_fusion.1
  62.8 20.3 %all_to_all.27 = bf16[16,16,1024]{2,1,0:T(8,128)(2,1)} all-to-all(bf16[16,16,1024]{2,1,0:T(8,128)(2,1)S(1)} %gather_fusion.1), channel_id=1, replica_groups=mesh['grp'=2,'smp'=16] {'smp'}, dimensions={0} | all-to-all | bytes 1048576 | tf_op jit(solution)/shard_map/all_to_all | solution.py:176
  83.1 1.8 %reshape.180 = bf16[16,16,16,64]{3,2,1,0:T(8,128)(2,1)S(1)} reshape(bf16[16,16,1024]{2,1,0:T(8,128)(2,1)} %all_to_all.27) | data formatting | bytes 1048576 | tf_op jit(solution)/shard_map/reshape | solution.py:180
  84.9 0.0 copy-start.3
  84.9 4.7 %fusion.9 = (f32[16,16,16]{2,1,0:T(8,128)S(1)}, f32[16,16,16,64]{3,2,1,0:T(8,128)S(1)}) fusion(pred[16,64]{1,0:T(8,128)(4,1)S(1)} %iota_compare_fusion, bf16[16,64,16,64]{3,2,1,0:T(8,128)(2,1)} %reshape.175, bf16[16,16,16,64]{3,2,1,0:T(8,128)(2,1)S(1)} %reshape.180), kind=kOutput, calls=%fused_computation.17 | convolution fusion | flops 34336768 | bytes 3687424 | tf_op jit(solution)/shard_map/blhd,bkhd->bhlk/dot_general | solution.py:23
  89.6 1.3 %fusion.12 = f32[16,16,16]{2,1,0:T(8,128)S(1)} fusion(f32[16,16,16,64]{3,2,1,0:T(8,128)S(1)} %get-tuple-element.21, f32[16,16,16]{2,1,0:T(8,128)S(1)} %get-tuple-element.20, pred[16,64]{1,0:T(8,128)(4,1)S(1)} %iota_compare_fusion), kind=kLoop, calls=%fused_computation.18 | loop fusion | flops 1044480 | bytes 1082368 | tf_op jit(solution)/shard_map/reduce_sum | solution.py:29
  90.9 0.0 copy-done.3
  90.9 2.0 %fusion.7 = bf16[16,16,16,64]{3,1,2,0:T(8,128)(2,1)S(1)} fusion(bf16[16,64,16,64]{3,2,1,0:T(8,128)(2,1)S(1)} %copy-done.3, f32[16,16,16,64]{3,2,1,0:T(8,128)S(1)} %get-tuple-element.21, f32[16,16,16]{1,2,0:T(8,128)S(1)} %bitcast.54, f32[16,16,16]{2,1,0:T(8,128)S(1)} %get-tuple-element.20, pred[16,64]{1,0:T(8,128)(4,1)S(1)} %iota_compare_fusion), kind=kOutput, calls=%fused_computation.13 | convolution fusion | flops 35127296 | bytes 3703808 | tf_op jit(solution)/shard_map/bhlk,bkhd->blhd/dot_general | solution.py:31
  92.9 0.3 copy.34
  93.2 1.5 %convert_element_type.64 = bf16[16,16,1024]{2,1,0:T(8,128)(2,1)} reshape(bf16[16,16,16,64]{3,2,1,0:T(8,128)(2,1)S(1)} %copy.34) | data formatting | bytes 1048576 | tf_op jit(solution)/shard_map/convert_element_type | solution.py:39
  94.7 4.1 %all-to-all-start.3 = ((bf16[16,16,1024]{2,1,0:T(8,128)(2,1)}), bf16[16,16,1024]{2,1,0:T(8,128)(2,1)S(1)}, u32[]{:S(2)}, u32[]{:S(2)}) async-start(bf16[16,16,1024]{2,1,0:T(8,128)(2,1)} %convert_element_type.64), calls=%async_computation.3 | async-start | bytes 1048576 | tf_op jit(solution)/shard_map/all_to_all | solution.py:185
  98.8 14.4 %all-to-all-done.3 = bf16[16,16,1024]{2,1,0:T(8,128)(2,1)S(1)} async-done(((bf16[16,16,1024]{2,1,0:T(8,128)(2,1)}), bf16[16,16,1024]{2,1,0:T(8,128)(2,1)S(1)}, u32[]{:S(2)}, u32[]{:S(2)}) %all-to-all-start.3) | async-done | bytes 524320 | tf_op jit(solution)/shard_map/all_to_all | solution.py:185
  113.3 0.6 gather_fusion.2
  113.9 3.2 %fusion.14 = bf16[256,1024]{1,0:T(8,128)(2,1)} fusion(bf16[256,1024]{1,0:T(8,128)(2,1)S(1)} %bitcast.52, bf16[1024,1024]{1,0:T(8,128)(2,1)} %param.27, bf16[256,1024]{1,0:T(8,128)(2,1)} %copy-done.6), kind=kOutput, calls=%fused_computation.24 | convolution fusion | flops 537657344 | bytes 3670016 | tf_op jit(solution)/shard_map/dot_general | solution.py:192
  (12 shorter events, 0.1 us)
Async XLA Ops:
  0.0 59.3 %copy-start = (bf16[1024,1024]{1,0:T(8,128)(2,1)S(1)}, bf16[1024,1024]{1,0:T(8,128)(2,1)}, u32[]{:S(2)}) copy-start(bf16[1024,1024]{1,0:T(8,128)(2,1)} %param.24) | copy-start | bytes 6291460
  3.7 13.8 %all-to-all-start = ((s32[16,1,65]{2,1,0:T(1,128)}), s32[16,1,65]{2,1,0:T(1,128)S(1)}, u32[]{:S(2)}, u32[]{:S(2)}) async-start(s32[16,1,65]{2,1,0:T(1,128)} %bitcast.4), calls=%async_computation | async-start | bytes 16384 | tf_op jit(solution)/shard_map/all_to_all | solution.py:127
  17.5 7.3 %copy-start.1 = (bf16[1,512,1024]{2,1,0:T(8,128)(2,1)S(1)}, bf16[1,512,1024]{2,1,0:T(8,128)(2,1)}, u32[]{:S(2)}) copy-start(bf16[1,512,1024]{2,1,0:T(8,128)(2,1)} %param.20) | copy-start | bytes 3145732
  18.6 36.5 %all-to-all-start.1 = ((bf16[16,16,2048]{2,1,0:T(8,128)(2,1)}), bf16[16,16,2048]{2,1,0:T(8,128)(2,1)}, u32[]{:S(2)}, u32[]{:S(2)}) async-start(bf16[16,16,2048]{2,1,0:T(8,128)(2,1)} %broadcast_in_dim.103), calls=%async_computation.1 | async-start | bytes 2097152 | tf_op jit(solution)/shard_map/all_to_all | solution.py:143
  30.2 2.2 %copy-start.2 = (bf16[1024,1024]{1,0:T(8,128)(2,1)S(1)}, bf16[1024,1024]{1,0:T(8,128)(2,1)}, u32[]{:S(2)}) copy-start(bf16[1024,1024]{1,0:T(8,128)(2,1)} %gather_fusion) | copy-start | bytes 6291460
  54.9 4.4 %copy-start.4 = (bf16[16,16,1024]{2,1,0:T(8,128)(2,1)S(1)}, bf16[16,16,1024]{2,1,0:T(8,128)(2,1)}, u32[]{:S(2)}) copy-start(bf16[16,16,1024]{2,1,0:T(8,128)(2,1)} %param.14) | copy-start | bytes 1572868
  59.3 2.0 %copy-start.5 = (bf16[1024,1024]{1,0:T(8,128)(2,1)S(1)}, bf16[1024,1024]{1,0:T(8,128)(2,1)}, u32[]{:S(2)}) copy-start(bf16[1024,1024]{1,0:T(8,128)(2,1)} %param.26) | copy-start | bytes 6291460
  61.3 0.9 copy-start.6
  84.9 6.1 %copy-start.3 = (bf16[16,64,16,64]{3,2,1,0:T(8,128)(2,1)S(1)}, bf16[16,64,16,64]{3,2,1,0:T(8,128)(2,1)}, u32[]{:S(2)}) copy-start(bf16[16,64,16,64]{3,2,1,0:T(8,128)(2,1)} %reshape.176) | copy-start | bytes 6291460
  94.7 18.6 %all-to-all-start.3 = ((bf16[16,16,1024]{2,1,0:T(8,128)(2,1)}), bf16[16,16,1024]{2,1,0:T(8,128)(2,1)S(1)}, u32[]{:S(2)}, u32[]{:S(2)}) async-start(bf16[16,16,1024]{2,1,0:T(8,128)(2,1)} %convert_element_type.64), calls=%async_computation.3 | async-start | bytes 1048576 | tf_op jit(solution)/shard_map/all_to_all | solution.py:185

commit v7 on v5

--- a/solution.py
+++ b/solution.py
@@ -30,6 +30,27 @@
     spike_mix = (
         jnp.einsum(
             "bhlk,bkhd->blhd",
+            spike_exp.astype(jnp.bfloat16),
+            value_rows,
+            preferred_element_type=jnp.float32,
+        )
+        / denominator
+    )
+    return spike_mix.reshape(samples, latents, head_count * head_size).astype(jnp.bfloat16)
+
+
+def attend_heads(queries, key_rows, value_rows, live_tokens):
+    samples, latents, head_count, head_size = queries.shape
+    spike_scores = jnp.einsum(
+        "blhd,bhkd->bhlk", queries, key_rows, preferred_element_type=jnp.float32
+    ) * HEAD_DIM ** (-0.5)
+    spike_scores = jnp.where(live_tokens[:, None, None, :], spike_scores, masked_score)
+    spike_max = jnp.max(spike_scores, axis=-1, keepdims=True)
+    spike_exp = jnp.exp(spike_scores - spike_max)
+    denominator = jnp.transpose(jnp.sum(spike_exp, axis=-1, keepdims=True), (0, 2, 1, 3))
+    spike_mix = (
+        jnp.einsum(
+            "bhlk,bhkd->blhd",
             spike_exp.astype(jnp.bfloat16),
             value_rows,
             preferred_element_type=jnp.float32,
@@ -147,6 +168,8 @@
         concat_axis=0,
         tiled=True,
     ).reshape(1, -1, 2 * model_width)
+    embed_normed = normed(served_embed).reshape(owners, token_total, model_width)
+    embed_normed, memory_rows = lax.optimization_barrier((embed_normed, memory_rows))
     memory_total = memory_rows.shape[1]
     read_mem = attend_kernel(
         queries.reshape(1, row_total, model_width),
@@ -164,16 +187,21 @@
     served_queries = lax.all_to_all(
         queries2[sample_pick], "smp", split_axis=0, concat_axis=0, tiled=True
     )
-    key_value = jnp.dot(
-        normed(served_embed),
-        kv_weight,
+    key_rows = jnp.einsum(
+        "btc,chd->bhtd",
+        embed_normed,
+        kv_weight[:, :model_width].reshape(model_width, head_count, HEAD_DIM),
         preferred_element_type=jnp.float32,
     ).astype(jnp.bfloat16)
-    key_value = key_value.reshape(owners, token_total, 2 * model_width)
-    key_rows = key_value[:, :, :model_width].reshape(owners, token_total, head_count, HEAD_DIM)
-    value_rows = key_value[:, :, model_width:].reshape(owners, token_total, head_count, HEAD_DIM)
+    value_rows = jnp.einsum(
+        "btc,chd->bhtd",
+        embed_normed,
+        kv_weight[:, model_width:].reshape(model_width, head_count, HEAD_DIM),
+        preferred_element_type=jnp.float32,
+    ).astype(jnp.bfloat16)
+    key_rows, value_rows = lax.optimization_barrier((key_rows, value_rows))
     live_tokens = jnp.arange(token_total, dtype=jnp.int32)[None, :] < served[:, token_total:]
-    served_read = attend(
+    served_read = attend_heads(
         served_queries.reshape(owners, latents, head_count, HEAD_DIM),
         key_rows,
         value_rows,

time: 121 us -> 113 us (0.934)
  waiting for transfers between devices: 29.6 us -> 15.5 us
  matrix products: 23.1 us -> 29.9 us
  local copies, waits for them, and re-layouts: 27.7 us -> 25.1 us
    reshape x2 -> x0, local copies, waits for them, and re-layouts: 12.7 us -> none  [the longest x1 6.37 us: per_device(): key_value[:, :, :model_width]]
    all_to_all x1, waiting for transfers between devices: 10.9 us -> 0.41 us  [per_device(): lax.all_to_all(jnp.broadcast_to(memory_pair[None], (owners,) + memory_pai...]
    slice x1 -> x3, local copies, waits for them, and re-layouts: 2.58 us -> 12.6 us  [the longest x2 8.66 us: per_device(): kv_weight[:, model_width:].reshape(model_width, head_count, HEAD_DIM)]
    dot_general x3 -> x4, matrix products: 14 us -> 20.5 us  [the longest x1 8.15 us: per_device(): jnp.einsum('btc,chd->bhtd', embed_normed, kv_weight[:, :model_width].resh...]
    all_to_all x1, waiting for transfers between devices: 4.33 us -> 0.42 us  [per_device(): lax.all_to_all(jnp.concatenate([request, count_pick[:, None]], axis=1), '...]
    convert_element_type x1 -> x2, other arithmetic: 1.28 us -> 4.29 us  [normed(): (wide * lax.rsqrt(jnp.mean(wide * wide, axis=-1, keepdims=True) + 1e-05))...]
    all_to_all x1, starting transfers between devices: 4.34 us -> 5.65 us  [per_device(): lax.all_to_all(jnp.broadcast_to(memory_pair[None], (owners,) + memory_pai...]
  transfers between devices with their start and end apart: 4 -> 4, of which waited for: 3 -> 4; matrix products, arithmetic and copies ran while one was open for 31% -> 38% of each run, Pallas kernels for 0% -> 0%
where the time goes in v7:
time: 113 us; the launch traced here: 112 us
  matrix products  29.9 us (26%)
  starting transfers between devices  25.6 us (23%)
  local copies, waits for them, and re-layouts  25.1 us (22%)
  waiting for transfers between devices  15.5 us (14%)
  other arithmetic  11.6 us (10%)
  Pallas kernels  4.11 us (4%)
    all_to_all x1, waiting for transfers between devices, per_device(): lax.all_to_all(served_read.reshape(owners, latents, model_width), 'smp',...  14.4 us
    slice x2, local copies, waits for them, and re-layouts, per_device(): kv_weight[:, model_width:].reshape(model_width, head_count, HEAD_DIM)  8.66 us
    dot_general x1, matrix products, per_device(): jnp.einsum('btc,chd->bhtd', embed_normed, kv_weight[:, :model_width].resh...  8.15 us
    all_to_all x1, starting transfers between devices, per_device(): lax.all_to_all(jnp.concatenate([request, count_pick[:, None]], axis=1), '...  7.39 us
    all_to_all x1, starting transfers between devices, per_device(): lax.all_to_all(queries2[sample_pick], 'smp', split_axis=0, concat_axis=0,...  6.93 us
    dot_general x1, matrix products, per_device(): jnp.einsum('btc,chd->bhtd', embed_normed, kv_weight[:, model_width:].resh...  6.07 us
    all_to_all x1, starting transfers between devices, per_device(): lax.all_to_all(served_read.reshape(owners, latents, model_width), 'smp',...  5.68 us
    all_to_all x1, starting transfers between devices, per_device(): lax.all_to_all(jnp.broadcast_to(memory_pair[None], (owners,) + memory_pai...  5.65 us
  transfers between devices with their start and end apart: 4, of which 4 were waited for; matrix products, arithmetic and copies ran while one was open for 38% of the time, Pallas kernels for 0%

profile of v7, /device:TPU:0, one launch (start us, length us, event | category | flops | bytes accessed | tf_op | source)
XLA Modules:
  0.0 112.2 jit_solution(3776582873516936247)
XLA Ops:
  0.0 0.0 copy-start
  0.0 1.0 select_reduce_fusion.4
  1.0 0.9 select_reduce_fusion.1
  1.9 0.1 copy.32
  2.0 0.9 add_select_fusion
  2.9 0.1 select_reduce_fusion
  3.0 0.7 pad_add_fusion
  3.7 7.4 %all-to-all-start = ((s32[16,1,65]{2,1,0:T(1,128)}), s32[16,1,65]{2,1,0:T(1,128)S(1)}, u32[]{:S(2)}, u32[]{:S(2)}) async-start(s32[16,1,65]{2,1,0:T(1,128)} %bitcast.4), calls=%async_computation | async-start | bytes 16384 | tf_op jit(solution)/shard_map/all_to_all | solution.py:148
  11.1 0.0 copy-start.2
  11.1 0.0 copy-start.6
  11.1 0.0 copy-start.7
  11.1 4.7 %fusion.26 = (bf16[1024,1024]{1,0:T(8,128)(2,1)}, bf16[1024,1024]{1,0:T(8,128)(2,1)}) fusion(bf16[1024,2048]{1,0:T(8,128)(2,1)} %param.25), kind=kLoop, calls=%fused_computation.66 | loop fusion | bytes 8388608 | tf_op jit(solution)/shard_map/slice | solution.py:199
  15.8 0.0 copy-done.2
  15.8 0.2 multiply_reduce_fusion.1
  16.0 0.1 rsqrt.31
  16.1 1.0 fusion.12
  17.1 0.0 copy-done.6
  17.1 0.0 copy-done.7
  17.1 0.4 all-to-all-done
  17.5 1.1 broadcast_in_dim.103
  18.6 5.7 %all-to-all-start.1 = ((bf16[16,16,2048]{2,1,0:T(8,128)(2,1)}), bf16[16,16,2048]{2,1,0:T(8,128)(2,1)}, u32[]{:S(2)}, u32[]{:S(2)}) async-start(bf16[16,16,2048]{2,1,0:T(8,128)(2,1)} %broadcast_in_dim.103), calls=%async_computation.1 | async-start | bytes 2097152 | tf_op jit(solution)/shard_map/all_to_all | solution.py:164
  24.3 4.0 %copy.33 = bf16[1024,1024]{0,1:T(8,128)(2,1)} copy(bf16[1024,1024]{1,0:T(8,128)(2,1)} %get-tuple-element.17) | data formatting | bytes 4194304 | tf_op jit(solution)/shard_map/slice | solution.py:193
  28.2 4.0 %copy.34 = bf16[1024,1024]{0,1:T(8,128)(2,1)} copy(bf16[1024,1024]{1,0:T(8,128)(2,1)} %get-tuple-element.16) | data formatting | bytes 4194304 | tf_op jit(solution)/shard_map/slice | solution.py:199
  32.2 0.0 copy-start.1
  32.2 3.4 %fusion.8.query_ref = bf16[1,256,1024]{2,1,0:T(8,128)(2,1)} fusion(bf16[256,1024]{1,0:T(8,128)(2,1)} %fusion.12, bf16[1024,1024]{1,0:T(8,128)(2,1)} %param.23), kind=kOutput, calls=%fused_computation.24 | convolution fusion | flops 537133056 | bytes 3145728 | tf_op jit(solution)/shard_map/dot_general | solution.py:160
  35.6 0.1 reshape.202
  35.7 0.0 copy-done.1
  35.7 5.4 %gather_fusion = bf16[1024,1024]{1,0:T(8,128)(2,1)} fusion(bf16[512,1024]{1,0:T(8,128)(2,1)S(1)} %bitcast.70, s32[1024]{0:T(1024)S(1)} %broadcast_clamp_fusion), kind=kCustom, calls=%fused_computation | custom fusion | bytes 4198400 | tf_op jit(solution)/shard_map/gather | solution.py:157
  41.1 2.1 %multiply_reduce_fusion = f32[1024]{0:T(1024)S(1)} fusion(bf16[1024,1024]{1,0:T(8,128)(2,1)} %gather_fusion), kind=kLoop, calls=%fused_computation.6 | loop fusion | flops 3144704 | bytes 2101248 | tf_op jit(solution)/shard_map/reduce_sum | solution.py:16
  43.2 0.1 rsqrt.33
  43.3 0.2 slice_reduce_fusion
  43.4 0.1 iota_compare_fusion
  43.5 3.3 %multiply_convert_fusion = bf16[16,64,1024]{2,1,0:T(8,128)(2,1)} fusion(f32[16,64]{1,0:T(8,128)S(1)} %rsqrt.33, bf16[16,64,1024]{2,1,0:T(8,128)(2,1)} %bitcast.71), kind=kLoop, calls=%fused_computation.5 | loop fusion | flops 3145728 | bytes 4198400 | tf_op jit(solution)/shard_map/convert_element_type | solution.py:16
  46.8 0.0 copy-start.3
  46.8 0.4 all-to-all-done.1
  47.3 4.1 %shard_map.136 = bf16[1,256,1024]{2,1,0:T(8,128)(2,1)} custom-call(s32[1]{0:T(128)} %constant.48.clone.1.counts_ref, bf16[1,256,1024]{2,1,0:T(8,128)(2,1)} %fusion.8.query_ref, bf16[1,256,2048]{2,1,0:T(8,128)(2,1)} %bitcast.8.key_ref.value_ref, bf16[1,256,2048]{2,1,0:T(8,128)(2,1)} %bitcast.8.key_ref.value_ref), custom_call_target="tpu_custom_call" | custom-call | tf_op jit(solution)/shard_map/pallas_call | solution.py:96
  51.4 0.0 copy-done
  51.4 0.0 copy-done.3
  51.4 0.0 copy-start.8
  51.4 2.0 %fusion.9 = (f32[256]{0:T(256)S(1)}, bf16[256,1024]{1,0:T(8,128)(2,1)S(1)}) fusion(bf16[1024,1024]{1,0:T(8,128)(2,1)S(1)} %copy-done, bf16[1,256,1024]{2,1,0:T(8,128)(2,1)} %shard_map.136, bf16[256,1024]{1,0:T(8,128)(2,1)S(1)} %bitcast.72), kind=kOutput, calls=%fused_computation.25 | convolution fusion | flops 538443520 | bytes 3671040 | tf_op jit(solution)/shard_map/dot_general | solution.py:181
  53.4 0.0 copy-done.8
  53.4 0.8 convolution_convert_fusion
  54.2 1.4 %gather_fusion.1 = bf16[16,16,1024]{2,1,0:T(8,128)(2,1)} fusion(bf16[16,16,1024]{2,1,0:T(8,128)(2,1)S(1)} %bitcast.76, s32[1024]{0:T(1024)S(1)} %pad_clamp_fusion.1), kind=kCustom, calls=%fused_computation.1 | custom fusion | bytes 1048640 | tf_op jit(solution)/shard_map/gather | solution.py:188
  55.6 0.0 copy-done.9
  55.6 6.9 %all-to-all-start.2 = ((bf16[16,16,1024]{2,1,0:T(8,128)(2,1)}), bf16[16,16,1024]{2,1,0:T(8,128)(2,1)}, u32[]{:S(2)}, u32[]{:S(2)}) async-start(bf16[16,16,1024]{2,1,0:T(8,128)(2,1)} %gather_fusion.1), calls=%async_computation.2 | async-start | bytes 1048576 | tf_op jit(solution)/shard_map/all_to_all | solution.py:187
  62.5 0.0 copy-start.4
  62.5 0.0 copy-start.5
  62.5 8.2 %convert_bitcast_fusion.1 = bf16[16,16,64,64]{3,2,1,0:T(8,128)(2,1)} fusion(bf16[1024,16,64,1]{0,2,1,3:T(8,128)(2,1)} %bitcast.73, bf16[16,64,1024]{2,1,0:T(8,128)(2,1)} %multiply_convert_fusion), kind=kOutput, calls=%fused_computation.4 | convolution fusion | flops 2148532224 | bytes 6291456 | tf_op jit(solution)/shard_map/btc,chd->bhtd/dot_general | solution.py:190
  70.7 0.0 copy-done.4
  70.7 0.0 copy-done.5
  70.7 6.1 %convert_bitcast_fusion = bf16[16,16,64,64]{3,2,1,0:T(8,128)(2,1)} fusion(bf16[1024,16,64,1]{0,2,1,3:T(8,128)(2,1)S(1)} %bitcast.74, bf16[16,64,1024]{2,1,0:T(8,128)(2,1)S(1)} %copy-done.5), kind=kOutput, calls=%fused_computation.3 | convolution fusion | flops 2148532224 | bytes 6291456 | tf_op jit(solution)/shard_map/btc,chd->bhtd/dot_general | solution.py:196
  76.7 0.3 all-to-all-done.2
  77.0 1.8 %reshape.208 = bf16[16,16,16,64]{3,2,1,0:T(8,128)(2,1)S(1)} reshape(bf16[16,16,1024]{2,1,0:T(8,128)(2,1)} %all-to-all-done.2) | data formatting | bytes 1048576 | tf_op jit(solution)/shard_map/reshape | solution.py:205
  78.8 0.0 copy-start.10
  78.8 4.7 %fusion.3 = (f32[16,16,16]{2,1,0:T(8,128)S(1)}, f32[16,16,16,64]{3,2,1,0:T(8,128)S(1)}) fusion(pred[16,64]{1,0:T(8,128)(4,1)S(1)} %iota_compare_fusion, bf16[16,16,64,64]{3,2,1,0:T(8,128)(2,1)} %convert_bitcast_fusion.1, bf16[16,16,16,64]{3,2,1,0:T(8,128)(2,1)S(1)} %reshape.208), kind=kOutput, calls=%fused_computation.13 | convolution fusion | flops 34336768 | bytes 3687424 | tf_op jit(solution)/shard_map/blhd,bhkd->bhlk/dot_general | solution.py:44
  83.5 1.3 %fusion.4 = f32[16,16,16]{2,1,0:T(8,128)S(1)} fusion(f32[16,16,16,64]{3,2,1,0:T(8,128)S(1)} %get-tuple-element.21, f32[16,16,16]{2,1,0:T(8,128)S(1)} %get-tuple-element.20, pred[16,64]{1,0:T(8,128)(4,1)S(1)} %iota_compare_fusion), kind=kLoop, calls=%fused_computation.14 | loop fusion | flops 1044480 | bytes 1082368 | tf_op jit(solution)/shard_map/reduce_sum | solution.py:50
  84.8 0.0 copy-done.10
  84.8 1.6 %fusion = bf16[16,16,16,64]{3,1,2,0:T(8,128)(2,1)S(1)} fusion(bf16[16,16,64,64]{3,2,1,0:T(8,128)(2,1)S(1)} %copy-done.10, f32[16,16,16,64]{3,2,1,0:T(8,128)S(1)} %get-tuple-element.21, f32[16,16,16]{1,2,0:T(8,128)S(1)} %bitcast.77, f32[16,16,16]{2,1,0:T(8,128)S(1)} %get-tuple-element.20, pred[16,64]{1,0:T(8,128)(4,1)S(1)} %iota_compare_fusion), kind=kOutput, calls=%fused_computation.8 | convolution fusion | flops 35127296 | bytes 3703808 | tf_op jit(solution)/shard_map/bhlk,bhkd->blhd/dot_general | solution.py:52
  86.4 0.3 copy.36
  86.7 1.5 %convert_element_type.85 = bf16[16,16,1024]{2,1,0:T(8,128)(2,1)} reshape(bf16[16,16,16,64]{3,2,1,0:T(8,128)(2,1)S(1)} %copy.36) | data formatting | bytes 1048576 | tf_op jit(solution)/shard_map/convert_element_type | solution.py:60
  88.2 5.7 %all-to-all-start.3 = ((bf16[16,16,1024]{2,1,0:T(8,128)(2,1)}), bf16[16,16,1024]{2,1,0:T(8,128)(2,1)S(1)}, u32[]{:S(2)}, u32[]{:S(2)}) async-start(bf16[16,16,1024]{2,1,0:T(8,128)(2,1)} %convert_element_type.85), calls=%async_computation.3 | async-start | bytes 1048576 | tf_op jit(solution)/shard_map/all_to_all | solution.py:210
  94.0 14.4 %all-to-all-done.3 = bf16[16,16,1024]{2,1,0:T(8,128)(2,1)S(1)} async-done(((bf16[16,16,1024]{2,1,0:T(8,128)(2,1)}), bf16[16,16,1024]{2,1,0:T(8,128)(2,1)S(1)}, u32[]{:S(2)}, u32[]{:S(2)}) %all-to-all-start.3) | async-done | bytes 524320 | tf_op jit(solution)/shard_map/all_to_all | solution.py:210
  108.4 0.6 gather_fusion.2
  109.0 3.2 %fusion.6 = bf16[256,1024]{1,0:T(8,128)(2,1)} fusion(bf16[256,1024]{1,0:T(8,128)(2,1)S(1)} %bitcast.75, bf16[1024,1024]{1,0:T(8,128)(2,1)} %param.27, bf16[256,1024]{1,0:T(8,128)(2,1)} %copy-done.9), kind=kOutput, calls=%fused_computation.20 | convolution fusion | flops 537657344 | bytes 3670016 | tf_op jit(solution)/shard_map/dot_general | solution.py:217
  (14 shorter events, 0.1 us)
Async XLA Ops:
  0.0 51.4 %copy-start = (bf16[1024,1024]{1,0:T(8,128)(2,1)S(1)}, bf16[1024,1024]{1,0:T(8,128)(2,1)}, u32[]{:S(2)}) copy-start(bf16[1024,1024]{1,0:T(8,128)(2,1)} %param.24) | copy-start | bytes 6291460
  3.7 13.8 %all-to-all-start = ((s32[16,1,65]{2,1,0:T(1,128)}), s32[16,1,65]{2,1,0:T(1,128)S(1)}, u32[]{:S(2)}, u32[]{:S(2)}) async-start(s32[16,1,65]{2,1,0:T(1,128)} %bitcast.4), calls=%async_computation | async-start | bytes 16384 | tf_op jit(solution)/shard_map/all_to_all | solution.py:148
  11.1 4.7 %copy-start.2 = (bf16[16,16,1024]{2,1,0:T(8,128)(2,1)S(1)}, bf16[16,16,1024]{2,1,0:T(8,128)(2,1)}, u32[]{:S(2)}) copy-start(bf16[16,16,1024]{2,1,0:T(8,128)(2,1)} %param.14) | copy-start | bytes 1572868
  11.1 6.0 %copy-start.6 = (bf16[16,1024]{1,0:T(8,128)(2,1)S(1)}, bf16[16,1024]{1,0:T(8,128)(2,1)}, u32[]{:S(2)}) copy-start(bf16[16,1024]{1,0:T(8,128)(2,1)} %param.22) | copy-start | bytes 98308
  11.1 6.0 %copy-start.7 = (bf16[16,1024]{1,0:T(8,128)(2,1)S(1)}, bf16[16,1024]{1,0:T(8,128)(2,1)}, u32[]{:S(2)}) copy-start(bf16[16,1024]{1,0:T(8,128)(2,1)} %param.21) | copy-start | bytes 98308
  18.6 28.7 %all-to-all-start.1 = ((bf16[16,16,2048]{2,1,0:T(8,128)(2,1)}), bf16[16,16,2048]{2,1,0:T(8,128)(2,1)}, u32[]{:S(2)}, u32[]{:S(2)}) async-start(bf16[16,16,2048]{2,1,0:T(8,128)(2,1)} %broadcast_in_dim.103), calls=%async_computation.1 | async-start | bytes 2097152 | tf_op jit(solution)/shard_map/all_to_all | solution.py:164
  32.2 3.5 %copy-start.1 = (bf16[1,512,1024]{2,1,0:T(8,128)(2,1)S(1)}, bf16[1,512,1024]{2,1,0:T(8,128)(2,1)}, u32[]{:S(2)}) copy-start(bf16[1,512,1024]{2,1,0:T(8,128)(2,1)} %param.20) | copy-start | bytes 3145732
  46.8 4.5 %copy-start.3 = (bf16[16,16,1024]{2,1,0:T(8,128)(2,1)S(1)}, bf16[16,16,1024]{2,1,0:T(8,128)(2,1)}, u32[]{:S(2)}) copy-start(bf16[16,16,1024]{2,1,0:T(8,128)(2,1)} %param.14) | copy-start | bytes 1572868
  51.4 2.0 %copy-start.8 = (bf16[1024,1024]{1,0:T(8,128)(2,1)S(1)}, bf16[1024,1024]{1,0:T(8,128)(2,1)}, u32[]{:S(2)}) copy-start(bf16[1024,1024]{1,0:T(8,128)(2,1)} %param.26) | copy-start | bytes 6291460
  53.4 2.2 %copy-start.9 = (bf16[256,1024]{1,0:T(8,128)(2,1)}, bf16[256,1024]{1,0:T(8,128)(2,1)S(1)}, u32[]{:S(2)}) copy-start(bf16[256,1024]{1,0:T(8,128)(2,1)S(1)} %get-tuple-element.19) | copy-start | bytes 1572868
  55.6 21.4 %all-to-all-start.2 = ((bf16[16,16,1024]{2,1,0:T(8,128)(2,1)}), bf16[16,16,1024]{2,1,0:T(8,128)(2,1)}, u32[]{:S(2)}, u32[]{:S(2)}) async-start(bf16[16,16,1024]{2,1,0:T(8,128)(2,1)} %gather_fusion.1), calls=%async_computation.2 | async-start | bytes 1048576 | tf_op jit(solution)/shard_map/all_to_all | solution.py:187
  62.5 8.2 %copy-start.4 = (bf16[1024,1024]{0,1:T(8,128)(2,1)S(1)}, bf16[1024,1024]{0,1:T(8,128)(2,1)}, u32[]{:S(2)}) copy-start(bf16[1024,1024]{0,1:T(8,128)(2,1)} %copy.34) | copy-start | bytes 6291460
  62.5 8.2 %copy-start.5 = (bf16[16,64,1024]{2,1,0:T(8,128)(2,1)S(1)}, bf16[16,64,1024]{2,1,0:T(8,128)(2,1)}, u32[]{:S(2)}) copy-start(bf16[16,64,1024]{2,1,0:T(8,128)(2,1)} %multiply_convert_fusion) | copy-start | bytes 6291460
  78.8 6.1 %copy-start.10 = (bf16[16,16,64,64]{3,2,1,0:T(8,128)(2,1)S(1)}, bf16[16,16,64,64]{3,2,1,0:T(8,128)(2,1)}, u32[]{:S(2)}) copy-start(bf16[16,16,64,64]{3,2,1,0:T(8,128)(2,1)} %convert_bitcast_fusion) | copy-start | bytes 6291460
  88.2 20.2 %all-to-all-start.3 = ((bf16[16,16,1024]{2,1,0:T(8,128)(2,1)}), bf16[16,16,1024]{2,1,0:T(8,128)(2,1)S(1)}, u32[]{:S(2)}, u32[]{:S(2)}) async-start(bf16[16,16,1024]{2,1,0:T(8,128)(2,1)} %convert_element_type.85), calls=%async_computation.3 | async-start | bytes 1048576 | tf_op jit(solution)/shard_map/all_to_all | solution.py:210

commit v8 on v7

--- a/solution.py
+++ b/solution.py
@@ -187,18 +187,13 @@
     served_queries = lax.all_to_all(
         queries2[sample_pick], "smp", split_axis=0, concat_axis=0, tiled=True
     )
-    key_rows = jnp.einsum(
-        "btc,chd->bhtd",
+    key_value = jnp.einsum(
+        "btc,cjhd->jbhtd",
         embed_normed,
-        kv_weight[:, :model_width].reshape(model_width, head_count, HEAD_DIM),
+        kv_weight.reshape(model_width, 2, head_count, HEAD_DIM),
         preferred_element_type=jnp.float32,
     ).astype(jnp.bfloat16)
-    value_rows = jnp.einsum(
-        "btc,chd->bhtd",
-        embed_normed,
-        kv_weight[:, model_width:].reshape(model_width, head_count, HEAD_DIM),
-        preferred_element_type=jnp.float32,
-    ).astype(jnp.bfloat16)
+    key_rows, value_rows = key_value[0], key_value[1]
     key_rows, value_rows = lax.optimization_barrier((key_rows, value_rows))
     live_tokens = jnp.arange(token_total, dtype=jnp.int32)[None, :] < served[:, token_total:]
     served_read = attend_heads(

time: 113 us -> 113 us (level)
  waiting for transfers between devices: 15.5 us -> 18.7 us
  other arithmetic: 11.6 us -> 14.5 us
  matrix products: 29.9 us -> 27.1 us
  local copies, waits for them, and re-layouts: 25.1 us -> 23.1 us
    slice x3 -> x0, local copies, waits for them, and re-layouts: 12.6 us -> none  [the longest x2 8.66 us: per_device(): kv_weight[:, model_width:].reshape(model_width, head_count, HEAD_DIM)]
    unnamed x22 -> x13, local copies, waits for them, and re-layouts: 0.05 us -> 6.43 us
    squeeze x0 -> x1, local copies, waits for them, and re-layouts: none -> 4.21 us  [per_device(): key_rows, value_rows = (key_value[0], key_value[1])]
    dot_general x2 -> x1, matrix products: 14.2 us -> 11.4 us  [per_device(): jnp.einsum('btc,cjhd->jbhtd', embed_normed, kv_weight.reshape(model_width...]
    all_to_all x1, waiting for transfers between devices: 0.42 us -> 2.32 us  [per_device(): lax.all_to_all(jnp.concatenate([request, count_pick[:, None]], axis=1), '...]
    all_to_all x1, waiting for transfers between devices: 0.41 us -> 1.9 us  [per_device(): lax.all_to_all(jnp.broadcast_to(memory_pair[None], (owners,) + memory_pai...]
    all_to_all x1, starting transfers between devices: 5.65 us -> 4.35 us  [per_device(): lax.all_to_all(jnp.broadcast_to(memory_pair[None], (owners,) + memory_pai...]
  transfers between devices with their start and end apart: 4 -> 4, of which waited for: 4 -> 3; matrix products, arithmetic and copies ran while one was open for 38% -> 36% of each run, Pallas kernels for 0% -> 0%
where the time goes in v8:
time: 113 us; the launch traced here: 112 us
  matrix products  27.1 us (24%)
  starting transfers between devices  24.6 us (22%)
  local copies, waits for them, and re-layouts  23.1 us (20%)
  waiting for transfers between devices  18.7 us (17%)
  other arithmetic  14.5 us (13%)
  Pallas kernels  4.11 us (4%)
    all_to_all x1, waiting for transfers between devices, per_device(): lax.all_to_all(served_read.reshape(owners, latents, model_width), 'smp',...  14.4 us
    dot_general x1, matrix products, per_device(): jnp.einsum('btc,cjhd->jbhtd', embed_normed, kv_weight.reshape(model_width...  11.4 us
    all_to_all x1, starting transfers between devices, per_device(): lax.all_to_all(jnp.concatenate([request, count_pick[:, None]], axis=1), '...  7.39 us
    all_to_all x1, starting transfers between devices, per_device(): lax.all_to_all(queries2[sample_pick], 'smp', split_axis=0, concat_axis=0,...  6.88 us
    unnamed x13, local copies, waits for them, and re-layouts  6.43 us
    all_to_all x1, starting transfers between devices, per_device(): lax.all_to_all(served_read.reshape(owners, latents, model_width), 'smp',...  5.95 us
    gather x1, local copies, waits for them, and re-layouts, per_device(): served_embed = panel_table[served_index.reshape(-1)]  5.37 us
    convert_element_type x2, other arithmetic, normed(): (wide * lax.rsqrt(jnp.mean(wide * wide, axis=-1, keepdims=True) + 1e-05))...  5.33 us
  transfers between devices with their start and end apart: 4, of which 3 were waited for; matrix products, arithmetic and copies ran while one was open for 36% of the time, Pallas kernels for 0%

profile of v8, /device:TPU:0, one launch (start us, length us, event | category | flops | bytes accessed | tf_op | source)
XLA Modules:
  0.0 112.2 jit_solution(10616940599074689077)
XLA Ops:
  0.0 0.0 copy-start
  0.0 1.0 select_reduce_fusion.4
  1.0 0.9 select_reduce_fusion.1
  1.9 0.1 copy.28
  2.0 0.9 add_select_fusion
  2.9 0.1 select_reduce_fusion
  3.0 0.7 pad_add_fusion
  3.7 7.4 %all-to-all-start = ((s32[16,1,65]{2,1,0:T(1,128)}), s32[16,1,65]{2,1,0:T(1,128)S(1)}, u32[]{:S(2)}, u32[]{:S(2)}) async-start(s32[16,1,65]{2,1,0:T(1,128)} %bitcast.4), calls=%async_computation | async-start | bytes 16384 | tf_op jit(solution)/shard_map/all_to_all | solution.py:148
  11.1 1.2 %multiply_reduce_fusion.1 = f32[16,16]{1,0:T(8,128)S(1)} fusion(bf16[16,16,1024]{2,1,0:T(8,128)(2,1)} %param.14), kind=kLoop, calls=%fused_computation.34 | loop fusion | flops 786176 | bytes 525312 | tf_op jit(solution)/shard_map/reduce_sum | solution.py:16
  12.3 0.1 rsqrt.31
  12.4 2.0 %fusion.11 = bf16[256,1024]{1,0:T(8,128)(2,1)} fusion(bf16[16,16,1024]{2,1,0:T(8,128)(2,1)} %param.14, f32[256]{0:T(256)S(1)} %rsqrt.31), kind=kLoop, calls=%fused_computation.28 | loop fusion | flops 786432 | bytes 1049600 | tf_op jit(solution)/shard_map/convert_element_type | solution.py:16
  14.4 0.8 pad_maximum_fusion
  15.2 2.3 %all-to-all-done = s32[16,1,65]{2,1,0:T(1,128)S(1)} async-done(((s32[16,1,65]{2,1,0:T(1,128)}), s32[16,1,65]{2,1,0:T(1,128)S(1)}, u32[]{:S(2)}, u32[]{:S(2)}) %all-to-all-start) | async-done | bytes 4192 | tf_op jit(solution)/shard_map/all_to_all | solution.py:148
  17.5 1.1 broadcast_in_dim.103
  18.6 4.3 %all-to-all-start.1 = ((bf16[16,16,2048]{2,1,0:T(8,128)(2,1)}), bf16[16,16,2048]{2,1,0:T(8,128)(2,1)}, u32[]{:S(2)}, u32[]{:S(2)}) async-start(bf16[16,16,2048]{2,1,0:T(8,128)(2,1)} %broadcast_in_dim.103), calls=%async_computation.1 | async-start | bytes 2097152 | tf_op jit(solution)/shard_map/all_to_all | solution.py:164
  23.0 6.4 %copy.29 = bf16[1024,2048]{0,1:T(8,128)(2,1)} copy(bf16[1024,2048]{1,0:T(8,128)(2,1)} %param.25) | data formatting | bytes 8388608 | tf_op args[11]
  29.4 0.0 copy-start.1
  29.4 3.4 %fusion.7.query_ref = bf16[1,256,1024]{2,1,0:T(8,128)(2,1)} fusion(bf16[256,1024]{1,0:T(8,128)(2,1)} %fusion.11, bf16[1024,1024]{1,0:T(8,128)(2,1)} %param.23), kind=kOutput, calls=%fused_computation.24 | convolution fusion | flops 537133056 | bytes 3145728 | tf_op jit(solution)/shard_map/dot_general | solution.py:160
  32.8 0.1 reshape.199
  32.9 0.0 copy-done.1
  32.9 5.4 %gather_fusion = bf16[1024,1024]{1,0:T(8,128)(2,1)} fusion(bf16[512,1024]{1,0:T(8,128)(2,1)S(1)} %bitcast.66, s32[1024]{0:T(1024)S(1)} %broadcast_clamp_fusion), kind=kCustom, calls=%fused_computation | custom fusion | bytes 4198400 | tf_op jit(solution)/shard_map/gather | solution.py:157
  38.2 2.1 %multiply_reduce_fusion = f32[1024]{0:T(1024)S(1)} fusion(bf16[1024,1024]{1,0:T(8,128)(2,1)} %gather_fusion), kind=kLoop, calls=%fused_computation.7 | loop fusion | flops 3144704 | bytes 2101248 | tf_op jit(solution)/shard_map/reduce_sum | solution.py:16
  40.3 0.1 rsqrt.33
  40.4 0.2 slice_reduce_fusion
  40.6 0.1 iota_compare_fusion
  40.7 3.3 %multiply_convert_fusion = bf16[16,64,1024]{2,1,0:T(8,128)(2,1)} fusion(f32[16,64]{1,0:T(8,128)S(1)} %rsqrt.33, bf16[16,64,1024]{2,1,0:T(8,128)(2,1)} %bitcast.67), kind=kLoop, calls=%fused_computation.6 | loop fusion | flops 3145728 | bytes 4198400 | tf_op jit(solution)/shard_map/convert_element_type | solution.py:16
  44.0 0.0 copy-start.3
  44.0 1.9 %all-to-all-done.1 = bf16[16,16,2048]{2,1,0:T(8,128)(2,1)} async-done(((bf16[16,16,2048]{2,1,0:T(8,128)(2,1)}), bf16[16,16,2048]{2,1,0:T(8,128)(2,1)}, u32[]{:S(2)}, u32[]{:S(2)}) %all-to-all-start.1) | async-done | bytes 1048608 | tf_op jit(solution)/shard_map/all_to_all | solution.py:164
  45.9 4.1 %shard_map.136 = bf16[1,256,1024]{2,1,0:T(8,128)(2,1)} custom-call(s32[1]{0:T(128)} %constant.48.clone.1.counts_ref, bf16[1,256,1024]{2,1,0:T(8,128)(2,1)} %fusion.7.query_ref, bf16[1,256,2048]{2,1,0:T(8,128)(2,1)} %bitcast.8.key_ref.value_ref, bf16[1,256,2048]{2,1,0:T(8,128)(2,1)} %bitcast.8.key_ref.value_ref), custom_call_target="tpu_custom_call" | custom-call | tf_op jit(solution)/shard_map/pallas_call | solution.py:96
  50.0 0.0 copy-done
  50.0 0.0 copy-done.3
  50.0 0.0 copy-start.4
  50.0 2.0 %fusion.8 = (f32[256]{0:T(256)S(1)}, bf16[256,1024]{1,0:T(8,128)(2,1)S(1)}) fusion(bf16[1024,1024]{1,0:T(8,128)(2,1)S(1)} %copy-done, bf16[1,256,1024]{2,1,0:T(8,128)(2,1)} %shard_map.136, bf16[256,1024]{1,0:T(8,128)(2,1)S(1)} %bitcast.69), kind=kOutput, calls=%fused_computation.25 | convolution fusion | flops 538443520 | bytes 3671040 | tf_op jit(solution)/shard_map/dot_general | solution.py:181
  52.0 0.0 copy-start.5
  52.0 0.0 copy-done.4
  52.1 0.8 convolution_convert_fusion
  52.8 1.4 %gather_fusion.1 = bf16[16,16,1024]{2,1,0:T(8,128)(2,1)} fusion(bf16[16,16,1024]{2,1,0:T(8,128)(2,1)S(1)} %bitcast.71, s32[1024]{0:T(1024)S(1)} %pad_clamp_fusion.1), kind=kCustom, calls=%fused_computation.1 | custom fusion | bytes 1048640 | tf_op jit(solution)/shard_map/gather | solution.py:188
  54.2 0.0 copy-done.5
  54.2 6.9 %all-to-all-start.2 = ((bf16[16,16,1024]{2,1,0:T(8,128)(2,1)}), bf16[16,16,1024]{2,1,0:T(8,128)(2,1)}, u32[]{:S(2)}, u32[]{:S(2)}) async-start(bf16[16,16,1024]{2,1,0:T(8,128)(2,1)} %gather_fusion.1), calls=%async_computation.2 | async-start | bytes 1048576 | tf_op jit(solution)/shard_map/all_to_all | solution.py:187
  61.1 11.4 %convert_bitcast_fusion = bf16[2,16,16,64,64]{4,3,2,0,1:T(8,128)(2,1)S(1)} fusion(bf16[1024,2,16,64,1]{0,3,2,1,4:T(8,128)(2,1)} %bitcast.68, bf16[16,64,1024]{2,1,0:T(8,128)(2,1)} %multiply_convert_fusion), kind=kOutput, calls=%fused_computation.3 | convolution fusion | flops 4297064448 | bytes 10485760 | tf_op jit(solution)/shard_map/btc,cjhd->jbhtd/dot_general | solution.py:190
  72.5 4.2 %slice_bitcast_fusion = (bf16[16,16,64,64]{3,2,1,0:T(8,128)(2,1)}, bf16[16,16,64,64]{3,2,1,0:T(8,128)(2,1)}) fusion(bf16[2,16,16,64,64]{4,3,2,0,1:T(8,128)(2,1)S(1)} %convert_bitcast_fusion), kind=kLoop, calls=%fused_computation.4 | loop fusion | bytes 8388608 | tf_op jit(solution)/shard_map/squeeze | solution.py:196
  76.7 0.0 all-to-all-done.2
  76.7 1.8 %reshape.204 = bf16[16,16,16,64]{3,2,1,0:T(8,128)(2,1)S(1)} reshape(bf16[16,16,1024]{2,1,0:T(8,128)(2,1)} %all-to-all-done.2) | data formatting | bytes 1048576 | tf_op jit(solution)/shard_map/reshape | solution.py:200
  78.5 0.0 copy-start.2
  78.5 4.7 %fusion.2 = (f32[16,16,16]{2,1,0:T(8,128)S(1)}, f32[16,16,16,64]{3,2,1,0:T(8,128)S(1)}) fusion(pred[16,64]{1,0:T(8,128)(4,1)S(1)} %iota_compare_fusion, bf16[16,16,64,64]{3,2,1,0:T(8,128)(2,1)} %get-tuple-element.12, bf16[16,16,16,64]{3,2,1,0:T(8,128)(2,1)S(1)} %reshape.204), kind=kOutput, calls=%fused_computation.13 | convolution fusion | flops 34336768 | bytes 3687424 | tf_op jit(solution)/shard_map/blhd,bhkd->bhlk/dot_general | solution.py:44
  83.2 1.3 %fusion.3 = f32[16,16,16]{2,1,0:T(8,128)S(1)} fusion(f32[16,16,16,64]{3,2,1,0:T(8,128)S(1)} %get-tuple-element.21, f32[16,16,16]{2,1,0:T(8,128)S(1)} %get-tuple-element.20, pred[16,64]{1,0:T(8,128)(4,1)S(1)} %iota_compare_fusion), kind=kLoop, calls=%fused_computation.14 | loop fusion | flops 1044480 | bytes 1082368 | tf_op jit(solution)/shard_map/reduce_sum | solution.py:50
  84.5 0.0 copy-done.2
  84.6 1.6 %fusion.1 = bf16[16,16,16,64]{3,1,2,0:T(8,128)(2,1)S(1)} fusion(bf16[16,16,64,64]{3,2,1,0:T(8,128)(2,1)S(1)} %copy-done.2, f32[16,16,16,64]{3,2,1,0:T(8,128)S(1)} %get-tuple-element.21, f32[16,16,16]{1,2,0:T(8,128)S(1)} %bitcast.72, f32[16,16,16]{2,1,0:T(8,128)S(1)} %get-tuple-element.20, pred[16,64]{1,0:T(8,128)(4,1)S(1)} %iota_compare_fusion), kind=kOutput, calls=%fused_computation.10 | convolution fusion | flops 35127296 | bytes 3703808 | tf_op jit(solution)/shard_map/bhlk,bhkd->blhd/dot_general | solution.py:52
  86.2 0.3 copy.31
  86.4 1.5 %convert_element_type.77 = bf16[16,16,1024]{2,1,0:T(8,128)(2,1)} reshape(bf16[16,16,16,64]{3,2,1,0:T(8,128)(2,1)S(1)} %copy.31) | data formatting | bytes 1048576 | tf_op jit(solution)/shard_map/convert_element_type | solution.py:60
  88.0 5.9 %all-to-all-start.3 = ((bf16[16,16,1024]{2,1,0:T(8,128)(2,1)}), bf16[16,16,1024]{2,1,0:T(8,128)(2,1)S(1)}, u32[]{:S(2)}, u32[]{:S(2)}) async-start(bf16[16,16,1024]{2,1,0:T(8,128)(2,1)} %convert_element_type.77), calls=%async_computation.3 | async-start | bytes 1048576 | tf_op jit(solution)/shard_map/all_to_all | solution.py:205
  93.9 14.4 %all-to-all-done.3 = bf16[16,16,1024]{2,1,0:T(8,128)(2,1)S(1)} async-done(((bf16[16,16,1024]{2,1,0:T(8,128)(2,1)}), bf16[16,16,1024]{2,1,0:T(8,128)(2,1)S(1)}, u32[]{:S(2)}, u32[]{:S(2)}) %all-to-all-start.3) | async-done | bytes 524320 | tf_op jit(solution)/shard_map/all_to_all | solution.py:205
  108.4 0.6 gather_fusion.2
  109.0 3.2 %fusion.5 = bf16[256,1024]{1,0:T(8,128)(2,1)} fusion(bf16[256,1024]{1,0:T(8,128)(2,1)S(1)} %bitcast.70, bf16[1024,1024]{1,0:T(8,128)(2,1)} %param.27, bf16[256,1024]{1,0:T(8,128)(2,1)} %copy-done.5), kind=kOutput, calls=%fused_computation.20 | convolution fusion | flops 537657344 | bytes 3670016 | tf_op jit(solution)/shard_map/dot_general | solution.py:212
  (12 shorter events, 0.1 us)
Async XLA Ops:
  0.0 50.0 %copy-start = (bf16[1024,1024]{1,0:T(8,128)(2,1)S(1)}, bf16[1024,1024]{1,0:T(8,128)(2,1)}, u32[]{:S(2)}) copy-start(bf16[1024,1024]{1,0:T(8,128)(2,1)} %param.24) | copy-start | bytes 6291460
  3.7 13.8 %all-to-all-start = ((s32[16,1,65]{2,1,0:T(1,128)}), s32[16,1,65]{2,1,0:T(1,128)S(1)}, u32[]{:S(2)}, u32[]{:S(2)}) async-start(s32[16,1,65]{2,1,0:T(1,128)} %bitcast.4), calls=%async_computation | async-start | bytes 16384 | tf_op jit(solution)/shard_map/all_to_all | solution.py:148
  18.6 27.3 %all-to-all-start.1 = ((bf16[16,16,2048]{2,1,0:T(8,128)(2,1)}), bf16[16,16,2048]{2,1,0:T(8,128)(2,1)}, u32[]{:S(2)}, u32[]{:S(2)}) async-start(bf16[16,16,2048]{2,1,0:T(8,128)(2,1)} %broadcast_in_dim.103), calls=%async_computation.1 | async-start | bytes 2097152 | tf_op jit(solution)/shard_map/all_to_all | solution.py:164
  29.4 3.5 %copy-start.1 = (bf16[1,512,1024]{2,1,0:T(8,128)(2,1)S(1)}, bf16[1,512,1024]{2,1,0:T(8,128)(2,1)}, u32[]{:S(2)}) copy-start(bf16[1,512,1024]{2,1,0:T(8,128)(2,1)} %param.20) | copy-start | bytes 3145732
  44.0 6.0 %copy-start.3 = (bf16[16,16,1024]{2,1,0:T(8,128)(2,1)S(1)}, bf16[16,16,1024]{2,1,0:T(8,128)(2,1)}, u32[]{:S(2)}) copy-start(bf16[16,16,1024]{2,1,0:T(8,128)(2,1)} %param.14) | copy-start | bytes 1572868
  50.0 2.0 %copy-start.4 = (bf16[1024,1024]{1,0:T(8,128)(2,1)S(1)}, bf16[1024,1024]{1,0:T(8,128)(2,1)}, u32[]{:S(2)}) copy-start(bf16[1024,1024]{1,0:T(8,128)(2,1)} %param.26) | copy-start | bytes 6291460
  52.0 2.2 %copy-start.5 = (bf16[256,1024]{1,0:T(8,128)(2,1)}, bf16[256,1024]{1,0:T(8,128)(2,1)S(1)}, u32[]{:S(2)}) copy-start(bf16[256,1024]{1,0:T(8,128)(2,1)S(1)} %get-tuple-element.19) | copy-start | bytes 1572868
  54.2 22.5 %all-to-all-start.2 = ((bf16[16,16,1024]{2,1,0:T(8,128)(2,1)}), bf16[16,16,1024]{2,1,0:T(8,128)(2,1)}, u32[]{:S(2)}, u32[]{:S(2)}) async-start(bf16[16,16,1024]{2,1,0:T(8,128)(2,1)} %gather_fusion.1), calls=%async_computation.2 | async-start | bytes 1048576 | tf_op jit(solution)/shard_map/all_to_all | solution.py:187
  78.5 6.1 %copy-start.2 = (bf16[16,16,64,64]{3,2,1,0:T(8,128)(2,1)S(1)}, bf16[16,16,64,64]{3,2,1,0:T(8,128)(2,1)}, u32[]{:S(2)}) copy-start(bf16[16,16,64,64]{3,2,1,0:T(8,128)(2,1)} %get-tuple-element.11) | copy-start | bytes 6291460
  88.0 20.4 %all-to-all-start.3 = ((bf16[16,16,1024]{2,1,0:T(8,128)(2,1)}), bf16[16,16,1024]{2,1,0:T(8,128)(2,1)S(1)}, u32[]{:S(2)}, u32[]{:S(2)}) async-start(bf16[16,16,1024]{2,1,0:T(8,128)(2,1)} %convert_element_type.77), calls=%async_computation.3 | async-start | bytes 1048576 | tf_op jit(solution)/shard_map/all_to_all | solution.py:205

commit v9 on v7

--- a/solution.py
+++ b/solution.py
@@ -145,13 +145,26 @@
     sample_pick = jnp.sum(
         jnp.where(slot_pick, jnp.arange(local_samples, dtype=jnp.int32)[None, :], 0), axis=1
     )
-    served = lax.all_to_all(
-        jnp.concatenate([request, count_pick[:, None]], axis=1),
+    table = jnp.concatenate([request, count_pick[:, None]], axis=1)
+    code_base = 64
+    codes = jnp.concatenate([table // code_base, table % code_base], axis=1).astype(jnp.bfloat16)
+    memory_pair = jnp.concatenate([memory_key, memory_value], axis=1)
+    memory_count = memory_pair.shape[0]
+    code_rows = jnp.zeros((owners, 8, 2 * model_width), jnp.bfloat16)
+    code_rows = code_rows.at[:, 0, : codes.shape[1]].set(codes)
+    arrived = lax.all_to_all(
+        jnp.concatenate(
+            [jnp.broadcast_to(memory_pair[None], (owners,) + memory_pair.shape), code_rows],
+            axis=1,
+        ),
         "smp",
         split_axis=0,
         concat_axis=0,
         tiled=True,
     )
+    memory_rows = arrived[:, :memory_count].reshape(1, -1, 2 * model_width)
+    code_back = arrived[:, memory_count, : codes.shape[1]].astype(jnp.int32)
+    served = code_back[:, : table.shape[1]] * code_base + code_back[:, table.shape[1] :]
     served_index = served[:, :token_total]
     panel_table = panels.reshape(sess_dev * unit_total, model_width)
     served_embed = panel_table[served_index.reshape(-1)]
@@ -160,16 +173,7 @@
     queries = jnp.dot(normed(flat_state), q1_weight, preferred_element_type=jnp.float32).astype(
         jnp.bfloat16
     )
-    memory_pair = jnp.concatenate([memory_key, memory_value], axis=1)
-    memory_rows = lax.all_to_all(
-        jnp.broadcast_to(memory_pair[None], (owners,) + memory_pair.shape),
-        "smp",
-        split_axis=0,
-        concat_axis=0,
-        tiled=True,
-    ).reshape(1, -1, 2 * model_width)
     embed_normed = normed(served_embed).reshape(owners, token_total, model_width)
-    embed_normed, memory_rows = lax.optimization_barrier((embed_normed, memory_rows))
     memory_total = memory_rows.shape[1]
     read_mem = attend_kernel(
         queries.reshape(1, row_total, model_width),

time: 113 us -> 128 us (1.13)
  waiting for transfers between devices: 15.5 us -> 30.4 us
  local copies, waits for them, and re-layouts: 25.1 us -> 28.6 us
  starting transfers between devices: 25.6 us -> 22.7 us
    all_to_all x2 -> x1, waiting for transfers between devices: 0.82 us -> 15.9 us  [per_device(): lax.all_to_all(jnp.concatenate([jnp.broadcast_to(memory_pair[None], (owne...]
    all_to_all x2 -> x1, starting transfers between devices: 13 us -> 7.56 us  [per_device(): lax.all_to_all(jnp.concatenate([jnp.broadcast_to(memory_pair[None], (owne...]
    convert_element_type x2, other arithmetic: 4.29 us -> 0.56 us  [normed(): (wide * lax.rsqrt(jnp.mean(wide * wide, axis=-1, keepdims=True) + 1e-05))...]
    dot_general x1, matrix products: 0.76 us -> 3.39 us  [per_device(): jnp.dot(normed(hidden), q2_weight, preferred_element_type=jnp.float32)]
    slice x0 -> x1, local copies, waits for them, and re-layouts: none -> 2.32 us  [per_device(): memory_rows = arrived[:, :memory_count].reshape(1, -1, 2 * model_width)]
    all_to_all x1, starting transfers between devices: 6.93 us -> 9.17 us  [per_device(): lax.all_to_all(queries2[sample_pick], 'smp', split_axis=0, concat_axis=0,...]
    dot_general x1, matrix products: 8.15 us -> 6.05 us  [per_device(): jnp.einsum('btc,chd->bhtd', embed_normed, kv_weight[:, :model_width].resh...]
  transfers between devices with their start and end apart: 4 -> 3, of which waited for: 4 -> 2; matrix products, arithmetic and copies ran while one was open for 38% -> 29% of each run, Pallas kernels for 0% -> 0%
where the time goes in v9:
time: 128 us; the launch traced here: 127 us
  matrix products  30.6 us (24%)
  waiting for transfers between devices  30.4 us (24%)
  local copies, waits for them, and re-layouts  28.6 us (22%)
  starting transfers between devices  22.7 us (18%)
  other arithmetic  10.6 us (8%)
  Pallas kernels  4.11 us (3%)
    all_to_all x1, waiting for transfers between devices, per_device(): lax.all_to_all(jnp.concatenate([jnp.broadcast_to(memory_pair[None], (owne...  15.9 us
    all_to_all x1, waiting for transfers between devices, per_device(): lax.all_to_all(served_read.reshape(owners, latents, model_width), 'smp',...  14.4 us
    all_to_all x1, starting transfers between devices, per_device(): lax.all_to_all(queries2[sample_pick], 'smp', split_axis=0, concat_axis=0,...  9.17 us
    slice x2, local copies, waits for them, and re-layouts, per_device(): kv_weight[:, model_width:].reshape(model_width, head_count, HEAD_DIM)  8.61 us
    all_to_all x1, starting transfers between devices, per_device(): lax.all_to_all(jnp.concatenate([jnp.broadcast_to(memory_pair[None], (owne...  7.56 us
    dot_general x1, matrix products, per_device(): jnp.einsum('btc,chd->bhtd', embed_normed, kv_weight[:, model_width:].resh...  6.05 us
    dot_general x1, matrix products, per_device(): jnp.einsum('btc,chd->bhtd', embed_normed, kv_weight[:, :model_width].resh...  6.05 us
    all_to_all x1, starting transfers between devices, per_device(): lax.all_to_all(served_read.reshape(owners, latents, model_width), 'smp',...  5.94 us
  transfers between devices with their start and end apart: 3, of which 2 were waited for; matrix products, arithmetic and copies ran while one was open for 29% of the time, Pallas kernels for 0%

profile of v9, /device:TPU:0, one launch (start us, length us, event | category | flops | bytes accessed | tf_op | source)
XLA Modules:
  0.0 127.3 jit_solution(13536348000053332919)
XLA Ops:
  0.0 0.0 copy-start
  0.0 1.0 select_reduce_fusion.4
  1.0 0.9 select_reduce_fusion.1
  1.9 0.1 copy.36
  2.0 0.9 add_select_fusion.2
  2.9 0.1 select_reduce_fusion
  3.0 0.1 fusion.29
  3.1 0.1 pad_maximum_fusion.1
  3.2 0.8 pad_maximum_fusion
  4.0 0.1 broadcast_in_dim.94
  4.1 1.4 %fusion.7 = bf16[16,24,2048]{2,1,0:T(8,128)(2,1)} fusion(bf16[16,1,130]{2,1,0:T(2,128)(2,1)S(1)} %copy.44, bf16[16,16,2048]{2,1,0:T(8,128)(2,1)S(1)} %broadcast_in_dim.94), kind=kLoop, calls=%fused_computation.18 | loop fusion | flops 4718592 | bytes 2625600 | tf_op jit(solution)/shard_map/concatenate | solution.py:156
  5.5 0.0 copy-start.3
  5.5 7.6 %all-to-all-start = ((bf16[16,24,2048]{2,1,0:T(8,128)(2,1)}), bf16[16,24,2048]{2,1,0:T(8,128)(2,1)}, u32[]{:S(2)}, u32[]{:S(2)}) async-start(bf16[16,24,2048]{2,1,0:T(8,128)(2,1)} %fusion.7), calls=%async_computation | async-start | bytes 3145728 | tf_op jit(solution)/shard_map/all_to_all | solution.py:155
  13.1 0.0 copy-done.3
  13.1 0.2 multiply_reduce_fusion
  13.3 0.1 rsqrt.31
  13.4 4.7 %fusion.34 = (bf16[1024,1024]{1,0:T(8,128)(2,1)}, bf16[1024,1024]{1,0:T(8,128)(2,1)}) fusion(bf16[1024,2048]{1,0:T(8,128)(2,1)} %param.27), kind=kLoop, calls=%fused_computation.86 | loop fusion | bytes 8388608 | tf_op jit(solution)/shard_map/slice | solution.py:203
  18.0 4.0 %copy.39 = bf16[1024,1024]{0,1:T(8,128)(2,1)} copy(bf16[1024,1024]{1,0:T(8,128)(2,1)} %get-tuple-element.24) | data formatting | bytes 4194304 | tf_op jit(solution)/shard_map/slice | solution.py:203
  22.0 3.9 %copy.38 = bf16[1024,1024]{0,1:T(8,128)(2,1)} copy(bf16[1024,1024]{1,0:T(8,128)(2,1)} %get-tuple-element.25) | data formatting | bytes 4194304 | tf_op jit(solution)/shard_map/slice | solution.py:197
  26.0 0.2 fusion.14
  26.1 3.1 %fusion.10.query_ref = bf16[1,256,1024]{2,1,0:T(8,128)(2,1)} fusion(bf16[256,1024]{1,0:T(8,128)(2,1)S(1)} %fusion.14, bf16[1024,1024]{1,0:T(8,128)(2,1)} %param.25), kind=kOutput, calls=%fused_computation.27 | convolution fusion | flops 537133056 | bytes 3145728 | tf_op jit(solution)/shard_map/dot_general | solution.py:173
  29.2 15.9 %all-to-all-done = bf16[16,24,2048]{2,1,0:T(8,128)(2,1)} async-done(((bf16[16,24,2048]{2,1,0:T(8,128)(2,1)}), bf16[16,24,2048]{2,1,0:T(8,128)(2,1)}, u32[]{:S(2)}, u32[]{:S(2)}) %all-to-all-start) | async-done | bytes 1572896 | tf_op jit(solution)/shard_map/all_to_all | solution.py:155
  45.1 0.9 slice_convert_fusion
  46.0 0.1 slice_add_fusion
  46.1 2.3 %slice.61 = bf16[16,16,2048]{2,1,0:T(8,128)(2,1)} slice(bf16[16,24,2048]{2,1,0:T(8,128)(2,1)} %all-to-all-done), slice={[0:16], [0:16], [0:2048]} | slice | bytes 2097152 | tf_op jit(solution)/shard_map/slice | solution.py:165
  48.4 4.1 %shard_map.136 = bf16[1,256,1024]{2,1,0:T(8,128)(2,1)} custom-call(s32[1]{0:T(128)} %constant.100.clone.1.counts_ref, bf16[1,256,1024]{2,1,0:T(8,128)(2,1)} %fusion.10.query_ref, bf16[1,256,2048]{2,1,0:T(8,128)(2,1)} %bitcast.74, bf16[1,256,2048]{2,1,0:T(8,128)(2,1)} %bitcast.75), custom_call_target="tpu_custom_call" | custom-call | tf_op jit(solution)/shard_map/pallas_call | solution.py:96
  52.5 0.0 copy-done
  52.5 2.6 %fusion.11 = (f32[256]{0:T(256)S(1)}, bf16[256,1024]{1,0:T(8,128)(2,1)}) fusion(bf16[1024,1024]{1,0:T(8,128)(2,1)S(1)} %copy-done, bf16[1,256,1024]{2,1,0:T(8,128)(2,1)} %shard_map.136, bf16[256,1024]{1,0:T(8,128)(2,1)S(1)} %bitcast.78), kind=kOutput, calls=%fused_computation.28 | convolution fusion | flops 538443520 | bytes 3671040 | tf_op jit(solution)/shard_map/dot_general | solution.py:185
  55.1 0.1 reshape.317
  55.2 0.0 copy-start.1
  55.2 3.4 %convolution_convert_fusion = bf16[256,1024]{1,0:T(8,128)(2,1)} fusion(bf16[1024,1024]{1,0:T(8,128)(2,1)} %param.28, bf16[256,1024]{1,0:T(8,128)(2,1)} %get-tuple-element.29, f32[256]{0:T(256)S(1)} %add_rsqrt_fusion.2), kind=kOutput, calls=%fused_computation.24 | convolution fusion | flops 537919488 | bytes 3146752 | tf_op jit(solution)/shard_map/dot_general | solution.py:187
  58.6 2.5 %gather_fusion.1 = bf16[16,16,1024]{2,1,0:T(8,128)(2,1)} fusion(bf16[16,16,1024]{2,1,0:T(8,128)(2,1)} %bitcast.82, s32[1024]{0:T(1024)S(1)} %pad_clamp_fusion.1), kind=kCustom, calls=%fused_computation.1 | custom fusion | bytes 1048640 | tf_op jit(solution)/shard_map/gather | solution.py:192
  61.1 9.2 %all-to-all-start.1 = ((bf16[16,16,1024]{2,1,0:T(8,128)(2,1)}), bf16[16,16,1024]{2,1,0:T(8,128)(2,1)}, u32[]{:S(2)}, u32[]{:S(2)}) async-start(bf16[16,16,1024]{2,1,0:T(8,128)(2,1)} %gather_fusion.1), calls=%async_computation.1 | async-start | bytes 1048576 | tf_op jit(solution)/shard_map/all_to_all | solution.py:191
  70.2 0.0 copy-done.1
  70.3 5.4 %gather_fusion = bf16[1024,1024]{1,0:T(8,128)(2,1)} fusion(bf16[512,1024]{1,0:T(8,128)(2,1)S(1)} %bitcast.73, s32[1024]{0:T(1024)S(1)} %broadcast_clamp_fusion), kind=kCustom, calls=%fused_computation | custom fusion | bytes 4198400 | tf_op jit(solution)/shard_map/gather | solution.py:170
  75.7 0.0 copy-start.2
  75.7 2.2 %fusion = f32[1024]{0:T(1024)S(1)} fusion(bf16[1024,1024]{1,0:T(8,128)(2,1)} %gather_fusion), kind=kLoop, calls=%fused_computation.5 | loop fusion | flops 3144704 | bytes 2101248 | tf_op jit(solution)/shard_map/reduce_sum | solution.py:16
  77.9 0.0 copy-done.2
  77.9 0.0 copy-start.4
  77.9 0.4 fusion.1
  78.3 1.2 copy-done.4
  79.5 0.0 copy-start.5
  79.5 6.0 %convert_bitcast_fusion = bf16[16,16,64,64]{3,2,1,0:T(8,128)(2,1)} fusion(bf16[16,64,1024,1]{2,1,3,0:T(8,128)(2,1)S(1)} %bitcast.76, bf16[1024,16,64,1]{0,2,1,3:T(8,128)(2,1)S(1)} %bitcast.79), kind=kOutput, calls=%fused_computation.7 | convolution fusion | flops 2148532224 | bytes 6291456 | tf_op jit(solution)/shard_map/btc,chd->bhtd/dot_general | solution.py:200
  85.5 0.0 copy-done.5
  85.5 6.0 %convert_bitcast_fusion.1 = bf16[16,16,64,64]{3,2,1,0:T(8,128)(2,1)} fusion(bf16[16,64,1024,1]{2,1,3,0:T(8,128)(2,1)S(1)} %bitcast.77, bf16[1024,16,64,1]{0,2,1,3:T(8,128)(2,1)S(1)} %bitcast.80), kind=kOutput, calls=%fused_computation.8 | convolution fusion | flops 2148532224 | bytes 6291456 | tf_op jit(solution)/shard_map/btc,chd->bhtd/dot_general | solution.py:194
  91.6 0.2 slice_reduce_fusion
  91.8 0.1 iota_compare_fusion.1
  91.8 0.0 all-to-all-done.1
  91.9 1.8 %reshape.321 = bf16[16,16,16,64]{3,2,1,0:T(8,128)(2,1)S(1)} reshape(bf16[16,16,1024]{2,1,0:T(8,128)(2,1)} %all-to-all-done.1) | data formatting | bytes 1048576 | tf_op jit(solution)/shard_map/reshape | solution.py:209
  93.6 0.0 copy-start.6
  93.6 4.7 %fusion.4 = (f32[16,16,16]{2,1,0:T(8,128)S(1)}, f32[16,16,16,64]{3,2,1,0:T(8,128)S(1)}) fusion(pred[16,64]{1,0:T(8,128)(4,1)S(1)} %iota_compare_fusion.1, bf16[16,16,64,64]{3,2,1,0:T(8,128)(2,1)} %convert_bitcast_fusion.1, bf16[16,16,16,64]{3,2,1,0:T(8,128)(2,1)S(1)} %reshape.321), kind=kOutput, calls=%fused_computation.15 | convolution fusion | flops 34336768 | bytes 3687424 | tf_op jit(solution)/shard_map/blhd,bhkd->bhlk/dot_general | solution.py:44
  98.3 1.3 %fusion.5 = f32[16,16,16]{2,1,0:T(8,128)S(1)} fusion(f32[16,16,16,64]{3,2,1,0:T(8,128)S(1)} %get-tuple-element.31, f32[16,16,16]{2,1,0:T(8,128)S(1)} %get-tuple-element.30, pred[16,64]{1,0:T(8,128)(4,1)S(1)} %iota_compare_fusion.1), kind=kLoop, calls=%fused_computation.16 | loop fusion | flops 1044480 | bytes 1082368 | tf_op jit(solution)/shard_map/reduce_sum | solution.py:50
  99.7 0.0 copy-done.6
  99.7 1.6 %fusion.3 = bf16[16,16,16,64]{3,1,2,0:T(8,128)(2,1)S(1)} fusion(bf16[16,16,64,64]{3,2,1,0:T(8,128)(2,1)S(1)} %copy-done.6, f32[16,16,16,64]{3,2,1,0:T(8,128)S(1)} %get-tuple-element.31, f32[16,16,16]{1,2,0:T(8,128)S(1)} %bitcast.83, f32[16,16,16]{2,1,0:T(8,128)S(1)} %get-tuple-element.30, pred[16,64]{1,0:T(8,128)(4,1)S(1)} %iota_compare_fusion.1), kind=kOutput, calls=%fused_computation.12 | convolution fusion | flops 35127296 | bytes 3703808 | tf_op jit(solution)/shard_map/bhlk,bhkd->blhd/dot_general | solution.py:52
  101.3 0.3 copy.41
  101.6 1.5 %convert_element_type.125 = bf16[16,16,1024]{2,1,0:T(8,128)(2,1)} reshape(bf16[16,16,16,64]{3,2,1,0:T(8,128)(2,1)S(1)} %copy.41) | data formatting | bytes 1048576 | tf_op jit(solution)/shard_map/convert_element_type | solution.py:60
  103.1 5.9 %all-to-all-start.2 = ((bf16[16,16,1024]{2,1,0:T(8,128)(2,1)}), bf16[16,16,1024]{2,1,0:T(8,128)(2,1)S(1)}, u32[]{:S(2)}, u32[]{:S(2)}) async-start(bf16[16,16,1024]{2,1,0:T(8,128)(2,1)} %convert_element_type.125), calls=%async_computation.2 | async-start | bytes 1048576 | tf_op jit(solution)/shard_map/all_to_all | solution.py:214
  109.1 14.4 %all-to-all-done.2 = bf16[16,16,1024]{2,1,0:T(8,128)(2,1)S(1)} async-done(((bf16[16,16,1024]{2,1,0:T(8,128)(2,1)}), bf16[16,16,1024]{2,1,0:T(8,128)(2,1)S(1)}, u32[]{:S(2)}, u32[]{:S(2)}) %all-to-all-start.2) | async-done | bytes 524320 | tf_op jit(solution)/shard_map/all_to_all | solution.py:214
  123.5 0.6 gather_fusion.2
  124.1 3.2 %fusion.8 = bf16[256,1024]{1,0:T(8,128)(2,1)} fusion(bf16[256,1024]{1,0:T(8,128)(2,1)S(1)} %bitcast.81, bf16[1024,1024]{1,0:T(8,128)(2,1)} %param.29, bf16[256,1024]{1,0:T(8,128)(2,1)} %get-tuple-element.29), kind=kOutput, calls=%fused_computation.23 | convolution fusion | flops 537657344 | bytes 3670016 | tf_op jit(solution)/shard_map/dot_general | solution.py:221
  (14 shorter events, 0.1 us)
Async XLA Ops:
  0.0 52.5 %copy-start = (bf16[1024,1024]{1,0:T(8,128)(2,1)S(1)}, bf16[1024,1024]{1,0:T(8,128)(2,1)}, u32[]{:S(2)}) copy-start(bf16[1024,1024]{1,0:T(8,128)(2,1)} %param.26) | copy-start | bytes 6291460
  5.5 7.6 %copy-start.3 = (bf16[16,16,1024]{2,1,0:T(8,128)(2,1)S(1)}, bf16[16,16,1024]{2,1,0:T(8,128)(2,1)}, u32[]{:S(2)}) copy-start(bf16[16,16,1024]{2,1,0:T(8,128)(2,1)} %param.16) | copy-start | bytes 1572868
  5.5 39.6 %all-to-all-start = ((bf16[16,24,2048]{2,1,0:T(8,128)(2,1)}), bf16[16,24,2048]{2,1,0:T(8,128)(2,1)}, u32[]{:S(2)}, u32[]{:S(2)}) async-start(bf16[16,24,2048]{2,1,0:T(8,128)(2,1)} %fusion.7), calls=%async_computation | async-start | bytes 3145728 | tf_op jit(solution)/shard_map/all_to_all | solution.py:155
  55.2 15.0 %copy-start.1 = (bf16[1,512,1024]{2,1,0:T(8,128)(2,1)S(1)}, bf16[1,512,1024]{2,1,0:T(8,128)(2,1)}, u32[]{:S(2)}) copy-start(bf16[1,512,1024]{2,1,0:T(8,128)(2,1)} %param.22) | copy-start | bytes 3145732
  61.1 30.8 %all-to-all-start.1 = ((bf16[16,16,1024]{2,1,0:T(8,128)(2,1)}), bf16[16,16,1024]{2,1,0:T(8,128)(2,1)}, u32[]{:S(2)}, u32[]{:S(2)}) async-start(bf16[16,16,1024]{2,1,0:T(8,128)(2,1)} %gather_fusion.1), calls=%async_computation.1 | async-start | bytes 1048576 | tf_op jit(solution)/shard_map/all_to_all | solution.py:191
  75.7 2.2 %copy-start.2 = (bf16[1024,1024]{1,0:T(8,128)(2,1)S(1)}, bf16[1024,1024]{1,0:T(8,128)(2,1)}, u32[]{:S(2)}) copy-start(bf16[1024,1024]{1,0:T(8,128)(2,1)} %gather_fusion) | copy-start | bytes 6291460
  77.9 1.6 %copy-start.4 = (bf16[1024,1024]{0,1:T(8,128)(2,1)S(1)}, bf16[1024,1024]{0,1:T(8,128)(2,1)}, u32[]{:S(2)}) copy-start(bf16[1024,1024]{0,1:T(8,128)(2,1)} %copy.39) | copy-start | bytes 6291460
  79.5 6.1 %copy-start.5 = (bf16[1024,1024]{0,1:T(8,128)(2,1)S(1)}, bf16[1024,1024]{0,1:T(8,128)(2,1)}, u32[]{:S(2)}) copy-start(bf16[1024,1024]{0,1:T(8,128)(2,1)} %copy.38) | copy-start | bytes 6291460
  93.6 6.1 %copy-start.6 = (bf16[16,16,64,64]{3,2,1,0:T(8,128)(2,1)S(1)}, bf16[16,16,64,64]{3,2,1,0:T(8,128)(2,1)}, u32[]{:S(2)}) copy-start(bf16[16,16,64,64]{3,2,1,0:T(8,128)(2,1)} %convert_bitcast_fusion) | copy-start | bytes 6291460
  103.1 20.4 %all-to-all-start.2 = ((bf16[16,16,1024]{2,1,0:T(8,128)(2,1)}), bf16[16,16,1024]{2,1,0:T(8,128)(2,1)S(1)}, u32[]{:S(2)}, u32[]{:S(2)}) async-start(bf16[16,16,1024]{2,1,0:T(8,128)(2,1)} %convert_element_type.125), calls=%async_computation.2 | async-start | bytes 1048576 | tf_op jit(solution)/shard_map/all_to_all | solution.py:214

commit v10 on v7

--- a/solution.py
+++ b/solution.py
@@ -58,6 +58,19 @@
         / denominator
     )
     return spike_mix.reshape(samples, latents, head_count * head_size).astype(jnp.bfloat16)
+
+
+def exchange(blocks, axis):
+    count = lax.axis_size(axis)
+    rank = lax.axis_index(axis)
+    pieces = [lax.dynamic_index_in_dim(blocks, rank, 0, keepdims=False)]
+    for shift in range(1, count):
+        outgoing = lax.dynamic_index_in_dim(blocks, (rank + shift) % count, 0, keepdims=False)
+        pieces.append(
+            lax.ppermute(outgoing, axis, [(i, (i + shift) % count) for i in range(count)])
+        )
+    stacked = jnp.stack(pieces)
+    return stacked[(rank - jnp.arange(count, dtype=jnp.int32)) % count]
 
 
 def attend_block(counts_ref, query_ref, key_ref, value_ref, out_ref):
@@ -207,13 +220,7 @@
         value_rows,
         live_tokens,
     )
-    read_spike = lax.all_to_all(
-        served_read.reshape(owners, latents, model_width),
-        "smp",
-        split_axis=0,
-        concat_axis=0,
-        tiled=True,
-    )[owner_rank]
+    read_spike = exchange(served_read.reshape(owners, latents, model_width), "smp")[owner_rank]
     result = hidden.astype(jnp.float32) + jnp.dot(
         read_spike.reshape(row_total, model_width), o2_weight, preferred_element_type=jnp.float32
     )

time: 113 us -> 119 us (1.053)
  starting transfers between devices: 25.6 us -> 41.8 us
  waiting for transfers between devices: 15.5 us -> 3.41 us
  local copies, waits for them, and re-layouts: 25.1 us -> 26.7 us
    ppermute x0 -> x15, starting transfers between devices: none -> 21.7 us  [exchange(): lax.ppermute(outgoing, axis, [(i, (i + shift) % count) for i in range(cou...]
    all_to_all x1 -> x0, waiting for transfers between devices: 14.4 us -> none  [per_device(): lax.all_to_all(served_read.reshape(owners, latents, model_width), 'smp',...]
    all_to_all x1 -> x0, starting transfers between devices: 5.68 us -> none  [per_device(): lax.all_to_all(served_read.reshape(owners, latents, model_width), 'smp',...]
    ppermute x0 -> x15, waiting for transfers between devices: none -> 2.37 us  [exchange(): lax.ppermute(outgoing, axis, [(i, (i + shift) % count) for i in range(cou...]
  transfers between devices with their start and end apart: 4 -> 18, of which waited for: 4 -> 7; matrix products, arithmetic and copies ran while one was open for 38% -> 36% of each run, Pallas kernels for 0% -> 0%
where the time goes in v10:
time: 119 us; the launch traced here: 118 us
  starting transfers between devices  41.8 us (35%)
  matrix products  29.8 us (25%)
  local copies, waits for them, and re-layouts  26.7 us (22%)
  other arithmetic  11.6 us (10%)
  Pallas kernels  4.11 us (3%)
  waiting for transfers between devices  3.41 us (3%)
    ppermute x15, starting transfers between devices, exchange(): lax.ppermute(outgoing, axis, [(i, (i + shift) % count) for i in range(cou...  21.7 us
    slice x2, local copies, waits for them, and re-layouts, per_device(): kv_weight[:, model_width:].reshape(model_width, head_count, HEAD_DIM)  8.63 us
    dot_general x1, matrix products, per_device(): jnp.einsum('btc,chd->bhtd', embed_normed, kv_weight[:, :model_width].resh...  8.13 us
    all_to_all x1, starting transfers between devices, per_device(): lax.all_to_all(jnp.concatenate([request, count_pick[:, None]], axis=1), '...  7.39 us
    all_to_all x1, starting transfers between devices, per_device(): lax.all_to_all(queries2[sample_pick], 'smp', split_axis=0, concat_axis=0,...  6.93 us
    dot_general x1, matrix products, per_device(): jnp.einsum('btc,chd->bhtd', embed_normed, kv_weight[:, model_width:].resh...  6.05 us
    all_to_all x1, starting transfers between devices, per_device(): lax.all_to_all(jnp.broadcast_to(memory_pair[None], (owners,) + memory_pai...  5.76 us
    gather x1, local copies, waits for them, and re-layouts, per_device(): served_embed = panel_table[served_index.reshape(-1)]  5.34 us
  transfers between devices with their start and end apart: 18, of which 7 were waited for; matrix products, arithmetic and copies ran while one was open for 36% of the time, Pallas kernels for 0%

profile of v10, /device:TPU:0, one launch (start us, length us, event | category | flops | bytes accessed | tf_op | source)
XLA Modules:
  0.0 118.0 jit_solution(1175867917576508198)
XLA Ops:
  0.0 1.0 select_reduce_fusion.4
  1.0 0.9 select_reduce_fusion.1
  1.9 0.1 copy.32
  2.0 0.9 add_select_fusion
  2.9 0.1 select_reduce_fusion
  3.0 0.7 pad_add_fusion
  3.7 7.4 %all-to-all-start = ((s32[16,1,65]{2,1,0:T(1,128)}), s32[16,1,65]{2,1,0:T(1,128)S(1)}, u32[]{:S(2)}, u32[]{:S(2)}) async-start(s32[16,1,65]{2,1,0:T(1,128)} %bitcast.4), calls=%async_computation | async-start | bytes 16384 | tf_op jit(solution)/shard_map/all_to_all | solution.py:161
  11.1 0.0 copy-start.2
  11.1 0.0 copy-start.6
  11.1 0.0 copy-start.7
  11.1 4.7 %fusion.28 = (bf16[1024,1024]{1,0:T(8,128)(2,1)}, bf16[1024,1024]{1,0:T(8,128)(2,1)}) fusion(bf16[1024,2048]{1,0:T(8,128)(2,1)} %param.25), kind=kLoop, calls=%fused_computation.105 | loop fusion | bytes 8388608 | tf_op jit(solution)/shard_map/slice | solution.py:212
  15.8 0.2 multiply_reduce_fusion.1
  16.0 0.1 rsqrt.31
  16.1 1.0 fusion.12
  17.2 0.3 all-to-all-done
  17.5 1.1 broadcast_in_dim.104
  18.6 5.8 %all-to-all-start.1 = ((bf16[16,16,2048]{2,1,0:T(8,128)(2,1)}), bf16[16,16,2048]{2,1,0:T(8,128)(2,1)}, u32[]{:S(2)}, u32[]{:S(2)}) async-start(bf16[16,16,2048]{2,1,0:T(8,128)(2,1)} %broadcast_in_dim.104), calls=%async_computation.1 | async-start | bytes 2097152 | tf_op jit(solution)/shard_map/all_to_all | solution.py:177
  24.5 3.9 %copy.33 = bf16[1024,1024]{0,1:T(8,128)(2,1)} copy(bf16[1024,1024]{1,0:T(8,128)(2,1)} %get-tuple-element.17) | data formatting | bytes 4194304 | tf_op jit(solution)/shard_map/slice | solution.py:206
  28.4 3.9 %copy.34 = bf16[1024,1024]{0,1:T(8,128)(2,1)} copy(bf16[1024,1024]{1,0:T(8,128)(2,1)} %get-tuple-element.16) | data formatting | bytes 4194304 | tf_op jit(solution)/shard_map/slice | solution.py:212
  32.4 3.4 %fusion.8.query_ref = bf16[1,256,1024]{2,1,0:T(8,128)(2,1)} fusion(bf16[256,1024]{1,0:T(8,128)(2,1)} %fusion.12, bf16[1024,1024]{1,0:T(8,128)(2,1)} %param.23), kind=kOutput, calls=%fused_computation.25 | convolution fusion | flops 537133056 | bytes 3145728 | tf_op jit(solution)/shard_map/dot_general | solution.py:173
  35.8 0.1 reshape.251
  35.9 5.3 %gather_fusion = bf16[1024,1024]{1,0:T(8,128)(2,1)} fusion(bf16[512,1024]{1,0:T(8,128)(2,1)S(1)} %bitcast.132, s32[1024]{0:T(1024)S(1)} %get-tuple-element.39), kind=kCustom, calls=%fused_computation | custom fusion | bytes 4198400 | tf_op jit(solution)/shard_map/gather | solution.py:170
  41.2 2.1 %multiply_reduce_fusion = f32[1024]{0:T(1024)S(1)} fusion(bf16[1024,1024]{1,0:T(8,128)(2,1)} %gather_fusion), kind=kLoop, calls=%fused_computation.7 | loop fusion | flops 3144704 | bytes 2101248 | tf_op jit(solution)/shard_map/reduce_sum | solution.py:16
  43.3 0.1 rsqrt.33
  43.4 0.2 slice_reduce_fusion
  43.5 0.1 iota_compare_fusion
  43.6 3.3 %multiply_convert_fusion = bf16[16,64,1024]{2,1,0:T(8,128)(2,1)} fusion(f32[16,64]{1,0:T(8,128)S(1)} %rsqrt.33, bf16[16,64,1024]{2,1,0:T(8,128)(2,1)} %bitcast.133), kind=kLoop, calls=%fused_computation.6 | loop fusion | flops 3145728 | bytes 4198400 | tf_op jit(solution)/shard_map/convert_element_type | solution.py:16
  46.9 0.4 all-to-all-done.1
  47.4 4.1 %shard_map.136 = bf16[1,256,1024]{2,1,0:T(8,128)(2,1)} custom-call(s32[1]{0:T(128)} %constant.170.clone.1.counts_ref, bf16[1,256,1024]{2,1,0:T(8,128)(2,1)} %fusion.8.query_ref, bf16[1,256,2048]{2,1,0:T(8,128)(2,1)} %bitcast.8.key_ref.value_ref, bf16[1,256,2048]{2,1,0:T(8,128)(2,1)} %bitcast.8.key_ref.value_ref), custom_call_target="tpu_custom_call" | custom-call | tf_op jit(solution)/shard_map/pallas_call | solution.py:109
  51.5 2.0 %fusion.9 = (f32[256]{0:T(256)S(1)}, bf16[256,1024]{1,0:T(8,128)(2,1)S(1)}) fusion(bf16[1024,1024]{1,0:T(8,128)(2,1)S(1)} %copy-done, bf16[1,256,1024]{2,1,0:T(8,128)(2,1)} %shard_map.136, bf16[256,1024]{1,0:T(8,128)(2,1)S(1)} %bitcast.134), kind=kOutput, calls=%fused_computation.26 | convolution fusion | flops 538443520 | bytes 3671040 | tf_op jit(solution)/shard_map/dot_general | solution.py:194
  53.5 0.8 convolution_convert_fusion
  54.3 1.4 %gather_fusion.1 = bf16[16,16,1024]{2,1,0:T(8,128)(2,1)} fusion(bf16[16,16,1024]{2,1,0:T(8,128)(2,1)S(1)} %bitcast.137, s32[1024]{0:T(1024)S(1)} %get-tuple-element.38), kind=kCustom, calls=%fused_computation.1 | custom fusion | bytes 1048640 | tf_op jit(solution)/shard_map/gather | solution.py:201
  55.7 6.9 %all-to-all-start.2 = ((bf16[16,16,1024]{2,1,0:T(8,128)(2,1)}), bf16[16,16,1024]{2,1,0:T(8,128)(2,1)}, u32[]{:S(2)}, u32[]{:S(2)}) async-start(bf16[16,16,1024]{2,1,0:T(8,128)(2,1)} %gather_fusion.1), calls=%async_computation.2 | async-start | bytes 1048576 | tf_op jit(solution)/shard_map/all_to_all | solution.py:200
  62.6 8.1 %convert_bitcast_fusion.1 = bf16[16,16,64,64]{3,2,1,0:T(8,128)(2,1)} fusion(bf16[1024,16,64,1]{0,2,1,3:T(8,128)(2,1)} %bitcast.135, bf16[16,64,1024]{2,1,0:T(8,128)(2,1)} %multiply_convert_fusion), kind=kOutput, calls=%fused_computation.5 | convolution fusion | flops 2148532224 | bytes 6291456 | tf_op jit(solution)/shard_map/btc,chd->bhtd/dot_general | solution.py:203
  70.8 6.0 %convert_bitcast_fusion = bf16[16,16,64,64]{3,2,1,0:T(8,128)(2,1)} fusion(bf16[1024,16,64,1]{0,2,1,3:T(8,128)(2,1)S(1)} %bitcast.136, bf16[16,64,1024]{2,1,0:T(8,128)(2,1)S(1)} %copy-done.5), kind=kOutput, calls=%fused_computation.4 | convolution fusion | flops 2148532224 | bytes 6291456 | tf_op jit(solution)/shard_map/btc,chd->bhtd/dot_general | solution.py:209
  76.8 0.3 all-to-all-done.2
  77.1 1.8 %reshape.257 = bf16[16,16,16,64]{3,2,1,0:T(8,128)(2,1)S(1)} reshape(bf16[16,16,1024]{2,1,0:T(8,128)(2,1)} %all-to-all-done.2) | data formatting | bytes 1048576 | tf_op jit(solution)/shard_map/reshape | solution.py:218
  78.9 4.7 %fusion.3 = (f32[16,16,16]{2,1,0:T(8,128)S(1)}, f32[16,16,16,64]{3,2,1,0:T(8,128)S(1)}) fusion(pred[16,64]{1,0:T(8,128)(4,1)S(1)} %iota_compare_fusion, bf16[16,16,64,64]{3,2,1,0:T(8,128)(2,1)} %convert_bitcast_fusion.1, bf16[16,16,16,64]{3,2,1,0:T(8,128)(2,1)S(1)} %reshape.257), kind=kOutput, calls=%fused_computation.14 | convolution fusion | flops 34336768 | bytes 3687424 | tf_op jit(solution)/shard_map/blhd,bhkd->bhlk/dot_general | solution.py:44
  83.6 1.3 %fusion.4 = f32[16,16,16]{2,1,0:T(8,128)S(1)} fusion(f32[16,16,16,64]{3,2,1,0:T(8,128)S(1)} %get-tuple-element.37, f32[16,16,16]{2,1,0:T(8,128)S(1)} %get-tuple-element.36, pred[16,64]{1,0:T(8,128)(4,1)S(1)} %iota_compare_fusion), kind=kLoop, calls=%fused_computation.15 | loop fusion | flops 1044480 | bytes 1082368 | tf_op jit(solution)/shard_map/reduce_sum | solution.py:50
  85.0 1.6 %fusion = bf16[16,16,16,64]{3,1,2,0:T(8,128)(2,1)S(1)} fusion(bf16[16,16,64,64]{3,2,1,0:T(8,128)(2,1)S(1)} %copy-done.10, f32[16,16,16,64]{3,2,1,0:T(8,128)S(1)} %get-tuple-element.37, f32[16,16,16]{1,2,0:T(8,128)S(1)} %bitcast.139, f32[16,16,16]{2,1,0:T(8,128)S(1)} %get-tuple-element.36, pred[16,64]{1,0:T(8,128)(4,1)S(1)} %iota_compare_fusion), kind=kOutput, calls=%fused_computation.9 | convolution fusion | flops 35127296 | bytes 3703808 | tf_op jit(solution)/shard_map/bhlk,bhkd->blhd/dot_general | solution.py:52
  86.6 0.3 copy.36
  86.9 1.5 %convert_element_type.85 = bf16[16,16,1024]{2,1,0:T(8,128)(2,1)} reshape(bf16[16,16,16,64]{3,2,1,0:T(8,128)(2,1)S(1)} %copy.36) | data formatting | bytes 1048576 | tf_op jit(solution)/shard_map/convert_element_type | solution.py:60
  88.4 1.0 dynamic-slice_bitcast_fusion
  89.4 0.1 collective-permute-start
  89.5 1.7 %collective-permute-start.1 = (bf16[16,1024]{1,0:T(8,128)(2,1)S(1)}, bf16[16,1024]{1,0:T(8,128)(2,1)S(1)}, u32[]{:S(2)}, u32[]{:S(2)}) collective-permute-start(bf16[16,1024]{1,0:T(8,128)(2,1)S(1)} %get-tuple-element.31), channel_id=1, source_target_pairs={{0,2},{1,3},{2,4},{3,5},{4,6},{5,7},{6,8},{7,9},{8,10},{9,11},{10,... | collective-permute-start | bytes 98312 | tf_op jit(solution)/shard_map/ppermute | solution.py:70
  91.2 2.2 %collective-permute-start.2 = (bf16[16,1024]{1,0:T(8,128)(2,1)S(1)}, bf16[16,1024]{1,0:T(8,128)(2,1)S(1)}, u32[]{:S(2)}, u32[]{:S(2)}) collective-permute-start(bf16[16,1024]{1,0:T(8,128)(2,1)S(1)} %get-tuple-element.30), channel_id=1, source_target_pairs={{0,3},{1,4},{2,5},{3,6},{4,7},{5,8},{6,9},{7,10},{8,11},{9,12},{10... | collective-permute-start | bytes 98312 | tf_op jit(solution)/shard_map/ppermute | solution.py:70
  93.4 1.5 %collective-permute-start.3 = (bf16[16,1024]{1,0:T(8,128)(2,1)S(1)}, bf16[16,1024]{1,0:T(8,128)(2,1)S(1)}, u32[]{:S(2)}, u32[]{:S(2)}) collective-permute-start(bf16[16,1024]{1,0:T(8,128)(2,1)S(1)} %get-tuple-element.29), channel_id=1, source_target_pairs={{0,4},{1,5},{2,6},{3,7},{4,8},{5,9},{6,10},{7,11},{8,12},{9,13},{1... | collective-permute-start | bytes 98312 | tf_op jit(solution)/shard_map/ppermute | solution.py:70
  94.9 0.2 collective-permute-start.4
  95.0 0.5 collective-permute-done
  95.5 1.0 collective-permute-start.5
  96.5 4.0 %collective-permute-start.6 = (bf16[16,1024]{1,0:T(8,128)(2,1)S(1)}, bf16[16,1024]{1,0:T(8,128)(2,1)S(1)}, u32[]{:S(2)}, u32[]{:S(2)}) collective-permute-start(bf16[16,1024]{1,0:T(8,128)(2,1)S(1)} %get-tuple-element.26), channel_id=1, source_target_pairs={{0,7},{1,8},{2,9},{3,10},{4,11},{5,12},{6,13},{7,14},{8,15},{9,0},... | collective-permute-start | bytes 98312 | tf_op jit(solution)/shard_map/ppermute | solution.py:70
  100.5 0.6 collective-permute-start.7
  101.1 0.2 collective-permute-start.8
  101.3 0.3 collective-permute-done.4
  101.6 2.0 %collective-permute-start.9 = (bf16[16,1024]{1,0:T(8,128)(2,1)S(1)}, bf16[16,1024]{1,0:T(8,128)(2,1)S(1)}, u32[]{:S(2)}, u32[]{:S(2)}) collective-permute-start(bf16[16,1024]{1,0:T(8,128)(2,1)S(1)} %get-tuple-element.23), channel_id=1, source_target_pairs={{0,10},{1,11},{2,12},{3,13},{4,14},{5,15},{6,0},{7,1},{8,2},{9,3},... | collective-permute-start | bytes 98312 | tf_op jit(solution)/shard_map/ppermute | solution.py:70
  103.5 3.2 %collective-permute-start.10 = (bf16[16,1024]{1,0:T(8,128)(2,1)S(1)}, bf16[16,1024]{1,0:T(8,128)(2,1)S(1)}, u32[]{:S(2)}, u32[]{:S(2)}) collective-permute-start(bf16[16,1024]{1,0:T(8,128)(2,1)S(1)} %get-tuple-element.22), channel_id=1, source_target_pairs={{0,11},{1,12},{2,13},{3,14},{4,15},{5,0},{6,1},{7,2},{8,3},{9,4},{... | collective-permute-start | bytes 98312 | tf_op jit(solution)/shard_map/ppermute | solution.py:70
  106.7 1.5 %collective-permute-start.11 = (bf16[16,1024]{1,0:T(8,128)(2,1)S(1)}, bf16[16,1024]{1,0:T(8,128)(2,1)S(1)}, u32[]{:S(2)}, u32[]{:S(2)}) collective-permute-start(bf16[16,1024]{1,0:T(8,128)(2,1)S(1)} %get-tuple-element.21), channel_id=1, source_target_pairs={{0,12},{1,13},{2,14},{3,15},{4,0},{5,1},{6,2},{7,3},{8,4},{9,5},{1... | collective-permute-start | bytes 98312 | tf_op jit(solution)/shard_map/ppermute | solution.py:70
  108.2 2.0 %collective-permute-start.13 = (bf16[16,1024]{1,0:T(8,128)(2,1)S(1)}, bf16[16,1024]{1,0:T(8,128)(2,1)S(1)}, u32[]{:S(2)}, u32[]{:S(2)}) collective-permute-start(bf16[16,1024]{1,0:T(8,128)(2,1)S(1)} %get-tuple-element.19), channel_id=1, source_target_pairs={{0,14},{1,15},{2,0},{3,1},{4,2},{5,3},{6,4},{7,5},{8,6},{9,7},{10,... | collective-permute-start | bytes 98312 | tf_op jit(solution)/shard_map/ppermute | solution.py:70
  110.2 1.8 %collective-permute-start.14 = (bf16[16,1024]{1,0:T(8,128)(2,1)S(1)}, bf16[16,1024]{1,0:T(8,128)(2,1)S(1)}, u32[]{:S(2)}, u32[]{:S(2)}) collective-permute-start(bf16[16,1024]{1,0:T(8,128)(2,1)S(1)} %get-tuple-element.18), channel_id=1, source_target_pairs={{0,15},{1,0},{2,1},{3,2},{4,3},{5,4},{6,5},{7,6},{8,7},{9,8},{10,9... | collective-permute-start | bytes 98312 | tf_op jit(solution)/shard_map/ppermute | solution.py:70
  112.1 0.1 collective-permute-done.13
  112.2 1.4 %collective-permute-done.14 = bf16[16,1024]{1,0:T(8,128)(2,1)S(1)} collective-permute-done((bf16[16,1024]{1,0:T(8,128)(2,1)S(1)}, bf16[16,1024]{1,0:T(8,128)(2,1)S(1)}, u32[]{:S(2)}, u32[]{:S(2)}) %collective-permute-start.14) | collective-permute-done | bytes 32800 | tf_op jit(solution)/shard_map/ppermute | solution.py:70
  113.7 0.6 gather_fusion.2
  114.2 0.6 gather_fusion.3
  114.8 3.2 %fusion.6 = bf16[256,1024]{1,0:T(8,128)(2,1)} fusion(bf16[256,1024]{1,0:T(8,128)(2,1)S(1)} %bitcast.138, bf16[1024,1024]{1,0:T(8,128)(2,1)} %param.27, bf16[256,1024]{1,0:T(8,128)(2,1)} %copy-done.9), kind=kOutput, calls=%fused_computation.21 | convolution fusion | flops 537657344 | bytes 3670016 | tf_op jit(solution)/shard_map/dot_general | solution.py:224
  (60 shorter events, 0.2 us)
Async XLA Ops:
  0.0 51.5 %copy-start = (bf16[1024,1024]{1,0:T(8,128)(2,1)S(1)}, bf16[1024,1024]{1,0:T(8,128)(2,1)}, u32[]{:S(2)}) copy-start(bf16[1024,1024]{1,0:T(8,128)(2,1)} %param.24) | copy-start | bytes 6291460
  3.7 13.8 %all-to-all-start = ((s32[16,1,65]{2,1,0:T(1,128)}), s32[16,1,65]{2,1,0:T(1,128)S(1)}, u32[]{:S(2)}, u32[]{:S(2)}) async-start(s32[16,1,65]{2,1,0:T(1,128)} %bitcast.4), calls=%async_computation | async-start | bytes 16384 | tf_op jit(solution)/shard_map/all_to_all | solution.py:161
  11.1 4.7 %copy-start.2 = (bf16[16,16,1024]{2,1,0:T(8,128)(2,1)S(1)}, bf16[16,16,1024]{2,1,0:T(8,128)(2,1)}, u32[]{:S(2)}) copy-start(bf16[16,16,1024]{2,1,0:T(8,128)(2,1)} %param.14) | copy-start | bytes 1572868
  11.1 6.0 %copy-start.6 = (bf16[16,1024]{1,0:T(8,128)(2,1)S(1)}, bf16[16,1024]{1,0:T(8,128)(2,1)}, u32[]{:S(2)}) copy-start(bf16[16,1024]{1,0:T(8,128)(2,1)} %param.22) | copy-start | bytes 98308
  11.1 5.9 %copy-start.7 = (bf16[16,1024]{1,0:T(8,128)(2,1)S(1)}, bf16[16,1024]{1,0:T(8,128)(2,1)}, u32[]{:S(2)}) copy-start(bf16[16,1024]{1,0:T(8,128)(2,1)} %param.21) | copy-start | bytes 98308
  18.6 28.8 %all-to-all-start.1 = ((bf16[16,16,2048]{2,1,0:T(8,128)(2,1)}), bf16[16,16,2048]{2,1,0:T(8,128)(2,1)}, u32[]{:S(2)}, u32[]{:S(2)}) async-start(bf16[16,16,2048]{2,1,0:T(8,128)(2,1)} %broadcast_in_dim.104), calls=%async_computation.1 | async-start | bytes 2097152 | tf_op jit(solution)/shard_map/all_to_all | solution.py:177
  32.4 3.5 %copy-start.1 = (bf16[1,512,1024]{2,1,0:T(8,128)(2,1)S(1)}, bf16[1,512,1024]{2,1,0:T(8,128)(2,1)}, u32[]{:S(2)}) copy-start(bf16[1,512,1024]{2,1,0:T(8,128)(2,1)} %param.20) | copy-start | bytes 3145732
  46.9 4.6 %copy-start.3 = (bf16[16,16,1024]{2,1,0:T(8,128)(2,1)S(1)}, bf16[16,16,1024]{2,1,0:T(8,128)(2,1)}, u32[]{:S(2)}) copy-start(bf16[16,16,1024]{2,1,0:T(8,128)(2,1)} %param.14) | copy-start | bytes 1572868
  51.5 2.0 %copy-start.8 = (bf16[1024,1024]{1,0:T(8,128)(2,1)S(1)}, bf16[1024,1024]{1,0:T(8,128)(2,1)}, u32[]{:S(2)}) copy-start(bf16[1024,1024]{1,0:T(8,128)(2,1)} %param.26) | copy-start | bytes 6291460
  53.5 2.2 %copy-start.9 = (bf16[256,1024]{1,0:T(8,128)(2,1)}, bf16[256,1024]{1,0:T(8,128)(2,1)S(1)}, u32[]{:S(2)}) copy-start(bf16[256,1024]{1,0:T(8,128)(2,1)S(1)} %get-tuple-element.35) | copy-start | bytes 1572868
  55.7 21.4 %all-to-all-start.2 = ((bf16[16,16,1024]{2,1,0:T(8,128)(2,1)}), bf16[16,16,1024]{2,1,0:T(8,128)(2,1)}, u32[]{:S(2)}, u32[]{:S(2)}) async-start(bf16[16,16,1024]{2,1,0:T(8,128)(2,1)} %gather_fusion.1), calls=%async_computation.2 | async-start | bytes 1048576 | tf_op jit(solution)/shard_map/all_to_all | solution.py:200
  62.6 8.2 %copy-start.4 = (bf16[1024,1024]{0,1:T(8,128)(2,1)S(1)}, bf16[1024,1024]{0,1:T(8,128)(2,1)}, u32[]{:S(2)}) copy-start(bf16[1024,1024]{0,1:T(8,128)(2,1)} %copy.34) | copy-start | bytes 6291460
  62.6 8.2 %copy-start.5 = (bf16[16,64,1024]{2,1,0:T(8,128)(2,1)S(1)}, bf16[16,64,1024]{2,1,0:T(8,128)(2,1)}, u32[]{:S(2)}) copy-start(bf16[16,64,1024]{2,1,0:T(8,128)(2,1)} %multiply_convert_fusion) | copy-start | bytes 6291460
  78.9 6.1 %copy-start.10 = (bf16[16,16,64,64]{3,2,1,0:T(8,128)(2,1)S(1)}, bf16[16,16,64,64]{3,2,1,0:T(8,128)(2,1)}, u32[]{:S(2)}) copy-start(bf16[16,16,64,64]{3,2,1,0:T(8,128)(2,1)} %convert_bitcast_fusion) | copy-start | bytes 6291460
  89.4 6.1 %collective-permute-start = (bf16[16,1024]{1,0:T(8,128)(2,1)S(1)}, bf16[16,1024]{1,0:T(8,128)(2,1)S(1)}, u32[]{:S(2)}, u32[]{:S(2)}) collective-permute-start(bf16[16,1024]{1,0:T(8,128)(2,1)S(1)} %get-tuple-element.32), channel_id=1, source_target_pairs={{0,1},{1,2},{2,3},{3,4},{4,5},{5,6},{6,7},{7,8},{8,9},{9,10},{10,1... | collective-permute-start | bytes 98312 | tf_op jit(solution)/shard_map/ppermute | solution.py:70
  89.5 7.0 %collective-permute-start.1 = (bf16[16,1024]{1,0:T(8,128)(2,1)S(1)}, bf16[16,1024]{1,0:T(8,128)(2,1)S(1)}, u32[]{:S(2)}, u32[]{:S(2)}) collective-permute-start(bf16[16,1024]{1,0:T(8,128)(2,1)S(1)} %get-tuple-element.31), channel_id=1, source_target_pairs={{0,2},{1,3},{2,4},{3,5},{4,6},{5,7},{6,8},{7,9},{8,10},{9,11},{10,... | collective-permute-start | bytes 98312 | tf_op jit(solution)/shard_map/ppermute | solution.py:70
  91.2 9.3 %collective-permute-start.2 = (bf16[16,1024]{1,0:T(8,128)(2,1)S(1)}, bf16[16,1024]{1,0:T(8,128)(2,1)S(1)}, u32[]{:S(2)}, u32[]{:S(2)}) collective-permute-start(bf16[16,1024]{1,0:T(8,128)(2,1)S(1)} %get-tuple-element.30), channel_id=1, source_target_pairs={{0,3},{1,4},{2,5},{3,6},{4,7},{5,8},{6,9},{7,10},{8,11},{9,12},{10... | collective-permute-start | bytes 98312 | tf_op jit(solution)/shard_map/ppermute | solution.py:70
  93.4 7.7 %collective-permute-start.3 = (bf16[16,1024]{1,0:T(8,128)(2,1)S(1)}, bf16[16,1024]{1,0:T(8,128)(2,1)S(1)}, u32[]{:S(2)}, u32[]{:S(2)}) collective-permute-start(bf16[16,1024]{1,0:T(8,128)(2,1)S(1)} %get-tuple-element.29), channel_id=1, source_target_pairs={{0,4},{1,5},{2,6},{3,7},{4,8},{5,9},{6,10},{7,11},{8,12},{9,13},{1... | collective-permute-start | bytes 98312 | tf_op jit(solution)/shard_map/ppermute | solution.py:70
  94.9 6.7 %collective-permute-start.4 = (bf16[16,1024]{1,0:T(8,128)(2,1)S(1)}, bf16[16,1024]{1,0:T(8,128)(2,1)S(1)}, u32[]{:S(2)}, u32[]{:S(2)}) collective-permute-start(bf16[16,1024]{1,0:T(8,128)(2,1)S(1)} %get-tuple-element.28), channel_id=1, source_target_pairs={{0,5},{1,6},{2,7},{3,8},{4,9},{5,10},{6,11},{7,12},{8,13},{9,14},{... | collective-permute-start | bytes 98312 | tf_op jit(solution)/shard_map/ppermute | solution.py:70
  95.5 8.0 %collective-permute-start.5 = (bf16[16,1024]{1,0:T(8,128)(2,1)S(1)}, bf16[16,1024]{1,0:T(8,128)(2,1)S(1)}, u32[]{:S(2)}, u32[]{:S(2)}) collective-permute-start(bf16[16,1024]{1,0:T(8,128)(2,1)S(1)} %get-tuple-element.27), channel_id=1, source_target_pairs={{0,6},{1,7},{2,8},{3,9},{4,10},{5,11},{6,12},{7,13},{8,14},{9,15},... | collective-permute-start | bytes 98312 | tf_op jit(solution)/shard_map/ppermute | solution.py:70
  96.5 10.2 %collective-permute-start.6 = (bf16[16,1024]{1,0:T(8,128)(2,1)S(1)}, bf16[16,1024]{1,0:T(8,128)(2,1)S(1)}, u32[]{:S(2)}, u32[]{:S(2)}) collective-permute-start(bf16[16,1024]{1,0:T(8,128)(2,1)S(1)} %get-tuple-element.26), channel_id=1, source_target_pairs={{0,7},{1,8},{2,9},{3,10},{4,11},{5,12},{6,13},{7,14},{8,15},{9,0},... | collective-permute-start | bytes 98312 | tf_op jit(solution)/shard_map/ppermute | solution.py:70
  100.5 7.7 %collective-permute-start.7 = (bf16[16,1024]{1,0:T(8,128)(2,1)S(1)}, bf16[16,1024]{1,0:T(8,128)(2,1)S(1)}, u32[]{:S(2)}, u32[]{:S(2)}) collective-permute-start(bf16[16,1024]{1,0:T(8,128)(2,1)S(1)} %get-tuple-element.25), channel_id=1, source_target_pairs={{0,8},{1,9},{2,10},{3,11},{4,12},{5,13},{6,14},{7,15},{8,0},{9,1},... | collective-permute-start | bytes 98312 | tf_op jit(solution)/shard_map/ppermute | solution.py:70
  101.1 7.1 %collective-permute-start.8 = (bf16[16,1024]{1,0:T(8,128)(2,1)S(1)}, bf16[16,1024]{1,0:T(8,128)(2,1)S(1)}, u32[]{:S(2)}, u32[]{:S(2)}) collective-permute-start(bf16[16,1024]{1,0:T(8,128)(2,1)S(1)} %get-tuple-element.24), channel_id=1, source_target_pairs={{0,9},{1,10},{2,11},{3,12},{4,13},{5,14},{6,15},{7,0},{8,1},{9,2},... | collective-permute-start | bytes 98312 | tf_op jit(solution)/shard_map/ppermute | solution.py:70
  101.6 8.7 %collective-permute-start.9 = (bf16[16,1024]{1,0:T(8,128)(2,1)S(1)}, bf16[16,1024]{1,0:T(8,128)(2,1)S(1)}, u32[]{:S(2)}, u32[]{:S(2)}) collective-permute-start(bf16[16,1024]{1,0:T(8,128)(2,1)S(1)} %get-tuple-element.23), channel_id=1, source_target_pairs={{0,10},{1,11},{2,12},{3,13},{4,14},{5,15},{6,0},{7,1},{8,2},{9,3},... | collective-permute-start | bytes 98312 | tf_op jit(solution)/shard_map/ppermute | solution.py:70
  103.5 8.5 %collective-permute-start.10 = (bf16[16,1024]{1,0:T(8,128)(2,1)S(1)}, bf16[16,1024]{1,0:T(8,128)(2,1)S(1)}, u32[]{:S(2)}, u32[]{:S(2)}) collective-permute-start(bf16[16,1024]{1,0:T(8,128)(2,1)S(1)} %get-tuple-element.22), channel_id=1, source_target_pairs={{0,11},{1,12},{2,13},{3,14},{4,15},{5,0},{6,1},{7,2},{8,3},{9,4},{... | collective-permute-start | bytes 98312 | tf_op jit(solution)/shard_map/ppermute | solution.py:70
  106.7 5.3 %collective-permute-start.11 = (bf16[16,1024]{1,0:T(8,128)(2,1)S(1)}, bf16[16,1024]{1,0:T(8,128)(2,1)S(1)}, u32[]{:S(2)}, u32[]{:S(2)}) collective-permute-start(bf16[16,1024]{1,0:T(8,128)(2,1)S(1)} %get-tuple-element.21), channel_id=1, source_target_pairs={{0,12},{1,13},{2,14},{3,15},{4,0},{5,1},{6,2},{7,3},{8,4},{9,5},{1... | collective-permute-start | bytes 98312 | tf_op jit(solution)/shard_map/ppermute | solution.py:70
  108.2 3.9 %collective-permute-start.12 = (bf16[16,1024]{1,0:T(8,128)(2,1)S(1)}, bf16[16,1024]{1,0:T(8,128)(2,1)S(1)}, u32[]{:S(2)}, u32[]{:S(2)}) collective-permute-start(bf16[16,1024]{1,0:T(8,128)(2,1)S(1)} %get-tuple-element.20), channel_id=1, source_target_pairs={{0,13},{1,14},{2,15},{3,0},{4,1},{5,2},{6,3},{7,4},{8,5},{9,6},{10... | collective-permute-start | bytes 98312 | tf_op jit(solution)/shard_map/ppermute | solution.py:70
  108.2 4.0 %collective-permute-start.13 = (bf16[16,1024]{1,0:T(8,128)(2,1)S(1)}, bf16[16,1024]{1,0:T(8,128)(2,1)S(1)}, u32[]{:S(2)}, u32[]{:S(2)}) collective-permute-start(bf16[16,1024]{1,0:T(8,128)(2,1)S(1)} %get-tuple-element.19), channel_id=1, source_target_pairs={{0,14},{1,15},{2,0},{3,1},{4,2},{5,3},{6,4},{7,5},{8,6},{9,7},{10,... | collective-permute-start | bytes 98312 | tf_op jit(solution)/shard_map/ppermute | solution.py:70
  110.2 3.4 %collective-permute-start.14 = (bf16[16,1024]{1,0:T(8,128)(2,1)S(1)}, bf16[16,1024]{1,0:T(8,128)(2,1)S(1)}, u32[]{:S(2)}, u32[]{:S(2)}) collective-permute-start(bf16[16,1024]{1,0:T(8,128)(2,1)S(1)} %get-tuple-element.18), channel_id=1, source_target_pairs={{0,15},{1,0},{2,1},{3,2},{4,3},{5,4},{6,5},{7,6},{8,7},{9,8},{10,9... | collective-permute-start | bytes 98312 | tf_op jit(solution)/shard_map/ppermute | solution.py:70

commit v11 on v9

--- a/solution.py
+++ b/solution.py
@@ -42,7 +42,7 @@
 def attend_heads(queries, key_rows, value_rows, live_tokens):
     samples, latents, head_count, head_size = queries.shape
     spike_scores = jnp.einsum(
-        "blhd,bhkd->bhlk", queries, key_rows, preferred_element_type=jnp.float32
+        "blhd,hbkd->bhlk", queries, key_rows, preferred_element_type=jnp.float32
     ) * HEAD_DIM ** (-0.5)
     spike_scores = jnp.where(live_tokens[:, None, None, :], spike_scores, masked_score)
     spike_max = jnp.max(spike_scores, axis=-1, keepdims=True)
@@ -50,7 +50,7 @@
     denominator = jnp.transpose(jnp.sum(spike_exp, axis=-1, keepdims=True), (0, 2, 1, 3))
     spike_mix = (
         jnp.einsum(
-            "bhlk,bhkd->blhd",
+            "bhlk,hbkd->blhd",
             spike_exp.astype(jnp.bfloat16),
             value_rows,
             preferred_element_type=jnp.float32,
@@ -145,35 +145,51 @@
     sample_pick = jnp.sum(
         jnp.where(slot_pick, jnp.arange(local_samples, dtype=jnp.int32)[None, :], 0), axis=1
     )
+    panel_table = panels.reshape(sess_dev * unit_total, model_width)
+    panel_normed = normed(panel_table)
+    key_table = jnp.einsum(
+        "pc,chd->hpd",
+        panel_normed,
+        kv_weight[:, :model_width].reshape(model_width, head_count, HEAD_DIM),
+        preferred_element_type=jnp.float32,
+    ).astype(jnp.bfloat16)
+    value_table = jnp.einsum(
+        "pc,chd->hpd",
+        panel_normed,
+        kv_weight[:, model_width:].reshape(model_width, head_count, HEAD_DIM),
+        preferred_element_type=jnp.float32,
+    ).astype(jnp.bfloat16)
+    row_total = local_samples * latents
+    flat_state = state.reshape(row_total, model_width)
+    queries = jnp.dot(normed(flat_state), q1_weight, preferred_element_type=jnp.float32).astype(
+        jnp.bfloat16
+    )
     table = jnp.concatenate([request, count_pick[:, None]], axis=1)
     code_base = 64
     codes = jnp.concatenate([table // code_base, table % code_base], axis=1).astype(jnp.bfloat16)
     memory_pair = jnp.concatenate([memory_key, memory_value], axis=1)
     memory_count = memory_pair.shape[0]
-    code_rows = jnp.zeros((owners, 8, 2 * model_width), jnp.bfloat16)
-    code_rows = code_rows.at[:, 0, : codes.shape[1]].set(codes)
+    code_lanes = 2 * HEAD_DIM
+    code_block = jnp.pad(codes, ((0, 0), (0, memory_count * code_lanes - codes.shape[1])))
     arrived = lax.all_to_all(
         jnp.concatenate(
-            [jnp.broadcast_to(memory_pair[None], (owners,) + memory_pair.shape), code_rows],
-            axis=1,
+            [
+                jnp.broadcast_to(memory_pair[None], (owners,) + memory_pair.shape),
+                code_block.reshape(owners, memory_count, code_lanes),
+            ],
+            axis=2,
         ),
         "smp",
         split_axis=0,
         concat_axis=0,
         tiled=True,
     )
-    memory_rows = arrived[:, :memory_count].reshape(1, -1, 2 * model_width)
-    code_back = arrived[:, memory_count, : codes.shape[1]].astype(jnp.int32)
+    memory_rows = arrived[:, :, : 2 * model_width].reshape(1, -1, 2 * model_width)
+    code_back = (
+        arrived[:, :, 2 * model_width :].reshape(owners, -1)[:, : codes.shape[1]].astype(jnp.int32)
+    )
     served = code_back[:, : table.shape[1]] * code_base + code_back[:, table.shape[1] :]
     served_index = served[:, :token_total]
-    panel_table = panels.reshape(sess_dev * unit_total, model_width)
-    served_embed = panel_table[served_index.reshape(-1)]
-    row_total = local_samples * latents
-    flat_state = state.reshape(row_total, model_width)
-    queries = jnp.dot(normed(flat_state), q1_weight, preferred_element_type=jnp.float32).astype(
-        jnp.bfloat16
-    )
-    embed_normed = normed(served_embed).reshape(owners, token_total, model_width)
     memory_total = memory_rows.shape[1]
     read_mem = attend_kernel(
         queries.reshape(1, row_total, model_width),
@@ -191,19 +207,8 @@
     served_queries = lax.all_to_all(
         queries2[sample_pick], "smp", split_axis=0, concat_axis=0, tiled=True
     )
-    key_rows = jnp.einsum(
-        "btc,chd->bhtd",
-        embed_normed,
-        kv_weight[:, :model_width].reshape(model_width, head_count, HEAD_DIM),
-        preferred_element_type=jnp.float32,
-    ).astype(jnp.bfloat16)
-    value_rows = jnp.einsum(
-        "btc,chd->bhtd",
-        embed_normed,
-        kv_weight[:, model_width:].reshape(model_width, head_count, HEAD_DIM),
-        preferred_element_type=jnp.float32,
-    ).astype(jnp.bfloat16)
-    key_rows, value_rows = lax.optimization_barrier((key_rows, value_rows))
+    key_rows = key_table[:, served_index]
+    value_rows = value_table[:, served_index]
     live_tokens = jnp.arange(token_total, dtype=jnp.int32)[None, :] < served[:, token_total:]
     served_read = attend_heads(
         served_queries.reshape(owners, latents, head_count, HEAD_DIM),

time: 128 us -> 113 us (0.88)
  waiting for transfers between devices: 30.4 us -> 14.8 us
  matrix products: 30.6 us -> 23.3 us
  local copies, waits for them, and re-layouts: 28.6 us -> 35.9 us
  other arithmetic: 10.6 us -> 12.7 us
  starting transfers between devices: 22.7 us -> 20.6 us
    all_to_all x1, waiting for transfers between devices: 15.9 us -> 0.33 us  [per_device(): lax.all_to_all(jnp.concatenate([jnp.broadcast_to(memory_pair[None], (owne...]
    gather x1 -> x2, local copies, waits for them, and re-layouts: 5.39 us -> 19.9 us  [the longest x1 9.98 us: per_device(): value_rows = value_table[:, served_index]]
    slice x4 -> x2, local copies, waits for them, and re-layouts: 14.9 us -> 1.14 us  [the longest x1 1.13 us: per_device(): arrived[:, :, :2 * model_width].reshape(1, -1, 2 * model_width)]
    dot_general x4 -> x2, matrix products: 18.4 us -> 6.67 us  [the longest x1 4.7 us: attend_heads(): jnp.einsum('blhd,hbkd->bhlk', queries, key_rows, preferred_element_type=j...]
    convert_element_type x0 -> x2, local copies, waits for them, and re-layouts: none -> 7.66 us  [the longest x1 3.85 us: per_device(): key_table = jnp.einsum('pc,chd->hpd', panel_normed, kv_weight[:, :model_w...]
    unnamed x0 -> x2, matrix products: none -> 6.6 us
    all_to_all x1, starting transfers between devices: 9.17 us -> 7.25 us  [per_device(): lax.all_to_all(queries2[sample_pick], 'smp', split_axis=0, concat_axis=0,...]
    dot_general x1, matrix products: 3.39 us -> 1.56 us  [per_device(): jnp.dot(normed(hidden), q2_weight, preferred_element_type=jnp.float32)]
  transfers between devices with their start and end apart: 3 -> 3, of which waited for: 2 -> 2; matrix products, arithmetic and copies ran while one was open for 29% -> 39% of each run, Pallas kernels for 0% -> 0%
where the time goes in v11:
time: 113 us; the launch traced here: 112 us
  local copies, waits for them, and re-layouts  35.9 us (32%)
  matrix products  23.3 us (21%)
  starting transfers between devices  20.6 us (18%)
  waiting for transfers between devices  14.8 us (13%)
  other arithmetic  12.7 us (11%)
  Pallas kernels  4.1 us (4%)
    all_to_all x1, waiting for transfers between devices, per_device(): lax.all_to_all(served_read.reshape(owners, latents, model_width), 'smp',...  14.4 us
    gather x1, local copies, waits for them, and re-layouts, per_device(): value_rows = value_table[:, served_index]  9.98 us
    gather x1, local copies, waits for them, and re-layouts, per_device(): key_rows = key_table[:, served_index]  9.97 us
    all_to_all x1, starting transfers between devices, per_device(): lax.all_to_all(jnp.concatenate([jnp.broadcast_to(memory_pair[None], (owne...  7.39 us
    all_to_all x1, starting transfers between devices, per_device(): lax.all_to_all(queries2[sample_pick], 'smp', split_axis=0, concat_axis=0,...  7.25 us
    unnamed x2, matrix products  6.6 us
    all_to_all x1, starting transfers between devices, per_device(): lax.all_to_all(served_read.reshape(owners, latents, model_width), 'smp',...  5.94 us
    dot_general x1, matrix products, attend_heads(): jnp.einsum('blhd,hbkd->bhlk', queries, key_rows, preferred_element_type=j...  4.7 us
  transfers between devices with their start and end apart: 3, of which 2 were waited for; matrix products, arithmetic and copies ran while one was open for 39% of the time, Pallas kernels for 0%

profile of v11, /device:TPU:0, one launch (start us, length us, event | category | flops | bytes accessed | tf_op | source)
XLA Modules:
  0.0 111.6 jit_solution(3641494442851458399)
XLA Ops:
  0.0 0.0 copy-start
  0.0 1.0 select_reduce_fusion.4
  1.0 0.9 select_reduce_fusion.1
  1.9 0.1 copy.29
  2.0 0.9 add_select_fusion.2
  2.9 0.1 select_reduce_fusion
  3.0 0.1 fusion.40
  3.1 0.1 fusion.39
  3.2 0.8 pad_maximum_fusion.1
  4.0 0.1 broadcast_in_dim.98
  4.1 1.1 pad_maximum_fusion
  5.2 7.4 %all-to-all-start = ((bf16[16,16,2176]{2,1,0:T(8,128)(2,1)}), bf16[16,16,2176]{2,1,0:T(8,128)(2,1)S(1)}, u32[]{:S(2)}, u32[]{:S(2)}) async-start(bf16[16,16,2176]{2,1,0:T(8,128)(2,1)} %pad_maximum_fusion), calls=%async_computation | async-start | bytes 2228224 | tf_op jit(solution)/shard_map/all_to_all | solution.py:174
  12.6 1.2 %multiply_reduce_fusion = f32[16,16]{1,0:T(8,128)S(1)} fusion(bf16[16,16,1024]{2,1,0:T(8,128)(2,1)} %param.14), kind=kLoop, calls=%fused_computation.46 | loop fusion | flops 786176 | bytes 525312 | tf_op jit(solution)/shard_map/reduce_sum | solution.py:16
  13.9 0.1 rsqrt.28
  13.9 1.5 %fusion.6 = f32[512]{0:T(512)S(1)} fusion(bf16[1,512,1024]{2,1,0:T(8,128)(2,1)} %param.20), kind=kLoop, calls=%fused_computation.12 | loop fusion | flops 1572352 | bytes 1050624 | tf_op jit(solution)/shard_map/reduce_sum | solution.py:16
  15.5 3.3 %fusion.9 = f32[512,1024]{0,1:S(1)} fusion(bf16[1024,2048]{1,0:T(8,128)(2,1)} %param.25, bf16[1,512,1024]{2,1,0:T(8,128)(2,1)} %param.20, f32[512]{0:T(512)S(1)} %add_rsqrt_fusion.1), kind=kOutput, calls=%fused_computation.18 | convolution fusion | flops 1075314688 | bytes 5244928
  18.8 1.1 %convert_bitcast_fusion = bf16[16,512,64]{1,2,0:T(8,128)(2,1)} fusion(f32[512,16,64]{0,2,1:T(8,128)S(1)} %bitcast.82), kind=kLoop, calls=%fused_computation.44 | loop fusion | flops 524288 | bytes 3145728 | tf_op jit(solution)/shard_map/convert_element_type | solution.py:155
  19.9 3.8 %copy.34 = bf16[16,512,64]{2,0,1:T(8,128)(2,1)} copy(bf16[16,512,64]{1,2,0:T(8,128)(2,1)} %convert_bitcast_fusion) | data formatting | bytes 2097152 | tf_op jit(solution)/shard_map/convert_element_type | solution.py:155
  23.8 3.3 %fusion.11 = f32[512,1024]{0,1:S(1)} fusion(bf16[1024,2048]{1,0:T(8,128)(2,1)} %param.25, bf16[1,512,1024]{2,1,0:T(8,128)(2,1)} %param.20, f32[512]{0:T(512)S(1)} %add_rsqrt_fusion.1), kind=kOutput, calls=%fused_computation.20 | convolution fusion | flops 1075314688 | bytes 5244928
  27.1 1.1 %convert_bitcast_fusion.1 = bf16[16,512,64]{1,2,0:T(8,128)(2,1)} fusion(f32[512,16,64]{0,2,1:T(8,128)S(1)} %bitcast.81), kind=kLoop, calls=%fused_computation.45 | loop fusion | flops 524288 | bytes 3145728 | tf_op jit(solution)/shard_map/convert_element_type | solution.py:161
  28.2 3.8 %copy.31 = bf16[16,512,64]{2,0,1:T(8,128)(2,1)} copy(bf16[16,512,64]{1,2,0:T(8,128)(2,1)} %convert_bitcast_fusion.1) | data formatting | bytes 2097152 | tf_op jit(solution)/shard_map/convert_element_type | solution.py:161
  32.0 1.2 %fusion.25 = bf16[256,1024]{1,0:T(8,128)(2,1)S(1)} fusion(bf16[16,16,1024]{2,1,0:T(8,128)(2,1)} %param.14, f32[256]{0:T(256)S(1)} %rsqrt.28), kind=kLoop, calls=%fused_computation.39 | loop fusion | flops 786432 | bytes 1049600 | tf_op jit(solution)/shard_map/convert_element_type | solution.py:16
  33.2 3.1 %fusion.20.query_ref = bf16[1,256,1024]{2,1,0:T(8,128)(2,1)} fusion(bf16[256,1024]{1,0:T(8,128)(2,1)S(1)} %fusion.25, bf16[1024,1024]{1,0:T(8,128)(2,1)} %param.23), kind=kOutput, calls=%fused_computation.33 | convolution fusion | flops 537133056 | bytes 3145728 | tf_op jit(solution)/shard_map/dot_general | solution.py:164
  36.3 0.3 all-to-all-done
  36.6 1.1 %slice.44 = bf16[16,16,2048]{2,1,0:T(8,128)(2,1)} slice(bf16[16,16,2176]{2,1,0:T(8,128)(2,1)S(1)} %all-to-all-done), slice={[0:16], [0:16], [0:2048]} | slice | bytes 2097152 | tf_op jit(solution)/shard_map/slice | solution.py:187
  37.8 4.1 %shard_map.136 = bf16[1,256,1024]{2,1,0:T(8,128)(2,1)} custom-call(s32[1]{0:T(128)} %constant.72.clone.1.counts_ref, bf16[1,256,1024]{2,1,0:T(8,128)(2,1)} %fusion.20.query_ref, bf16[1,256,2048]{2,1,0:T(8,128)(2,1)} %bitcast.78, bf16[1,256,2048]{2,1,0:T(8,128)(2,1)} %bitcast.79), custom_call_target="tpu_custom_call" | custom-call | tf_op jit(solution)/shard_map/pallas_call | solution.py:96
  41.9 0.0 copy-done
  41.9 0.0 copy-start.2
  41.9 2.2 %fusion.21 = (f32[256]{0:T(256)S(1)}, bf16[256,1024]{1,0:T(8,128)(2,1)S(1)}) fusion(bf16[1024,1024]{1,0:T(8,128)(2,1)S(1)} %copy-done, bf16[1,256,1024]{2,1,0:T(8,128)(2,1)} %shard_map.136, bf16[256,1024]{1,0:T(8,128)(2,1)} %bitcast.83), kind=kOutput, calls=%fused_computation.35 | convolution fusion | flops 538443520 | bytes 3671040 | tf_op jit(solution)/shard_map/dot_general | solution.py:201
  44.1 0.0 copy-start.3
  44.1 0.0 copy-done.2
  44.1 1.6 %convolution_convert_fusion = bf16[256,1024]{1,0:T(8,128)(2,1)} fusion(bf16[1024,1024]{1,0:T(8,128)(2,1)S(1)} %copy-done.2, bf16[256,1024]{1,0:T(8,128)(2,1)S(1)} %get-tuple-element.11, f32[256]{0:T(256)S(1)} %add_rsqrt_fusion.2), kind=kOutput, calls=%fused_computation.30 | convolution fusion | flops 537919488 | bytes 3146752 | tf_op jit(solution)/shard_map/dot_general | solution.py:203
  45.7 0.0 copy-done.3
  45.7 2.4 %gather_fusion.1 = bf16[16,16,1024]{2,1,0:T(8,128)(2,1)} fusion(bf16[16,16,1024]{2,1,0:T(8,128)(2,1)} %bitcast.85, s32[1024]{0:T(1024)S(1)} %pad_clamp_fusion.1), kind=kCustom, calls=%fused_computation.1 | custom fusion | bytes 1048640 | tf_op jit(solution)/shard_map/gather | solution.py:208
  48.1 7.2 %all-to-all-start.1 = ((bf16[16,16,1024]{2,1,0:T(8,128)(2,1)}), bf16[16,16,1024]{2,1,0:T(8,128)(2,1)}, u32[]{:S(2)}, u32[]{:S(2)}) async-start(bf16[16,16,1024]{2,1,0:T(8,128)(2,1)} %gather_fusion.1), calls=%async_computation.1 | async-start | bytes 1048576 | tf_op jit(solution)/shard_map/all_to_all | solution.py:207
  55.4 0.1 slice_add_fusion
  55.5 0.1 reshape.188
  55.6 10.0 %gather_fusion.2 = bf16[1024,16,64]{2,1,0:T(8,128)(2,1)} fusion(bf16[16,512,64]{2,0,1:T(8,128)(2,1)} %copy.34, s32[1024]{0:T(1024)S(1)} %broadcast_clamp_fusion), kind=kCustom, calls=%fused_computation.2 | custom fusion | bytes 4198400 | tf_op jit(solution)/shard_map/gather | solution.py:210
  65.5 10.0 %gather_fusion = bf16[1024,16,64]{2,1,0:T(8,128)(2,1)} fusion(bf16[16,512,64]{2,0,1:T(8,128)(2,1)} %copy.31, s32[1024]{0:T(1024)S(1)} %broadcast_clamp_fusion), kind=kCustom, calls=%fused_computation | custom fusion | bytes 4198400 | tf_op jit(solution)/shard_map/gather | solution.py:211
  75.5 0.2 slice_reduce_fusion
  75.7 0.1 iota_compare_fusion.1
  75.8 0.0 all-to-all-done.1
  75.8 1.8 %reshape.181 = bf16[16,16,16,64]{3,2,1,0:T(8,128)(2,1)S(1)} reshape(bf16[16,16,1024]{2,1,0:T(8,128)(2,1)} %all-to-all-done.1) | data formatting | bytes 1048576 | tf_op jit(solution)/shard_map/reshape | solution.py:214
  77.5 0.0 copy-start.1
  77.5 4.7 %fusion.13 = (f32[16,16,16]{2,1,0:T(8,128)S(1)}, f32[16,16,16,64]{3,2,1,0:T(8,128)S(1)}) fusion(pred[16,64]{1,0:T(8,128)(4,1)S(1)} %iota_compare_fusion.1, bf16[16,64,16,64]{3,2,1,0:T(8,128)(2,1)} %bitcast.77, bf16[16,16,16,64]{3,2,1,0:T(8,128)(2,1)S(1)} %reshape.181), kind=kOutput, calls=%fused_computation.22 | convolution fusion | flops 34336768 | bytes 3687424 | tf_op jit(solution)/shard_map/blhd,hbkd->bhlk/dot_general | solution.py:44
  82.2 1.3 %fusion.16 = f32[16,16,16]{2,1,0:T(8,128)S(1)} fusion(f32[16,16,16,64]{3,2,1,0:T(8,128)S(1)} %get-tuple-element.13, f32[16,16,16]{2,1,0:T(8,128)S(1)} %get-tuple-element.12, pred[16,64]{1,0:T(8,128)(4,1)S(1)} %iota_compare_fusion.1), kind=kLoop, calls=%fused_computation.23 | loop fusion | flops 1044480 | bytes 1082368 | tf_op jit(solution)/shard_map/reduce_sum | solution.py:50
  83.6 0.0 copy-done.1
  83.6 2.0 %fusion.8 = bf16[16,16,16,64]{3,1,2,0:T(8,128)(2,1)S(1)} fusion(bf16[16,64,16,64]{3,2,1,0:T(8,128)(2,1)S(1)} %bitcast.80, f32[16,16,16,64]{3,2,1,0:T(8,128)S(1)} %get-tuple-element.13, f32[16,16,16]{1,2,0:T(8,128)S(1)} %bitcast.88, f32[16,16,16]{2,1,0:T(8,128)S(1)} %get-tuple-element.12, pred[16,64]{1,0:T(8,128)(4,1)S(1)} %iota_compare_fusion.1), kind=kOutput, calls=%fused_computation.15 | convolution fusion | flops 35127296 | bytes 3703808 | tf_op jit(solution)/shard_map/bhlk,hbkd->blhd/dot_general | solution.py:52
  85.6 0.3 copy.37
  85.9 1.5 %convert_element_type.91 = bf16[16,16,1024]{2,1,0:T(8,128)(2,1)} reshape(bf16[16,16,16,64]{3,2,1,0:T(8,128)(2,1)S(1)} %copy.37) | data formatting | bytes 1048576 | tf_op jit(solution)/shard_map/convert_element_type | solution.py:60
  87.4 5.9 %all-to-all-start.2 = ((bf16[16,16,1024]{2,1,0:T(8,128)(2,1)}), bf16[16,16,1024]{2,1,0:T(8,128)(2,1)S(1)}, u32[]{:S(2)}, u32[]{:S(2)}) async-start(bf16[16,16,1024]{2,1,0:T(8,128)(2,1)} %convert_element_type.91), calls=%async_computation.2 | async-start | bytes 1048576 | tf_op jit(solution)/shard_map/all_to_all | solution.py:219
  93.3 14.4 %all-to-all-done.2 = bf16[16,16,1024]{2,1,0:T(8,128)(2,1)S(1)} async-done(((bf16[16,16,1024]{2,1,0:T(8,128)(2,1)}), bf16[16,16,1024]{2,1,0:T(8,128)(2,1)S(1)}, u32[]{:S(2)}, u32[]{:S(2)}) %all-to-all-start.2) | async-done | bytes 524320 | tf_op jit(solution)/shard_map/all_to_all | solution.py:219
  107.8 0.6 gather_fusion.3
  108.4 3.2 %fusion.18 = bf16[256,1024]{1,0:T(8,128)(2,1)} fusion(bf16[256,1024]{1,0:T(8,128)(2,1)S(1)} %bitcast.84, bf16[1024,1024]{1,0:T(8,128)(2,1)} %param.27, bf16[256,1024]{1,0:T(8,128)(2,1)} %copy-done.3), kind=kOutput, calls=%fused_computation.29 | convolution fusion | flops 537657344 | bytes 3670016 | tf_op jit(solution)/shard_map/dot_general | solution.py:226
  (16 shorter events, 0.1 us)
Async XLA Ops:
  0.0 41.9 %copy-start = (bf16[1024,1024]{1,0:T(8,128)(2,1)S(1)}, bf16[1024,1024]{1,0:T(8,128)(2,1)}, u32[]{:S(2)}) copy-start(bf16[1024,1024]{1,0:T(8,128)(2,1)} %param.24) | copy-start | bytes 6291460
  5.2 31.4 %all-to-all-start = ((bf16[16,16,2176]{2,1,0:T(8,128)(2,1)}), bf16[16,16,2176]{2,1,0:T(8,128)(2,1)S(1)}, u32[]{:S(2)}, u32[]{:S(2)}) async-start(bf16[16,16,2176]{2,1,0:T(8,128)(2,1)} %pad_maximum_fusion), calls=%async_computation | async-start | bytes 2228224 | tf_op jit(solution)/shard_map/all_to_all | solution.py:174
  41.9 2.2 %copy-start.2 = (bf16[1024,1024]{1,0:T(8,128)(2,1)S(1)}, bf16[1024,1024]{1,0:T(8,128)(2,1)}, u32[]{:S(2)}) copy-start(bf16[1024,1024]{1,0:T(8,128)(2,1)} %param.26) | copy-start | bytes 6291460
  44.1 1.6 %copy-start.3 = (bf16[256,1024]{1,0:T(8,128)(2,1)}, bf16[256,1024]{1,0:T(8,128)(2,1)S(1)}, u32[]{:S(2)}) copy-start(bf16[256,1024]{1,0:T(8,128)(2,1)S(1)} %get-tuple-element.11) | copy-start | bytes 1572868
  48.1 27.7 %all-to-all-start.1 = ((bf16[16,16,1024]{2,1,0:T(8,128)(2,1)}), bf16[16,16,1024]{2,1,0:T(8,128)(2,1)}, u32[]{:S(2)}, u32[]{:S(2)}) async-start(bf16[16,16,1024]{2,1,0:T(8,128)(2,1)} %gather_fusion.1), calls=%async_computation.1 | async-start | bytes 1048576 | tf_op jit(solution)/shard_map/all_to_all | solution.py:207
  77.5 6.1 %copy-start.1 = (bf16[1024,16,64]{2,1,0:T(8,128)(2,1)S(1)}, bf16[1024,16,64]{2,1,0:T(8,128)(2,1)}, u32[]{:S(2)}) copy-start(bf16[1024,16,64]{2,1,0:T(8,128)(2,1)} %gather_fusion) | copy-start | bytes 6291460
  87.4 20.4 %all-to-all-start.2 = ((bf16[16,16,1024]{2,1,0:T(8,128)(2,1)}), bf16[16,16,1024]{2,1,0:T(8,128)(2,1)S(1)}, u32[]{:S(2)}, u32[]{:S(2)}) async-start(bf16[16,16,1024]{2,1,0:T(8,128)(2,1)} %convert_element_type.91), calls=%async_computation.2 | async-start | bytes 1048576 | tf_op jit(solution)/shard_map/all_to_all | solution.py:219

commit v12 on v11

--- a/solution.py
+++ b/solution.py
@@ -207,8 +207,20 @@
     served_queries = lax.all_to_all(
         queries2[sample_pick], "smp", split_axis=0, concat_axis=0, tiled=True
     )
-    key_rows = key_table[:, served_index]
-    value_rows = value_table[:, served_index]
+    pick = (
+        served_index.reshape(-1)[:, None]
+        == jnp.arange(key_table.shape[1], dtype=jnp.int32)[None, :]
+    ).astype(jnp.bfloat16)
+    key_rows = (
+        jnp.einsum("np,hpd->hnd", pick, key_table, preferred_element_type=jnp.float32)
+        .astype(jnp.bfloat16)
+        .reshape(head_count, owners, token_total, HEAD_DIM)
+    )
+    value_rows = (
+        jnp.einsum("np,hpd->hnd", pick, value_table, preferred_element_type=jnp.float32)
+        .astype(jnp.bfloat16)
+        .reshape(head_count, owners, token_total, HEAD_DIM)
+    )
     live_tokens = jnp.arange(token_total, dtype=jnp.int32)[None, :] < served[:, token_total:]
     served_read = attend_heads(
         served_queries.reshape(owners, latents, head_count, HEAD_DIM),

time: 113 us -> 115 us (1.018)
  local copies, waits for them, and re-layouts: 35.9 us -> 21 us
  waiting for transfers between devices: 14.8 us -> 25.6 us
  matrix products: 23.3 us -> 32.1 us
  other arithmetic: 12.7 us -> 10.7 us
    gather x2 -> x0, local copies, waits for them, and re-layouts: 19.9 us -> none  [the longest x1 9.98 us: per_device(): value_rows = value_table[:, served_index]]
    reshape x0 -> x2, local copies, waits for them, and re-layouts: none -> 12.7 us  [the longest x1 6.37 us: per_device(): key_rows = jnp.einsum('np,hpd->hnd', pick, key_table, preferred_element_t...]
    all_to_all x1, waiting for transfers between devices: 0.33 us -> 11.2 us  [per_device(): lax.all_to_all(jnp.concatenate([jnp.broadcast_to(memory_pair[None], (owne...]
    dot_general x0 -> x2, matrix products: none -> 8.83 us  [the longest x1 4.44 us: per_device(): jnp.einsum('np,hpd->hnd', pick, value_table, preferred_element_type=jnp.f...]
    convert_element_type x2 -> x0, local copies, waits for them, and re-layouts: 7.66 us -> none  [the longest x1 3.85 us: per_device(): key_table = jnp.einsum('pc,chd->hpd', panel_normed, kv_weight[:, :model_w...]
    convert_element_type x2 -> x0, other arithmetic: 2.28 us -> none  [the longest x1 1.14 us: per_device(): key_table = jnp.einsum('pc,chd->hpd', panel_normed, kv_weight[:, :model_w...]
  transfers between devices with their start and end apart: 3 -> 3, of which waited for: 2 -> 2; matrix products, arithmetic and copies ran while one was open for 39% -> 30% of each run, Pallas kernels for 0% -> 0%
where the time goes in v12:
time: 115 us; the launch traced here: 114 us
  matrix products  32.1 us (28%)
  waiting for transfers between devices  25.6 us (22%)
  local copies, waits for them, and re-layouts  21 us (18%)
  starting transfers between devices  20.6 us (18%)
  other arithmetic  10.7 us (9%)
  Pallas kernels  4.11 us (4%)
    all_to_all x1, waiting for transfers between devices, per_device(): lax.all_to_all(served_read.reshape(owners, latents, model_width), 'smp',...  14.4 us
    all_to_all x1, waiting for transfers between devices, per_device(): lax.all_to_all(jnp.concatenate([jnp.broadcast_to(memory_pair[None], (owne...  11.2 us
    all_to_all x1, starting transfers between devices, per_device(): lax.all_to_all(jnp.concatenate([jnp.broadcast_to(memory_pair[None], (owne...  7.39 us
    all_to_all x1, starting transfers between devices, per_device(): lax.all_to_all(queries2[sample_pick], 'smp', split_axis=0, concat_axis=0,...  7.25 us
    reshape x1, local copies, waits for them, and re-layouts, per_device(): key_rows = jnp.einsum('np,hpd->hnd', pick, key_table, preferred_element_t...  6.37 us
    reshape x1, local copies, waits for them, and re-layouts, per_device(): value_rows = jnp.einsum('np,hpd->hnd', pick, value_table, preferred_eleme...  6.37 us
    all_to_all x1, starting transfers between devices, per_device(): lax.all_to_all(served_read.reshape(owners, latents, model_width), 'smp',...  5.94 us
    unnamed x2, matrix products  5.45 us
  transfers between devices with their start and end apart: 3, of which 2 were waited for; matrix products, arithmetic and copies ran while one was open for 30% of the time, Pallas kernels for 0%

profile of v12, /device:TPU:0, one launch (start us, length us, event | category | flops | bytes accessed | tf_op | source)
XLA Modules:
  0.0 114.3 jit_solution(9030178133265728140)
XLA Ops:
  0.0 0.0 copy-start
  0.0 1.0 select_reduce_fusion.4
  1.0 0.9 select_reduce_fusion.1
  1.9 0.1 copy.42
  2.0 0.9 add_select_fusion.2
  2.9 0.1 select_reduce_fusion
  3.0 0.1 fusion.53
  3.1 0.1 fusion.52
  3.2 0.8 pad_maximum_fusion.1
  4.0 0.1 broadcast_in_dim.95
  4.1 1.1 pad_maximum_fusion
  5.2 7.4 %all-to-all-start = ((bf16[16,16,2176]{2,1,0:T(8,128)(2,1)}), bf16[16,16,2176]{2,1,0:T(8,128)(2,1)S(1)}, u32[]{:S(2)}, u32[]{:S(2)}) async-start(bf16[16,16,2176]{2,1,0:T(8,128)(2,1)} %pad_maximum_fusion), calls=%async_computation | async-start | bytes 2228224 | tf_op jit(solution)/shard_map/all_to_all | solution.py:174
  12.6 1.2 %multiply_reduce_fusion = f32[16,16]{1,0:T(8,128)S(1)} fusion(bf16[16,16,1024]{2,1,0:T(8,128)(2,1)} %param.14), kind=kLoop, calls=%fused_computation.52 | loop fusion | flops 786176 | bytes 525312 | tf_op jit(solution)/shard_map/reduce_sum | solution.py:16
  13.9 0.1 rsqrt.28
  14.0 0.0 copy-start.3
  14.0 1.7 %fusion.4 = f32[512]{0:T(512)S(1)} fusion(bf16[1,512,1024]{2,1,0:T(8,128)(2,1)} %param.20), kind=kLoop, calls=%fused_computation.8 | loop fusion | flops 1572352 | bytes 1050624 | tf_op jit(solution)/shard_map/reduce_sum | solution.py:16
  15.6 0.0 copy-start.2
  15.7 1.3 %fusion.34 = bf16[256,1024]{1,0:T(8,128)(2,1)S(1)} fusion(bf16[16,16,1024]{2,1,0:T(8,128)(2,1)} %param.14, f32[256]{0:T(256)S(1)} %rsqrt.28), kind=kLoop, calls=%fused_computation.43 | loop fusion | flops 786432 | bytes 1049600 | tf_op jit(solution)/shard_map/convert_element_type | solution.py:16
  16.9 3.1 %fusion.27.query_ref = bf16[1,256,1024]{2,1,0:T(8,128)(2,1)} fusion(bf16[256,1024]{1,0:T(8,128)(2,1)S(1)} %fusion.34, bf16[1024,1024]{1,0:T(8,128)(2,1)} %param.23), kind=kOutput, calls=%fused_computation.35 | convolution fusion | flops 537133056 | bytes 3145728 | tf_op jit(solution)/shard_map/dot_general | solution.py:164
  20.0 0.0 copy-done.3
  20.0 0.0 copy-done.2
  20.0 2.7 %fusion.7 = f32[512,1024]{0,1} fusion(bf16[1024,2048]{1,0:T(8,128)(2,1)S(1)} %copy-done.3, bf16[1,512,1024]{2,1,0:T(8,128)(2,1)S(1)} %copy-done.2, f32[512]{0:T(512)S(1)} %add_rsqrt_fusion.1), kind=kOutput, calls=%fused_computation.15 | convolution fusion | flops 1075314688 | bytes 5244928
  22.8 2.7 %fusion.9 = f32[512,1024]{0,1} fusion(bf16[1024,2048]{1,0:T(8,128)(2,1)S(1)} %copy-done.3, bf16[1,512,1024]{2,1,0:T(8,128)(2,1)S(1)} %copy-done.2, f32[512]{0:T(512)S(1)} %add_rsqrt_fusion.1), kind=kOutput, calls=%fused_computation.19 | convolution fusion | flops 1075314688 | bytes 5244928
  25.5 11.2 %all-to-all-done = bf16[16,16,2176]{2,1,0:T(8,128)(2,1)S(1)} async-done(((bf16[16,16,2176]{2,1,0:T(8,128)(2,1)}), bf16[16,16,2176]{2,1,0:T(8,128)(2,1)S(1)}, u32[]{:S(2)}, u32[]{:S(2)}) %all-to-all-start) | async-done | bytes 1114144 | tf_op jit(solution)/shard_map/all_to_all | solution.py:174
  36.6 1.1 slice.40
  37.8 4.1 %shard_map.136 = bf16[1,256,1024]{2,1,0:T(8,128)(2,1)} custom-call(s32[1]{0:T(128)} %constant.70.clone.1.counts_ref, bf16[1,256,1024]{2,1,0:T(8,128)(2,1)} %fusion.27.query_ref, bf16[1,256,2048]{2,1,0:T(8,128)(2,1)} %bitcast.84, bf16[1,256,2048]{2,1,0:T(8,128)(2,1)} %bitcast.85), custom_call_target="tpu_custom_call" | custom-call | tf_op jit(solution)/shard_map/pallas_call | solution.py:96
  41.9 0.0 copy-done
  41.9 0.0 copy-start.4
  41.9 2.2 %fusion.28 = (f32[256]{0:T(256)S(1)}, bf16[256,1024]{1,0:T(8,128)(2,1)S(1)}) fusion(bf16[1024,1024]{1,0:T(8,128)(2,1)S(1)} %copy-done, bf16[1,256,1024]{2,1,0:T(8,128)(2,1)} %shard_map.136, bf16[256,1024]{1,0:T(8,128)(2,1)} %bitcast.86), kind=kOutput, calls=%fused_computation.37 | convolution fusion | flops 538443520 | bytes 3671040 | tf_op jit(solution)/shard_map/dot_general | solution.py:201
  44.0 0.0 copy-start.5
  44.1 0.0 copy-done.4
  44.1 1.6 %convolution_convert_fusion = bf16[256,1024]{1,0:T(8,128)(2,1)} fusion(bf16[1024,1024]{1,0:T(8,128)(2,1)S(1)} %copy-done.4, bf16[256,1024]{1,0:T(8,128)(2,1)S(1)} %get-tuple-element.11, f32[256]{0:T(256)S(1)} %add_rsqrt_fusion.2), kind=kOutput, calls=%fused_computation.32 | convolution fusion | flops 537919488 | bytes 3146752 | tf_op jit(solution)/shard_map/dot_general | solution.py:203
  45.6 0.0 copy-done.5
  45.6 2.4 %gather_fusion = bf16[16,16,1024]{2,1,0:T(8,128)(2,1)} fusion(bf16[16,16,1024]{2,1,0:T(8,128)(2,1)} %bitcast.88, s32[1024]{0:T(1024)S(1)} %pad_clamp_fusion.1), kind=kCustom, calls=%fused_computation | custom fusion | bytes 1048640 | tf_op jit(solution)/shard_map/gather | solution.py:208
  48.1 7.2 %all-to-all-start.1 = ((bf16[16,16,1024]{2,1,0:T(8,128)(2,1)}), bf16[16,16,1024]{2,1,0:T(8,128)(2,1)}, u32[]{:S(2)}, u32[]{:S(2)}) async-start(bf16[16,16,1024]{2,1,0:T(8,128)(2,1)} %gather_fusion), calls=%async_computation.1 | async-start | bytes 1048576 | tf_op jit(solution)/shard_map/all_to_all | solution.py:207
  55.4 0.1 slice_add_fusion
  55.4 0.1 eq.86
  55.5 4.4 %convert_bitcast_fusion = bf16[16,1024,64]{1,2,0:T(8,128)(2,1)} fusion(f32[512,16,64]{0,2,1:T(8,128)} %bitcast.96, s32[1024]{0:T(1024)S(1)} %eq.86), kind=kOutput, calls=%fused_computation.14 | convolution fusion | flops 1075838976 | bytes 4198400 | tf_op jit(solution)/shard_map/np,hpd->hnd/dot_general | solution.py:215
  59.9 6.4 %reshape.191 = bf16[16,16,64,64]{2,1,3,0:T(8,128)(2,1)} reshape(bf16[16,1024,64]{1,2,0:T(8,128)(2,1)} %convert_bitcast_fusion) | data formatting | bytes 4194304 | tf_op jit(solution)/shard_map/reshape | solution.py:217
  66.3 4.4 %convert_bitcast_fusion.1 = bf16[16,1024,64]{1,2,0:T(8,128)(2,1)} fusion(s32[1024]{0:T(1024)S(1)} %eq.86, f32[512,16,64]{0,2,1:T(8,128)} %bitcast.95), kind=kOutput, calls=%fused_computation.17 | convolution fusion | flops 1075838976 | bytes 4198400 | tf_op jit(solution)/shard_map/np,hpd->hnd/dot_general | solution.py:220
  70.7 6.4 %reshape.187 = bf16[16,16,64,64]{2,1,3,0:T(8,128)(2,1)} reshape(bf16[16,1024,64]{1,2,0:T(8,128)(2,1)} %convert_bitcast_fusion.1) | data formatting | bytes 4194304 | tf_op jit(solution)/shard_map/reshape | solution.py:222
  77.1 0.2 slice_reduce_fusion
  77.3 0.1 iota_compare_fusion.2
  77.3 0.0 all-to-all-done.1
  77.3 1.8 %reshape.189 = bf16[16,16,16,64]{3,2,1,0:T(8,128)(2,1)S(1)} reshape(bf16[16,16,1024]{2,1,0:T(8,128)(2,1)} %all-to-all-done.1) | data formatting | bytes 1048576 | tf_op jit(solution)/shard_map/reshape | solution.py:226
  79.1 0.0 copy-start.1
  79.1 4.7 %fusion.20 = (f32[16,16,16]{2,1,0:T(8,128)S(1)}, f32[16,16,16,64]{3,2,1,0:T(8,128)S(1)}) fusion(pred[16,64]{1,0:T(8,128)(4,1)S(1)} %iota_compare_fusion.2, bf16[16,16,64,64]{2,1,3,0:T(8,128)(2,1)} %reshape.191, bf16[16,16,16,64]{3,2,1,0:T(8,128)(2,1)S(1)} %reshape.189), kind=kOutput, calls=%fused_computation.24 | convolution fusion | flops 34336768 | bytes 3687424 | tf_op jit(solution)/shard_map/blhd,hbkd->bhlk/dot_general | solution.py:44
  83.8 1.4 %fusion.23 = f32[16,16,16]{2,1,0:T(8,128)S(1)} fusion(f32[16,16,16,64]{3,2,1,0:T(8,128)S(1)} %get-tuple-element.13, f32[16,16,16]{2,1,0:T(8,128)S(1)} %get-tuple-element.12, pred[16,64]{1,0:T(8,128)(4,1)S(1)} %iota_compare_fusion.2), kind=kLoop, calls=%fused_computation.25 | loop fusion | flops 1044480 | bytes 1082368 | tf_op jit(solution)/shard_map/reduce_sum | solution.py:50
  85.2 0.0 copy-done.1
  85.2 3.1 %fusion.6 = bf16[16,16,16,64]{3,1,2,0:T(8,128)(2,1)S(1)} fusion(bf16[16,16,64,64]{2,1,3,0:T(8,128)(2,1)S(1)} %copy-done.1, f32[16,16,16,64]{3,2,1,0:T(8,128)S(1)} %get-tuple-element.13, f32[16,16,16]{1,2,0:T(8,128)S(1)} %bitcast.91, f32[16,16,16]{2,1,0:T(8,128)S(1)} %get-tuple-element.12, pred[16,64]{1,0:T(8,128)(4,1)S(1)} %iota_compare_fusion.2), kind=kOutput, calls=%fused_computation.11 | convolution fusion | flops 35127296 | bytes 3703808 | tf_op jit(solution)/shard_map/bhlk,hbkd->blhd/dot_general | solution.py:52
  88.3 0.3 copy.48
  88.6 1.5 %convert_element_type.108 = bf16[16,16,1024]{2,1,0:T(8,128)(2,1)} reshape(bf16[16,16,16,64]{3,2,1,0:T(8,128)(2,1)S(1)} %copy.48) | data formatting | bytes 1048576 | tf_op jit(solution)/shard_map/convert_element_type | solution.py:60
  90.1 5.9 %all-to-all-start.2 = ((bf16[16,16,1024]{2,1,0:T(8,128)(2,1)}), bf16[16,16,1024]{2,1,0:T(8,128)(2,1)S(1)}, u32[]{:S(2)}, u32[]{:S(2)}) async-start(bf16[16,16,1024]{2,1,0:T(8,128)(2,1)} %convert_element_type.108), calls=%async_computation.2 | async-start | bytes 1048576 | tf_op jit(solution)/shard_map/all_to_all | solution.py:231
  96.1 14.4 %all-to-all-done.2 = bf16[16,16,1024]{2,1,0:T(8,128)(2,1)S(1)} async-done(((bf16[16,16,1024]{2,1,0:T(8,128)(2,1)}), bf16[16,16,1024]{2,1,0:T(8,128)(2,1)S(1)}, u32[]{:S(2)}, u32[]{:S(2)}) %all-to-all-start.2) | async-done | bytes 524320 | tf_op jit(solution)/shard_map/all_to_all | solution.py:231
  110.5 0.6 gather_fusion.1
  111.1 3.2 %fusion.25 = bf16[256,1024]{1,0:T(8,128)(2,1)} fusion(bf16[256,1024]{1,0:T(8,128)(2,1)S(1)} %bitcast.87, bf16[1024,1024]{1,0:T(8,128)(2,1)} %param.27, bf16[256,1024]{1,0:T(8,128)(2,1)} %copy-done.5), kind=kOutput, calls=%fused_computation.31 | convolution fusion | flops 537657344 | bytes 3670016 | tf_op jit(solution)/shard_map/dot_general | solution.py:238
  (14 shorter events, 0.1 us)
Async XLA Ops:
  0.0 41.9 %copy-start = (bf16[1024,1024]{1,0:T(8,128)(2,1)S(1)}, bf16[1024,1024]{1,0:T(8,128)(2,1)}, u32[]{:S(2)}) copy-start(bf16[1024,1024]{1,0:T(8,128)(2,1)} %param.24) | copy-start | bytes 6291460
  5.2 31.4 %all-to-all-start = ((bf16[16,16,2176]{2,1,0:T(8,128)(2,1)}), bf16[16,16,2176]{2,1,0:T(8,128)(2,1)S(1)}, u32[]{:S(2)}, u32[]{:S(2)}) async-start(bf16[16,16,2176]{2,1,0:T(8,128)(2,1)} %pad_maximum_fusion), calls=%async_computation | async-start | bytes 2228224 | tf_op jit(solution)/shard_map/all_to_all | solution.py:174
  14.0 6.1 %copy-start.3 = (bf16[1024,2048]{1,0:T(8,128)(2,1)S(1)}, bf16[1024,2048]{1,0:T(8,128)(2,1)}, u32[]{:S(2)}) copy-start(bf16[1024,2048]{1,0:T(8,128)(2,1)} %param.25) | copy-start | bytes 12582916
  15.6 4.4 %copy-start.2 = (bf16[1,512,1024]{2,1,0:T(8,128)(2,1)S(1)}, bf16[1,512,1024]{2,1,0:T(8,128)(2,1)}, u32[]{:S(2)}) copy-start(bf16[1,512,1024]{2,1,0:T(8,128)(2,1)} %param.20) | copy-start | bytes 3145732
  41.9 2.2 %copy-start.4 = (bf16[1024,1024]{1,0:T(8,128)(2,1)S(1)}, bf16[1024,1024]{1,0:T(8,128)(2,1)}, u32[]{:S(2)}) copy-start(bf16[1024,1024]{1,0:T(8,128)(2,1)} %param.26) | copy-start | bytes 6291460
  44.0 1.6 %copy-start.5 = (bf16[256,1024]{1,0:T(8,128)(2,1)}, bf16[256,1024]{1,0:T(8,128)(2,1)S(1)}, u32[]{:S(2)}) copy-start(bf16[256,1024]{1,0:T(8,128)(2,1)S(1)} %get-tuple-element.11) | copy-start | bytes 1572868
  48.1 29.3 %all-to-all-start.1 = ((bf16[16,16,1024]{2,1,0:T(8,128)(2,1)}), bf16[16,16,1024]{2,1,0:T(8,128)(2,1)}, u32[]{:S(2)}, u32[]{:S(2)}) async-start(bf16[16,16,1024]{2,1,0:T(8,128)(2,1)} %gather_fusion), calls=%async_computation.1 | async-start | bytes 1048576 | tf_op jit(solution)/shard_map/all_to_all | solution.py:207
  79.1 6.1 %copy-start.1 = (bf16[16,16,64,64]{2,1,3,0:T(8,128)(2,1)S(1)}, bf16[16,16,64,64]{2,1,3,0:T(8,128)(2,1)}, u32[]{:S(2)}) copy-start(bf16[16,16,64,64]{2,1,3,0:T(8,128)(2,1)} %reshape.187) | copy-start | bytes 6291460
  90.1 20.4 %all-to-all-start.2 = ((bf16[16,16,1024]{2,1,0:T(8,128)(2,1)}), bf16[16,16,1024]{2,1,0:T(8,128)(2,1)S(1)}, u32[]{:S(2)}, u32[]{:S(2)}) async-start(bf16[16,16,1024]{2,1,0:T(8,128)(2,1)} %convert_element_type.108), calls=%async_computation.2 | async-start | bytes 1048576 | tf_op jit(solution)/shard_map/all_to_all | solution.py:231

commit v13 on v11

--- a/solution.py
+++ b/solution.py
@@ -184,7 +184,7 @@
         concat_axis=0,
         tiled=True,
     )
-    memory_rows = arrived[:, :, : 2 * model_width].reshape(1, -1, 2 * model_width)
+    memory_rows = arrived.reshape(1, -1, arrived.shape[2])
     code_back = (
         arrived[:, :, 2 * model_width :].reshape(owners, -1)[:, : codes.shape[1]].astype(jnp.int32)
     )
@@ -205,7 +205,18 @@
     )
     queries2 = queries2.reshape(local_samples, latents, model_width)
     served_queries = lax.all_to_all(
-        queries2[sample_pick], "smp", split_axis=0, concat_axis=0, tiled=True
+        jnp.einsum(
+            "ob,bld->old",
+            (sample_pick[:, None] == jnp.arange(local_samples, dtype=jnp.int32)[None, :]).astype(
+                jnp.bfloat16
+            ),
+            queries2,
+            preferred_element_type=jnp.float32,
+        ).astype(jnp.bfloat16),
+        "smp",
+        split_axis=0,
+        concat_axis=0,
+        tiled=True,
     )
     key_rows = key_table[:, served_index]
     value_rows = value_table[:, served_index]

time: 113 us -> 112 us (level)
    gather x1 -> x0, local copies, waits for them, and re-layouts: 2.41 us -> none  [per_device(): queries2[sample_pick]]
    slice x1 -> x0, local copies, waits for them, and re-layouts: 1.13 us -> none  [per_device(): arrived[:, :, :2 * model_width].reshape(1, -1, 2 * model_width)]
  transfers between devices with their start and end apart: 3 -> 3, of which waited for: 2 -> 2; matrix products, arithmetic and copies ran while one was open for 39% -> 41% of each run, Pallas kernels for 0% -> 0%
where the time goes in v13:
time: 112 us; the launch traced here: 111 us
  local copies, waits for them, and re-layouts  35.2 us (31%)
  matrix products  22.9 us (20%)
  starting transfers between devices  20.6 us (18%)
  waiting for transfers between devices  14.8 us (13%)
  other arithmetic  12.7 us (11%)
  Pallas kernels  4.1 us (4%)
    all_to_all x1, waiting for transfers between devices, per_device(): lax.all_to_all(served_read.reshape(owners, latents, model_width), 'smp',...  14.4 us
    gather x1, local copies, waits for them, and re-layouts, per_device(): value_rows = value_table[:, served_index]  9.98 us
    gather x1, local copies, waits for them, and re-layouts, per_device(): key_rows = key_table[:, served_index]  9.96 us
    all_to_all x1, starting transfers between devices, per_device(): lax.all_to_all(jnp.concatenate([jnp.broadcast_to(memory_pair[None], (owne...  7.39 us
    all_to_all x1, starting transfers between devices, per_device(): lax.all_to_all(jnp.einsum('ob,bld->old', (sample_pick[:, None] == jnp.ara...  7.25 us
    unnamed x2, matrix products  6.6 us
    all_to_all x1, starting transfers between devices, per_device(): lax.all_to_all(served_read.reshape(owners, latents, model_width), 'smp',...  5.96 us
    dot_general x1, matrix products, attend_heads(): jnp.einsum('blhd,hbkd->bhlk', queries, key_rows, preferred_element_type=j...  4.7 us
  transfers between devices with their start and end apart: 3, of which 2 were waited for; matrix products, arithmetic and copies ran while one was open for 41% of the time, Pallas kernels for 0%

profile of v13, /device:TPU:0, one launch (start us, length us, event | category | flops | bytes accessed | tf_op | source)
XLA Modules:
  0.0 110.6 jit_solution(10945489564059834860)
XLA Ops:
  0.0 0.0 copy-start
  0.0 1.0 select_reduce_fusion.4
  1.0 0.9 select_reduce_fusion.1
  1.9 0.1 copy.53
  2.0 0.9 add_select_fusion.2
  2.9 0.1 select_reduce_fusion
  3.0 0.1 fusion.41
  3.1 0.1 fusion.40
  3.2 0.8 pad_maximum_fusion.1
  4.0 0.1 broadcast_in_dim.99
  4.1 1.1 %pad_maximum_fusion = bf16[16,16,2176]{2,1,0:T(8,128)(2,1)} fusion(bf16[16,16,128]{2,1,0:T(8,128)(2,1)S(1)} %bitcast.85, bf16[16,16,2048]{2,1,0:T(8,128)(2,1)S(1)} %broadcast_in_dim.99), kind=kLoop, calls=%fused_computation.34 | loop fusion | flops 2228224 | bytes 2228224 | tf_op jit(solution)/shard_map/concatenate | solution.py:175
  5.2 7.4 %all-to-all-start = ((bf16[16,16,2176]{2,1,0:T(8,128)(2,1)}), bf16[16,16,2176]{2,1,0:T(8,128)(2,1)S(1)}, u32[]{:S(2)}, u32[]{:S(2)}) async-start(bf16[16,16,2176]{2,1,0:T(8,128)(2,1)} %pad_maximum_fusion), calls=%async_computation | async-start | bytes 2228224 | tf_op jit(solution)/shard_map/all_to_all | solution.py:174
  12.6 1.2 %multiply_reduce_fusion = f32[16,16]{1,0:T(8,128)S(1)} fusion(bf16[16,16,1024]{2,1,0:T(8,128)(2,1)} %param.14), kind=kLoop, calls=%fused_computation.46 | loop fusion | flops 786176 | bytes 525312 | tf_op jit(solution)/shard_map/reduce_sum | solution.py:16
  13.9 1.5 %fusion.6 = f32[512]{0:T(512)S(1)} fusion(bf16[1,512,1024]{2,1,0:T(8,128)(2,1)} %param.20), kind=kLoop, calls=%fused_computation.11 | loop fusion | flops 1572352 | bytes 1050624 | tf_op jit(solution)/shard_map/reduce_sum | solution.py:16
  15.4 0.1 rsqrt.28
  15.5 3.3 %fusion.9 = f32[512,1024]{0,1:S(1)} fusion(bf16[1024,2048]{1,0:T(8,128)(2,1)} %param.25, bf16[1,512,1024]{2,1,0:T(8,128)(2,1)} %param.20, f32[512]{0:T(512)S(1)} %add_rsqrt_fusion.1), kind=kOutput, calls=%fused_computation.17 | convolution fusion | flops 1075314688 | bytes 5244928
  18.8 1.1 %convert_bitcast_fusion = bf16[16,512,64]{1,2,0:T(8,128)(2,1)} fusion(f32[512,16,64]{0,2,1:T(8,128)S(1)} %bitcast.81), kind=kLoop, calls=%fused_computation.44 | loop fusion | flops 524288 | bytes 3145728 | tf_op jit(solution)/shard_map/convert_element_type | solution.py:155
  19.9 3.8 %copy.60 = bf16[16,512,64]{2,0,1:T(8,128)(2,1)} copy(bf16[16,512,64]{1,2,0:T(8,128)(2,1)} %convert_bitcast_fusion) | data formatting | bytes 2097152 | tf_op jit(solution)/shard_map/convert_element_type | solution.py:155
  23.7 3.3 %fusion.11 = f32[512,1024]{0,1:S(1)} fusion(bf16[1024,2048]{1,0:T(8,128)(2,1)} %param.25, bf16[1,512,1024]{2,1,0:T(8,128)(2,1)} %param.20, f32[512]{0:T(512)S(1)} %add_rsqrt_fusion.1), kind=kOutput, calls=%fused_computation.19 | convolution fusion | flops 1075314688 | bytes 5244928
  27.0 1.1 %convert_bitcast_fusion.1 = bf16[16,512,64]{1,2,0:T(8,128)(2,1)} fusion(f32[512,16,64]{0,2,1:T(8,128)S(1)} %bitcast.80), kind=kLoop, calls=%fused_computation.45 | loop fusion | flops 524288 | bytes 3145728 | tf_op jit(solution)/shard_map/convert_element_type | solution.py:161
  28.2 3.8 %copy.55 = bf16[16,512,64]{2,0,1:T(8,128)(2,1)} copy(bf16[16,512,64]{1,2,0:T(8,128)(2,1)} %convert_bitcast_fusion.1) | data formatting | bytes 2097152 | tf_op jit(solution)/shard_map/convert_element_type | solution.py:161
  32.0 1.2 %fusion.25 = bf16[256,1024]{1,0:T(8,128)(2,1)S(1)} fusion(bf16[16,16,1024]{2,1,0:T(8,128)(2,1)} %param.14, f32[256]{0:T(256)S(1)} %rsqrt.28), kind=kLoop, calls=%fused_computation.39 | loop fusion | flops 786432 | bytes 1049600 | tf_op jit(solution)/shard_map/convert_element_type | solution.py:16
  33.2 3.1 %fusion.20.query_ref = bf16[1,256,1024]{2,1,0:T(8,128)(2,1)} fusion(bf16[256,1024]{1,0:T(8,128)(2,1)S(1)} %fusion.25, bf16[1024,1024]{1,0:T(8,128)(2,1)} %param.23), kind=kOutput, calls=%fused_computation.33 | convolution fusion | flops 537133056 | bytes 3145728 | tf_op jit(solution)/shard_map/dot_general | solution.py:164
  36.3 0.4 all-to-all-done
  36.6 0.0 copy-start.1
  36.7 1.0 copy-done.1
  37.7 4.1 %shard_map.136 = bf16[1,256,1024]{2,1,0:T(8,128)(2,1)} custom-call(s32[1]{0:T(128)} %constant.72.clone.1.counts_ref, bf16[1,256,1024]{2,1,0:T(8,128)(2,1)} %fusion.20.query_ref, bf16[1,256,2176]{2,1,0:T(8,128)(2,1)} %bitcast.77, bf16[1,256,2176]{2,1,0:T(8,128)(2,1)} %bitcast.78), custom_call_target="tpu_custom_call" | custom-call | tf_op jit(solution)/shard_map/pallas_call | solution.py:96
  41.8 0.0 copy-done
  41.8 0.0 copy-start.3
  41.8 2.2 %fusion.21 = (f32[256]{0:T(256)S(1)}, bf16[256,1024]{1,0:T(8,128)(2,1)S(1)}) fusion(bf16[1024,1024]{1,0:T(8,128)(2,1)S(1)} %copy-done, bf16[1,256,1024]{2,1,0:T(8,128)(2,1)} %shard_map.136, bf16[256,1024]{1,0:T(8,128)(2,1)} %bitcast.82), kind=kOutput, calls=%fused_computation.35 | convolution fusion | flops 538443520 | bytes 3671040 | tf_op jit(solution)/shard_map/dot_general | solution.py:201
  43.9 0.0 copy-start.4
  44.0 0.0 copy-done.3
  44.0 0.8 convolution_convert_fusion.1
  44.8 0.5 convolution_convert_fusion
  45.2 0.0 copy-done.4
  45.2 1.1 copy.58
  46.3 7.2 %all-to-all-start.1 = ((bf16[16,16,1024]{2,1,0:T(8,128)(2,1)}), bf16[16,16,1024]{2,1,0:T(8,128)(2,1)}, u32[]{:S(2)}, u32[]{:S(2)}) async-start(bf16[16,16,1024]{2,1,0:T(8,128)(2,1)} %copy.58), calls=%async_computation.1 | async-start | bytes 1048576 | tf_op jit(solution)/shard_map/all_to_all | solution.py:207
  53.6 0.8 slice.38
  54.5 0.1 slice_add_fusion
  54.5 0.1 reshape.176
  54.6 10.0 %gather_fusion.1 = bf16[1024,16,64]{2,1,0:T(8,128)(2,1)} fusion(bf16[16,512,64]{2,0,1:T(8,128)(2,1)} %copy.60, s32[1024]{0:T(1024)S(1)} %broadcast_clamp_fusion), kind=kCustom, calls=%fused_computation.1 | custom fusion | bytes 4198400 | tf_op jit(solution)/shard_map/gather | solution.py:221
  64.6 10.0 %gather_fusion = bf16[1024,16,64]{2,1,0:T(8,128)(2,1)} fusion(bf16[16,512,64]{2,0,1:T(8,128)(2,1)} %copy.55, s32[1024]{0:T(1024)S(1)} %broadcast_clamp_fusion), kind=kCustom, calls=%fused_computation | custom fusion | bytes 4198400 | tf_op jit(solution)/shard_map/gather | solution.py:222
  74.6 0.2 slice_reduce_fusion
  74.7 0.1 iota_compare_fusion.2
  74.8 0.0 all-to-all-done.1
  74.8 1.8 %reshape.169 = bf16[16,16,16,64]{3,2,1,0:T(8,128)(2,1)S(1)} reshape(bf16[16,16,1024]{2,1,0:T(8,128)(2,1)} %all-to-all-done.1) | data formatting | bytes 1048576 | tf_op jit(solution)/shard_map/reshape | solution.py:225
  76.6 0.0 copy-start.2
  76.6 4.7 %fusion.13 = (f32[16,16,16]{2,1,0:T(8,128)S(1)}, f32[16,16,16,64]{3,2,1,0:T(8,128)S(1)}) fusion(pred[16,64]{1,0:T(8,128)(4,1)S(1)} %iota_compare_fusion.2, bf16[16,64,16,64]{3,2,1,0:T(8,128)(2,1)} %bitcast.76, bf16[16,16,16,64]{3,2,1,0:T(8,128)(2,1)S(1)} %reshape.169), kind=kOutput, calls=%fused_computation.21 | convolution fusion | flops 34336768 | bytes 3687424 | tf_op jit(solution)/shard_map/blhd,hbkd->bhlk/dot_general | solution.py:44
  81.3 1.3 %fusion.16 = f32[16,16,16]{2,1,0:T(8,128)S(1)} fusion(f32[16,16,16,64]{3,2,1,0:T(8,128)S(1)} %get-tuple-element.13, f32[16,16,16]{2,1,0:T(8,128)S(1)} %get-tuple-element.12, pred[16,64]{1,0:T(8,128)(4,1)S(1)} %iota_compare_fusion.2), kind=kLoop, calls=%fused_computation.22 | loop fusion | flops 1044480 | bytes 1082368 | tf_op jit(solution)/shard_map/reduce_sum | solution.py:50
  82.6 0.0 copy-done.2
  82.7 2.0 %fusion.8 = bf16[16,16,16,64]{3,1,2,0:T(8,128)(2,1)S(1)} fusion(bf16[16,64,16,64]{3,2,1,0:T(8,128)(2,1)S(1)} %bitcast.79, f32[16,16,16,64]{3,2,1,0:T(8,128)S(1)} %get-tuple-element.13, f32[16,16,16]{1,2,0:T(8,128)S(1)} %bitcast.87, f32[16,16,16]{2,1,0:T(8,128)S(1)} %get-tuple-element.12, pred[16,64]{1,0:T(8,128)(4,1)S(1)} %iota_compare_fusion.2), kind=kOutput, calls=%fused_computation.14 | convolution fusion | flops 35127296 | bytes 3703808 | tf_op jit(solution)/shard_map/bhlk,hbkd->blhd/dot_general | solution.py:52
  84.6 0.3 copy.63
  84.9 1.5 %convert_element_type.96 = bf16[16,16,1024]{2,1,0:T(8,128)(2,1)} reshape(bf16[16,16,16,64]{3,2,1,0:T(8,128)(2,1)S(1)} %copy.63) | data formatting | bytes 1048576 | tf_op jit(solution)/shard_map/convert_element_type | solution.py:60
  86.4 6.0 %all-to-all-start.2 = ((bf16[16,16,1024]{2,1,0:T(8,128)(2,1)}), bf16[16,16,1024]{2,1,0:T(8,128)(2,1)S(1)}, u32[]{:S(2)}, u32[]{:S(2)}) async-start(bf16[16,16,1024]{2,1,0:T(8,128)(2,1)} %convert_element_type.96), calls=%async_computation.2 | async-start | bytes 1048576 | tf_op jit(solution)/shard_map/all_to_all | solution.py:230
  92.4 14.4 %all-to-all-done.2 = bf16[16,16,1024]{2,1,0:T(8,128)(2,1)S(1)} async-done(((bf16[16,16,1024]{2,1,0:T(8,128)(2,1)}), bf16[16,16,1024]{2,1,0:T(8,128)(2,1)S(1)}, u32[]{:S(2)}, u32[]{:S(2)}) %all-to-all-start.2) | async-done | bytes 524320 | tf_op jit(solution)/shard_map/all_to_all | solution.py:230
  106.9 0.6 gather_fusion.2
  107.5 3.2 %fusion.18 = bf16[256,1024]{1,0:T(8,128)(2,1)} fusion(bf16[256,1024]{1,0:T(8,128)(2,1)S(1)} %bitcast.84, bf16[1024,1024]{1,0:T(8,128)(2,1)} %param.27, bf16[256,1024]{1,0:T(8,128)(2,1)} %copy-done.4), kind=kOutput, calls=%fused_computation.28 | convolution fusion | flops 537657344 | bytes 3670016 | tf_op jit(solution)/shard_map/dot_general | solution.py:237
  (13 shorter events, 0.1 us)
Async XLA Ops:
  0.0 41.8 %copy-start = (bf16[1024,1024]{1,0:T(8,128)(2,1)S(1)}, bf16[1024,1024]{1,0:T(8,128)(2,1)}, u32[]{:S(2)}) copy-start(bf16[1024,1024]{1,0:T(8,128)(2,1)} %param.24) | copy-start | bytes 6291460
  5.2 31.4 %all-to-all-start = ((bf16[16,16,2176]{2,1,0:T(8,128)(2,1)}), bf16[16,16,2176]{2,1,0:T(8,128)(2,1)S(1)}, u32[]{:S(2)}, u32[]{:S(2)}) async-start(bf16[16,16,2176]{2,1,0:T(8,128)(2,1)} %pad_maximum_fusion), calls=%async_computation | async-start | bytes 2228224 | tf_op jit(solution)/shard_map/all_to_all | solution.py:174
  36.6 1.0 copy-start.1
  41.8 2.2 %copy-start.3 = (bf16[1024,1024]{1,0:T(8,128)(2,1)S(1)}, bf16[1024,1024]{1,0:T(8,128)(2,1)}, u32[]{:S(2)}) copy-start(bf16[1024,1024]{1,0:T(8,128)(2,1)} %param.26) | copy-start | bytes 6291460
  43.9 1.3 %copy-start.4 = (bf16[256,1024]{1,0:T(8,128)(2,1)}, bf16[256,1024]{1,0:T(8,128)(2,1)S(1)}, u32[]{:S(2)}) copy-start(bf16[256,1024]{1,0:T(8,128)(2,1)S(1)} %get-tuple-element.11) | copy-start | bytes 1572868
  46.3 28.5 %all-to-all-start.1 = ((bf16[16,16,1024]{2,1,0:T(8,128)(2,1)}), bf16[16,16,1024]{2,1,0:T(8,128)(2,1)}, u32[]{:S(2)}, u32[]{:S(2)}) async-start(bf16[16,16,1024]{2,1,0:T(8,128)(2,1)} %copy.58), calls=%async_computation.1 | async-start | bytes 1048576 | tf_op jit(solution)/shard_map/all_to_all | solution.py:207
  76.6 6.1 %copy-start.2 = (bf16[1024,16,64]{2,1,0:T(8,128)(2,1)S(1)}, bf16[1024,16,64]{2,1,0:T(8,128)(2,1)}, u32[]{:S(2)}) copy-start(bf16[1024,16,64]{2,1,0:T(8,128)(2,1)} %gather_fusion) | copy-start | bytes 6291460
  86.4 20.4 %all-to-all-start.2 = ((bf16[16,16,1024]{2,1,0:T(8,128)(2,1)}), bf16[16,16,1024]{2,1,0:T(8,128)(2,1)S(1)}, u32[]{:S(2)}, u32[]{:S(2)}) async-start(bf16[16,16,1024]{2,1,0:T(8,128)(2,1)} %convert_element_type.96), calls=%async_computation.2 | async-start | bytes 1048576 | tf_op jit(solution)/shard_map/all_to_all | solution.py:230

commit v14 on v13

--- a/solution.py
+++ b/solution.py
@@ -42,7 +42,7 @@
 def attend_heads(queries, key_rows, value_rows, live_tokens):
     samples, latents, head_count, head_size = queries.shape
     spike_scores = jnp.einsum(
-        "blhd,hbkd->bhlk", queries, key_rows, preferred_element_type=jnp.float32
+        "blhd,bkhd->bhlk", queries, key_rows, preferred_element_type=jnp.float32
     ) * HEAD_DIM ** (-0.5)
     spike_scores = jnp.where(live_tokens[:, None, None, :], spike_scores, masked_score)
     spike_max = jnp.max(spike_scores, axis=-1, keepdims=True)
@@ -50,7 +50,7 @@
     denominator = jnp.transpose(jnp.sum(spike_exp, axis=-1, keepdims=True), (0, 2, 1, 3))
     spike_mix = (
         jnp.einsum(
-            "bhlk,hbkd->blhd",
+            "bhlk,bkhd->blhd",
             spike_exp.astype(jnp.bfloat16),
             value_rows,
             preferred_element_type=jnp.float32,
@@ -148,13 +148,13 @@
     panel_table = panels.reshape(sess_dev * unit_total, model_width)
     panel_normed = normed(panel_table)
     key_table = jnp.einsum(
-        "pc,chd->hpd",
+        "pc,chd->phd",
         panel_normed,
         kv_weight[:, :model_width].reshape(model_width, head_count, HEAD_DIM),
         preferred_element_type=jnp.float32,
     ).astype(jnp.bfloat16)
     value_table = jnp.einsum(
-        "pc,chd->hpd",
+        "pc,chd->phd",
         panel_normed,
         kv_weight[:, model_width:].reshape(model_width, head_count, HEAD_DIM),
         preferred_element_type=jnp.float32,
@@ -218,8 +218,8 @@
         concat_axis=0,
         tiled=True,
     )
-    key_rows = key_table[:, served_index]
-    value_rows = value_table[:, served_index]
+    key_rows = key_table[served_index]
+    value_rows = value_table[served_index]
     live_tokens = jnp.arange(token_total, dtype=jnp.int32)[None, :] < served[:, token_total:]
     served_read = attend_heads(
         served_queries.reshape(owners, latents, head_count, HEAD_DIM),

time: 112 us -> 112 us (level)
  no operation moved by 1% of the time
where the time goes in v14:
time: 112 us; the launch traced here: 111 us
  local copies, waits for them, and re-layouts  35.2 us (31%)
  matrix products  22.9 us (20%)
  starting transfers between devices  20.6 us (18%)
  waiting for transfers between devices  14.8 us (13%)
  other arithmetic  12.7 us (11%)
  Pallas kernels  4.1 us (4%)
    all_to_all x1, waiting for transfers between devices, per_device(): lax.all_to_all(served_read.reshape(owners, latents, model_width), 'smp',...  14.4 us
    gather x1, local copies, waits for them, and re-layouts, per_device(): value_rows = value_table[served_index]  9.98 us
    gather x1, local copies, waits for them, and re-layouts, per_device(): key_rows = key_table[served_index]  9.96 us
    all_to_all x1, starting transfers between devices, per_device(): lax.all_to_all(jnp.concatenate([jnp.broadcast_to(memory_pair[None], (owne...  7.39 us
    all_to_all x1, starting transfers between devices, per_device(): lax.all_to_all(jnp.einsum('ob,bld->old', (sample_pick[:, None] == jnp.ara...  7.25 us
    unnamed x2, matrix products  6.6 us
    all_to_all x1, starting transfers between devices, per_device(): lax.all_to_all(served_read.reshape(owners, latents, model_width), 'smp',...  5.97 us
    dot_general x1, matrix products, attend_heads(): jnp.einsum('blhd,bkhd->bhlk', queries, key_rows, preferred_element_type=j...  4.7 us
  transfers between devices with their start and end apart: 3, of which 2 were waited for; matrix products, arithmetic and copies ran while one was open for 41% of the time, Pallas kernels for 0%

profile of v14, /device:TPU:0, one launch (start us, length us, event | category | flops | bytes accessed | tf_op | source)
XLA Modules:
  0.0 110.6 jit_solution(2462383022111342043)
XLA Ops:
  0.0 0.0 copy-start
  0.0 1.0 select_reduce_fusion.4
  1.0 0.9 select_reduce_fusion.1
  1.9 0.1 copy.53
  2.0 0.9 add_select_fusion.2
  2.9 0.1 select_reduce_fusion
  3.0 0.1 fusion.39
  3.1 0.1 fusion.38
  3.2 0.8 pad_maximum_fusion.1
  4.0 0.1 broadcast_in_dim.99
  4.1 1.1 %pad_maximum_fusion = bf16[16,16,2176]{2,1,0:T(8,128)(2,1)} fusion(bf16[16,16,128]{2,1,0:T(8,128)(2,1)S(1)} %bitcast.71, bf16[16,16,2048]{2,1,0:T(8,128)(2,1)S(1)} %broadcast_in_dim.99), kind=kLoop, calls=%fused_computation.32 | loop fusion | flops 2228224 | bytes 2228224 | tf_op jit(solution)/shard_map/concatenate | solution.py:175
  5.2 7.4 %all-to-all-start = ((bf16[16,16,2176]{2,1,0:T(8,128)(2,1)}), bf16[16,16,2176]{2,1,0:T(8,128)(2,1)S(1)}, u32[]{:S(2)}, u32[]{:S(2)}) async-start(bf16[16,16,2176]{2,1,0:T(8,128)(2,1)} %pad_maximum_fusion), calls=%async_computation | async-start | bytes 2228224 | tf_op jit(solution)/shard_map/all_to_all | solution.py:174
  12.6 1.2 %multiply_reduce_fusion = f32[16,16]{1,0:T(8,128)S(1)} fusion(bf16[16,16,1024]{2,1,0:T(8,128)(2,1)} %param.14), kind=kLoop, calls=%fused_computation.42 | loop fusion | flops 786176 | bytes 525312 | tf_op jit(solution)/shard_map/reduce_sum | solution.py:16
  13.9 0.1 rsqrt.28
  13.9 1.5 %fusion.4 = f32[512]{0:T(512)S(1)} fusion(bf16[1,512,1024]{2,1,0:T(8,128)(2,1)} %param.20), kind=kLoop, calls=%fused_computation.9 | loop fusion | flops 1572352 | bytes 1050624 | tf_op jit(solution)/shard_map/reduce_sum | solution.py:16
  15.5 3.3 %fusion.7 = f32[512,1024]{0,1:S(1)} fusion(bf16[1024,2048]{1,0:T(8,128)(2,1)} %param.25, bf16[1,512,1024]{2,1,0:T(8,128)(2,1)} %param.20, f32[512]{0:T(512)S(1)} %add_rsqrt_fusion.1), kind=kOutput, calls=%fused_computation.15 | convolution fusion | flops 1075314688 | bytes 5244928
  18.8 1.1 %convert_element_type.85 = bf16[512,16,64]{0,2,1:T(8,128)(2,1)} convert(f32[512,16,64]{0,2,1:T(8,128)S(1)} %bitcast.67) | non-fusion elementwise | flops 524288 | bytes 3145728 | tf_op jit(solution)/shard_map/convert_element_type | solution.py:155
  19.9 3.8 %copy.59 = bf16[512,16,64]{2,1,0:T(8,128)(2,1)} copy(bf16[512,16,64]{0,2,1:T(8,128)(2,1)} %convert_element_type.85) | data formatting | bytes 2097152 | tf_op jit(solution)/shard_map/convert_element_type | solution.py:155
  23.8 3.3 %fusion.9 = f32[512,1024]{0,1:S(1)} fusion(bf16[1024,2048]{1,0:T(8,128)(2,1)} %param.25, bf16[1,512,1024]{2,1,0:T(8,128)(2,1)} %param.20, f32[512]{0:T(512)S(1)} %add_rsqrt_fusion.1), kind=kOutput, calls=%fused_computation.17 | convolution fusion | flops 1075314688 | bytes 5244928
  27.1 1.1 %convert_element_type.80 = bf16[512,16,64]{0,2,1:T(8,128)(2,1)} convert(f32[512,16,64]{0,2,1:T(8,128)S(1)} %bitcast.66) | non-fusion elementwise | flops 524288 | bytes 3145728 | tf_op jit(solution)/shard_map/convert_element_type | solution.py:161
  28.2 3.8 %copy.55 = bf16[512,16,64]{2,1,0:T(8,128)(2,1)} copy(bf16[512,16,64]{0,2,1:T(8,128)(2,1)} %convert_element_type.80) | data formatting | bytes 2097152 | tf_op jit(solution)/shard_map/convert_element_type | solution.py:161
  32.0 1.2 %fusion.23 = bf16[256,1024]{1,0:T(8,128)(2,1)S(1)} fusion(bf16[16,16,1024]{2,1,0:T(8,128)(2,1)} %param.14, f32[256]{0:T(256)S(1)} %rsqrt.28), kind=kLoop, calls=%fused_computation.37 | loop fusion | flops 786432 | bytes 1049600 | tf_op jit(solution)/shard_map/convert_element_type | solution.py:16
  33.2 3.1 %fusion.18.query_ref = bf16[1,256,1024]{2,1,0:T(8,128)(2,1)} fusion(bf16[256,1024]{1,0:T(8,128)(2,1)S(1)} %fusion.23, bf16[1024,1024]{1,0:T(8,128)(2,1)} %param.23), kind=kOutput, calls=%fused_computation.31 | convolution fusion | flops 537133056 | bytes 3145728 | tf_op jit(solution)/shard_map/dot_general | solution.py:164
  36.3 0.3 all-to-all-done
  36.6 0.0 copy-start.1
  36.7 1.0 copy-done.1
  37.7 4.1 %shard_map.136 = bf16[1,256,1024]{2,1,0:T(8,128)(2,1)} custom-call(s32[1]{0:T(128)} %constant.72.clone.1.counts_ref, bf16[1,256,1024]{2,1,0:T(8,128)(2,1)} %fusion.18.query_ref, bf16[1,256,2176]{2,1,0:T(8,128)(2,1)} %bitcast.63, bf16[1,256,2176]{2,1,0:T(8,128)(2,1)} %bitcast.64), custom_call_target="tpu_custom_call" | custom-call | tf_op jit(solution)/shard_map/pallas_call | solution.py:96
  41.8 0.0 copy-done
  41.8 0.0 copy-start.3
  41.8 2.2 %fusion.19 = (f32[256]{0:T(256)S(1)}, bf16[256,1024]{1,0:T(8,128)(2,1)S(1)}) fusion(bf16[1024,1024]{1,0:T(8,128)(2,1)S(1)} %copy-done, bf16[1,256,1024]{2,1,0:T(8,128)(2,1)} %shard_map.136, bf16[256,1024]{1,0:T(8,128)(2,1)} %bitcast.68), kind=kOutput, calls=%fused_computation.33 | convolution fusion | flops 538443520 | bytes 3671040 | tf_op jit(solution)/shard_map/dot_general | solution.py:201
  43.9 0.0 copy-start.4
  44.0 0.0 copy-done.3
  44.0 0.8 convolution_convert_fusion.1
  44.7 0.5 convolution_convert_fusion
  45.2 0.0 copy-done.4
  45.2 1.1 copy.57
  46.3 7.2 %all-to-all-start.1 = ((bf16[16,16,1024]{2,1,0:T(8,128)(2,1)}), bf16[16,16,1024]{2,1,0:T(8,128)(2,1)}, u32[]{:S(2)}, u32[]{:S(2)}) async-start(bf16[16,16,1024]{2,1,0:T(8,128)(2,1)} %copy.57), calls=%async_computation.1 | async-start | bytes 1048576 | tf_op jit(solution)/shard_map/all_to_all | solution.py:207
  53.6 0.8 slice.38
  54.5 0.1 slice_add_fusion
  54.5 0.1 reshape.176
  54.6 10.0 %gather_fusion.1 = bf16[1024,16,64]{2,1,0:T(8,128)(2,1)} fusion(bf16[512,16,64]{2,1,0:T(8,128)(2,1)} %copy.59, s32[1024]{0:T(1024)S(1)} %broadcast_clamp_fusion), kind=kCustom, calls=%fused_computation.1 | custom fusion | bytes 4198400 | tf_op jit(solution)/shard_map/gather | solution.py:221
  64.6 10.0 %gather_fusion = bf16[1024,16,64]{2,1,0:T(8,128)(2,1)} fusion(bf16[512,16,64]{2,1,0:T(8,128)(2,1)} %copy.55, s32[1024]{0:T(1024)S(1)} %broadcast_clamp_fusion), kind=kCustom, calls=%fused_computation | custom fusion | bytes 4198400 | tf_op jit(solution)/shard_map/gather | solution.py:222
  74.6 0.2 slice_reduce_fusion
  74.7 0.1 iota_compare_fusion.2
  74.8 0.0 all-to-all-done.1
  74.8 1.8 %reshape.169 = bf16[16,16,16,64]{3,2,1,0:T(8,128)(2,1)S(1)} reshape(bf16[16,16,1024]{2,1,0:T(8,128)(2,1)} %all-to-all-done.1) | data formatting | bytes 1048576 | tf_op jit(solution)/shard_map/reshape | solution.py:225
  76.6 0.0 copy-start.2
  76.6 4.7 %fusion.11 = (f32[16,16,16]{2,1,0:T(8,128)S(1)}, f32[16,16,16,64]{3,2,1,0:T(8,128)S(1)}) fusion(pred[16,64]{1,0:T(8,128)(4,1)S(1)} %iota_compare_fusion.2, bf16[16,64,16,64]{3,2,1,0:T(8,128)(2,1)} %bitcast.62, bf16[16,16,16,64]{3,2,1,0:T(8,128)(2,1)S(1)} %reshape.169), kind=kOutput, calls=%fused_computation.19 | convolution fusion | flops 34336768 | bytes 3687424 | tf_op jit(solution)/shard_map/blhd,bkhd->bhlk/dot_general | solution.py:44
  81.3 1.3 %fusion.14 = f32[16,16,16]{2,1,0:T(8,128)S(1)} fusion(f32[16,16,16,64]{3,2,1,0:T(8,128)S(1)} %get-tuple-element.13, f32[16,16,16]{2,1,0:T(8,128)S(1)} %get-tuple-element.12, pred[16,64]{1,0:T(8,128)(4,1)S(1)} %iota_compare_fusion.2), kind=kLoop, calls=%fused_computation.20 | loop fusion | flops 1044480 | bytes 1082368 | tf_op jit(solution)/shard_map/reduce_sum | solution.py:50
  82.6 0.0 copy-done.2
  82.7 2.0 %fusion.6 = bf16[16,16,16,64]{3,1,2,0:T(8,128)(2,1)S(1)} fusion(bf16[16,64,16,64]{3,2,1,0:T(8,128)(2,1)S(1)} %bitcast.65, f32[16,16,16,64]{3,2,1,0:T(8,128)S(1)} %get-tuple-element.13, f32[16,16,16]{1,2,0:T(8,128)S(1)} %bitcast.73, f32[16,16,16]{2,1,0:T(8,128)S(1)} %get-tuple-element.12, pred[16,64]{1,0:T(8,128)(4,1)S(1)} %iota_compare_fusion.2), kind=kOutput, calls=%fused_computation.12 | convolution fusion | flops 35127296 | bytes 3703808 | tf_op jit(solution)/shard_map/bhlk,bkhd->blhd/dot_general | solution.py:52
  84.6 0.3 copy.63
  84.9 1.5 %convert_element_type.88 = bf16[16,16,1024]{2,1,0:T(8,128)(2,1)} reshape(bf16[16,16,16,64]{3,2,1,0:T(8,128)(2,1)S(1)} %copy.63) | data formatting | bytes 1048576 | tf_op jit(solution)/shard_map/convert_element_type | solution.py:60
  86.4 6.0 %all-to-all-start.2 = ((bf16[16,16,1024]{2,1,0:T(8,128)(2,1)}), bf16[16,16,1024]{2,1,0:T(8,128)(2,1)S(1)}, u32[]{:S(2)}, u32[]{:S(2)}) async-start(bf16[16,16,1024]{2,1,0:T(8,128)(2,1)} %convert_element_type.88), calls=%async_computation.2 | async-start | bytes 1048576 | tf_op jit(solution)/shard_map/all_to_all | solution.py:230
  92.4 14.4 %all-to-all-done.2 = bf16[16,16,1024]{2,1,0:T(8,128)(2,1)S(1)} async-done(((bf16[16,16,1024]{2,1,0:T(8,128)(2,1)}), bf16[16,16,1024]{2,1,0:T(8,128)(2,1)S(1)}, u32[]{:S(2)}, u32[]{:S(2)}) %all-to-all-start.2) | async-done | bytes 524320 | tf_op jit(solution)/shard_map/all_to_all | solution.py:230
  106.9 0.6 gather_fusion.2
  107.5 3.2 %fusion.16 = bf16[256,1024]{1,0:T(8,128)(2,1)} fusion(bf16[256,1024]{1,0:T(8,128)(2,1)S(1)} %bitcast.70, bf16[1024,1024]{1,0:T(8,128)(2,1)} %param.27, bf16[256,1024]{1,0:T(8,128)(2,1)} %copy-done.4), kind=kOutput, calls=%fused_computation.26 | convolution fusion | flops 537657344 | bytes 3670016 | tf_op jit(solution)/shard_map/dot_general | solution.py:237
  (13 shorter events, 0.1 us)
Async XLA Ops:
  0.0 41.8 %copy-start = (bf16[1024,1024]{1,0:T(8,128)(2,1)S(1)}, bf16[1024,1024]{1,0:T(8,128)(2,1)}, u32[]{:S(2)}) copy-start(bf16[1024,1024]{1,0:T(8,128)(2,1)} %param.24) | copy-start | bytes 6291460
  5.2 31.4 %all-to-all-start = ((bf16[16,16,2176]{2,1,0:T(8,128)(2,1)}), bf16[16,16,2176]{2,1,0:T(8,128)(2,1)S(1)}, u32[]{:S(2)}, u32[]{:S(2)}) async-start(bf16[16,16,2176]{2,1,0:T(8,128)(2,1)} %pad_maximum_fusion), calls=%async_computation | async-start | bytes 2228224 | tf_op jit(solution)/shard_map/all_to_all | solution.py:174
  36.6 1.0 copy-start.1
  41.8 2.2 %copy-start.3 = (bf16[1024,1024]{1,0:T(8,128)(2,1)S(1)}, bf16[1024,1024]{1,0:T(8,128)(2,1)}, u32[]{:S(2)}) copy-start(bf16[1024,1024]{1,0:T(8,128)(2,1)} %param.26) | copy-start | bytes 6291460
  43.9 1.3 %copy-start.4 = (bf16[256,1024]{1,0:T(8,128)(2,1)}, bf16[256,1024]{1,0:T(8,128)(2,1)S(1)}, u32[]{:S(2)}) copy-start(bf16[256,1024]{1,0:T(8,128)(2,1)S(1)} %get-tuple-element.11) | copy-start | bytes 1572868
  46.3 28.5 %all-to-all-start.1 = ((bf16[16,16,1024]{2,1,0:T(8,128)(2,1)}), bf16[16,16,1024]{2,1,0:T(8,128)(2,1)}, u32[]{:S(2)}, u32[]{:S(2)}) async-start(bf16[16,16,1024]{2,1,0:T(8,128)(2,1)} %copy.57), calls=%async_computation.1 | async-start | bytes 1048576 | tf_op jit(solution)/shard_map/all_to_all | solution.py:207
  76.6 6.1 %copy-start.2 = (bf16[1024,16,64]{2,1,0:T(8,128)(2,1)S(1)}, bf16[1024,16,64]{2,1,0:T(8,128)(2,1)}, u32[]{:S(2)}) copy-start(bf16[1024,16,64]{2,1,0:T(8,128)(2,1)} %gather_fusion) | copy-start | bytes 6291460
  86.4 20.4 %all-to-all-start.2 = ((bf16[16,16,1024]{2,1,0:T(8,128)(2,1)}), bf16[16,16,1024]{2,1,0:T(8,128)(2,1)S(1)}, u32[]{:S(2)}, u32[]{:S(2)}) async-start(bf16[16,16,1024]{2,1,0:T(8,128)(2,1)} %convert_element_type.88), calls=%async_computation.2 | async-start | bytes 1048576 | tf_op jit(solution)/shard_map/all_to_all | solution.py:230

commit v15 on v14

--- a/solution.py
+++ b/solution.py
@@ -58,6 +58,32 @@
         / denominator
     )
     return spike_mix.reshape(samples, latents, head_count * head_size).astype(jnp.bfloat16)
+
+
+def attend_pairs(queries, key_rows, value_rows, live_tokens):
+    samples, latents, pair_count, pair_width = queries.shape
+    halves = (
+        lax.broadcasted_iota(jnp.int32, (2, pair_width), 1) // HEAD_DIM
+        == lax.broadcasted_iota(jnp.int32, (2, pair_width), 0)
+    )
+    masked = jnp.where(halves[None, None, None], queries[:, :, :, None, :], 0).astype(jnp.bfloat16)
+    scores = jnp.einsum(
+        "blqje,btqe->bqjlt", masked, key_rows, preferred_element_type=jnp.float32
+    ) * HEAD_DIM ** (-0.5)
+    scores = jnp.where(live_tokens[:, None, None, None, :], scores, masked_score)
+    row_max = jnp.max(scores, axis=-1, keepdims=True)
+    exponent = jnp.exp(scores - row_max)
+    denominator = jnp.sum(exponent, axis=-1, keepdims=True)
+    mix = jnp.einsum(
+        "bqjlt,btqe->bqjle",
+        exponent.astype(jnp.bfloat16),
+        value_rows,
+        preferred_element_type=jnp.float32,
+    ) / denominator
+    mix = jnp.sum(jnp.where(halves[None, None, :, None, :], mix, 0.0), axis=2)
+    return jnp.transpose(mix, (0, 2, 1, 3)).reshape(samples, latents, pair_count * pair_width).astype(
+        jnp.bfloat16
+    )
 
 
 def attend_block(counts_ref, query_ref, key_ref, value_ref, out_ref):
@@ -150,13 +176,13 @@
     key_table = jnp.einsum(
         "pc,chd->phd",
         panel_normed,
-        kv_weight[:, :model_width].reshape(model_width, head_count, HEAD_DIM),
+        kv_weight[:, :model_width].reshape(model_width, head_count // 2, 2 * HEAD_DIM),
         preferred_element_type=jnp.float32,
     ).astype(jnp.bfloat16)
     value_table = jnp.einsum(
         "pc,chd->phd",
         panel_normed,
-        kv_weight[:, model_width:].reshape(model_width, head_count, HEAD_DIM),
+        kv_weight[:, model_width:].reshape(model_width, head_count // 2, 2 * HEAD_DIM),
         preferred_element_type=jnp.float32,
     ).astype(jnp.bfloat16)
     row_total = local_samples * latents
@@ -221,10 +247,10 @@
     key_rows = key_table[served_index]
     value_rows = value_table[served_index]
     live_tokens = jnp.arange(token_total, dtype=jnp.int32)[None, :] < served[:, token_total:]
-    served_read = attend_heads(
-        served_queries.reshape(owners, latents, head_count, HEAD_DIM),
-        key_rows,
-        value_rows,
+    served_read = attend_pairs(
+        served_queries.reshape(owners, latents, head_count // 2, 2 * HEAD_DIM),
+        key_rows.reshape(owners, token_total, head_count // 2, 2 * HEAD_DIM),
+        value_rows.reshape(owners, token_total, head_count // 2, 2 * HEAD_DIM),
         live_tokens,
     )
     read_spike = lax.all_to_all(

time: 112 us -> 104 us (0.929)
  other arithmetic: 12.7 us -> 7.2 us
  matrix products: 22.9 us -> 19 us
  local copies, waits for them, and re-layouts: 35.2 us -> 37.8 us
    unnamed x12 -> x24, local copies, waits for them, and re-layouts: 1.07 us -> 9.13 us
    unnamed x2 -> x0, matrix products: 6.6 us -> none
    slice x0 -> x1, local copies, waits for them, and re-layouts: none -> 4.68 us  [per_device(): kv_weight[:, :model_width]]
    dot_general x2 -> x4, matrix products: 6.67 us -> 11 us  [the longest x1 3.22 us: per_device(): jnp.einsum('pc,chd->phd', panel_normed, kv_weight[:, :model_width].reshap...]
    gather x1, local copies, waits for them, and re-layouts: 9.98 us -> 7.59 us  [per_device(): value_rows = value_table[served_index]]
    reduce_sum x2, other arithmetic: 2.73 us -> 0.45 us  [normed(): jnp.mean(wide * wide, axis=-1, keepdims=True) + 1e-05]
    convert_element_type x2 -> x0, other arithmetic: 2.28 us -> none  [the longest x1 1.14 us: per_device(): key_table = jnp.einsum('pc,chd->phd', panel_normed, kv_weight[:, :model_w...]
    convert_element_type x1, local copies, waits for them, and re-layouts: 3.85 us -> 1.7 us  [per_device(): key_table = jnp.einsum('pc,chd->phd', panel_normed, kv_weight[:, :model_w...]
  transfers between devices with their start and end apart: 3 -> 3, of which waited for: 2 -> 1; matrix products, arithmetic and copies ran while one was open for 41% -> 40% of each run, Pallas kernels for 0% -> 0%
where the time goes in v15:
time: 104 us; the launch traced here: 103 us
  local copies, waits for them, and re-layouts  37.8 us (36%)
  starting transfers between devices  19.9 us (19%)
  matrix products  19 us (18%)
  waiting for transfers between devices  14.4 us (14%)
  other arithmetic  7.2 us (7%)
  Pallas kernels  4.13 us (4%)
    all_to_all x1, waiting for transfers between devices, per_device(): lax.all_to_all(served_read.reshape(owners, latents, model_width), 'smp',...  14.4 us
    unnamed x24, local copies, waits for them, and re-layouts  9.13 us
    gather x1, local copies, waits for them, and re-layouts, per_device(): key_rows = key_table[served_index]  8.88 us
    gather x1, local copies, waits for them, and re-layouts, per_device(): value_rows = value_table[served_index]  7.59 us
    all_to_all x1, starting transfers between devices, per_device(): lax.all_to_all(jnp.concatenate([jnp.broadcast_to(memory_pair[None], (owne...  7.39 us
    all_to_all x1, starting transfers between devices, per_device(): lax.all_to_all(jnp.einsum('ob,bld->old', (sample_pick[:, None] == jnp.ara...  6.53 us
    all_to_all x1, starting transfers between devices, per_device(): lax.all_to_all(served_read.reshape(owners, latents, model_width), 'smp',...  5.95 us
    slice x1, local copies, waits for them, and re-layouts, per_device(): kv_weight[:, :model_width]  4.68 us
  transfers between devices with their start and end apart: 3, of which 1 were waited for; matrix products, arithmetic and copies ran while one was open for 40% of the time, Pallas kernels for 0%

profile of v15, /device:TPU:0, one launch (start us, length us, event | category | flops | bytes accessed | tf_op | source)
XLA Modules:
  0.0 102.8 jit_solution(9400080677937521667)
XLA Ops:
  0.0 0.0 copy-start
  0.0 1.0 select_reduce_fusion.5
  1.0 0.9 select_reduce_fusion.2
  1.9 0.1 copy.44
  2.0 0.9 add_select_fusion.2
  2.9 0.1 select_reduce_fusion.1
  3.0 0.1 fusion.37
  3.1 0.1 fusion.36
  3.2 0.8 pad_maximum_fusion.1
  4.0 0.1 broadcast_in_dim.133
  4.1 1.1 %pad_maximum_fusion = bf16[16,16,2176]{2,1,0:T(8,128)(2,1)} fusion(bf16[16,16,128]{2,1,0:T(8,128)(2,1)S(1)} %bitcast.84, bf16[16,16,2048]{2,1,0:T(8,128)(2,1)S(1)} %broadcast_in_dim.133), kind=kLoop, calls=%fused_computation.30 | loop fusion | flops 2228224 | bytes 2228224 | tf_op jit(solution)/shard_map/concatenate | solution.py:201
  5.2 7.4 %all-to-all-start = ((bf16[16,16,2176]{2,1,0:T(8,128)(2,1)}), bf16[16,16,2176]{2,1,0:T(8,128)(2,1)S(1)}, u32[]{:S(2)}, u32[]{:S(2)}) async-start(bf16[16,16,2176]{2,1,0:T(8,128)(2,1)} %pad_maximum_fusion), calls=%async_computation | async-start | bytes 2228224 | tf_op jit(solution)/shard_map/all_to_all | solution.py:200
  12.6 0.0 copy-start.6
  12.6 4.7 %fusion.48 = (bf16[1024,1024]{1,0:T(8,128)(2,1)}, bf16[1024,1024]{1,0:T(8,128)(2,1)}) fusion(bf16[1024,2048]{1,0:T(8,128)(2,1)} %param.25), kind=kLoop, calls=%fused_computation.105 | loop fusion | bytes 8388608 | tf_op jit(solution)/shard_map/slice | solution.py:179
  17.3 0.0 copy-done.6
  17.3 0.3 fusion
  17.6 4.0 %copy.66 = bf16[1024,1024]{0,1:T(8,128)(2,1)} copy(bf16[1024,1024]{1,0:T(8,128)(2,1)} %get-tuple-element.9) | data formatting | bytes 4194304
  21.6 3.2 %convolution_convert_fusion = bf16[512,8,128]{2,0,1:T(8,128)(2,1)S(1)} fusion(bf16[1024,8,128]{0,2,1:T(8,128)(2,1)} %bitcast.81, bf16[1,512,1024]{2,1,0:T(8,128)(2,1)} %param.20, f32[512]{0:T(512)S(1)} %add_rsqrt_fusion.1), kind=kOutput, calls=%fused_computation.21 | convolution fusion | flops 1075838976 | bytes 4196352 | tf_op jit(solution)/shard_map/pc,chd->phd/dot_general | solution.py:182
  24.8 0.0 copy-start.3
  24.8 1.7 %copy.54 = bf16[512,8,128]{2,1,0:T(8,128)(2,1)} copy(bf16[512,8,128]{2,0,1:T(8,128)(2,1)S(1)} %convolution_convert_fusion) | data formatting | bytes 2097152 | tf_op jit(solution)/shard_map/convert_element_type | solution.py:187
  26.5 0.0 copy-done.3
  26.5 0.2 multiply_reduce_fusion
  26.6 0.1 rsqrt.28
  26.7 4.0 %copy.65 = bf16[1024,1024]{0,1:T(8,128)(2,1)} copy(bf16[1024,1024]{1,0:T(8,128)(2,1)} %get-tuple-element.8) | data formatting | bytes 4194304
  30.7 3.2 %convolution_convert_fusion.1 = bf16[512,8,128]{2,0,1:T(8,128)(2,1)S(1)} fusion(bf16[1024,8,128]{0,2,1:T(8,128)(2,1)} %bitcast.80, bf16[1,512,1024]{2,1,0:T(8,128)(2,1)} %param.20, f32[512]{0:T(512)S(1)} %add_rsqrt_fusion.1), kind=kOutput, calls=%fused_computation.22 | convolution fusion | flops 1075838976 | bytes 4196352 | tf_op jit(solution)/shard_map/pc,chd->phd/dot_general | solution.py:176
  33.9 0.0 copy-start.4
  33.9 0.0 copy-start.7
  33.9 1.7 %copy.47 = bf16[512,8,128]{2,1,0:T(8,128)(2,1)} copy(bf16[512,8,128]{2,0,1:T(8,128)(2,1)S(1)} %convolution_convert_fusion.1) | data formatting | bytes 2097152 | tf_op jit(solution)/shard_map/convert_element_type | solution.py:181
  35.7 0.0 copy-done.4
  35.7 0.2 fusion.18
  35.8 0.0 copy-done.7
  35.9 1.5 %fusion.13.query_ref = bf16[1,256,1024]{2,1,0:T(8,128)(2,1)} fusion(bf16[256,1024]{1,0:T(8,128)(2,1)S(1)} %fusion.18, bf16[1024,1024]{1,0:T(8,128)(2,1)S(1)} %copy-done.7), kind=kOutput, calls=%fused_computation.29 | convolution fusion | flops 537133056 | bytes 3145728 | tf_op jit(solution)/shard_map/dot_general | solution.py:190
  37.4 0.0 all-to-all-done
  37.4 0.0 copy-start.1
  37.4 0.9 copy-done.1
  38.4 4.1 %shard_map.136 = bf16[1,256,1024]{2,1,0:T(8,128)(2,1)} custom-call(s32[1]{0:T(128)} %constant.85.clone.1.counts_ref, bf16[1,256,1024]{2,1,0:T(8,128)(2,1)} %fusion.13.query_ref, bf16[1,256,2176]{2,1,0:T(8,128)(2,1)} %bitcast.75, bf16[1,256,2176]{2,1,0:T(8,128)(2,1)} %bitcast.76), custom_call_target="tpu_custom_call" | custom-call | tf_op jit(solution)/shard_map/pallas_call | solution.py:122
  42.5 0.0 copy-done
  42.5 2.2 %fusion.14 = (f32[256]{0:T(256)S(1)}, bf16[256,1024]{1,0:T(8,128)(2,1)S(1)}) fusion(bf16[1024,1024]{1,0:T(8,128)(2,1)S(1)} %copy-done, bf16[1,256,1024]{2,1,0:T(8,128)(2,1)} %shard_map.136, bf16[256,1024]{1,0:T(8,128)(2,1)} %bitcast.77), kind=kOutput, calls=%fused_computation.31 | convolution fusion | flops 538443520 | bytes 3671040 | tf_op jit(solution)/shard_map/dot_general | solution.py:227
  44.7 0.0 copy-done.8
  44.7 0.8 convolution_convert_fusion.3
  45.5 0.0 copy-start.2
  45.5 0.5 convolution_convert_fusion.2
  45.9 0.0 copy-done.9
  46.0 1.1 %copy.49 = bf16[16,16,1024]{2,1,0:T(8,128)(2,1)} copy(bf16[16,16,1024]{2,0,1:T(8,128)(2,1)S(1)} %convolution_convert_fusion.2) | data formatting | bytes 1048576 | tf_op jit(solution)/shard_map/convert_element_type | solution.py:241
  47.0 6.5 %all-to-all-start.1 = ((bf16[16,16,1024]{2,1,0:T(8,128)(2,1)}), bf16[16,16,1024]{2,1,0:T(8,128)(2,1)}, u32[]{:S(2)}, u32[]{:S(2)}) async-start(bf16[16,16,1024]{2,1,0:T(8,128)(2,1)} %copy.49), calls=%async_computation.1 | async-start | bytes 1048576 | tf_op jit(solution)/shard_map/all_to_all | solution.py:233
  53.6 0.1 slice_add_fusion
  53.7 0.1 reshape.269
  53.7 0.0 copy-done.2
  53.7 7.6 %gather_fusion.1 = bf16[1024,8,128]{2,1,0:T(8,128)(2,1)} fusion(bf16[512,8,128]{2,1,0:T(8,128)(2,1)S(1)} %copy-done.2, s32[1024]{0:T(1024)S(1)} %broadcast_clamp_fusion), kind=kCustom, calls=%fused_computation.1 | custom fusion | bytes 4198400 | tf_op jit(solution)/shard_map/gather | solution.py:248
  61.3 8.9 %gather_fusion = bf16[1024,8,128]{2,1,0:T(8,128)(2,1)} fusion(bf16[512,8,128]{2,1,0:T(8,128)(2,1)} %copy.47, s32[1024]{0:T(1024)S(1)} %broadcast_clamp_fusion), kind=kCustom, calls=%fused_computation | custom fusion | bytes 4198400 | tf_op jit(solution)/shard_map/gather | solution.py:247
  70.2 0.2 slice_reduce_fusion
  70.4 0.1 iota_compare_fusion.2
  70.5 0.0 all-to-all-done.1
  70.5 1.1 %copy_bitcast_fusion.1 = bf16[16,16,8,128]{3,1,2,0:T(8,128)(2,1)S(1)} fusion(bf16[16,16,1024]{2,1,0:T(8,128)(2,1)} %all-to-all-done.1), kind=kLoop, calls=%fused_computation.44 | loop fusion | bytes 1048576 | tf_op jit(solution)/shard_map/jit(_where)/broadcast_in_dim | solution.py:69
  71.6 3.0 %bitcast_reduce_fusion = (f32[16,8,2,16]{3,2,1,0:T(2,128)S(1)}, f32[16,8,64,16,2]{2,3,4,1,0:T(8,128)S(1)}) fusion(pred[16,64]{1,0:T(8,128)(4,1)S(1)} %iota_compare_fusion.2, pred[2,128]{1,0:T(4,128)(4,1)S(1)} %iota_compare_fusion.6, bf16[16,16,8,128]{3,1,2,0:T(8,128)(2,1)S(1)} %copy_bitcast_fusion.1, bf16[16,64,8,128,1]{3,2,1,0,4:T(8,128)(2,1)} %bitcast.79), kind=kOutput, calls=%fused_computation.10 | convolution fusion | flops 68415488 | bytes 3687680 | tf_op jit(solution)/shard_map/blqje,btqe->bqjlt/dot_general | solution.py:70
  74.6 0.0 copy-start.5
  74.6 1.4 %fusion.7 = f32[16,8,2,16]{3,2,1,0:T(2,128)S(1)} fusion(f32[16,8,64,16,2]{2,3,4,1,0:T(8,128)S(1)} %get-tuple-element.15, f32[16,8,2,16]{3,2,1,0:T(2,128)S(1)} %get-tuple-element.14, pred[16,64]{1,0:T(8,128)(4,1)S(1)} %iota_compare_fusion.2), kind=kLoop, calls=%fused_computation.16 | loop fusion | flops 1044480 | bytes 1082368 | tf_op jit(solution)/shard_map/reduce_sum | solution.py:76
  76.0 0.2 copy-done.5
  76.2 1.6 %select_reduce_fusion = bf16[16,8,16,128]{3,2,1,0:T(8,128)(2,1)S(1)} fusion(bf16[16,64,8,128,1]{3,2,1,0,4:T(8,128)(2,1)S(1)} %bitcast.78, f32[16,8,64,16,2]{2,3,4,1,0:T(8,128)S(1)} %get-tuple-element.15, f32[16,8,2,16]{3,2,1,0:T(2,128)S(1)} %fusion.7, f32[16,8,2,16]{3,2,1,0:T(2,128)S(1)} %get-tuple-element.14, pred[16,64]{1,0:T(8,128)(4,1)S(1)} %iota_compare_fusion.2, ...), kind=kOutput, calls=%fused_computation.14 | convolution fusion | flops 69468160 | bytes 3704064 | tf_op jit(solution)/shard_map/bqjlt,btqe->bqjle/dot_general | solution.py:77
  77.7 0.9 copy_bitcast_fusion
  78.6 5.9 %all-to-all-start.2 = ((bf16[16,16,1024]{2,1,0:T(8,128)(2,1)}), bf16[16,16,1024]{2,1,0:T(8,128)(2,1)S(1)}, u32[]{:S(2)}, u32[]{:S(2)}) async-start(bf16[16,16,1024]{2,1,0:T(8,128)(2,1)} %copy_bitcast_fusion), calls=%async_computation.2 | async-start | bytes 1048576 | tf_op jit(solution)/shard_map/all_to_all | solution.py:256
  84.6 14.4 %all-to-all-done.2 = bf16[16,16,1024]{2,1,0:T(8,128)(2,1)S(1)} async-done(((bf16[16,16,1024]{2,1,0:T(8,128)(2,1)}), bf16[16,16,1024]{2,1,0:T(8,128)(2,1)S(1)}, u32[]{:S(2)}, u32[]{:S(2)}) %all-to-all-start.2) | async-done | bytes 524320 | tf_op jit(solution)/shard_map/all_to_all | solution.py:256
  99.0 0.6 gather_fusion.2
  99.6 3.2 %fusion.11 = bf16[256,1024]{1,0:T(8,128)(2,1)} fusion(bf16[256,1024]{1,0:T(8,128)(2,1)S(1)} %bitcast.83, bf16[1024,1024]{1,0:T(8,128)(2,1)} %param.27, bf16[256,1024]{1,0:T(8,128)(2,1)} %copy-done.9), kind=kOutput, calls=%fused_computation.24 | convolution fusion | flops 537657344 | bytes 3670016 | tf_op jit(solution)/shard_map/dot_general | solution.py:263
  (19 shorter events, 0.1 us)
Async XLA Ops:
  0.0 42.5 %copy-start = (bf16[1024,1024]{1,0:T(8,128)(2,1)S(1)}, bf16[1024,1024]{1,0:T(8,128)(2,1)}, u32[]{:S(2)}) copy-start(bf16[1024,1024]{1,0:T(8,128)(2,1)} %param.24) | copy-start | bytes 6291460
  5.2 32.1 %all-to-all-start = ((bf16[16,16,2176]{2,1,0:T(8,128)(2,1)}), bf16[16,16,2176]{2,1,0:T(8,128)(2,1)S(1)}, u32[]{:S(2)}, u32[]{:S(2)}) async-start(bf16[16,16,2176]{2,1,0:T(8,128)(2,1)} %pad_maximum_fusion), calls=%async_computation | async-start | bytes 2228224 | tf_op jit(solution)/shard_map/all_to_all | solution.py:200
  12.6 4.7 %copy-start.6 = (bf16[1,512,1024]{2,1,0:T(8,128)(2,1)S(1)}, bf16[1,512,1024]{2,1,0:T(8,128)(2,1)}, u32[]{:S(2)}) copy-start(bf16[1,512,1024]{2,1,0:T(8,128)(2,1)} %param.20) | copy-start | bytes 3145732
  24.8 1.7 %copy-start.3 = (bf16[16,16,1024]{2,1,0:T(8,128)(2,1)S(1)}, bf16[16,16,1024]{2,1,0:T(8,128)(2,1)}, u32[]{:S(2)}) copy-start(bf16[16,16,1024]{2,1,0:T(8,128)(2,1)} %param.14) | copy-start | bytes 1572868
  33.9 1.7 %copy-start.4 = (bf16[16,16,1024]{2,1,0:T(8,128)(2,1)S(1)}, bf16[16,16,1024]{2,1,0:T(8,128)(2,1)}, u32[]{:S(2)}) copy-start(bf16[16,16,1024]{2,1,0:T(8,128)(2,1)} %param.14) | copy-start | bytes 1572868
  33.9 1.9 %copy-start.7 = (bf16[1024,1024]{1,0:T(8,128)(2,1)S(1)}, bf16[1024,1024]{1,0:T(8,128)(2,1)}, u32[]{:S(2)}) copy-start(bf16[1024,1024]{1,0:T(8,128)(2,1)} %param.23) | copy-start | bytes 6291460
  37.4 1.0 copy-start.1
  42.5 2.2 %copy-start.8 = (bf16[1024,1024]{1,0:T(8,128)(2,1)S(1)}, bf16[1024,1024]{1,0:T(8,128)(2,1)}, u32[]{:S(2)}) copy-start(bf16[1024,1024]{1,0:T(8,128)(2,1)} %param.26) | copy-start | bytes 6291460
  44.7 1.3 %copy-start.9 = (bf16[256,1024]{1,0:T(8,128)(2,1)}, bf16[256,1024]{1,0:T(8,128)(2,1)S(1)}, u32[]{:S(2)}) copy-start(bf16[256,1024]{1,0:T(8,128)(2,1)S(1)} %get-tuple-element.13) | copy-start | bytes 1572868
  45.5 8.3 %copy-start.2 = (bf16[512,8,128]{2,1,0:T(8,128)(2,1)S(1)}, bf16[512,8,128]{2,1,0:T(8,128)(2,1)}, u32[]{:S(2)}) copy-start(bf16[512,8,128]{2,1,0:T(8,128)(2,1)} %copy.54) | copy-start | bytes 3145732
  47.0 23.4 %all-to-all-start.1 = ((bf16[16,16,1024]{2,1,0:T(8,128)(2,1)}), bf16[16,16,1024]{2,1,0:T(8,128)(2,1)}, u32[]{:S(2)}, u32[]{:S(2)}) async-start(bf16[16,16,1024]{2,1,0:T(8,128)(2,1)} %copy.49), calls=%async_computation.1 | async-start | bytes 1048576 | tf_op jit(solution)/shard_map/all_to_all | solution.py:233
  74.6 1.6 %copy-start.5 = (bf16[1024,8,128]{2,1,0:T(8,128)(2,1)S(1)}, bf16[1024,8,128]{2,1,0:T(8,128)(2,1)}, u32[]{:S(2)}) copy-start(bf16[1024,8,128]{2,1,0:T(8,128)(2,1)} %gather_fusion.1) | copy-start | bytes 6291460
  78.6 20.4 %all-to-all-start.2 = ((bf16[16,16,1024]{2,1,0:T(8,128)(2,1)}), bf16[16,16,1024]{2,1,0:T(8,128)(2,1)S(1)}, u32[]{:S(2)}, u32[]{:S(2)}) async-start(bf16[16,16,1024]{2,1,0:T(8,128)(2,1)} %copy_bitcast_fusion), calls=%async_computation.2 | async-start | bytes 1048576 | tf_op jit(solution)/shard_map/all_to_all | solution.py:256

commit v16 on v15

--- a/solution.py
+++ b/solution.py
@@ -173,18 +173,12 @@
     )
     panel_table = panels.reshape(sess_dev * unit_total, model_width)
     panel_normed = normed(panel_table)
-    key_table = jnp.einsum(
-        "pc,chd->phd",
-        panel_normed,
-        kv_weight[:, :model_width].reshape(model_width, head_count // 2, 2 * HEAD_DIM),
-        preferred_element_type=jnp.float32,
-    ).astype(jnp.bfloat16)
-    value_table = jnp.einsum(
-        "pc,chd->phd",
-        panel_normed,
-        kv_weight[:, model_width:].reshape(model_width, head_count // 2, 2 * HEAD_DIM),
-        preferred_element_type=jnp.float32,
-    ).astype(jnp.bfloat16)
+    kv_flat = jnp.dot(panel_normed, kv_weight, preferred_element_type=jnp.float32).astype(
+        jnp.bfloat16
+    )
+    panel_total = kv_flat.shape[0]
+    key_table = kv_flat[:, :model_width].reshape(panel_total, head_count // 2, 2 * HEAD_DIM)
+    value_table = kv_flat[:, model_width:].reshape(panel_total, head_count // 2, 2 * HEAD_DIM)
     row_total = local_samples * latents
     flat_state = state.reshape(row_total, model_width)
     queries = jnp.dot(normed(flat_state), q1_weight, preferred_element_type=jnp.float32).astype(

time: 104 us -> 105 us (level)
  local copies, waits for them, and re-layouts: 37.8 us -> 26 us
  waiting for transfers between devices: 14.4 us -> 25.7 us
  other arithmetic: 7.2 us -> 9.45 us
  matrix products: 19 us -> 17.5 us
    all_to_all x1, waiting for transfers between devices: 0.01 us -> 11.3 us  [per_device(): lax.all_to_all(jnp.concatenate([jnp.broadcast_to(memory_pair[None], (owne...]
    slice x1 -> x0, local copies, waits for them, and re-layouts: 4.68 us -> none  [per_device(): kv_weight[:, :model_width]]
    unnamed x24 -> x21, local copies, waits for them, and re-layouts: 9.13 us -> 4.48 us
    convert_element_type x2 -> x0, local copies, waits for them, and re-layouts: 3.35 us -> none  [the longest x1 1.7 us: per_device(): key_table = jnp.einsum('pc,chd->phd', panel_normed, kv_weight[:, :model_w...]
    reduce_sum x2, other arithmetic: 0.45 us -> 2.73 us  [normed(): jnp.mean(wide * wide, axis=-1, keepdims=True) + 1e-05]
    dot_general x2 -> x1, matrix products: 6.44 us -> 4.92 us  [per_device(): jnp.dot(panel_normed, kv_weight, preferred_element_type=jnp.float32)]
    gather x1, local copies, waits for them, and re-layouts: 7.59 us -> 8.85 us  [per_device(): value_rows = value_table[served_index]]
    gather x1, local copies, waits for them, and re-layouts: 8.88 us -> 7.62 us  [per_device(): key_rows = key_table[served_index]]
  transfers between devices with their start and end apart: 3 -> 3, of which waited for: 1 -> 2; matrix products, arithmetic and copies ran while one was open for 40% -> 29% of each run, Pallas kernels for 0% -> 0%
where the time goes in v16:
time: 105 us; the launch traced here: 104 us
  local copies, waits for them, and re-layouts  26 us (25%)
  waiting for transfers between devices  25.7 us (24%)
  starting transfers between devices  20.6 us (20%)
  matrix products  17.5 us (17%)
  other arithmetic  9.45 us (9%)
  Pallas kernels  4.12 us (4%)
    all_to_all x1, waiting for transfers between devices, per_device(): lax.all_to_all(served_read.reshape(owners, latents, model_width), 'smp',...  14.4 us
    all_to_all x1, waiting for transfers between devices, per_device(): lax.all_to_all(jnp.concatenate([jnp.broadcast_to(memory_pair[None], (owne...  11.3 us
    gather x1, local copies, waits for them, and re-layouts, per_device(): value_rows = value_table[served_index]  8.85 us
    gather x1, local copies, waits for them, and re-layouts, per_device(): key_rows = key_table[served_index]  7.62 us
    all_to_all x1, starting transfers between devices, per_device(): lax.all_to_all(jnp.concatenate([jnp.broadcast_to(memory_pair[None], (owne...  7.39 us
    all_to_all x1, starting transfers between devices, per_device(): lax.all_to_all(jnp.einsum('ob,bld->old', (sample_pick[:, None] == jnp.ara...  7.24 us
    all_to_all x1, starting transfers between devices, per_device(): lax.all_to_all(served_read.reshape(owners, latents, model_width), 'smp',...  5.96 us
    dot_general x1, matrix products, per_device(): jnp.dot(panel_normed, kv_weight, preferred_element_type=jnp.float32)  4.92 us
  transfers between devices with their start and end apart: 3, of which 2 were waited for; matrix products, arithmetic and copies ran while one was open for 29% of the time, Pallas kernels for 0%

profile of v16, /device:TPU:0, one launch (start us, length us, event | category | flops | bytes accessed | tf_op | source)
XLA Modules:
  0.0 103.6 jit_solution(10828183314069974845)
XLA Ops:
  0.0 0.0 copy-start
  0.0 1.0 select_reduce_fusion.5
  1.0 0.9 select_reduce_fusion.2
  1.9 0.1 copy.30
  2.0 0.9 add_select_fusion.2
  2.9 0.1 select_reduce_fusion.1
  3.0 0.1 fusion.37
  3.1 0.1 fusion.36
  3.2 0.8 pad_maximum_fusion.1
  4.0 0.1 broadcast_in_dim.133
  4.1 1.1 %pad_maximum_fusion = bf16[16,16,2176]{2,1,0:T(8,128)(2,1)} fusion(bf16[16,16,128]{2,1,0:T(8,128)(2,1)S(1)} %bitcast.89, bf16[16,16,2048]{2,1,0:T(8,128)(2,1)S(1)} %broadcast_in_dim.133), kind=kLoop, calls=%fused_computation.29 | loop fusion | flops 2228224 | bytes 2228224 | tf_op jit(solution)/shard_map/concatenate | solution.py:195
  5.2 7.4 %all-to-all-start = ((bf16[16,16,2176]{2,1,0:T(8,128)(2,1)}), bf16[16,16,2176]{2,1,0:T(8,128)(2,1)S(1)}, u32[]{:S(2)}, u32[]{:S(2)}) async-start(bf16[16,16,2176]{2,1,0:T(8,128)(2,1)} %pad_maximum_fusion), calls=%async_computation | async-start | bytes 2228224 | tf_op jit(solution)/shard_map/all_to_all | solution.py:194
  12.6 1.2 %multiply_reduce_fusion = f32[16,16]{1,0:T(8,128)S(1)} fusion(bf16[16,16,1024]{2,1,0:T(8,128)(2,1)} %param.14), kind=kLoop, calls=%fused_computation.42 | loop fusion | flops 786176 | bytes 525312 | tf_op jit(solution)/shard_map/reduce_sum | solution.py:16
  13.8 0.1 rsqrt.28
  13.9 1.5 %fusion = f32[512]{0:T(512)S(1)} fusion(bf16[1,512,1024]{2,1,0:T(8,128)(2,1)} %param.20), kind=kLoop, calls=%fused_computation.6 | loop fusion | flops 1572352 | bytes 1050624 | tf_op jit(solution)/shard_map/reduce_sum | solution.py:16
  15.4 4.9 %convolution_convert_fusion = bf16[512,2048]{1,0:T(8,128)(2,1)S(1)} fusion(bf16[1024,2048]{1,0:T(8,128)(2,1)} %param.25, bf16[1,512,1024]{2,1,0:T(8,128)(2,1)} %param.20, f32[512]{0:T(512)S(1)} %add_rsqrt_fusion.1), kind=kOutput, calls=%fused_computation.3 | convolution fusion | flops 2150105088 | bytes 7342080 | tf_op jit(solution)/shard_map/dot_general | solution.py:176
  20.4 0.2 slice_bitcast_fusion.1
  20.6 0.0 copy-start.3
  20.6 1.3 %copy.47 = bf16[64,8,8,128]{3,2,1,0:T(8,128)(2,1)} copy(bf16[64,8,8,128]{3,1,2,0:T(8,128)(2,1)S(1)} %get-tuple-element.8) | data formatting | bytes 2097152
  21.9 0.0 copy-start.5
  21.9 1.3 %copy.48 = bf16[64,8,8,128]{3,2,1,0:T(8,128)(2,1)} copy(bf16[64,8,8,128]{3,1,2,0:T(8,128)(2,1)S(1)} %get-tuple-element.9) | data formatting | bytes 2097152
  23.1 0.0 copy-done.3
  23.2 0.2 fusion.19
  23.3 0.5 copy-done.5
  23.8 1.5 %fusion.13.query_ref = bf16[1,256,1024]{2,1,0:T(8,128)(2,1)} fusion(bf16[256,1024]{1,0:T(8,128)(2,1)S(1)} %fusion.19, bf16[1024,1024]{1,0:T(8,128)(2,1)S(1)} %copy-done.5), kind=kOutput, calls=%fused_computation.28 | convolution fusion | flops 537133056 | bytes 3145728 | tf_op jit(solution)/shard_map/dot_general | solution.py:184
  25.3 11.3 %all-to-all-done = bf16[16,16,2176]{2,1,0:T(8,128)(2,1)S(1)} async-done(((bf16[16,16,2176]{2,1,0:T(8,128)(2,1)}), bf16[16,16,2176]{2,1,0:T(8,128)(2,1)S(1)}, u32[]{:S(2)}, u32[]{:S(2)}) %all-to-all-start) | async-done | bytes 1114144 | tf_op jit(solution)/shard_map/all_to_all | solution.py:194
  36.6 0.0 copy-start.1
  36.6 1.0 copy-done.1
  37.6 4.1 %shard_map.136 = bf16[1,256,1024]{2,1,0:T(8,128)(2,1)} custom-call(s32[1]{0:T(128)} %constant.85.clone.1.counts_ref, bf16[1,256,1024]{2,1,0:T(8,128)(2,1)} %fusion.13.query_ref, bf16[1,256,2176]{2,1,0:T(8,128)(2,1)} %bitcast.80, bf16[1,256,2176]{2,1,0:T(8,128)(2,1)} %bitcast.81), custom_call_target="tpu_custom_call" | custom-call | tf_op jit(solution)/shard_map/pallas_call | solution.py:122
  41.7 0.0 copy-done
  41.7 0.0 copy-start.6
  41.7 2.2 %fusion.14 = (f32[256]{0:T(256)S(1)}, bf16[256,1024]{1,0:T(8,128)(2,1)S(1)}) fusion(bf16[1024,1024]{1,0:T(8,128)(2,1)S(1)} %copy-done, bf16[1,256,1024]{2,1,0:T(8,128)(2,1)} %shard_map.136, bf16[256,1024]{1,0:T(8,128)(2,1)} %bitcast.84), kind=kOutput, calls=%fused_computation.30 | convolution fusion | flops 538443520 | bytes 3671040 | tf_op jit(solution)/shard_map/dot_general | solution.py:221
  43.9 0.0 copy-start.7
  43.9 0.0 copy-done.6
  43.9 0.8 convolution_convert_fusion.2
  44.7 0.0 copy-start.2
  44.7 0.5 convolution_convert_fusion.1
  45.2 0.0 copy-done.7
  45.2 1.1 %copy.32 = bf16[16,16,1024]{2,1,0:T(8,128)(2,1)} copy(bf16[16,16,1024]{2,0,1:T(8,128)(2,1)S(1)} %convolution_convert_fusion.1) | data formatting | bytes 1048576 | tf_op jit(solution)/shard_map/convert_element_type | solution.py:235
  46.3 7.2 %all-to-all-start.1 = ((bf16[16,16,1024]{2,1,0:T(8,128)(2,1)}), bf16[16,16,1024]{2,1,0:T(8,128)(2,1)}, u32[]{:S(2)}, u32[]{:S(2)}) async-start(bf16[16,16,1024]{2,1,0:T(8,128)(2,1)} %copy.32), calls=%async_computation.1 | async-start | bytes 1048576 | tf_op jit(solution)/shard_map/all_to_all | solution.py:227
  53.5 0.8 slice.38
  54.4 0.1 slice_add_fusion
  54.5 0.1 reshape.254
  54.6 0.0 copy-done.2
  54.6 7.6 %gather_fusion = bf16[1024,8,128]{2,1,0:T(8,128)(2,1)} fusion(bf16[512,8,128]{2,1,0:T(8,128)(2,1)S(1)} %bitcast.82, s32[1024]{0:T(1024)S(1)} %broadcast_clamp_fusion), kind=kCustom, calls=%fused_computation | custom fusion | bytes 4198400 | tf_op jit(solution)/shard_map/gather | solution.py:241
  62.2 8.9 %gather_fusion.1 = bf16[1024,8,128]{2,1,0:T(8,128)(2,1)} fusion(bf16[512,8,128]{2,1,0:T(8,128)(2,1)} %bitcast.83, s32[1024]{0:T(1024)S(1)} %broadcast_clamp_fusion), kind=kCustom, calls=%fused_computation.1 | custom fusion | bytes 4198400 | tf_op jit(solution)/shard_map/gather | solution.py:242
  71.0 0.2 slice_reduce_fusion
  71.2 0.1 iota_compare_fusion.2
  71.3 0.0 all-to-all-done.1
  71.3 1.1 %copy_bitcast_fusion.1 = bf16[16,16,8,128]{3,1,2,0:T(8,128)(2,1)S(1)} fusion(bf16[16,16,1024]{2,1,0:T(8,128)(2,1)} %all-to-all-done.1), kind=kLoop, calls=%fused_computation.46 | loop fusion | bytes 1048576 | tf_op jit(solution)/shard_map/jit(_where)/broadcast_in_dim | solution.py:69
  72.5 3.0 %bitcast_reduce_fusion = (f32[16,8,2,16]{3,2,1,0:T(2,128)S(1)}, f32[16,8,64,16,2]{2,3,4,1,0:T(8,128)S(1)}) fusion(pred[16,64]{1,0:T(8,128)(4,1)S(1)} %iota_compare_fusion.2, pred[2,128]{1,0:T(4,128)(4,1)S(1)} %iota_compare_fusion.6, bf16[16,16,8,128]{3,1,2,0:T(8,128)(2,1)S(1)} %copy_bitcast_fusion.1, bf16[16,64,8,128,1]{3,2,1,0,4:T(8,128)(2,1)} %bitcast.86), kind=kOutput, calls=%fused_computation.11 | convolution fusion | flops 68415488 | bytes 3687680 | tf_op jit(solution)/shard_map/blqje,btqe->bqjlt/dot_general | solution.py:70
  75.4 0.0 copy-start.4
  75.4 1.4 %fusion.7 = f32[16,8,2,16]{3,2,1,0:T(2,128)S(1)} fusion(f32[16,8,64,16,2]{2,3,4,1,0:T(8,128)S(1)} %get-tuple-element.15, f32[16,8,2,16]{3,2,1,0:T(2,128)S(1)} %get-tuple-element.14, pred[16,64]{1,0:T(8,128)(4,1)S(1)} %iota_compare_fusion.2), kind=kLoop, calls=%fused_computation.17 | loop fusion | flops 1044480 | bytes 1082368 | tf_op jit(solution)/shard_map/reduce_sum | solution.py:76
  76.8 0.2 copy-done.4
  77.0 1.6 %select_reduce_fusion = bf16[16,8,16,128]{3,2,1,0:T(8,128)(2,1)S(1)} fusion(bf16[16,64,8,128,1]{3,2,1,0,4:T(8,128)(2,1)S(1)} %bitcast.85, f32[16,8,64,16,2]{2,3,4,1,0:T(8,128)S(1)} %get-tuple-element.15, f32[16,8,2,16]{3,2,1,0:T(2,128)S(1)} %fusion.7, f32[16,8,2,16]{3,2,1,0:T(2,128)S(1)} %get-tuple-element.14, pred[16,64]{1,0:T(8,128)(4,1)S(1)} %iota_compare_fusion.2, ...), kind=kOutput, calls=%fused_computation.15 | convolution fusion | flops 69468160 | bytes 3704064 | tf_op jit(solution)/shard_map/bqjlt,btqe->bqjle/dot_general | solution.py:77
  78.6 0.9 copy_bitcast_fusion
  79.4 6.0 %all-to-all-start.2 = ((bf16[16,16,1024]{2,1,0:T(8,128)(2,1)}), bf16[16,16,1024]{2,1,0:T(8,128)(2,1)S(1)}, u32[]{:S(2)}, u32[]{:S(2)}) async-start(bf16[16,16,1024]{2,1,0:T(8,128)(2,1)} %copy_bitcast_fusion), calls=%async_computation.2 | async-start | bytes 1048576 | tf_op jit(solution)/shard_map/all_to_all | solution.py:250
  85.4 14.4 %all-to-all-done.2 = bf16[16,16,1024]{2,1,0:T(8,128)(2,1)S(1)} async-done(((bf16[16,16,1024]{2,1,0:T(8,128)(2,1)}), bf16[16,16,1024]{2,1,0:T(8,128)(2,1)S(1)}, u32[]{:S(2)}, u32[]{:S(2)}) %all-to-all-start.2) | async-done | bytes 524320 | tf_op jit(solution)/shard_map/all_to_all | solution.py:250
  99.9 0.6 gather_fusion.2
  100.5 3.2 %fusion.11 = bf16[256,1024]{1,0:T(8,128)(2,1)} fusion(bf16[256,1024]{1,0:T(8,128)(2,1)S(1)} %bitcast.88, bf16[1024,1024]{1,0:T(8,128)(2,1)} %param.27, bf16[256,1024]{1,0:T(8,128)(2,1)} %copy-done.7), kind=kOutput, calls=%fused_computation.23 | convolution fusion | flops 537657344 | bytes 3670016 | tf_op jit(solution)/shard_map/dot_general | solution.py:257
  (16 shorter events, 0.1 us)
Async XLA Ops:
  0.0 41.7 %copy-start = (bf16[1024,1024]{1,0:T(8,128)(2,1)S(1)}, bf16[1024,1024]{1,0:T(8,128)(2,1)}, u32[]{:S(2)}) copy-start(bf16[1024,1024]{1,0:T(8,128)(2,1)} %param.24) | copy-start | bytes 6291460
  5.2 31.4 %all-to-all-start = ((bf16[16,16,2176]{2,1,0:T(8,128)(2,1)}), bf16[16,16,2176]{2,1,0:T(8,128)(2,1)S(1)}, u32[]{:S(2)}, u32[]{:S(2)}) async-start(bf16[16,16,2176]{2,1,0:T(8,128)(2,1)} %pad_maximum_fusion), calls=%async_computation | async-start | bytes 2228224 | tf_op jit(solution)/shard_map/all_to_all | solution.py:194
  20.6 2.6 %copy-start.3 = (bf16[16,16,1024]{2,1,0:T(8,128)(2,1)S(1)}, bf16[16,16,1024]{2,1,0:T(8,128)(2,1)}, u32[]{:S(2)}) copy-start(bf16[16,16,1024]{2,1,0:T(8,128)(2,1)} %param.14) | copy-start | bytes 1572868
  21.9 2.0 %copy-start.5 = (bf16[1024,1024]{1,0:T(8,128)(2,1)S(1)}, bf16[1024,1024]{1,0:T(8,128)(2,1)}, u32[]{:S(2)}) copy-start(bf16[1024,1024]{1,0:T(8,128)(2,1)} %param.23) | copy-start | bytes 6291460
  36.6 1.0 copy-start.1
  41.7 2.2 %copy-start.6 = (bf16[1024,1024]{1,0:T(8,128)(2,1)S(1)}, bf16[1024,1024]{1,0:T(8,128)(2,1)}, u32[]{:S(2)}) copy-start(bf16[1024,1024]{1,0:T(8,128)(2,1)} %param.26) | copy-start | bytes 6291460
  43.9 1.3 %copy-start.7 = (bf16[256,1024]{1,0:T(8,128)(2,1)}, bf16[256,1024]{1,0:T(8,128)(2,1)S(1)}, u32[]{:S(2)}) copy-start(bf16[256,1024]{1,0:T(8,128)(2,1)S(1)} %get-tuple-element.13) | copy-start | bytes 1572868
  44.7 9.9 %copy-start.2 = (bf16[64,8,8,128]{3,2,1,0:T(8,128)(2,1)S(1)}, bf16[64,8,8,128]{3,2,1,0:T(8,128)(2,1)}, u32[]{:S(2)}) copy-start(bf16[64,8,8,128]{3,2,1,0:T(8,128)(2,1)} %copy.47) | copy-start | bytes 3145732
  46.3 25.0 %all-to-all-start.1 = ((bf16[16,16,1024]{2,1,0:T(8,128)(2,1)}), bf16[16,16,1024]{2,1,0:T(8,128)(2,1)}, u32[]{:S(2)}, u32[]{:S(2)}) async-start(bf16[16,16,1024]{2,1,0:T(8,128)(2,1)} %copy.32), calls=%async_computation.1 | async-start | bytes 1048576 | tf_op jit(solution)/shard_map/all_to_all | solution.py:227
  75.4 1.6 %copy-start.4 = (bf16[1024,8,128]{2,1,0:T(8,128)(2,1)S(1)}, bf16[1024,8,128]{2,1,0:T(8,128)(2,1)}, u32[]{:S(2)}) copy-start(bf16[1024,8,128]{2,1,0:T(8,128)(2,1)} %gather_fusion.1) | copy-start | bytes 6291460
  79.4 20.4 %all-to-all-start.2 = ((bf16[16,16,1024]{2,1,0:T(8,128)(2,1)}), bf16[16,16,1024]{2,1,0:T(8,128)(2,1)S(1)}, u32[]{:S(2)}, u32[]{:S(2)}) async-start(bf16[16,16,1024]{2,1,0:T(8,128)(2,1)} %copy_bitcast_fusion), calls=%async_computation.2 | async-start | bytes 1048576 | tf_op jit(solution)/shard_map/all_to_all | solution.py:250

commit v17 on v16

--- a/solution.py
+++ b/solution.py
@@ -177,8 +177,7 @@
         jnp.bfloat16
     )
     panel_total = kv_flat.shape[0]
-    key_table = kv_flat[:, :model_width].reshape(panel_total, head_count // 2, 2 * HEAD_DIM)
-    value_table = kv_flat[:, model_width:].reshape(panel_total, head_count // 2, 2 * HEAD_DIM)
+    kv_table = kv_flat.reshape(panel_total, head_count, 2 * HEAD_DIM)
     row_total = local_samples * latents
     flat_state = state.reshape(row_total, model_width)
     queries = jnp.dot(normed(flat_state), q1_weight, preferred_element_type=jnp.float32).astype(
@@ -238,8 +237,9 @@
         concat_axis=0,
         tiled=True,
     )
-    key_rows = key_table[served_index]
-    value_rows = value_table[served_index]
+    kv_rows = kv_table[served_index]
+    key_rows = kv_rows[:, :, : head_count // 2]
+    value_rows = kv_rows[:, :, head_count // 2 :]
     live_tokens = jnp.arange(token_total, dtype=jnp.int32)[None, :] < served[:, token_total:]
     served_read = attend_pairs(
         served_queries.reshape(owners, latents, head_count // 2, 2 * HEAD_DIM),

time: 105 us -> 102 us (0.971)
  local copies, waits for them, and re-layouts: 26 us -> 21.8 us
  waiting for transfers between devices: 25.7 us -> 27 us
    gather x2 -> x1, local copies, waits for them, and re-layouts: 16.5 us -> 9.97 us  [per_device(): kv_rows = kv_table[served_index]]
    slice x0 -> x1, local copies, waits for them, and re-layouts: none -> 4.65 us  [per_device(): key_rows = kv_rows[:, :, :head_count // 2]]
    unnamed x21 -> x17, local copies, waits for them, and re-layouts: 4.48 us -> 3.19 us
    all_to_all x1, waiting for transfers between devices: 11.3 us -> 12.5 us  [per_device(): lax.all_to_all(jnp.concatenate([jnp.broadcast_to(memory_pair[None], (owne...]
  transfers between devices with their start and end apart: 3 -> 3, of which waited for: 2 -> 2; matrix products, arithmetic and copies ran while one was open for 29% -> 27% of each run, Pallas kernels for 0% -> 0%
where the time goes in v17:
time: 102 us; the launch traced here: 101 us
  waiting for transfers between devices  27 us (26%)
  local copies, waits for them, and re-layouts  21.8 us (21%)
  starting transfers between devices  20.6 us (20%)
  matrix products  17.6 us (17%)
  other arithmetic  9.45 us (9%)
  Pallas kernels  4.13 us (4%)
    all_to_all x1, waiting for transfers between devices, per_device(): lax.all_to_all(served_read.reshape(owners, latents, model_width), 'smp',...  14.4 us
    all_to_all x1, waiting for transfers between devices, per_device(): lax.all_to_all(jnp.concatenate([jnp.broadcast_to(memory_pair[None], (owne...  12.5 us
    gather x1, local copies, waits for them, and re-layouts, per_device(): kv_rows = kv_table[served_index]  9.97 us
    all_to_all x1, starting transfers between devices, per_device(): lax.all_to_all(jnp.concatenate([jnp.broadcast_to(memory_pair[None], (owne...  7.39 us
    all_to_all x1, starting transfers between devices, per_device(): lax.all_to_all(jnp.einsum('ob,bld->old', (sample_pick[:, None] == jnp.ara...  7.19 us
    all_to_all x1, starting transfers between devices, per_device(): lax.all_to_all(served_read.reshape(owners, latents, model_width), 'smp',...  6.01 us
    dot_general x1, matrix products, per_device(): jnp.dot(panel_normed, kv_weight, preferred_element_type=jnp.float32)  4.93 us
    slice x1, local copies, waits for them, and re-layouts, per_device(): key_rows = kv_rows[:, :, :head_count // 2]  4.65 us
  transfers between devices with their start and end apart: 3, of which 2 were waited for; matrix products, arithmetic and copies ran while one was open for 27% of the time, Pallas kernels for 0%

profile of v17, /device:TPU:0, one launch (start us, length us, event | category | flops | bytes accessed | tf_op | source)
XLA Modules:
  0.0 100.7 jit_solution(14661938109617655047)
XLA Ops:
  0.0 0.0 copy-start
  0.0 1.0 select_reduce_fusion.5
  1.0 0.9 select_reduce_fusion.2
  1.9 0.1 copy.30
  2.0 0.9 add_select_fusion.2
  2.9 0.1 select_reduce_fusion.1
  3.0 0.1 fusion.34
  3.1 0.1 fusion.33
  3.2 0.8 pad_maximum_fusion.1
  4.0 0.1 broadcast_in_dim.132
  4.1 1.1 %pad_maximum_fusion = bf16[16,16,2176]{2,1,0:T(8,128)(2,1)} fusion(bf16[16,16,128]{2,1,0:T(8,128)(2,1)S(1)} %bitcast.93, bf16[16,16,2048]{2,1,0:T(8,128)(2,1)S(1)} %broadcast_in_dim.132), kind=kLoop, calls=%fused_computation.29 | loop fusion | flops 2228224 | bytes 2228224 | tf_op jit(solution)/shard_map/concatenate | solution.py:194
  5.2 7.4 %all-to-all-start = ((bf16[16,16,2176]{2,1,0:T(8,128)(2,1)}), bf16[16,16,2176]{2,1,0:T(8,128)(2,1)S(1)}, u32[]{:S(2)}, u32[]{:S(2)}) async-start(bf16[16,16,2176]{2,1,0:T(8,128)(2,1)} %pad_maximum_fusion), calls=%async_computation | async-start | bytes 2228224 | tf_op jit(solution)/shard_map/all_to_all | solution.py:193
  12.6 1.2 %multiply_reduce_fusion = f32[16,16]{1,0:T(8,128)S(1)} fusion(bf16[16,16,1024]{2,1,0:T(8,128)(2,1)} %param.14), kind=kLoop, calls=%fused_computation.40 | loop fusion | flops 786176 | bytes 525312 | tf_op jit(solution)/shard_map/reduce_sum | solution.py:16
  13.8 0.1 rsqrt.28
  13.9 1.5 %fusion = f32[512]{0:T(512)S(1)} fusion(bf16[1,512,1024]{2,1,0:T(8,128)(2,1)} %param.20), kind=kLoop, calls=%fused_computation.5 | loop fusion | flops 1572352 | bytes 1050624 | tf_op jit(solution)/shard_map/reduce_sum | solution.py:16
  15.4 4.9 %fusion.5 = bf16[64,8,16,128]{3,1,2,0:T(8,128)(2,1)S(1)} fusion(bf16[1024,2048]{1,0:T(8,128)(2,1)} %param.25, bf16[1,512,1024]{2,1,0:T(8,128)(2,1)} %param.20, f32[512]{0:T(512)S(1)} %add_rsqrt_fusion.1), kind=kOutput, calls=%fused_computation.16 | convolution fusion | flops 2150105088 | bytes 7342080 | tf_op jit(solution)/shard_map/dot_general | solution.py:176
  20.4 0.0 copy-start.2
  20.4 0.0 copy-start.4
  20.4 2.0 %copy.45 = bf16[64,8,16,128]{3,2,1,0:T(8,128)(2,1)} copy(bf16[64,8,16,128]{3,1,2,0:T(8,128)(2,1)S(1)} %fusion.5) | data formatting | bytes 4194304
  22.4 0.0 copy-done.2
  22.4 0.2 fusion.16
  22.6 0.0 copy-done.4
  22.6 1.5 %fusion.10.query_ref = bf16[1,256,1024]{2,1,0:T(8,128)(2,1)} fusion(bf16[256,1024]{1,0:T(8,128)(2,1)S(1)} %fusion.16, bf16[1024,1024]{1,0:T(8,128)(2,1)S(1)} %copy-done.4), kind=kOutput, calls=%fused_computation.28 | convolution fusion | flops 537133056 | bytes 3145728 | tf_op jit(solution)/shard_map/dot_general | solution.py:183
  24.1 12.5 %all-to-all-done = bf16[16,16,2176]{2,1,0:T(8,128)(2,1)S(1)} async-done(((bf16[16,16,2176]{2,1,0:T(8,128)(2,1)}), bf16[16,16,2176]{2,1,0:T(8,128)(2,1)S(1)}, u32[]{:S(2)}, u32[]{:S(2)}) %all-to-all-start) | async-done | bytes 1114144 | tf_op jit(solution)/shard_map/all_to_all | solution.py:193
  36.6 0.0 copy-start.1
  36.6 1.0 copy-done.1
  37.6 4.1 %shard_map.136 = bf16[1,256,1024]{2,1,0:T(8,128)(2,1)} custom-call(s32[1]{0:T(128)} %constant.85.clone.1.counts_ref, bf16[1,256,1024]{2,1,0:T(8,128)(2,1)} %fusion.10.query_ref, bf16[1,256,2176]{2,1,0:T(8,128)(2,1)} %bitcast.88, bf16[1,256,2176]{2,1,0:T(8,128)(2,1)} %bitcast.89), custom_call_target="tpu_custom_call" | custom-call | tf_op jit(solution)/shard_map/pallas_call | solution.py:122
  41.7 0.0 copy-done
  41.7 0.0 copy-start.5
  41.7 2.2 %fusion.11 = (f32[256]{0:T(256)S(1)}, bf16[256,1024]{1,0:T(8,128)(2,1)S(1)}) fusion(bf16[1024,1024]{1,0:T(8,128)(2,1)S(1)} %copy-done, bf16[1,256,1024]{2,1,0:T(8,128)(2,1)} %shard_map.136, bf16[256,1024]{1,0:T(8,128)(2,1)} %bitcast.90), kind=kOutput, calls=%fused_computation.30 | convolution fusion | flops 538443520 | bytes 3671040 | tf_op jit(solution)/shard_map/dot_general | solution.py:220
  43.9 0.0 copy-start.6
  43.9 0.0 copy-done.5
  43.9 0.8 convolution_convert_fusion.2
  44.7 0.5 convolution_convert_fusion.1
  45.2 0.0 copy-done.6
  45.2 1.1 %copy.33 = bf16[16,16,1024]{2,1,0:T(8,128)(2,1)} copy(bf16[16,16,1024]{2,0,1:T(8,128)(2,1)S(1)} %convolution_convert_fusion.1) | data formatting | bytes 1048576 | tf_op jit(solution)/shard_map/convert_element_type | solution.py:234
  46.3 7.2 %all-to-all-start.1 = ((bf16[16,16,1024]{2,1,0:T(8,128)(2,1)}), bf16[16,16,1024]{2,1,0:T(8,128)(2,1)S(1)}, u32[]{:S(2)}, u32[]{:S(2)}) async-start(bf16[16,16,1024]{2,1,0:T(8,128)(2,1)} %copy.33), calls=%async_computation.1 | async-start | bytes 1048576 | tf_op jit(solution)/shard_map/all_to_all | solution.py:226
  53.5 0.8 slice.36
  54.4 0.1 slice_add_fusion
  54.4 0.1 reshape.250
  54.5 10.0 %gather_fusion = bf16[1024,16,128]{2,1,0:T(8,128)(2,1)} fusion(bf16[512,16,128]{2,1,0:T(8,128)(2,1)} %bitcast.86, s32[1024]{0:T(1024)S(1)} %broadcast_clamp_fusion), kind=kCustom, calls=%fused_computation | custom fusion | bytes 8392704 | tf_op jit(solution)/shard_map/gather | solution.py:240
  64.5 0.2 slice_reduce_fusion
  64.7 0.1 iota_compare_fusion.2
  64.7 4.7 %fusion.45 = (bf16[16,64,8,128]{3,2,1,0:T(8,128)(2,1)}, bf16[16,64,8,128]{3,2,1,0:T(8,128)(2,1)}) fusion(bf16[16,64,16,128]{3,2,1,0:T(8,128)(2,1)} %bitcast.87), kind=kLoop, calls=%fused_computation.105 | loop fusion | bytes 8388608 | tf_op jit(solution)/shard_map/slice | solution.py:241
  69.4 0.0 all-to-all-done.1
  69.4 0.1 copy_bitcast_fusion.7
  69.5 3.0 %bitcast_reduce_fusion = (f32[16,8,2,16]{3,2,1,0:T(2,128)S(1)}, f32[16,8,64,16,2]{2,3,4,1,0:T(8,128)S(1)}) fusion(pred[16,64]{1,0:T(8,128)(4,1)S(1)} %iota_compare_fusion.2, pred[2,128]{1,0:T(4,128)(4,1)S(1)} %iota_compare_fusion.6, bf16[16,16,8,128]{3,1,2,0:T(8,128)(2,1)S(1)} %copy_bitcast_fusion.7, bf16[16,64,8,128]{3,2,1,0:T(8,128)(2,1)} %get-tuple-element.8), kind=kOutput, calls=%fused_computation.12 | convolution fusion | flops 68415488 | bytes 3687680 | tf_op jit(solution)/shard_map/blqje,btqe->bqjlt/dot_general | solution.py:70
  72.5 0.0 copy-start.3
  72.5 1.4 %fusion.6 = f32[16,8,2,16]{3,2,1,0:T(2,128)S(1)} fusion(f32[16,8,64,16,2]{2,3,4,1,0:T(8,128)S(1)} %get-tuple-element.15, f32[16,8,2,16]{3,2,1,0:T(2,128)S(1)} %get-tuple-element.14, pred[16,64]{1,0:T(8,128)(4,1)S(1)} %iota_compare_fusion.2), kind=kLoop, calls=%fused_computation.17 | loop fusion | flops 1044480 | bytes 1082368 | tf_op jit(solution)/shard_map/reduce_sum | solution.py:76
  73.9 0.2 copy-done.3
  74.1 1.6 %select_reduce_fusion = bf16[16,8,16,128]{3,2,1,0:T(8,128)(2,1)S(1)} fusion(bf16[16,64,8,128]{3,2,1,0:T(8,128)(2,1)S(1)} %copy-done.3, f32[16,8,64,16,2]{2,3,4,1,0:T(8,128)S(1)} %get-tuple-element.15, f32[16,8,2,16]{3,2,1,0:T(2,128)S(1)} %fusion.6, f32[16,8,2,16]{3,2,1,0:T(2,128)S(1)} %get-tuple-element.14, pred[16,64]{1,0:T(8,128)(4,1)S(1)} %iota_compare_fusion.2, ...), kind=kOutput, calls=%fused_computation.14 | convolution fusion | flops 69468160 | bytes 3704064 | tf_op jit(solution)/shard_map/bqjlt,btqe->bqjle/dot_general | solution.py:77
  75.6 0.9 copy_bitcast_fusion.6
  76.5 6.0 %all-to-all-start.2 = ((bf16[16,16,1024]{2,1,0:T(8,128)(2,1)}), bf16[16,16,1024]{2,1,0:T(8,128)(2,1)S(1)}, u32[]{:S(2)}, u32[]{:S(2)}) async-start(bf16[16,16,1024]{2,1,0:T(8,128)(2,1)} %copy_bitcast_fusion.6), calls=%async_computation.2 | async-start | bytes 1048576 | tf_op jit(solution)/shard_map/all_to_all | solution.py:250
  82.5 14.4 %all-to-all-done.2 = bf16[16,16,1024]{2,1,0:T(8,128)(2,1)S(1)} async-done(((bf16[16,16,1024]{2,1,0:T(8,128)(2,1)}), bf16[16,16,1024]{2,1,0:T(8,128)(2,1)S(1)}, u32[]{:S(2)}, u32[]{:S(2)}) %all-to-all-start.2) | async-done | bytes 524320 | tf_op jit(solution)/shard_map/all_to_all | solution.py:250
  97.0 0.6 gather_fusion.1
  97.5 3.2 %fusion.8 = bf16[256,1024]{1,0:T(8,128)(2,1)} fusion(bf16[256,1024]{1,0:T(8,128)(2,1)S(1)} %bitcast.92, bf16[1024,1024]{1,0:T(8,128)(2,1)} %param.27, bf16[256,1024]{1,0:T(8,128)(2,1)} %copy-done.6), kind=kOutput, calls=%fused_computation.23 | convolution fusion | flops 537657344 | bytes 3670016 | tf_op jit(solution)/shard_map/dot_general | solution.py:257
  (16 shorter events, 0.1 us)
Async XLA Ops:
  0.0 41.7 %copy-start = (bf16[1024,1024]{1,0:T(8,128)(2,1)S(1)}, bf16[1024,1024]{1,0:T(8,128)(2,1)}, u32[]{:S(2)}) copy-start(bf16[1024,1024]{1,0:T(8,128)(2,1)} %param.24) | copy-start | bytes 6291460
  5.2 31.4 %all-to-all-start = ((bf16[16,16,2176]{2,1,0:T(8,128)(2,1)}), bf16[16,16,2176]{2,1,0:T(8,128)(2,1)S(1)}, u32[]{:S(2)}, u32[]{:S(2)}) async-start(bf16[16,16,2176]{2,1,0:T(8,128)(2,1)} %pad_maximum_fusion), calls=%async_computation | async-start | bytes 2228224 | tf_op jit(solution)/shard_map/all_to_all | solution.py:193
  20.4 2.0 %copy-start.2 = (bf16[16,16,1024]{2,1,0:T(8,128)(2,1)S(1)}, bf16[16,16,1024]{2,1,0:T(8,128)(2,1)}, u32[]{:S(2)}) copy-start(bf16[16,16,1024]{2,1,0:T(8,128)(2,1)} %param.14) | copy-start | bytes 1572868
  20.4 2.2 %copy-start.4 = (bf16[1024,1024]{1,0:T(8,128)(2,1)S(1)}, bf16[1024,1024]{1,0:T(8,128)(2,1)}, u32[]{:S(2)}) copy-start(bf16[1024,1024]{1,0:T(8,128)(2,1)} %param.23) | copy-start | bytes 6291460
  36.6 1.0 copy-start.1
  41.7 2.2 %copy-start.5 = (bf16[1024,1024]{1,0:T(8,128)(2,1)S(1)}, bf16[1024,1024]{1,0:T(8,128)(2,1)}, u32[]{:S(2)}) copy-start(bf16[1024,1024]{1,0:T(8,128)(2,1)} %param.26) | copy-start | bytes 6291460
  43.9 1.3 %copy-start.6 = (bf16[256,1024]{1,0:T(8,128)(2,1)}, bf16[256,1024]{1,0:T(8,128)(2,1)S(1)}, u32[]{:S(2)}) copy-start(bf16[256,1024]{1,0:T(8,128)(2,1)S(1)} %get-tuple-element.13) | copy-start | bytes 1572868
  46.3 23.1 %all-to-all-start.1 = ((bf16[16,16,1024]{2,1,0:T(8,128)(2,1)}), bf16[16,16,1024]{2,1,0:T(8,128)(2,1)S(1)}, u32[]{:S(2)}, u32[]{:S(2)}) async-start(bf16[16,16,1024]{2,1,0:T(8,128)(2,1)} %copy.33), calls=%async_computation.1 | async-start | bytes 1048576 | tf_op jit(solution)/shard_map/all_to_all | solution.py:226
  72.5 1.6 %copy-start.3 = (bf16[16,64,8,128]{3,2,1,0:T(8,128)(2,1)S(1)}, bf16[16,64,8,128]{3,2,1,0:T(8,128)(2,1)}, u32[]{:S(2)}) copy-start(bf16[16,64,8,128]{3,2,1,0:T(8,128)(2,1)} %get-tuple-element.9) | copy-start | bytes 6291460
  76.5 20.5 %all-to-all-start.2 = ((bf16[16,16,1024]{2,1,0:T(8,128)(2,1)}), bf16[16,16,1024]{2,1,0:T(8,128)(2,1)S(1)}, u32[]{:S(2)}, u32[]{:S(2)}) async-start(bf16[16,16,1024]{2,1,0:T(8,128)(2,1)} %copy_bitcast_fusion.6), calls=%async_computation.2 | async-start | bytes 1048576 | tf_op jit(solution)/shard_map/all_to_all | solution.py:250

commit v18 on v17

--- a/solution.py
+++ b/solution.py
@@ -156,13 +156,8 @@
     owners = lax.axis_size("smp")
     sess_dev, unit_total = (panels.shape[0], panels.shape[1])
     head_count = model_width // HEAD_DIM
-    session_ids = jnp.arange(session_row.shape[0], dtype=jnp.int32)
-    panel_row = jnp.sum(
-        jnp.where(session[:, None] == session_ids[None, :], session_row[None, :], 0), axis=1
-    )
-    unit_limit = jnp.sum(
-        jnp.where(panel_row[:, None] == session_ids[None, :], unit_count[None, :], 0), axis=1
-    )
+    panel_row = session_row[session]
+    unit_limit = unit_count[panel_row]
     owner_rank = panel_row // sess_dev
     token_index = (panel_row % sess_dev * unit_total)[:, None] + unit_slot % unit_limit[:, None]
     slot_pick = owner_rank[None, :] == jnp.arange(owners, dtype=jnp.int32)[:, None]

time: 102 us -> 103 us (level)
  blocking collectives: 0 us -> 20.3 us
  waiting for transfers between devices: 27 us -> 12.5 us
  starting transfers between devices: 20.6 us -> 14.6 us
  local copies, waits for them, and re-layouts: 21.8 us -> 23.6 us
    all_to_all x0 -> x1, blocking collectives: none -> 20.3 us  [per_device(): lax.all_to_all(served_read.reshape(owners, latents, model_width), 'smp',...]
    all_to_all x1 -> x0, waiting for transfers between devices: 14.4 us -> none  [per_device(): lax.all_to_all(served_read.reshape(owners, latents, model_width), 'smp',...]
    all_to_all x1 -> x0, starting transfers between devices: 6.01 us -> none  [per_device(): lax.all_to_all(served_read.reshape(owners, latents, model_width), 'smp',...]
    gather x0 -> x2, local copies, waits for them, and re-layouts: none -> 2.63 us  [the longest x1 1.32 us: per_device(): unit_limit = unit_count[panel_row]]
  transfers between devices with their start and end apart: 3 -> 2, of which waited for: 2 -> 1; matrix products, arithmetic and copies ran while one was open for 27% -> 27% of each run, Pallas kernels for 0% -> 0%
where the time goes in v18:
time: 103 us; the launch traced here: 102 us
  local copies, waits for them, and re-layouts  23.6 us (23%)
  blocking collectives  20.3 us (20%)
  matrix products  17.6 us (17%)
  starting transfers between devices  14.6 us (14%)
  waiting for transfers between devices  12.5 us (12%)
  other arithmetic  9.15 us (9%)
  Pallas kernels  4.13 us (4%)
    all_to_all x1, blocking collectives, per_device(): lax.all_to_all(served_read.reshape(owners, latents, model_width), 'smp',...  20.3 us
    all_to_all x1, waiting for transfers between devices, per_device(): lax.all_to_all(jnp.concatenate([jnp.broadcast_to(memory_pair[None], (owne...  12.5 us
    gather x1, local copies, waits for them, and re-layouts, per_device(): kv_rows = kv_table[served_index]  9.97 us
    all_to_all x1, starting transfers between devices, per_device(): lax.all_to_all(jnp.concatenate([jnp.broadcast_to(memory_pair[None], (owne...  7.39 us
    all_to_all x1, starting transfers between devices, per_device(): lax.all_to_all(jnp.einsum('ob,bld->old', (sample_pick[:, None] == jnp.ara...  7.19 us
    dot_general x1, matrix products, per_device(): jnp.dot(panel_normed, kv_weight, preferred_element_type=jnp.float32)  4.93 us
    slice x1, local copies, waits for them, and re-layouts, per_device(): key_rows = kv_rows[:, :, :head_count // 2]  4.65 us
    pallas_call x1, Pallas kernels, attend_kernel(): pl.pallas_call(attend_block, grid_spec=pltpu.PrefetchScalarGridSpec(num_s...  4.13 us
  transfers between devices with their start and end apart: 2, of which 1 were waited for; matrix products, arithmetic and copies ran while one was open for 27% of the time, Pallas kernels for 0%

profile of v18, /device:TPU:0, one launch (start us, length us, event | category | flops | bytes accessed | tf_op | source)
XLA Modules:
  0.0 102.1 jit_solution(14283687888868526849)
XLA Ops:
  0.0 0.0 copy-start
  0.0 0.8 compare_select_fusion.3
  0.8 1.3 %gather_fusion = s32[16]{0:T(128)S(1)} fusion(s32[16]{0:T(128)} %param.18, s32[1024]{0:T(1024)S(1)} %pad_clamp_fusion.1), kind=kCustom, calls=%fused_computation | custom fusion | bytes 192 | tf_op jit(solution)/shard_map/gather | solution.py:159
  2.2 1.3 %gather_fusion.1 = s32[16]{0:T(128)S(1)} fusion(s32[16]{0:T(128)} %param.19, s32[1024]{0:T(1024)S(1)} %pad_clamp_fusion), kind=kCustom, calls=%fused_computation.1 | custom fusion | bytes 192 | tf_op jit(solution)/shard_map/gather | solution.py:160
  3.5 0.8 select_reduce_fusion.2
  4.3 0.1 copy.30
  4.4 0.9 add_select_fusion.2
  5.3 0.1 select_reduce_fusion.1
  5.4 0.1 fusion.34
  5.5 0.1 fusion.33
  5.6 0.8 pad_maximum_fusion.1
  6.4 0.1 broadcast_in_dim.122
  6.5 1.1 %pad_maximum_fusion = bf16[16,16,2176]{2,1,0:T(8,128)(2,1)} fusion(bf16[16,16,128]{2,1,0:T(8,128)(2,1)S(1)} %bitcast.93, bf16[16,16,2048]{2,1,0:T(8,128)(2,1)S(1)} %broadcast_in_dim.122), kind=kLoop, calls=%fused_computation.31 | loop fusion | flops 2228224 | bytes 2228224 | tf_op jit(solution)/shard_map/concatenate | solution.py:189
  7.6 7.4 %all-to-all-start = ((bf16[16,16,2176]{2,1,0:T(8,128)(2,1)}), bf16[16,16,2176]{2,1,0:T(8,128)(2,1)S(1)}, u32[]{:S(2)}, u32[]{:S(2)}) async-start(bf16[16,16,2176]{2,1,0:T(8,128)(2,1)} %pad_maximum_fusion), calls=%async_computation | async-start | bytes 2228224 | tf_op jit(solution)/shard_map/all_to_all | solution.py:188
  14.9 1.2 %multiply_reduce_fusion = f32[16,16]{1,0:T(8,128)S(1)} fusion(bf16[16,16,1024]{2,1,0:T(8,128)(2,1)} %param.14), kind=kLoop, calls=%fused_computation.42 | loop fusion | flops 786176 | bytes 525312 | tf_op jit(solution)/shard_map/reduce_sum | solution.py:16
  16.2 0.1 rsqrt.28
  16.3 1.5 %fusion = f32[512]{0:T(512)S(1)} fusion(bf16[1,512,1024]{2,1,0:T(8,128)(2,1)} %param.20), kind=kLoop, calls=%fused_computation.7 | loop fusion | flops 1572352 | bytes 1050624 | tf_op jit(solution)/shard_map/reduce_sum | solution.py:16
  17.8 4.9 %fusion.5 = bf16[64,8,16,128]{3,1,2,0:T(8,128)(2,1)S(1)} fusion(bf16[1024,2048]{1,0:T(8,128)(2,1)} %param.25, bf16[1,512,1024]{2,1,0:T(8,128)(2,1)} %param.20, f32[512]{0:T(512)S(1)} %add_rsqrt_fusion.1), kind=kOutput, calls=%fused_computation.18 | convolution fusion | flops 2150105088 | bytes 7342080 | tf_op jit(solution)/shard_map/dot_general | solution.py:171
  22.7 0.0 copy-start.2
  22.7 0.0 copy-start.4
  22.7 2.0 %copy.45 = bf16[64,8,16,128]{3,2,1,0:T(8,128)(2,1)} copy(bf16[64,8,16,128]{3,1,2,0:T(8,128)(2,1)S(1)} %fusion.5) | data formatting | bytes 4194304
  24.7 0.0 copy-done.2
  24.7 0.2 fusion.16
  24.9 0.0 copy-done.4
  24.9 1.5 %fusion.10.query_ref = bf16[1,256,1024]{2,1,0:T(8,128)(2,1)} fusion(bf16[256,1024]{1,0:T(8,128)(2,1)S(1)} %fusion.16, bf16[1024,1024]{1,0:T(8,128)(2,1)S(1)} %copy-done.4), kind=kOutput, calls=%fused_computation.30 | convolution fusion | flops 537133056 | bytes 3145728 | tf_op jit(solution)/shard_map/dot_general | solution.py:178
  26.5 12.5 %all-to-all-done = bf16[16,16,2176]{2,1,0:T(8,128)(2,1)S(1)} async-done(((bf16[16,16,2176]{2,1,0:T(8,128)(2,1)}), bf16[16,16,2176]{2,1,0:T(8,128)(2,1)S(1)}, u32[]{:S(2)}, u32[]{:S(2)}) %all-to-all-start) | async-done | bytes 1114144 | tf_op jit(solution)/shard_map/all_to_all | solution.py:188
  39.0 0.0 copy-start.1
  39.0 1.0 copy-done.1
  40.0 4.1 %shard_map.136 = bf16[1,256,1024]{2,1,0:T(8,128)(2,1)} custom-call(s32[1]{0:T(128)} %constant.85.clone.1.counts_ref, bf16[1,256,1024]{2,1,0:T(8,128)(2,1)} %fusion.10.query_ref, bf16[1,256,2176]{2,1,0:T(8,128)(2,1)} %bitcast.88, bf16[1,256,2176]{2,1,0:T(8,128)(2,1)} %bitcast.89), custom_call_target="tpu_custom_call" | custom-call | tf_op jit(solution)/shard_map/pallas_call | solution.py:122
  44.1 0.0 copy-done
  44.1 0.0 copy-start.5
  44.1 2.2 %fusion.11 = (f32[256]{0:T(256)S(1)}, bf16[256,1024]{1,0:T(8,128)(2,1)S(1)}) fusion(bf16[1024,1024]{1,0:T(8,128)(2,1)S(1)} %copy-done, bf16[1,256,1024]{2,1,0:T(8,128)(2,1)} %shard_map.136, bf16[256,1024]{1,0:T(8,128)(2,1)} %bitcast.90), kind=kOutput, calls=%fused_computation.32 | convolution fusion | flops 538443520 | bytes 3671040 | tf_op jit(solution)/shard_map/dot_general | solution.py:215
  46.3 0.0 copy-start.6
  46.3 0.0 copy-done.5
  46.3 0.8 convolution_convert_fusion.2
  47.1 0.5 convolution_convert_fusion.1
  47.5 0.0 copy-done.6
  47.5 1.1 %copy.33 = bf16[16,16,1024]{2,1,0:T(8,128)(2,1)} copy(bf16[16,16,1024]{2,0,1:T(8,128)(2,1)S(1)} %convolution_convert_fusion.1) | data formatting | bytes 1048576 | tf_op jit(solution)/shard_map/convert_element_type | solution.py:229
  48.6 7.2 %all-to-all-start.1 = ((bf16[16,16,1024]{2,1,0:T(8,128)(2,1)}), bf16[16,16,1024]{2,1,0:T(8,128)(2,1)S(1)}, u32[]{:S(2)}, u32[]{:S(2)}) async-start(bf16[16,16,1024]{2,1,0:T(8,128)(2,1)} %copy.33), calls=%async_computation.1 | async-start | bytes 1048576 | tf_op jit(solution)/shard_map/all_to_all | solution.py:221
  55.8 0.8 slice.40
  56.7 0.1 slice_add_fusion
  56.8 0.1 reshape.267
  56.9 10.0 %gather_fusion.2 = bf16[1024,16,128]{2,1,0:T(8,128)(2,1)} fusion(bf16[512,16,128]{2,1,0:T(8,128)(2,1)} %bitcast.86, s32[1024]{0:T(1024)S(1)} %broadcast_clamp_fusion), kind=kCustom, calls=%fused_computation.2 | custom fusion | bytes 8392704 | tf_op jit(solution)/shard_map/gather | solution.py:235
  66.8 0.2 slice_reduce_fusion
  67.0 0.1 iota_compare_fusion.2
  67.1 4.7 %fusion.45 = (bf16[16,64,8,128]{3,2,1,0:T(8,128)(2,1)}, bf16[16,64,8,128]{3,2,1,0:T(8,128)(2,1)}) fusion(bf16[16,64,16,128]{3,2,1,0:T(8,128)(2,1)} %bitcast.87), kind=kLoop, calls=%fused_computation.105 | loop fusion | bytes 8388608 | tf_op jit(solution)/shard_map/slice | solution.py:236
  71.7 0.0 all-to-all-done.1
  71.7 0.1 copy_bitcast_fusion.7
  71.8 3.0 %bitcast_reduce_fusion = (f32[16,8,2,16]{3,2,1,0:T(2,128)S(1)}, f32[16,8,64,16,2]{2,3,4,1,0:T(8,128)S(1)}) fusion(pred[16,64]{1,0:T(8,128)(4,1)S(1)} %iota_compare_fusion.2, pred[2,128]{1,0:T(4,128)(4,1)S(1)} %iota_compare_fusion.4, bf16[16,16,8,128]{3,1,2,0:T(8,128)(2,1)S(1)} %copy_bitcast_fusion.7, bf16[16,64,8,128]{3,2,1,0:T(8,128)(2,1)} %get-tuple-element.7), kind=kOutput, calls=%fused_computation.14 | convolution fusion | flops 68415488 | bytes 3687680 | tf_op jit(solution)/shard_map/blqje,btqe->bqjlt/dot_general | solution.py:70
  74.8 0.0 copy-start.3
  74.8 1.4 %fusion.6 = f32[16,8,2,16]{3,2,1,0:T(2,128)S(1)} fusion(f32[16,8,64,16,2]{2,3,4,1,0:T(8,128)S(1)} %get-tuple-element.14, f32[16,8,2,16]{3,2,1,0:T(2,128)S(1)} %get-tuple-element.13, pred[16,64]{1,0:T(8,128)(4,1)S(1)} %iota_compare_fusion.2), kind=kLoop, calls=%fused_computation.19 | loop fusion | flops 1044480 | bytes 1082368 | tf_op jit(solution)/shard_map/reduce_sum | solution.py:76
  76.2 0.2 copy-done.3
  76.4 1.6 %select_reduce_fusion = bf16[16,8,16,128]{3,2,1,0:T(8,128)(2,1)S(1)} fusion(bf16[16,64,8,128]{3,2,1,0:T(8,128)(2,1)S(1)} %copy-done.3, f32[16,8,64,16,2]{2,3,4,1,0:T(8,128)S(1)} %get-tuple-element.14, f32[16,8,2,16]{3,2,1,0:T(2,128)S(1)} %fusion.6, f32[16,8,2,16]{3,2,1,0:T(2,128)S(1)} %get-tuple-element.13, pred[16,64]{1,0:T(8,128)(4,1)S(1)} %iota_compare_fusion.2, ...), kind=kOutput, calls=%fused_computation.16 | convolution fusion | flops 69468160 | bytes 3704064 | tf_op jit(solution)/shard_map/bqjlt,btqe->bqjle/dot_general | solution.py:77
  78.0 0.1 copy_bitcast_fusion.6
  78.0 20.3 %all_to_all.15 = bf16[16,16,1024]{2,1,0:T(8,128)(2,1)S(1)} all-to-all(bf16[16,16,1024]{2,1,0:T(8,128)(2,1)S(1)} %copy_bitcast_fusion.6), channel_id=1, replica_groups=mesh['grp'=2,'smp'=16] {'smp'}, dimensions={0} | all-to-all | bytes 1048576 | tf_op jit(solution)/shard_map/all_to_all | solution.py:245
  98.3 0.6 gather_fusion.3
  98.9 3.2 %fusion.8 = bf16[256,1024]{1,0:T(8,128)(2,1)} fusion(bf16[256,1024]{1,0:T(8,128)(2,1)S(1)} %bitcast.92, bf16[1024,1024]{1,0:T(8,128)(2,1)} %param.27, bf16[256,1024]{1,0:T(8,128)(2,1)} %copy-done.6), kind=kOutput, calls=%fused_computation.25 | convolution fusion | flops 537657344 | bytes 3670016 | tf_op jit(solution)/shard_map/dot_general | solution.py:252
  (17 shorter events, 0.1 us)
Async XLA Ops:
  0.0 44.1 %copy-start = (bf16[1024,1024]{1,0:T(8,128)(2,1)S(1)}, bf16[1024,1024]{1,0:T(8,128)(2,1)}, u32[]{:S(2)}) copy-start(bf16[1024,1024]{1,0:T(8,128)(2,1)} %param.24) | copy-start | bytes 6291460
  7.6 31.4 %all-to-all-start = ((bf16[16,16,2176]{2,1,0:T(8,128)(2,1)}), bf16[16,16,2176]{2,1,0:T(8,128)(2,1)S(1)}, u32[]{:S(2)}, u32[]{:S(2)}) async-start(bf16[16,16,2176]{2,1,0:T(8,128)(2,1)} %pad_maximum_fusion), calls=%async_computation | async-start | bytes 2228224 | tf_op jit(solution)/shard_map/all_to_all | solution.py:188
  22.7 2.0 %copy-start.2 = (bf16[16,16,1024]{2,1,0:T(8,128)(2,1)S(1)}, bf16[16,16,1024]{2,1,0:T(8,128)(2,1)}, u32[]{:S(2)}) copy-start(bf16[16,16,1024]{2,1,0:T(8,128)(2,1)} %param.14) | copy-start | bytes 1572868
  22.7 2.2 %copy-start.4 = (bf16[1024,1024]{1,0:T(8,128)(2,1)S(1)}, bf16[1024,1024]{1,0:T(8,128)(2,1)}, u32[]{:S(2)}) copy-start(bf16[1024,1024]{1,0:T(8,128)(2,1)} %param.23) | copy-start | bytes 6291460
  39.0 1.0 copy-start.1
  44.1 2.2 %copy-start.5 = (bf16[1024,1024]{1,0:T(8,128)(2,1)S(1)}, bf16[1024,1024]{1,0:T(8,128)(2,1)}, u32[]{:S(2)}) copy-start(bf16[1024,1024]{1,0:T(8,128)(2,1)} %param.26) | copy-start | bytes 6291460
  46.3 1.3 %copy-start.6 = (bf16[256,1024]{1,0:T(8,128)(2,1)}, bf16[256,1024]{1,0:T(8,128)(2,1)S(1)}, u32[]{:S(2)}) copy-start(bf16[256,1024]{1,0:T(8,128)(2,1)S(1)} %get-tuple-element.12) | copy-start | bytes 1572868
  48.6 23.1 %all-to-all-start.1 = ((bf16[16,16,1024]{2,1,0:T(8,128)(2,1)}), bf16[16,16,1024]{2,1,0:T(8,128)(2,1)S(1)}, u32[]{:S(2)}, u32[]{:S(2)}) async-start(bf16[16,16,1024]{2,1,0:T(8,128)(2,1)} %copy.33), calls=%async_computation.1 | async-start | bytes 1048576 | tf_op jit(solution)/shard_map/all_to_all | solution.py:221
  74.8 1.6 %copy-start.3 = (bf16[16,64,8,128]{3,2,1,0:T(8,128)(2,1)S(1)}, bf16[16,64,8,128]{3,2,1,0:T(8,128)(2,1)}, u32[]{:S(2)}) copy-start(bf16[16,64,8,128]{3,2,1,0:T(8,128)(2,1)} %get-tuple-element.8) | copy-start | bytes 6291460

commit v19 on v17

--- a/solution.py
+++ b/solution.py
@@ -80,6 +80,32 @@
         value_rows,
         preferred_element_type=jnp.float32,
     ) / denominator
+    mix = jnp.sum(jnp.where(halves[None, None, :, None, :], mix, 0.0), axis=2)
+    return jnp.transpose(mix, (0, 2, 1, 3)).reshape(samples, latents, pair_count * pair_width).astype(
+        jnp.bfloat16
+    )
+
+
+def attend_stacked(queries, kv_rows, live_tokens):
+    samples, latents, pair_count, pair_width = queries.shape
+    halves = (
+        lax.broadcasted_iota(jnp.int32, (2, pair_width), 1) // HEAD_DIM
+        == lax.broadcasted_iota(jnp.int32, (2, pair_width), 0)
+    )
+    masked = jnp.where(halves[None, None, None], queries[:, :, :, None, :], 0).astype(jnp.bfloat16)
+    masked = jnp.concatenate([masked, jnp.zeros_like(masked)], axis=2)
+    scores = jnp.einsum(
+        "blqje,btqe->bqjlt", masked, kv_rows, preferred_element_type=jnp.float32
+    )[:, :pair_count] * HEAD_DIM ** (-0.5)
+    scores = jnp.where(live_tokens[:, None, None, None, :], scores, masked_score)
+    row_max = jnp.max(scores, axis=-1, keepdims=True)
+    exponent = jnp.exp(scores - row_max)
+    denominator = jnp.sum(exponent, axis=-1, keepdims=True)
+    weights = exponent.astype(jnp.bfloat16)
+    weights = jnp.concatenate([jnp.zeros_like(weights), weights], axis=1)
+    mix = jnp.einsum(
+        "bqjlt,btqe->bqjle", weights, kv_rows, preferred_element_type=jnp.float32
+    )[:, pair_count:] / denominator
     mix = jnp.sum(jnp.where(halves[None, None, :, None, :], mix, 0.0), axis=2)
     return jnp.transpose(mix, (0, 2, 1, 3)).reshape(samples, latents, pair_count * pair_width).astype(
         jnp.bfloat16
@@ -238,13 +264,10 @@
         tiled=True,
     )
     kv_rows = kv_table[served_index]
-    key_rows = kv_rows[:, :, : head_count // 2]
-    value_rows = kv_rows[:, :, head_count // 2 :]
     live_tokens = jnp.arange(token_total, dtype=jnp.int32)[None, :] < served[:, token_total:]
-    served_read = attend_pairs(
+    served_read = attend_stacked(
         served_queries.reshape(owners, latents, head_count // 2, 2 * HEAD_DIM),
-        key_rows.reshape(owners, token_total, head_count // 2, 2 * HEAD_DIM),
-        value_rows.reshape(owners, token_total, head_count // 2, 2 * HEAD_DIM),
+        kv_rows.reshape(owners, token_total, head_count, 2 * HEAD_DIM),
         live_tokens,
     )
     read_spike = lax.all_to_all(

time: 102 us -> 101 us (level)
  local copies, waits for them, and re-layouts: 21.8 us -> 17 us
  waiting for transfers between devices: 27 us -> 31 us
  starting transfers between devices: 20.6 us -> 18.7 us
  matrix products: 17.6 us -> 19.1 us
    slice x1 -> x0, local copies, waits for them, and re-layouts: 4.65 us -> none  [per_device(): key_rows = kv_rows[:, :, :head_count // 2]]
    all_to_all x1, waiting for transfers between devices: 0.01 us -> 4.07 us  [per_device(): lax.all_to_all(jnp.einsum('ob,bld->old', (sample_pick[:, None] == jnp.ara...]
    all_to_all x1, starting transfers between devices: 6.01 us -> 4.1 us  [per_device(): lax.all_to_all(served_read.reshape(owners, latents, model_width), 'smp',...]
    slice x0 -> x1, matrix products: none -> 1.61 us  [attend_stacked(): jnp.einsum('bqjlt,btqe->bqjle', weights, kv_rows, preferred_element_type=...]
    dot_general x2 -> x1, matrix products: 4.52 us -> 4.48 us  [attend_stacked(): jnp.einsum('blqje,btqe->bqjlt', masked, kv_rows, preferred_element_type=j...]
  transfers between devices with their start and end apart: 3 -> 3, of which waited for: 2 -> 3; matrix products, arithmetic and copies ran while one was open for 27% -> 22% of each run, Pallas kernels for 0% -> 0%
where the time goes in v19:
time: 101 us
  waiting for transfers between devices  31 us (31%)
  matrix products  19.1 us (19%)
  starting transfers between devices  18.7 us (19%)
  local copies, waits for them, and re-layouts  17 us (17%)
  other arithmetic  10.4 us (10%)
  Pallas kernels  4.13 us (4%)
    all_to_all x1, waiting for transfers between devices, per_device(): lax.all_to_all(served_read.reshape(owners, latents, model_width), 'smp',...  14.4 us
    all_to_all x1, waiting for transfers between devices, per_device(): lax.all_to_all(jnp.concatenate([jnp.broadcast_to(memory_pair[None], (owne...  12.5 us
    gather x1, local copies, waits for them, and re-layouts, per_device(): kv_rows = kv_table[served_index]  9.97 us
    all_to_all x1, starting transfers between devices, per_device(): lax.all_to_all(jnp.concatenate([jnp.broadcast_to(memory_pair[None], (owne...  7.39 us
    all_to_all x1, starting transfers between devices, per_device(): lax.all_to_all(jnp.einsum('ob,bld->old', (sample_pick[:, None] == jnp.ara...  7.19 us
    dot_general x1, matrix products, per_device(): jnp.dot(panel_normed, kv_weight, preferred_element_type=jnp.float32)  4.92 us
    dot_general x1, matrix products, attend_stacked(): jnp.einsum('blqje,btqe->bqjlt', masked, kv_rows, preferred_element_type=j...  4.48 us
    pallas_call x1, Pallas kernels, attend_kernel(): pl.pallas_call(attend_block, grid_spec=pltpu.PrefetchScalarGridSpec(num_s...  4.13 us
  transfers between devices with their start and end apart: 3, of which 3 were waited for; matrix products, arithmetic and copies ran while one was open for 22% of the time, Pallas kernels for 0%

profile of v19, /device:TPU:0, one launch (start us, length us, event | category | flops | bytes accessed | tf_op | source)
XLA Modules:
  0.0 100.6 jit_solution(833454414435209794)
XLA Ops:
  0.0 0.0 copy-start
  0.0 1.0 select_reduce_fusion.5
  1.0 0.9 select_reduce_fusion.2
  1.9 0.1 copy.30
  2.0 0.9 add_select_fusion.2
  2.9 0.1 select_reduce_fusion.1
  3.0 0.1 fusion.39
  3.1 0.1 fusion.38
  3.2 0.8 pad_maximum_fusion.1
  4.0 0.1 broadcast_in_dim.134
  4.1 1.1 %pad_maximum_fusion = bf16[16,16,2176]{2,1,0:T(8,128)(2,1)} fusion(bf16[16,16,128]{2,1,0:T(8,128)(2,1)S(1)} %bitcast.75, bf16[16,16,2048]{2,1,0:T(8,128)(2,1)S(1)} %broadcast_in_dim.134), kind=kLoop, calls=%fused_computation.31 | loop fusion | flops 2228224 | bytes 2228224 | tf_op jit(solution)/shard_map/concatenate | solution.py:220
  5.2 7.4 %all-to-all-start = ((bf16[16,16,2176]{2,1,0:T(8,128)(2,1)}), bf16[16,16,2176]{2,1,0:T(8,128)(2,1)S(1)}, u32[]{:S(2)}, u32[]{:S(2)}) async-start(bf16[16,16,2176]{2,1,0:T(8,128)(2,1)} %pad_maximum_fusion), calls=%async_computation | async-start | bytes 2228224 | tf_op jit(solution)/shard_map/all_to_all | solution.py:219
  12.6 1.2 %multiply_reduce_fusion = f32[16,16]{1,0:T(8,128)S(1)} fusion(bf16[16,16,1024]{2,1,0:T(8,128)(2,1)} %param.14), kind=kLoop, calls=%fused_computation.41 | loop fusion | flops 786176 | bytes 525312 | tf_op jit(solution)/shard_map/reduce_sum | solution.py:16
  13.8 0.1 rsqrt.28
  13.9 1.5 %fusion.7 = f32[512]{0:T(512)S(1)} fusion(bf16[1,512,1024]{2,1,0:T(8,128)(2,1)} %param.20), kind=kLoop, calls=%fused_computation.10 | loop fusion | flops 1572352 | bytes 1050624 | tf_op jit(solution)/shard_map/reduce_sum | solution.py:16
  15.4 4.9 %fusion.13 = bf16[64,8,16,128]{3,1,2,0:T(8,128)(2,1)S(1)} fusion(bf16[1024,2048]{1,0:T(8,128)(2,1)} %param.25, bf16[1,512,1024]{2,1,0:T(8,128)(2,1)} %param.20, f32[512]{0:T(512)S(1)} %add_rsqrt_fusion.1), kind=kOutput, calls=%fused_computation.19 | convolution fusion | flops 2150105088 | bytes 7342080 | tf_op jit(solution)/shard_map/dot_general | solution.py:202
  20.4 0.0 copy-start.3
  20.4 0.0 copy-start.4
  20.4 2.0 %copy.47 = bf16[64,8,16,128]{3,2,1,0:T(8,128)(2,1)} copy(bf16[64,8,16,128]{3,1,2,0:T(8,128)(2,1)S(1)} %fusion.13) | data formatting | bytes 4194304
  22.4 0.0 copy-done.3
  22.4 0.2 fusion.25
  22.5 0.0 copy-done.4
  22.6 1.5 %fusion.17.query_ref = bf16[1,256,1024]{2,1,0:T(8,128)(2,1)} fusion(bf16[256,1024]{1,0:T(8,128)(2,1)S(1)} %fusion.25, bf16[1024,1024]{1,0:T(8,128)(2,1)S(1)} %copy-done.4), kind=kOutput, calls=%fused_computation.30 | convolution fusion | flops 537133056 | bytes 3145728 | tf_op jit(solution)/shard_map/dot_general | solution.py:209
  24.1 12.5 %all-to-all-done = bf16[16,16,2176]{2,1,0:T(8,128)(2,1)S(1)} async-done(((bf16[16,16,2176]{2,1,0:T(8,128)(2,1)}), bf16[16,16,2176]{2,1,0:T(8,128)(2,1)S(1)}, u32[]{:S(2)}, u32[]{:S(2)}) %all-to-all-start) | async-done | bytes 1114144 | tf_op jit(solution)/shard_map/all_to_all | solution.py:219
  36.6 0.0 copy-start.2
  36.6 1.0 copy-done.2
  37.6 4.1 %shard_map.136 = bf16[1,256,1024]{2,1,0:T(8,128)(2,1)} custom-call(s32[1]{0:T(128)} %constant.87.clone.1.counts_ref, bf16[1,256,1024]{2,1,0:T(8,128)(2,1)} %fusion.17.query_ref, bf16[1,256,2176]{2,1,0:T(8,128)(2,1)} %bitcast.70, bf16[1,256,2176]{2,1,0:T(8,128)(2,1)} %bitcast.71), custom_call_target="tpu_custom_call" | custom-call | tf_op jit(solution)/shard_map/pallas_call | solution.py:148
  41.7 0.0 copy-done
  41.7 0.0 copy-start.5
  41.7 2.2 %fusion.20 = (f32[256]{0:T(256)S(1)}, bf16[256,1024]{1,0:T(8,128)(2,1)S(1)}) fusion(bf16[1024,1024]{1,0:T(8,128)(2,1)S(1)} %copy-done, bf16[1,256,1024]{2,1,0:T(8,128)(2,1)} %shard_map.136, bf16[256,1024]{1,0:T(8,128)(2,1)} %bitcast.72), kind=kOutput, calls=%fused_computation.32 | convolution fusion | flops 538443520 | bytes 3671040 | tf_op jit(solution)/shard_map/dot_general | solution.py:246
  43.9 0.0 copy-start.6
  43.9 0.9 slice.36
  44.9 0.0 copy-done.5
  44.9 0.8 convolution_convert_fusion.2
  45.7 0.5 convolution_convert_fusion.1
  46.1 0.0 copy-done.6
  46.2 1.1 %copy.32 = bf16[16,16,1024]{2,1,0:T(8,128)(2,1)} copy(bf16[16,16,1024]{2,0,1:T(8,128)(2,1)S(1)} %convolution_convert_fusion.1) | data formatting | bytes 1048576 | tf_op jit(solution)/shard_map/convert_element_type | solution.py:260
  47.2 7.2 %all-to-all-start.1 = ((bf16[16,16,1024]{2,1,0:T(8,128)(2,1)}), bf16[16,16,1024]{2,1,0:T(8,128)(2,1)S(1)}, u32[]{:S(2)}, u32[]{:S(2)}) async-start(bf16[16,16,1024]{2,1,0:T(8,128)(2,1)} %copy.32), calls=%async_computation.1 | async-start | bytes 1048576 | tf_op jit(solution)/shard_map/all_to_all | solution.py:252
  54.4 0.1 slice_add_fusion
  54.5 0.1 reshape.250
  54.6 10.0 %gather_fusion = bf16[1024,16,128]{2,1,0:T(8,128)(2,1)} fusion(bf16[512,16,128]{2,1,0:T(8,128)(2,1)} %bitcast.67, s32[1024]{0:T(1024)S(1)} %broadcast_clamp_fusion), kind=kCustom, calls=%fused_computation | custom fusion | bytes 8392704 | tf_op jit(solution)/shard_map/gather | solution.py:266
  64.6 0.2 slice_reduce_fusion
  64.7 0.1 iota_compare_fusion.2
  64.8 4.1 %all-to-all-done.1 = bf16[16,16,1024]{2,1,0:T(8,128)(2,1)S(1)} async-done(((bf16[16,16,1024]{2,1,0:T(8,128)(2,1)}), bf16[16,16,1024]{2,1,0:T(8,128)(2,1)S(1)}, u32[]{:S(2)}, u32[]{:S(2)}) %all-to-all-start.1) | async-done | bytes 524320 | tf_op jit(solution)/shard_map/all_to_all | solution.py:252
  68.9 0.1 copy_bitcast_fusion.1
  69.0 0.1 broadcast_select_fusion
  69.1 4.5 %fusion.4 = f32[16,16,2,16,64]{4,3,2,1,0:T(8,128)S(1)} fusion(bf16[16,64,16,128,1]{3,2,1,0,4:T(8,128)(2,1)} %bitcast.68, bf16[16,16,8,2,128]{4,1,3,2,0:T(8,128)(2,1)S(1)} %broadcast_select_fusion), kind=kOutput, calls=%fused_computation.9 | convolution fusion | flops 134217728 | bytes 7340032 | tf_op jit(solution)/shard_map/blqje,btqe->bqjlt/dot_general | solution.py:97
  73.6 0.0 copy-start.1
  73.6 0.8 fusion.14
  74.4 1.4 %fusion.11 = f32[16,8,2,16]{3,2,1,0:T(2,128)S(1)} fusion(f32[16,16,2,16,64]{4,3,2,1,0:T(8,128)S(1)} %fusion.4, f32[16,8,2,16]{3,2,1,0:T(2,128)S(1)} %fusion.14, pred[16,64]{1,0:T(8,128)(4,1)S(1)} %iota_compare_fusion.2), kind=kLoop, calls=%fused_computation.17 | loop fusion | flops 1044480 | bytes 1082368 | tf_op jit(solution)/shard_map/reduce_sum | solution.py:103
  75.8 0.0 copy-done.1
  75.8 1.6 %select_reduce_fusion = bf16[16,8,16,128]{3,2,1,0:T(8,128)(2,1)S(1)} fusion(bf16[16,64,16,128,1]{3,2,1,0,4:T(8,128)(2,1)S(1)} %bitcast.69, f32[16,16,2,16,64]{4,3,2,1,0:T(8,128)S(1)} %fusion.4, f32[16,8,2,16]{3,2,1,0:T(2,128)S(1)} %fusion.11, f32[16,8,2,16]{3,2,1,0:T(2,128)S(1)} %fusion.14, pred[16,64]{1,0:T(8,128)(4,1)S(1)} %iota_compare_fusion.2, ...), kind=kOutput, calls=%fused_computation.14 | convolution fusion | flops 69468160 | bytes 7080448 | tf_op jit(solution)/shard_map/slice | solution.py:106
  77.4 0.9 copy_bitcast_fusion
  78.3 4.1 %all-to-all-start.2 = ((bf16[16,16,1024]{2,1,0:T(8,128)(2,1)}), bf16[16,16,1024]{2,1,0:T(8,128)(2,1)S(1)}, u32[]{:S(2)}, u32[]{:S(2)}) async-start(bf16[16,16,1024]{2,1,0:T(8,128)(2,1)} %copy_bitcast_fusion), calls=%async_computation.2 | async-start | bytes 1048576 | tf_op jit(solution)/shard_map/all_to_all | solution.py:273
  82.4 14.4 %all-to-all-done.2 = bf16[16,16,1024]{2,1,0:T(8,128)(2,1)S(1)} async-done(((bf16[16,16,1024]{2,1,0:T(8,128)(2,1)}), bf16[16,16,1024]{2,1,0:T(8,128)(2,1)S(1)}, u32[]{:S(2)}, u32[]{:S(2)}) %all-to-all-start.2) | async-done | bytes 524320 | tf_op jit(solution)/shard_map/all_to_all | solution.py:273
  96.9 0.6 gather_fusion.1
  97.4 3.2 %fusion.15 = bf16[256,1024]{1,0:T(8,128)(2,1)} fusion(bf16[256,1024]{1,0:T(8,128)(2,1)S(1)} %bitcast.74, bf16[1024,1024]{1,0:T(8,128)(2,1)} %param.27, bf16[256,1024]{1,0:T(8,128)(2,1)} %copy-done.6), kind=kOutput, calls=%fused_computation.25 | convolution fusion | flops 537657344 | bytes 3670016 | tf_op jit(solution)/shard_map/dot_general | solution.py:280
  (16 shorter events, 0.1 us)
Async XLA Ops:
  0.0 41.7 %copy-start = (bf16[1024,1024]{1,0:T(8,128)(2,1)S(1)}, bf16[1024,1024]{1,0:T(8,128)(2,1)}, u32[]{:S(2)}) copy-start(bf16[1024,1024]{1,0:T(8,128)(2,1)} %param.24) | copy-start | bytes 6291460
  5.2 31.4 %all-to-all-start = ((bf16[16,16,2176]{2,1,0:T(8,128)(2,1)}), bf16[16,16,2176]{2,1,0:T(8,128)(2,1)S(1)}, u32[]{:S(2)}, u32[]{:S(2)}) async-start(bf16[16,16,2176]{2,1,0:T(8,128)(2,1)} %pad_maximum_fusion), calls=%async_computation | async-start | bytes 2228224 | tf_op jit(solution)/shard_map/all_to_all | solution.py:219
  20.4 2.0 %copy-start.3 = (bf16[16,16,1024]{2,1,0:T(8,128)(2,1)S(1)}, bf16[16,16,1024]{2,1,0:T(8,128)(2,1)}, u32[]{:S(2)}) copy-start(bf16[16,16,1024]{2,1,0:T(8,128)(2,1)} %param.14) | copy-start | bytes 1572868
  20.4 2.2 %copy-start.4 = (bf16[1024,1024]{1,0:T(8,128)(2,1)S(1)}, bf16[1024,1024]{1,0:T(8,128)(2,1)}, u32[]{:S(2)}) copy-start(bf16[1024,1024]{1,0:T(8,128)(2,1)} %param.23) | copy-start | bytes 6291460
  36.6 1.0 copy-start.2
  41.7 3.2 %copy-start.5 = (bf16[1024,1024]{1,0:T(8,128)(2,1)S(1)}, bf16[1024,1024]{1,0:T(8,128)(2,1)}, u32[]{:S(2)}) copy-start(bf16[1024,1024]{1,0:T(8,128)(2,1)} %param.26) | copy-start | bytes 6291460
  43.9 2.2 %copy-start.6 = (bf16[256,1024]{1,0:T(8,128)(2,1)}, bf16[256,1024]{1,0:T(8,128)(2,1)S(1)}, u32[]{:S(2)}) copy-start(bf16[256,1024]{1,0:T(8,128)(2,1)S(1)} %get-tuple-element.11) | copy-start | bytes 1572868
  47.2 21.7 %all-to-all-start.1 = ((bf16[16,16,1024]{2,1,0:T(8,128)(2,1)}), bf16[16,16,1024]{2,1,0:T(8,128)(2,1)S(1)}, u32[]{:S(2)}, u32[]{:S(2)}) async-start(bf16[16,16,1024]{2,1,0:T(8,128)(2,1)} %copy.32), calls=%async_computation.1 | async-start | bytes 1048576 | tf_op jit(solution)/shard_map/all_to_all | solution.py:252
  73.6 2.2 %copy-start.1 = (bf16[1024,16,128]{2,1,0:T(8,128)(2,1)S(1)}, bf16[1024,16,128]{2,1,0:T(8,128)(2,1)}, u32[]{:S(2)}) copy-start(bf16[1024,16,128]{2,1,0:T(8,128)(2,1)} %gather_fusion) | copy-start | bytes 12582916
  78.3 18.6 %all-to-all-start.2 = ((bf16[16,16,1024]{2,1,0:T(8,128)(2,1)}), bf16[16,16,1024]{2,1,0:T(8,128)(2,1)S(1)}, u32[]{:S(2)}, u32[]{:S(2)}) async-start(bf16[16,16,1024]{2,1,0:T(8,128)(2,1)} %copy_bitcast_fusion), calls=%async_computation.2 | async-start | bytes 1048576 | tf_op jit(solution)/shard_map/all_to_all | solution.py:273

commit v20 on v17

--- a/solution.py
+++ b/solution.py
@@ -1,3 +1,5 @@
+import functools
+
 import jax
 import jax.numpy as jnp
 from jax import lax
@@ -86,7 +88,7 @@
     )
 
 
-def attend_block(counts_ref, query_ref, key_ref, value_ref, out_ref):
+def attend_block(counts_ref, query_ref, key_ref, value_ref, out_ref, all_live=False):
     group = pl.program_id(0)
     latents = query_ref.shape[1]
     tokens = key_ref.shape[1]
@@ -105,7 +107,8 @@
                 (((1,), (1,)), ((), ())),
                 preferred_element_type=jnp.float32,
             ) * HEAD_DIM ** (-0.5)
-            scores = jnp.where(live, scores, masked_score)
+            if not all_live:
+                scores = jnp.where(live, scores, masked_score)
             row_max = jnp.max(scores, axis=1, keepdims=True)
             exponent = jnp.exp(scores - row_max)
             denominator = jnp.sum(exponent, axis=1, keepdims=True)
@@ -116,11 +119,11 @@
         out_ref[0, :, cols] = jnp.where(first_head, mixes[0], mixes[1]).astype(jnp.bfloat16)
 
 
-def attend_kernel(queries, key_value, counts):
+def attend_kernel(queries, key_value, counts, all_live=False):
     groups, latents, width = queries.shape
     tokens = key_value.shape[1]
     return pl.pallas_call(
-        attend_block,
+        functools.partial(attend_block, all_live=all_live),
         grid_spec=pltpu.PrefetchScalarGridSpec(
             num_scalar_prefetch=1,
             grid=(groups,),
@@ -214,6 +217,7 @@
         queries.reshape(1, row_total, model_width),
         memory_rows,
         jnp.full((1,), memory_total, jnp.int32),
+        all_live=True,
     ).reshape(row_total, model_width)
     hidden = (
         flat_state.astype(jnp.float32)

time: 102 us -> 102 us (level)
  no operation moved by 1% of the time
where the time goes in v20:
time: 102 us; the launch traced here: 101 us
  waiting for transfers between devices  27 us (26%)
  local copies, waits for them, and re-layouts  21.8 us (21%)
  starting transfers between devices  20.6 us (20%)
  matrix products  17.6 us (17%)
  other arithmetic  9.45 us (9%)
  Pallas kernels  4.07 us (4%)
    all_to_all x1, waiting for transfers between devices, per_device(): lax.all_to_all(served_read.reshape(owners, latents, model_width), 'smp',...  14.4 us
    all_to_all x1, waiting for transfers between devices, per_device(): lax.all_to_all(jnp.concatenate([jnp.broadcast_to(memory_pair[None], (owne...  12.5 us
    gather x1, local copies, waits for them, and re-layouts, per_device(): kv_rows = kv_table[served_index]  9.97 us
    all_to_all x1, starting transfers between devices, per_device(): lax.all_to_all(jnp.concatenate([jnp.broadcast_to(memory_pair[None], (owne...  7.39 us
    all_to_all x1, starting transfers between devices, per_device(): lax.all_to_all(jnp.einsum('ob,bld->old', (sample_pick[:, None] == jnp.ara...  7.19 us
    all_to_all x1, starting transfers between devices, per_device(): lax.all_to_all(served_read.reshape(owners, latents, model_width), 'smp',...  6.01 us
    dot_general x1, matrix products, per_device(): jnp.dot(panel_normed, kv_weight, preferred_element_type=jnp.float32)  4.93 us
    slice x1, local copies, waits for them, and re-layouts, per_device(): key_rows = kv_rows[:, :, :head_count // 2]  4.65 us
  transfers between devices with their start and end apart: 3, of which 2 were waited for; matrix products, arithmetic and copies ran while one was open for 27% of the time, Pallas kernels for 0%

profile of v20, /device:TPU:0, one launch (start us, length us, event | category | flops | bytes accessed | tf_op | source)
XLA Modules:
  0.0 100.7 jit_solution(15214696588198927829)
XLA Ops:
  0.0 0.0 copy-start
  0.0 1.0 select_reduce_fusion.5
  1.0 0.9 select_reduce_fusion.2
  1.9 0.1 copy.30
  2.0 0.9 add_select_fusion.2
  2.9 0.1 select_reduce_fusion.1
  3.0 0.1 fusion.34
  3.1 0.1 fusion.33
  3.2 0.8 pad_maximum_fusion.1
  4.0 0.1 broadcast_in_dim.132
  4.1 1.1 %pad_maximum_fusion = bf16[16,16,2176]{2,1,0:T(8,128)(2,1)} fusion(bf16[16,16,128]{2,1,0:T(8,128)(2,1)S(1)} %bitcast.93, bf16[16,16,2048]{2,1,0:T(8,128)(2,1)S(1)} %broadcast_in_dim.132), kind=kLoop, calls=%fused_computation.29 | loop fusion | flops 2228224 | bytes 2228224 | tf_op jit(solution)/shard_map/concatenate | solution.py:197
  5.2 7.4 %all-to-all-start = ((bf16[16,16,2176]{2,1,0:T(8,128)(2,1)}), bf16[16,16,2176]{2,1,0:T(8,128)(2,1)S(1)}, u32[]{:S(2)}, u32[]{:S(2)}) async-start(bf16[16,16,2176]{2,1,0:T(8,128)(2,1)} %pad_maximum_fusion), calls=%async_computation | async-start | bytes 2228224 | tf_op jit(solution)/shard_map/all_to_all | solution.py:196
  12.6 1.2 %multiply_reduce_fusion = f32[16,16]{1,0:T(8,128)S(1)} fusion(bf16[16,16,1024]{2,1,0:T(8,128)(2,1)} %param.14), kind=kLoop, calls=%fused_computation.40 | loop fusion | flops 786176 | bytes 525312 | tf_op jit(solution)/shard_map/reduce_sum | solution.py:18
  13.8 0.1 rsqrt.28
  13.9 1.5 %fusion = f32[512]{0:T(512)S(1)} fusion(bf16[1,512,1024]{2,1,0:T(8,128)(2,1)} %param.20), kind=kLoop, calls=%fused_computation.5 | loop fusion | flops 1572352 | bytes 1050624 | tf_op jit(solution)/shard_map/reduce_sum | solution.py:18
  15.4 4.9 %fusion.5 = bf16[64,8,16,128]{3,1,2,0:T(8,128)(2,1)S(1)} fusion(bf16[1024,2048]{1,0:T(8,128)(2,1)} %param.25, bf16[1,512,1024]{2,1,0:T(8,128)(2,1)} %param.20, f32[512]{0:T(512)S(1)} %add_rsqrt_fusion.1), kind=kOutput, calls=%fused_computation.16 | convolution fusion | flops 2150105088 | bytes 7342080 | tf_op jit(solution)/shard_map/dot_general | solution.py:179
  20.4 0.0 copy-start.2
  20.4 0.0 copy-start.4
  20.4 2.0 %copy.45 = bf16[64,8,16,128]{3,2,1,0:T(8,128)(2,1)} copy(bf16[64,8,16,128]{3,1,2,0:T(8,128)(2,1)S(1)} %fusion.5) | data formatting | bytes 4194304
  22.4 0.0 copy-done.2
  22.4 0.2 fusion.16
  22.6 0.0 copy-done.4
  22.6 1.5 %fusion.10.query_ref = bf16[1,256,1024]{2,1,0:T(8,128)(2,1)} fusion(bf16[256,1024]{1,0:T(8,128)(2,1)S(1)} %fusion.16, bf16[1024,1024]{1,0:T(8,128)(2,1)S(1)} %copy-done.4), kind=kOutput, calls=%fused_computation.28 | convolution fusion | flops 537133056 | bytes 3145728 | tf_op jit(solution)/shard_map/dot_general | solution.py:186
  24.1 12.5 %all-to-all-done = bf16[16,16,2176]{2,1,0:T(8,128)(2,1)S(1)} async-done(((bf16[16,16,2176]{2,1,0:T(8,128)(2,1)}), bf16[16,16,2176]{2,1,0:T(8,128)(2,1)S(1)}, u32[]{:S(2)}, u32[]{:S(2)}) %all-to-all-start) | async-done | bytes 1114144 | tf_op jit(solution)/shard_map/all_to_all | solution.py:196
  36.6 0.0 copy-start.1
  36.6 1.0 copy-done.1
  37.6 4.1 %shard_map.136 = bf16[1,256,1024]{2,1,0:T(8,128)(2,1)} custom-call(s32[1]{0:T(128)} %constant.85.clone.1.counts_ref, bf16[1,256,1024]{2,1,0:T(8,128)(2,1)} %fusion.10.query_ref, bf16[1,256,2176]{2,1,0:T(8,128)(2,1)} %bitcast.88, bf16[1,256,2176]{2,1,0:T(8,128)(2,1)} %bitcast.89), custom_call_target="tpu_custom_call" | custom-call | tf_op jit(solution)/shard_map/pallas_call | solution.py:125
  41.7 0.0 copy-done
  41.7 0.0 copy-start.5
  41.7 2.2 %fusion.11 = (f32[256]{0:T(256)S(1)}, bf16[256,1024]{1,0:T(8,128)(2,1)S(1)}) fusion(bf16[1024,1024]{1,0:T(8,128)(2,1)S(1)} %copy-done, bf16[1,256,1024]{2,1,0:T(8,128)(2,1)} %shard_map.136, bf16[256,1024]{1,0:T(8,128)(2,1)} %bitcast.90), kind=kOutput, calls=%fused_computation.30 | convolution fusion | flops 538443520 | bytes 3671040 | tf_op jit(solution)/shard_map/dot_general | solution.py:224
  43.9 0.0 copy-start.6
  43.9 0.0 copy-done.5
  43.9 0.8 convolution_convert_fusion.2
  44.7 0.5 convolution_convert_fusion.1
  45.1 0.0 copy-done.6
  45.1 1.1 %copy.33 = bf16[16,16,1024]{2,1,0:T(8,128)(2,1)} copy(bf16[16,16,1024]{2,0,1:T(8,128)(2,1)S(1)} %convolution_convert_fusion.1) | data formatting | bytes 1048576 | tf_op jit(solution)/shard_map/convert_element_type | solution.py:238
  46.2 7.2 %all-to-all-start.1 = ((bf16[16,16,1024]{2,1,0:T(8,128)(2,1)}), bf16[16,16,1024]{2,1,0:T(8,128)(2,1)S(1)}, u32[]{:S(2)}, u32[]{:S(2)}) async-start(bf16[16,16,1024]{2,1,0:T(8,128)(2,1)} %copy.33), calls=%async_computation.1 | async-start | bytes 1048576 | tf_op jit(solution)/shard_map/all_to_all | solution.py:230
  53.4 0.8 slice.36
  54.3 0.1 slice_add_fusion
  54.4 0.1 reshape.250
  54.5 10.0 %gather_fusion = bf16[1024,16,128]{2,1,0:T(8,128)(2,1)} fusion(bf16[512,16,128]{2,1,0:T(8,128)(2,1)} %bitcast.86, s32[1024]{0:T(1024)S(1)} %broadcast_clamp_fusion), kind=kCustom, calls=%fused_computation | custom fusion | bytes 8392704 | tf_op jit(solution)/shard_map/gather | solution.py:244
  64.4 0.2 slice_reduce_fusion
  64.6 0.1 iota_compare_fusion.2
  64.7 4.7 %fusion.45 = (bf16[16,64,8,128]{3,2,1,0:T(8,128)(2,1)}, bf16[16,64,8,128]{3,2,1,0:T(8,128)(2,1)}) fusion(bf16[16,64,16,128]{3,2,1,0:T(8,128)(2,1)} %bitcast.87), kind=kLoop, calls=%fused_computation.105 | loop fusion | bytes 8388608 | tf_op jit(solution)/shard_map/slice | solution.py:245
  69.3 0.0 all-to-all-done.1
  69.3 0.1 copy_bitcast_fusion.7
  69.4 3.0 %bitcast_reduce_fusion = (f32[16,8,2,16]{3,2,1,0:T(2,128)S(1)}, f32[16,8,64,16,2]{2,3,4,1,0:T(8,128)S(1)}) fusion(pred[16,64]{1,0:T(8,128)(4,1)S(1)} %iota_compare_fusion.2, pred[2,128]{1,0:T(4,128)(4,1)S(1)} %iota_compare_fusion.6, bf16[16,16,8,128]{3,1,2,0:T(8,128)(2,1)S(1)} %copy_bitcast_fusion.7, bf16[16,64,8,128]{3,2,1,0:T(8,128)(2,1)} %get-tuple-element.8), kind=kOutput, calls=%fused_computation.12 | convolution fusion | flops 68415488 | bytes 3687680 | tf_op jit(solution)/shard_map/blqje,btqe->bqjlt/dot_general | solution.py:72
  72.4 0.0 copy-start.3
  72.4 1.4 %fusion.6 = f32[16,8,2,16]{3,2,1,0:T(2,128)S(1)} fusion(f32[16,8,64,16,2]{2,3,4,1,0:T(8,128)S(1)} %get-tuple-element.15, f32[16,8,2,16]{3,2,1,0:T(2,128)S(1)} %get-tuple-element.14, pred[16,64]{1,0:T(8,128)(4,1)S(1)} %iota_compare_fusion.2), kind=kLoop, calls=%fused_computation.17 | loop fusion | flops 1044480 | bytes 1082368 | tf_op jit(solution)/shard_map/reduce_sum | solution.py:78
  73.8 0.2 copy-done.3
  74.0 1.6 %select_reduce_fusion = bf16[16,8,16,128]{3,2,1,0:T(8,128)(2,1)S(1)} fusion(bf16[16,64,8,128]{3,2,1,0:T(8,128)(2,1)S(1)} %copy-done.3, f32[16,8,64,16,2]{2,3,4,1,0:T(8,128)S(1)} %get-tuple-element.15, f32[16,8,2,16]{3,2,1,0:T(2,128)S(1)} %fusion.6, f32[16,8,2,16]{3,2,1,0:T(2,128)S(1)} %get-tuple-element.14, pred[16,64]{1,0:T(8,128)(4,1)S(1)} %iota_compare_fusion.2, ...), kind=kOutput, calls=%fused_computation.14 | convolution fusion | flops 69468160 | bytes 3704064 | tf_op jit(solution)/shard_map/bqjlt,btqe->bqjle/dot_general | solution.py:79
  75.6 0.9 copy_bitcast_fusion.6
  76.4 6.0 %all-to-all-start.2 = ((bf16[16,16,1024]{2,1,0:T(8,128)(2,1)}), bf16[16,16,1024]{2,1,0:T(8,128)(2,1)S(1)}, u32[]{:S(2)}, u32[]{:S(2)}) async-start(bf16[16,16,1024]{2,1,0:T(8,128)(2,1)} %copy_bitcast_fusion.6), calls=%async_computation.2 | async-start | bytes 1048576 | tf_op jit(solution)/shard_map/all_to_all | solution.py:254
  82.5 14.4 %all-to-all-done.2 = bf16[16,16,1024]{2,1,0:T(8,128)(2,1)S(1)} async-done(((bf16[16,16,1024]{2,1,0:T(8,128)(2,1)}), bf16[16,16,1024]{2,1,0:T(8,128)(2,1)S(1)}, u32[]{:S(2)}, u32[]{:S(2)}) %all-to-all-start.2) | async-done | bytes 524320 | tf_op jit(solution)/shard_map/all_to_all | solution.py:254
  96.9 0.6 gather_fusion.1
  97.5 3.2 %fusion.8 = bf16[256,1024]{1,0:T(8,128)(2,1)} fusion(bf16[256,1024]{1,0:T(8,128)(2,1)S(1)} %bitcast.92, bf16[1024,1024]{1,0:T(8,128)(2,1)} %param.27, bf16[256,1024]{1,0:T(8,128)(2,1)} %copy-done.6), kind=kOutput, calls=%fused_computation.23 | convolution fusion | flops 537657344 | bytes 3670016 | tf_op jit(solution)/shard_map/dot_general | solution.py:261
  (16 shorter events, 0.1 us)
Async XLA Ops:
  0.0 41.7 %copy-start = (bf16[1024,1024]{1,0:T(8,128)(2,1)S(1)}, bf16[1024,1024]{1,0:T(8,128)(2,1)}, u32[]{:S(2)}) copy-start(bf16[1024,1024]{1,0:T(8,128)(2,1)} %param.24) | copy-start | bytes 6291460
  5.2 31.4 %all-to-all-start = ((bf16[16,16,2176]{2,1,0:T(8,128)(2,1)}), bf16[16,16,2176]{2,1,0:T(8,128)(2,1)S(1)}, u32[]{:S(2)}, u32[]{:S(2)}) async-start(bf16[16,16,2176]{2,1,0:T(8,128)(2,1)} %pad_maximum_fusion), calls=%async_computation | async-start | bytes 2228224 | tf_op jit(solution)/shard_map/all_to_all | solution.py:196
  20.4 2.0 %copy-start.2 = (bf16[16,16,1024]{2,1,0:T(8,128)(2,1)S(1)}, bf16[16,16,1024]{2,1,0:T(8,128)(2,1)}, u32[]{:S(2)}) copy-start(bf16[16,16,1024]{2,1,0:T(8,128)(2,1)} %param.14) | copy-start | bytes 1572868
  20.4 2.2 %copy-start.4 = (bf16[1024,1024]{1,0:T(8,128)(2,1)S(1)}, bf16[1024,1024]{1,0:T(8,128)(2,1)}, u32[]{:S(2)}) copy-start(bf16[1024,1024]{1,0:T(8,128)(2,1)} %param.23) | copy-start | bytes 6291460
  36.6 1.0 copy-start.1
  41.7 2.2 %copy-start.5 = (bf16[1024,1024]{1,0:T(8,128)(2,1)S(1)}, bf16[1024,1024]{1,0:T(8,128)(2,1)}, u32[]{:S(2)}) copy-start(bf16[1024,1024]{1,0:T(8,128)(2,1)} %param.26) | copy-start | bytes 6291460
  43.9 1.3 %copy-start.6 = (bf16[256,1024]{1,0:T(8,128)(2,1)}, bf16[256,1024]{1,0:T(8,128)(2,1)S(1)}, u32[]{:S(2)}) copy-start(bf16[256,1024]{1,0:T(8,128)(2,1)S(1)} %get-tuple-element.13) | copy-start | bytes 1572868
  46.2 23.1 %all-to-all-start.1 = ((bf16[16,16,1024]{2,1,0:T(8,128)(2,1)}), bf16[16,16,1024]{2,1,0:T(8,128)(2,1)S(1)}, u32[]{:S(2)}, u32[]{:S(2)}) async-start(bf16[16,16,1024]{2,1,0:T(8,128)(2,1)} %copy.33), calls=%async_computation.1 | async-start | bytes 1048576 | tf_op jit(solution)/shard_map/all_to_all | solution.py:230
  72.4 1.6 %copy-start.3 = (bf16[16,64,8,128]{3,2,1,0:T(8,128)(2,1)S(1)}, bf16[16,64,8,128]{3,2,1,0:T(8,128)(2,1)}, u32[]{:S(2)}) copy-start(bf16[16,64,8,128]{3,2,1,0:T(8,128)(2,1)} %get-tuple-element.9) | copy-start | bytes 6291460
  76.4 20.5 %all-to-all-start.2 = ((bf16[16,16,1024]{2,1,0:T(8,128)(2,1)}), bf16[16,16,1024]{2,1,0:T(8,128)(2,1)S(1)}, u32[]{:S(2)}, u32[]{:S(2)}) async-start(bf16[16,16,1024]{2,1,0:T(8,128)(2,1)} %copy_bitcast_fusion.6), calls=%async_computation.2 | async-start | bytes 1048576 | tf_op jit(solution)/shard_map/all_to_all | solution.py:254

commit v21 on v17

--- a/solution.py
+++ b/solution.py
@@ -178,8 +178,14 @@
     )
     panel_total = kv_flat.shape[0]
     kv_table = kv_flat.reshape(panel_total, head_count, 2 * HEAD_DIM)
-    row_total = local_samples * latents
-    flat_state = state.reshape(row_total, model_width)
+    slot_onehot = (
+        sample_pick[:, None] == jnp.arange(local_samples, dtype=jnp.int32)[None, :]
+    ).astype(jnp.bfloat16)
+    slot_state = jnp.einsum(
+        "ob,bld->old", slot_onehot, state, preferred_element_type=jnp.float32
+    ).astype(jnp.bfloat16)
+    row_total = owners * latents
+    flat_state = slot_state.reshape(row_total, model_width)
     queries = jnp.dot(normed(flat_state), q1_weight, preferred_element_type=jnp.float32).astype(
         jnp.bfloat16
     )
@@ -222,16 +228,8 @@
     queries2 = jnp.dot(normed(hidden), q2_weight, preferred_element_type=jnp.float32).astype(
         jnp.bfloat16
     )
-    queries2 = queries2.reshape(local_samples, latents, model_width)
     served_queries = lax.all_to_all(
-        jnp.einsum(
-            "ob,bld->old",
-            (sample_pick[:, None] == jnp.arange(local_samples, dtype=jnp.int32)[None, :]).astype(
-                jnp.bfloat16
-            ),
-            queries2,
-            preferred_element_type=jnp.float32,
-        ).astype(jnp.bfloat16),
+        queries2.reshape(owners, latents, model_width),
         "smp",
         split_axis=0,
         concat_axis=0,
@@ -253,11 +251,14 @@
         split_axis=0,
         concat_axis=0,
         tiled=True,
-    )[owner_rank]
-    result = hidden.astype(jnp.float32) + jnp.dot(
-        read_spike.reshape(row_total, model_width), o2_weight, preferred_element_type=jnp.float32
-    )
-    return result.astype(jnp.bfloat16).reshape(local_samples, latents, model_width)
+    )
+    result = (
+        hidden.astype(jnp.float32)
+        + jnp.dot(
+            read_spike.reshape(row_total, model_width), o2_weight, preferred_element_type=jnp.float32
+        )
+    ).astype(jnp.bfloat16)
+    return result.reshape(owners, latents, model_width)[owner_rank]
 
 
 def solution(mesh):

time: 102 us -> 103 us (level)
  local copies, waits for them, and re-layouts: 21.8 us -> 24.7 us
  waiting for transfers between devices: 27 us -> 24.5 us
  matrix products: 17.6 us -> 19.5 us
  other arithmetic: 9.45 us -> 8.19 us
    all_to_all x1, waiting for transfers between devices: 12.5 us -> 10 us  [per_device(): lax.all_to_all(jnp.concatenate([jnp.broadcast_to(memory_pair[None], (owne...]
    gather x1, local copies, waits for them, and re-layouts: 0.58 us -> 2.41 us  [per_device(): return result.reshape(owners, latents, model_width)[owner_rank]]
    reduce_sum x2 -> x1, other arithmetic: 2.73 us -> 1.51 us  [normed(): jnp.mean(wide * wide, axis=-1, keepdims=True) + 1e-05]
    dot_general x1, matrix products: 0.46 us -> 1.57 us  [per_device(): jnp.einsum('ob,bld->old', slot_onehot, state, preferred_element_type=jnp....]
    unnamed x17 -> x15, local copies, waits for them, and re-layouts: 3.19 us -> 3.64 us
  transfers between devices with their start and end apart: 3 -> 3, of which waited for: 2 -> 2; matrix products, arithmetic and copies ran while one was open for 27% -> 29% of each run, Pallas kernels for 0% -> 0%
where the time goes in v21:
time: 103 us; the launch traced here: 102 us
  local copies, waits for them, and re-layouts  24.7 us (24%)
  waiting for transfers between devices  24.5 us (24%)
  starting transfers between devices  20.6 us (20%)
  matrix products  19.5 us (19%)
  other arithmetic  8.19 us (8%)
  Pallas kernels  4.12 us (4%)
    all_to_all x1, waiting for transfers between devices, per_device(): lax.all_to_all(served_read.reshape(owners, latents, model_width), 'smp',...  14.4 us
    all_to_all x1, waiting for transfers between devices, per_device(): lax.all_to_all(jnp.concatenate([jnp.broadcast_to(memory_pair[None], (owne...  10 us
    gather x1, local copies, waits for them, and re-layouts, per_device(): kv_rows = kv_table[served_index]  9.97 us
    all_to_all x1, starting transfers between devices, per_device(): lax.all_to_all(jnp.concatenate([jnp.broadcast_to(memory_pair[None], (owne...  7.39 us
    all_to_all x1, starting transfers between devices, per_device(): lax.all_to_all(queries2.reshape(owners, latents, model_width), 'smp', spl...  7.18 us
    all_to_all x1, starting transfers between devices, per_device(): lax.all_to_all(served_read.reshape(owners, latents, model_width), 'smp',...  6.01 us
    dot_general x1, matrix products, per_device(): jnp.dot(panel_normed, kv_weight, preferred_element_type=jnp.float32)  4.93 us
    slice x1, local copies, waits for them, and re-layouts, per_device(): key_rows = kv_rows[:, :, :head_count // 2]  4.65 us
  transfers between devices with their start and end apart: 3, of which 2 were waited for; matrix products, arithmetic and copies ran while one was open for 29% of the time, Pallas kernels for 0%

profile of v21, /device:TPU:0, one launch (start us, length us, event | category | flops | bytes accessed | tf_op | source)
XLA Modules:
  0.0 101.8 jit_solution(16808901876321416200)
XLA Ops:
  0.0 0.0 copy-start
  0.0 1.0 select_reduce_fusion.5
  1.0 0.9 select_reduce_fusion.4
  1.9 0.1 copy.42
  2.0 0.9 add_select_fusion.2
  2.9 0.1 select_reduce_fusion.1
  3.0 0.1 fusion.35
  3.1 0.1 fusion.34
  3.2 0.8 pad_maximum_fusion.1
  4.0 0.1 broadcast_in_dim.134
  4.1 1.1 %pad_maximum_fusion = bf16[16,16,2176]{2,1,0:T(8,128)(2,1)} fusion(bf16[16,16,128]{2,1,0:T(8,128)(2,1)S(1)} %bitcast.95, bf16[16,16,2048]{2,1,0:T(8,128)(2,1)S(1)} %broadcast_in_dim.134), kind=kLoop, calls=%fused_computation.30 | loop fusion | flops 2228224 | bytes 2228224 | tf_op jit(solution)/shard_map/concatenate | solution.py:200
  5.2 7.4 %all-to-all-start = ((bf16[16,16,2176]{2,1,0:T(8,128)(2,1)}), bf16[16,16,2176]{2,1,0:T(8,128)(2,1)S(1)}, u32[]{:S(2)}, u32[]{:S(2)}) async-start(bf16[16,16,2176]{2,1,0:T(8,128)(2,1)} %pad_maximum_fusion), calls=%async_computation | async-start | bytes 2228224 | tf_op jit(solution)/shard_map/all_to_all | solution.py:199
  12.6 1.6 %multiply_reduce_fusion = (f32[16,16]{0,1:T(8,128)S(1)}, f32[16,16,1024]{2,0,1:T(8,128)S(1)}) fusion(bf16[16,16,1024]{2,1,0:T(8,128)(2,1)} %param.14, s32[16]{0:T(128)S(1)} %get-tuple-element.5), kind=kOutput, calls=%fused_computation.41 | convolution fusion | flops 9437184 | bytes 1573952 | tf_op jit(solution)/shard_map/ob,bld->old/dot_general | solution.py:184
  14.2 1.6 %copy.40 = f32[16,16,1024]{2,1,0:T(8,128)} copy(f32[16,16,1024]{2,0,1:T(8,128)S(1)} %get-tuple-element.13) | data formatting | bytes 2097152 | tf_op jit(solution)/shard_map/convert_element_type | solution.py:225
  15.8 0.1 copy.41
  15.9 0.1 rsqrt.28
  16.0 1.5 %fusion = f32[512]{0:T(512)S(1)} fusion(bf16[1,512,1024]{2,1,0:T(8,128)(2,1)} %param.20), kind=kLoop, calls=%fused_computation.5 | loop fusion | flops 1572352 | bytes 1050624 | tf_op jit(solution)/shard_map/reduce_sum | solution.py:16
  17.5 4.9 %fusion.5 = bf16[64,8,16,128]{3,1,2,0:T(8,128)(2,1)S(1)} fusion(bf16[1024,2048]{1,0:T(8,128)(2,1)} %param.25, bf16[1,512,1024]{2,1,0:T(8,128)(2,1)} %param.20, f32[512]{0:T(512)S(1)} %add_rsqrt_fusion.1), kind=kOutput, calls=%fused_computation.16 | convolution fusion | flops 2150105088 | bytes 7342080 | tf_op jit(solution)/shard_map/dot_general | solution.py:176
  22.4 0.0 copy-start.2
  22.4 0.0 copy-start.4
  22.4 2.0 %copy.55 = bf16[64,8,16,128]{3,2,1,0:T(8,128)(2,1)} copy(bf16[64,8,16,128]{3,1,2,0:T(8,128)(2,1)S(1)} %fusion.5) | data formatting | bytes 4194304
  24.4 0.0 copy-done.2
  24.4 0.1 fusion.17
  24.6 0.5 copy-done.4
  25.0 1.5 %fusion.11.query_ref = bf16[1,256,1024]{2,1,0:T(8,128)(2,1)} fusion(bf16[256,1024]{1,0:T(8,128)(2,1)S(1)} %fusion.17, bf16[1024,1024]{1,0:T(8,128)(2,1)S(1)} %copy-done.4), kind=kOutput, calls=%fused_computation.29 | convolution fusion | flops 537133056 | bytes 3145728 | tf_op jit(solution)/shard_map/dot_general | solution.py:189
  26.6 10.0 %all-to-all-done = bf16[16,16,2176]{2,1,0:T(8,128)(2,1)S(1)} async-done(((bf16[16,16,2176]{2,1,0:T(8,128)(2,1)}), bf16[16,16,2176]{2,1,0:T(8,128)(2,1)S(1)}, u32[]{:S(2)}, u32[]{:S(2)}) %all-to-all-start) | async-done | bytes 1114144 | tf_op jit(solution)/shard_map/all_to_all | solution.py:199
  36.6 0.0 copy-start.1
  36.6 1.0 copy-done.1
  37.6 4.1 %shard_map.136 = bf16[1,256,1024]{2,1,0:T(8,128)(2,1)} custom-call(s32[1]{0:T(128)} %constant.86.clone.1.counts_ref, bf16[1,256,1024]{2,1,0:T(8,128)(2,1)} %fusion.11.query_ref, bf16[1,256,2176]{2,1,0:T(8,128)(2,1)} %bitcast.89, bf16[1,256,2176]{2,1,0:T(8,128)(2,1)} %bitcast.90), custom_call_target="tpu_custom_call" | custom-call | tf_op jit(solution)/shard_map/pallas_call | solution.py:122
  41.7 0.0 copy-done
  41.7 0.0 copy-start.5
  41.7 2.3 %fusion.12 = (f32[256]{0:T(256)S(1)}, bf16[256,1024]{1,0:T(8,128)(2,1)S(1)}) fusion(f32[256,1024]{1,0:T(8,128)} %bitcast.91, bf16[1024,1024]{1,0:T(8,128)(2,1)S(1)} %copy-done, bf16[1,256,1024]{2,1,0:T(8,128)(2,1)} %shard_map.136), kind=kOutput, calls=%fused_computation.31 | convolution fusion | flops 538181376 | bytes 4195328 | tf_op jit(solution)/shard_map/dot_general | solution.py:226
  44.1 0.0 copy-done.5
  44.1 1.6 %convolution_convert_fusion.1 = bf16[256,1024]{1,0:T(8,128)(2,1)} fusion(bf16[1024,1024]{1,0:T(8,128)(2,1)S(1)} %copy-done.5, bf16[256,1024]{1,0:T(8,128)(2,1)S(1)} %get-tuple-element.15, f32[256]{0:T(256)S(1)} %add_rsqrt_fusion.2), kind=kOutput, calls=%fused_computation.24 | convolution fusion | flops 537919488 | bytes 3146752 | tf_op jit(solution)/shard_map/dot_general | solution.py:228
  45.6 7.2 %all-to-all-start.1 = ((bf16[16,16,1024]{2,1,0:T(8,128)(2,1)}), bf16[16,16,1024]{2,1,0:T(8,128)(2,1)S(1)}, u32[]{:S(2)}, u32[]{:S(2)}) async-start(bf16[16,16,1024]{2,1,0:T(8,128)(2,1)} %bitcast.92), calls=%async_computation.1 | async-start | bytes 1048576 | tf_op jit(solution)/shard_map/all_to_all | solution.py:231
  52.8 0.8 slice.36
  53.7 0.1 slice_add_fusion
  53.8 0.1 reshape.250
  53.9 10.0 %gather_fusion = bf16[1024,16,128]{2,1,0:T(8,128)(2,1)} fusion(bf16[512,16,128]{2,1,0:T(8,128)(2,1)} %bitcast.87, s32[1024]{0:T(1024)S(1)} %broadcast_clamp_fusion), kind=kCustom, calls=%fused_computation | custom fusion | bytes 8392704 | tf_op jit(solution)/shard_map/gather | solution.py:238
  63.9 0.2 slice_reduce_fusion
  64.0 0.1 iota_compare_fusion.1
  64.1 4.7 %fusion.46 = (bf16[16,64,8,128]{3,2,1,0:T(8,128)(2,1)}, bf16[16,64,8,128]{3,2,1,0:T(8,128)(2,1)}) fusion(bf16[16,64,16,128]{3,2,1,0:T(8,128)(2,1)} %bitcast.88), kind=kLoop, calls=%fused_computation.106 | loop fusion | bytes 8388608 | tf_op jit(solution)/shard_map/slice | solution.py:239
  68.8 0.0 all-to-all-done.1
  68.8 0.1 copy_bitcast_fusion.7
  68.9 3.0 %bitcast_reduce_fusion = (f32[16,8,2,16]{3,2,1,0:T(2,128)S(1)}, f32[16,8,64,16,2]{2,3,4,1,0:T(8,128)S(1)}) fusion(pred[16,64]{1,0:T(8,128)(4,1)S(1)} %iota_compare_fusion.1, pred[2,128]{1,0:T(4,128)(4,1)S(1)} %iota_compare_fusion.6, bf16[16,16,8,128]{3,1,2,0:T(8,128)(2,1)S(1)} %copy_bitcast_fusion.7, bf16[16,64,8,128]{3,2,1,0:T(8,128)(2,1)} %get-tuple-element.8), kind=kOutput, calls=%fused_computation.12 | convolution fusion | flops 68415488 | bytes 3687680 | tf_op jit(solution)/shard_map/blqje,btqe->bqjlt/dot_general | solution.py:70
  71.8 0.0 copy-start.3
  71.8 1.4 %fusion.6 = f32[16,8,2,16]{3,2,1,0:T(2,128)S(1)} fusion(f32[16,8,64,16,2]{2,3,4,1,0:T(8,128)S(1)} %get-tuple-element.17, f32[16,8,2,16]{3,2,1,0:T(2,128)S(1)} %get-tuple-element.16, pred[16,64]{1,0:T(8,128)(4,1)S(1)} %iota_compare_fusion.1), kind=kLoop, calls=%fused_computation.17 | loop fusion | flops 1044480 | bytes 1082368 | tf_op jit(solution)/shard_map/reduce_sum | solution.py:76
  73.2 0.2 copy-done.3
  73.4 1.6 %select_reduce_fusion = bf16[16,8,16,128]{3,2,1,0:T(8,128)(2,1)S(1)} fusion(bf16[16,64,8,128]{3,2,1,0:T(8,128)(2,1)S(1)} %copy-done.3, f32[16,8,64,16,2]{2,3,4,1,0:T(8,128)S(1)} %get-tuple-element.17, f32[16,8,2,16]{3,2,1,0:T(2,128)S(1)} %fusion.6, f32[16,8,2,16]{3,2,1,0:T(2,128)S(1)} %get-tuple-element.16, pred[16,64]{1,0:T(8,128)(4,1)S(1)} %iota_compare_fusion.1, ...), kind=kOutput, calls=%fused_computation.14 | convolution fusion | flops 69468160 | bytes 3704064 | tf_op jit(solution)/shard_map/bqjlt,btqe->bqjle/dot_general | solution.py:77
  75.0 0.9 copy_bitcast_fusion.6
  75.8 6.0 %all-to-all-start.2 = ((bf16[16,16,1024]{2,1,0:T(8,128)(2,1)}), bf16[16,16,1024]{2,1,0:T(8,128)(2,1)S(1)}, u32[]{:S(2)}, u32[]{:S(2)}) async-start(bf16[16,16,1024]{2,1,0:T(8,128)(2,1)} %copy_bitcast_fusion.6), calls=%async_computation.2 | async-start | bytes 1048576 | tf_op jit(solution)/shard_map/all_to_all | solution.py:248
  81.9 14.4 %all-to-all-done.2 = bf16[16,16,1024]{2,1,0:T(8,128)(2,1)S(1)} async-done(((bf16[16,16,1024]{2,1,0:T(8,128)(2,1)}), bf16[16,16,1024]{2,1,0:T(8,128)(2,1)S(1)}, u32[]{:S(2)}, u32[]{:S(2)}) %all-to-all-start.2) | async-done | bytes 524320 | tf_op jit(solution)/shard_map/all_to_all | solution.py:248
  96.3 3.1 %fusion.8 = bf16[256,1024]{1,0:T(8,128)(2,1)} fusion(bf16[256,1024]{1,0:T(8,128)(2,1)S(1)} %bitcast.93, bf16[1024,1024]{1,0:T(8,128)(2,1)} %param.27, bf16[256,1024]{1,0:T(8,128)(2,1)S(1)} %get-tuple-element.15), kind=kOutput, calls=%fused_computation.23 | convolution fusion | flops 537657344 | bytes 3670016 | tf_op jit(solution)/shard_map/dot_general | solution.py:257
  99.4 2.4 %gather_fusion.1 = bf16[16,16,1024]{2,1,0:T(8,128)(2,1)} fusion(bf16[16,16,1024]{2,1,0:T(8,128)(2,1)} %bitcast.94, s32[1024]{0:T(1024)S(1)} %pad_clamp_fusion), kind=kCustom, calls=%fused_computation.1 | custom fusion | bytes 1048640 | tf_op jit(solution)/shard_map/gather | solution.py:261
  (16 shorter events, 0.1 us)
Async XLA Ops:
  0.0 41.7 %copy-start = (bf16[1024,1024]{1,0:T(8,128)(2,1)S(1)}, bf16[1024,1024]{1,0:T(8,128)(2,1)}, u32[]{:S(2)}) copy-start(bf16[1024,1024]{1,0:T(8,128)(2,1)} %param.24) | copy-start | bytes 6291460
  5.2 31.4 %all-to-all-start = ((bf16[16,16,2176]{2,1,0:T(8,128)(2,1)}), bf16[16,16,2176]{2,1,0:T(8,128)(2,1)S(1)}, u32[]{:S(2)}, u32[]{:S(2)}) async-start(bf16[16,16,2176]{2,1,0:T(8,128)(2,1)} %pad_maximum_fusion), calls=%async_computation | async-start | bytes 2228224 | tf_op jit(solution)/shard_map/all_to_all | solution.py:199
  22.4 2.0 %copy-start.2 = (f32[16,16,1024]{2,1,0:T(8,128)S(1)}, f32[16,16,1024]{2,1,0:T(8,128)}, u32[]{:S(2)}) copy-start(f32[16,16,1024]{2,1,0:T(8,128)} %copy.40) | copy-start | bytes 3145732
  22.4 2.6 %copy-start.4 = (bf16[1024,1024]{1,0:T(8,128)(2,1)S(1)}, bf16[1024,1024]{1,0:T(8,128)(2,1)}, u32[]{:S(2)}) copy-start(bf16[1024,1024]{1,0:T(8,128)(2,1)} %param.23) | copy-start | bytes 6291460
  36.6 1.0 copy-start.1
  41.7 2.3 %copy-start.5 = (bf16[1024,1024]{1,0:T(8,128)(2,1)S(1)}, bf16[1024,1024]{1,0:T(8,128)(2,1)}, u32[]{:S(2)}) copy-start(bf16[1024,1024]{1,0:T(8,128)(2,1)} %param.26) | copy-start | bytes 6291460
  45.6 23.1 %all-to-all-start.1 = ((bf16[16,16,1024]{2,1,0:T(8,128)(2,1)}), bf16[16,16,1024]{2,1,0:T(8,128)(2,1)S(1)}, u32[]{:S(2)}, u32[]{:S(2)}) async-start(bf16[16,16,1024]{2,1,0:T(8,128)(2,1)} %bitcast.92), calls=%async_computation.1 | async-start | bytes 1048576 | tf_op jit(solution)/shard_map/all_to_all | solution.py:231
  71.8 1.6 %copy-start.3 = (bf16[16,64,8,128]{3,2,1,0:T(8,128)(2,1)S(1)}, bf16[16,64,8,128]{3,2,1,0:T(8,128)(2,1)}, u32[]{:S(2)}) copy-start(bf16[16,64,8,128]{3,2,1,0:T(8,128)(2,1)} %get-tuple-element.9) | copy-start | bytes 6291460
  75.8 20.5 %all-to-all-start.2 = ((bf16[16,16,1024]{2,1,0:T(8,128)(2,1)}), bf16[16,16,1024]{2,1,0:T(8,128)(2,1)S(1)}, u32[]{:S(2)}, u32[]{:S(2)}) async-start(bf16[16,16,1024]{2,1,0:T(8,128)(2,1)} %copy_bitcast_fusion.6), calls=%async_computation.2 | async-start | bytes 1048576 | tf_op jit(solution)/shard_map/all_to_all | solution.py:248

commit v22 on v19

--- a/solution.py
+++ b/solution.py
@@ -1,3 +1,5 @@
+import functools
+
 import jax
 import jax.numpy as jnp
 from jax import lax
@@ -112,7 +114,7 @@
     )
 
 
-def attend_block(counts_ref, query_ref, key_ref, value_ref, out_ref):
+def attend_block(counts_ref, query_ref, key_ref, value_ref, out_ref, all_live=False):
     group = pl.program_id(0)
     latents = query_ref.shape[1]
     tokens = key_ref.shape[1]
@@ -131,7 +133,8 @@
                 (((1,), (1,)), ((), ())),
                 preferred_element_type=jnp.float32,
             ) * HEAD_DIM ** (-0.5)
-            scores = jnp.where(live, scores, masked_score)
+            if not all_live:
+                scores = jnp.where(live, scores, masked_score)
             row_max = jnp.max(scores, axis=1, keepdims=True)
             exponent = jnp.exp(scores - row_max)
             denominator = jnp.sum(exponent, axis=1, keepdims=True)
@@ -142,11 +145,11 @@
         out_ref[0, :, cols] = jnp.where(first_head, mixes[0], mixes[1]).astype(jnp.bfloat16)
 
 
-def attend_kernel(queries, key_value, counts):
+def attend_kernel(queries, key_value, counts, all_live=False):
     groups, latents, width = queries.shape
     tokens = key_value.shape[1]
     return pl.pallas_call(
-        attend_block,
+        functools.partial(attend_block, all_live=all_live),
         grid_spec=pltpu.PrefetchScalarGridSpec(
             num_scalar_prefetch=1,
             grid=(groups,),
@@ -240,6 +243,7 @@
         queries.reshape(1, row_total, model_width),
         memory_rows,
         jnp.full((1,), memory_total, jnp.int32),
+        all_live=True,
     ).reshape(row_total, model_width)
     hidden = (
         flat_state.astype(jnp.float32)

time: 101 us -> 101 us (level)
  no operation moved by 1% of the time
where the time goes in v22:
time: 101 us
  waiting for transfers between devices  31 us (31%)
  matrix products  19.1 us (19%)
  starting transfers between devices  18.7 us (19%)
  local copies, waits for them, and re-layouts  17 us (17%)
  other arithmetic  10.4 us (10%)
  Pallas kernels  4.07 us (4%)
    all_to_all x1, waiting for transfers between devices, per_device(): lax.all_to_all(served_read.reshape(owners, latents, model_width), 'smp',...  14.4 us
    all_to_all x1, waiting for transfers between devices, per_device(): lax.all_to_all(jnp.concatenate([jnp.broadcast_to(memory_pair[None], (owne...  12.5 us
    gather x1, local copies, waits for them, and re-layouts, per_device(): kv_rows = kv_table[served_index]  9.97 us
    all_to_all x1, starting transfers between devices, per_device(): lax.all_to_all(jnp.concatenate([jnp.broadcast_to(memory_pair[None], (owne...  7.39 us
    all_to_all x1, starting transfers between devices, per_device(): lax.all_to_all(jnp.einsum('ob,bld->old', (sample_pick[:, None] == jnp.ara...  7.19 us
    dot_general x1, matrix products, per_device(): jnp.dot(panel_normed, kv_weight, preferred_element_type=jnp.float32)  4.92 us
    dot_general x1, matrix products, attend_stacked(): jnp.einsum('blqje,btqe->bqjlt', masked, kv_rows, preferred_element_type=j...  4.48 us
    all_to_all x1, starting transfers between devices, per_device(): lax.all_to_all(served_read.reshape(owners, latents, model_width), 'smp',...  4.1 us
  transfers between devices with their start and end apart: 3, of which 3 were waited for; matrix products, arithmetic and copies ran while one was open for 22% of the time, Pallas kernels for 0%

profile of v22, /device:TPU:0, one launch (start us, length us, event | category | flops | bytes accessed | tf_op | source)
XLA Modules:
  0.0 100.6 jit_solution(5578030723534974122)
XLA Ops:
  0.0 0.0 copy-start
  0.0 1.0 select_reduce_fusion.5
  1.0 0.9 select_reduce_fusion.2
  1.9 0.1 copy.30
  2.0 0.9 add_select_fusion.2
  2.9 0.1 select_reduce_fusion.1
  3.0 0.1 fusion.39
  3.1 0.1 fusion.38
  3.2 0.8 pad_maximum_fusion.1
  4.0 0.1 broadcast_in_dim.134
  4.1 1.1 %pad_maximum_fusion = bf16[16,16,2176]{2,1,0:T(8,128)(2,1)} fusion(bf16[16,16,128]{2,1,0:T(8,128)(2,1)S(1)} %bitcast.75, bf16[16,16,2048]{2,1,0:T(8,128)(2,1)S(1)} %broadcast_in_dim.134), kind=kLoop, calls=%fused_computation.31 | loop fusion | flops 2228224 | bytes 2228224 | tf_op jit(solution)/shard_map/concatenate | solution.py:223
  5.2 7.4 %all-to-all-start = ((bf16[16,16,2176]{2,1,0:T(8,128)(2,1)}), bf16[16,16,2176]{2,1,0:T(8,128)(2,1)S(1)}, u32[]{:S(2)}, u32[]{:S(2)}) async-start(bf16[16,16,2176]{2,1,0:T(8,128)(2,1)} %pad_maximum_fusion), calls=%async_computation | async-start | bytes 2228224 | tf_op jit(solution)/shard_map/all_to_all | solution.py:222
  12.6 1.2 %multiply_reduce_fusion = f32[16,16]{1,0:T(8,128)S(1)} fusion(bf16[16,16,1024]{2,1,0:T(8,128)(2,1)} %param.14), kind=kLoop, calls=%fused_computation.41 | loop fusion | flops 786176 | bytes 525312 | tf_op jit(solution)/shard_map/reduce_sum | solution.py:18
  13.8 0.1 rsqrt.28
  13.9 1.5 %fusion.7 = f32[512]{0:T(512)S(1)} fusion(bf16[1,512,1024]{2,1,0:T(8,128)(2,1)} %param.20), kind=kLoop, calls=%fused_computation.10 | loop fusion | flops 1572352 | bytes 1050624 | tf_op jit(solution)/shard_map/reduce_sum | solution.py:18
  15.4 4.9 %fusion.13 = bf16[64,8,16,128]{3,1,2,0:T(8,128)(2,1)S(1)} fusion(bf16[1024,2048]{1,0:T(8,128)(2,1)} %param.25, bf16[1,512,1024]{2,1,0:T(8,128)(2,1)} %param.20, f32[512]{0:T(512)S(1)} %add_rsqrt_fusion.1), kind=kOutput, calls=%fused_computation.19 | convolution fusion | flops 2150105088 | bytes 7342080 | tf_op jit(solution)/shard_map/dot_general | solution.py:205
  20.4 0.0 copy-start.3
  20.4 0.0 copy-start.4
  20.4 2.0 %copy.47 = bf16[64,8,16,128]{3,2,1,0:T(8,128)(2,1)} copy(bf16[64,8,16,128]{3,1,2,0:T(8,128)(2,1)S(1)} %fusion.13) | data formatting | bytes 4194304
  22.4 0.0 copy-done.3
  22.4 0.2 fusion.25
  22.5 0.0 copy-done.4
  22.6 1.5 %fusion.17.query_ref = bf16[1,256,1024]{2,1,0:T(8,128)(2,1)} fusion(bf16[256,1024]{1,0:T(8,128)(2,1)S(1)} %fusion.25, bf16[1024,1024]{1,0:T(8,128)(2,1)S(1)} %copy-done.4), kind=kOutput, calls=%fused_computation.30 | convolution fusion | flops 537133056 | bytes 3145728 | tf_op jit(solution)/shard_map/dot_general | solution.py:212
  24.1 12.5 %all-to-all-done = bf16[16,16,2176]{2,1,0:T(8,128)(2,1)S(1)} async-done(((bf16[16,16,2176]{2,1,0:T(8,128)(2,1)}), bf16[16,16,2176]{2,1,0:T(8,128)(2,1)S(1)}, u32[]{:S(2)}, u32[]{:S(2)}) %all-to-all-start) | async-done | bytes 1114144 | tf_op jit(solution)/shard_map/all_to_all | solution.py:222
  36.6 0.0 copy-start.2
  36.6 1.0 copy-done.2
  37.6 4.1 %shard_map.136 = bf16[1,256,1024]{2,1,0:T(8,128)(2,1)} custom-call(s32[1]{0:T(128)} %constant.87.clone.1.counts_ref, bf16[1,256,1024]{2,1,0:T(8,128)(2,1)} %fusion.17.query_ref, bf16[1,256,2176]{2,1,0:T(8,128)(2,1)} %bitcast.70, bf16[1,256,2176]{2,1,0:T(8,128)(2,1)} %bitcast.71), custom_call_target="tpu_custom_call" | custom-call | tf_op jit(solution)/shard_map/pallas_call | solution.py:151
  41.7 0.0 copy-done
  41.7 0.0 copy-start.5
  41.7 2.2 %fusion.20 = (f32[256]{0:T(256)S(1)}, bf16[256,1024]{1,0:T(8,128)(2,1)S(1)}) fusion(bf16[1024,1024]{1,0:T(8,128)(2,1)S(1)} %copy-done, bf16[1,256,1024]{2,1,0:T(8,128)(2,1)} %shard_map.136, bf16[256,1024]{1,0:T(8,128)(2,1)} %bitcast.72), kind=kOutput, calls=%fused_computation.32 | convolution fusion | flops 538443520 | bytes 3671040 | tf_op jit(solution)/shard_map/dot_general | solution.py:250
  43.9 0.0 copy-start.6
  43.9 0.9 slice.36
  44.8 0.0 copy-done.5
  44.8 0.8 convolution_convert_fusion.2
  45.6 0.5 convolution_convert_fusion.1
  46.1 0.0 copy-done.6
  46.1 1.1 %copy.32 = bf16[16,16,1024]{2,1,0:T(8,128)(2,1)} copy(bf16[16,16,1024]{2,0,1:T(8,128)(2,1)S(1)} %convolution_convert_fusion.1) | data formatting | bytes 1048576 | tf_op jit(solution)/shard_map/convert_element_type | solution.py:264
  47.2 7.2 %all-to-all-start.1 = ((bf16[16,16,1024]{2,1,0:T(8,128)(2,1)}), bf16[16,16,1024]{2,1,0:T(8,128)(2,1)S(1)}, u32[]{:S(2)}, u32[]{:S(2)}) async-start(bf16[16,16,1024]{2,1,0:T(8,128)(2,1)} %copy.32), calls=%async_computation.1 | async-start | bytes 1048576 | tf_op jit(solution)/shard_map/all_to_all | solution.py:256
  54.4 0.1 slice_add_fusion
  54.5 0.1 reshape.250
  54.5 10.0 %gather_fusion = bf16[1024,16,128]{2,1,0:T(8,128)(2,1)} fusion(bf16[512,16,128]{2,1,0:T(8,128)(2,1)} %bitcast.67, s32[1024]{0:T(1024)S(1)} %broadcast_clamp_fusion), kind=kCustom, calls=%fused_computation | custom fusion | bytes 8392704 | tf_op jit(solution)/shard_map/gather | solution.py:270
  64.5 0.2 slice_reduce_fusion
  64.7 0.1 iota_compare_fusion.2
  64.8 4.1 %all-to-all-done.1 = bf16[16,16,1024]{2,1,0:T(8,128)(2,1)S(1)} async-done(((bf16[16,16,1024]{2,1,0:T(8,128)(2,1)}), bf16[16,16,1024]{2,1,0:T(8,128)(2,1)S(1)}, u32[]{:S(2)}, u32[]{:S(2)}) %all-to-all-start.1) | async-done | bytes 524320 | tf_op jit(solution)/shard_map/all_to_all | solution.py:256
  68.8 0.1 copy_bitcast_fusion.1
  68.9 0.1 broadcast_select_fusion
  69.0 4.5 %fusion.4 = f32[16,16,2,16,64]{4,3,2,1,0:T(8,128)S(1)} fusion(bf16[16,64,16,128,1]{3,2,1,0,4:T(8,128)(2,1)} %bitcast.68, bf16[16,16,8,2,128]{4,1,3,2,0:T(8,128)(2,1)S(1)} %broadcast_select_fusion), kind=kOutput, calls=%fused_computation.9 | convolution fusion | flops 134217728 | bytes 7340032 | tf_op jit(solution)/shard_map/blqje,btqe->bqjlt/dot_general | solution.py:99
  73.5 0.0 copy-start.1
  73.5 0.8 fusion.14
  74.3 1.4 %fusion.11 = f32[16,8,2,16]{3,2,1,0:T(2,128)S(1)} fusion(f32[16,16,2,16,64]{4,3,2,1,0:T(8,128)S(1)} %fusion.4, f32[16,8,2,16]{3,2,1,0:T(2,128)S(1)} %fusion.14, pred[16,64]{1,0:T(8,128)(4,1)S(1)} %iota_compare_fusion.2), kind=kLoop, calls=%fused_computation.17 | loop fusion | flops 1044480 | bytes 1082368 | tf_op jit(solution)/shard_map/reduce_sum | solution.py:105
  75.7 0.0 copy-done.1
  75.8 1.6 %select_reduce_fusion = bf16[16,8,16,128]{3,2,1,0:T(8,128)(2,1)S(1)} fusion(bf16[16,64,16,128,1]{3,2,1,0,4:T(8,128)(2,1)S(1)} %bitcast.69, f32[16,16,2,16,64]{4,3,2,1,0:T(8,128)S(1)} %fusion.4, f32[16,8,2,16]{3,2,1,0:T(2,128)S(1)} %fusion.11, f32[16,8,2,16]{3,2,1,0:T(2,128)S(1)} %fusion.14, pred[16,64]{1,0:T(8,128)(4,1)S(1)} %iota_compare_fusion.2, ...), kind=kOutput, calls=%fused_computation.14 | convolution fusion | flops 69468160 | bytes 7080448 | tf_op jit(solution)/shard_map/slice | solution.py:108
  77.4 0.9 copy_bitcast_fusion
  78.2 4.1 %all-to-all-start.2 = ((bf16[16,16,1024]{2,1,0:T(8,128)(2,1)}), bf16[16,16,1024]{2,1,0:T(8,128)(2,1)S(1)}, u32[]{:S(2)}, u32[]{:S(2)}) async-start(bf16[16,16,1024]{2,1,0:T(8,128)(2,1)} %copy_bitcast_fusion), calls=%async_computation.2 | async-start | bytes 1048576 | tf_op jit(solution)/shard_map/all_to_all | solution.py:277
  82.4 14.4 %all-to-all-done.2 = bf16[16,16,1024]{2,1,0:T(8,128)(2,1)S(1)} async-done(((bf16[16,16,1024]{2,1,0:T(8,128)(2,1)}), bf16[16,16,1024]{2,1,0:T(8,128)(2,1)S(1)}, u32[]{:S(2)}, u32[]{:S(2)}) %all-to-all-start.2) | async-done | bytes 524320 | tf_op jit(solution)/shard_map/all_to_all | solution.py:277
  96.8 0.6 gather_fusion.1
  97.4 3.2 %fusion.15 = bf16[256,1024]{1,0:T(8,128)(2,1)} fusion(bf16[256,1024]{1,0:T(8,128)(2,1)S(1)} %bitcast.74, bf16[1024,1024]{1,0:T(8,128)(2,1)} %param.27, bf16[256,1024]{1,0:T(8,128)(2,1)} %copy-done.6), kind=kOutput, calls=%fused_computation.25 | convolution fusion | flops 537657344 | bytes 3670016 | tf_op jit(solution)/shard_map/dot_general | solution.py:284
  (16 shorter events, 0.1 us)
Async XLA Ops:
  0.0 41.7 %copy-start = (bf16[1024,1024]{1,0:T(8,128)(2,1)S(1)}, bf16[1024,1024]{1,0:T(8,128)(2,1)}, u32[]{:S(2)}) copy-start(bf16[1024,1024]{1,0:T(8,128)(2,1)} %param.24) | copy-start | bytes 6291460
  5.2 31.4 %all-to-all-start = ((bf16[16,16,2176]{2,1,0:T(8,128)(2,1)}), bf16[16,16,2176]{2,1,0:T(8,128)(2,1)S(1)}, u32[]{:S(2)}, u32[]{:S(2)}) async-start(bf16[16,16,2176]{2,1,0:T(8,128)(2,1)} %pad_maximum_fusion), calls=%async_computation | async-start | bytes 2228224 | tf_op jit(solution)/shard_map/all_to_all | solution.py:222
  20.4 2.0 %copy-start.3 = (bf16[16,16,1024]{2,1,0:T(8,128)(2,1)S(1)}, bf16[16,16,1024]{2,1,0:T(8,128)(2,1)}, u32[]{:S(2)}) copy-start(bf16[16,16,1024]{2,1,0:T(8,128)(2,1)} %param.14) | copy-start | bytes 1572868
  20.4 2.2 %copy-start.4 = (bf16[1024,1024]{1,0:T(8,128)(2,1)S(1)}, bf16[1024,1024]{1,0:T(8,128)(2,1)}, u32[]{:S(2)}) copy-start(bf16[1024,1024]{1,0:T(8,128)(2,1)} %param.23) | copy-start | bytes 6291460
  36.6 1.0 copy-start.2
  41.7 3.2 %copy-start.5 = (bf16[1024,1024]{1,0:T(8,128)(2,1)S(1)}, bf16[1024,1024]{1,0:T(8,128)(2,1)}, u32[]{:S(2)}) copy-start(bf16[1024,1024]{1,0:T(8,128)(2,1)} %param.26) | copy-start | bytes 6291460
  43.9 2.2 %copy-start.6 = (bf16[256,1024]{1,0:T(8,128)(2,1)}, bf16[256,1024]{1,0:T(8,128)(2,1)S(1)}, u32[]{:S(2)}) copy-start(bf16[256,1024]{1,0:T(8,128)(2,1)S(1)} %get-tuple-element.11) | copy-start | bytes 1572868
  47.2 21.7 %all-to-all-start.1 = ((bf16[16,16,1024]{2,1,0:T(8,128)(2,1)}), bf16[16,16,1024]{2,1,0:T(8,128)(2,1)S(1)}, u32[]{:S(2)}, u32[]{:S(2)}) async-start(bf16[16,16,1024]{2,1,0:T(8,128)(2,1)} %copy.32), calls=%async_computation.1 | async-start | bytes 1048576 | tf_op jit(solution)/shard_map/all_to_all | solution.py:256
  73.5 2.2 %copy-start.1 = (bf16[1024,16,128]{2,1,0:T(8,128)(2,1)S(1)}, bf16[1024,16,128]{2,1,0:T(8,128)(2,1)}, u32[]{:S(2)}) copy-start(bf16[1024,16,128]{2,1,0:T(8,128)(2,1)} %gather_fusion) | copy-start | bytes 12582916
  78.2 18.6 %all-to-all-start.2 = ((bf16[16,16,1024]{2,1,0:T(8,128)(2,1)}), bf16[16,16,1024]{2,1,0:T(8,128)(2,1)S(1)}, u32[]{:S(2)}, u32[]{:S(2)}) async-start(bf16[16,16,1024]{2,1,0:T(8,128)(2,1)} %copy_bitcast_fusion), calls=%async_computation.2 | async-start | bytes 1048576 | tf_op jit(solution)/shard_map/all_to_all | solution.py:277
